TPU v7x, 32 devices: a whole 2x2x4 slice. The times are simulated.
32 devices in a mesh: grp: 8 (over y, x, core), ent: 4 (over z).
Axes of the slice: x: 2, y: 2, z: 4, core: 2. Of those that a mesh axis runs over, the one named last changes fastest.
Arguments:
- factor: bfloat16 [4096, 256], P(('grp', 'ent')), may hold values from -1.5 to 1.5
- cores: bfloat16 [16, 256, 256], replicated, may hold values from -0.375 to 0.375
- adjacency: int32 [768, 128, 128], P(('grp', 'ent')), may hold values 0 or 1
- tile_rels: int32 [32, 24], P(('grp', 'ent')), may hold values from 0 to 15
- tile_count: int32 [32], P(('grp', 'ent')), may hold values from 1 to 24, 480 in all
- send_lists: int32 [32, 4, 6], P(('grp', 'ent')), may hold values from 0 to 7
Outputs:
- factor_grad: float32 [4096, 256], P(('grp', 'ent'))
All inputs are finite; a program needn't handle non-finite values. No bound on the sum of `adjacency` or of `tile_count` on one device may be relied on, other than what follows from the above.
Results may differ from a plain program's by a relative error of at most 0.002.
Values may be sent and summed in bfloat16 or wider, within the bound.
No kernel may reach another device: no remote copies, remote signals or barrier semaphores. Data moves between devices by JAX's collectives and lax.ppermute only.
A program may use at most 64 MiB of HBM per device.

v0:
```python
import jax
import jax.numpy as jnp
from jax import lax
from jax.sharding import PartitionSpec as P

LOSS_SCALE = 0.0625


def on_device(factor, cores, adjacency, tile_rels, tile_count, send_lists):
    ent_count = lax.axis_size("ent")
    grp_count = lax.axis_size("grp")
    my_ent = lax.axis_index("ent")
    tiles = tile_rels.shape[1]
    block = factor.shape[0]
    width = factor.shape[1]
    per_relay = tiles // ent_count
    slots = ent_count * per_relay
    relations = tile_rels[0]
    routes = send_lists[0].reshape(slots)
    group_blocks = lax.all_gather(factor[None], "grp", axis=0, tiled=True)
    outgoing = group_blocks[routes].reshape(ent_count, per_relay, block, width)
    arrived = lax.all_to_all(outgoing, "ent", split_axis=0, concat_axis=0, tiled=True).reshape(
        slots, block, width
    )
    tile_ids = jnp.arange(tiles, dtype=jnp.int32)
    slot_of_tile = (my_ent + tile_ids) % ent_count * per_relay + tile_ids // ent_count
    factor_panels = arrived[slot_of_tile]
    live = (tile_ids < tile_count[0]).astype(jnp.float32)
    by_relation = jnp.einsum(
        "br,krs->kbs", factor, cores, preferred_element_type=jnp.float32
    ).astype(jnp.bfloat16)
    mapped_tiles = by_relation[relations]
    predicted_scores = jnp.einsum(
        "ogj,omj->ogm", mapped_tiles, factor_panels, preferred_element_type=jnp.float32
    )
    score_residual = (
        (predicted_scores - adjacency.astype(jnp.float32)) * (LOSS_SCALE * live)[:, None, None]
    ).astype(jnp.bfloat16)
    relation_product = jnp.einsum(
        "xmw,xwe->xme", score_residual, factor_panels, preferred_element_type=jnp.float32
    ).astype(jnp.bfloat16)
    row_grad = jnp.einsum(
        "tbs,trs->br", relation_product, cores[relations], preferred_element_type=jnp.float32
    )
    slot_ids = jnp.arange(slots, dtype=jnp.int32)
    tile_of_slot = slot_ids % per_relay * ent_count + (slot_ids // per_relay - my_ent) % ent_count
    column_terms = jnp.einsum(
        "yzj,yzh->yjh", score_residual, mapped_tiles, preferred_element_type=jnp.float32
    ).astype(jnp.bfloat16)
    sent_terms = column_terms[tile_of_slot].reshape(ent_count, per_relay, block, width)
    returned = (
        lax.all_to_all(sent_terms, "ent", split_axis=0, concat_axis=0, tiled=True)
        .reshape(slots, block * width)
        .astype(jnp.float32)
    )
    owner_onehot = (routes[:, None] == jnp.arange(grp_count, dtype=jnp.int32)[None, :]).astype(
        jnp.float32
    )
    owner_terms = jnp.dot(
        owner_onehot.T,
        returned,
        precision=lax.Precision.HIGHEST,
        preferred_element_type=jnp.float32,
    )
    owner_part = lax.psum_scatter(
        owner_terms.reshape(grp_count, block, width), "grp", scatter_dimension=0, tiled=True
    )
    return row_grad + owner_part[0]


def solution(mesh):
    in_specs = (
        P(("grp", "ent"), None),
        P(),
        P(("grp", "ent"), None, None),
        P(("grp", "ent"), None),
        P(("grp", "ent")),
        P(("grp", "ent"), None, None),
    )
    out_specs = P(("grp", "ent"), None)
    return jax.shard_map(
        on_device, mesh=mesh, in_specs=in_specs, out_specs=out_specs, check_vma=False
    )
```

profile of v0, /device:TPU:0, one launch (start us, length us, event | category | flops | bytes accessed | tf_op | source)
XLA Modules:
  0.0 166.0 jit_solution(857811333616795226)
XLA Ops:
  6.5 0.0 copy-start
  6.5 0.9 reshape_squeeze.3
  7.5 11.6 %all-gather = bf16[1024,256]{1,0:T(8,128)(2,1)S(1)} all-gather(bf16[128,256]{1,0:T(8,128)(2,1)} %param.6), channel_id=2, replica_groups=mesh['grp'=8,'ent'=4] {'grp'}, dimensions={0}, use_global_device_ids=true | all-gather | bytes 589824 | tf_op jit(solution)/shard_map/all_gather | solution.py:20
  19.1 1.9 %gather_fusion.1 = bf16[24,128,256]{2,1,0:T(8,128)(2,1)} fusion(bf16[8,128,256]{2,1,0:T(8,128)(2,1)S(1)} %bitcast.50, s32[1024]{0:T(1024)S(1)} %pad_clamp_fusion.2), kind=kCustom, calls=%fused_computation.1 | custom fusion | bytes 3145824 | tf_op jit(solution)/shard_map/gather | solution.py:21
  20.9 0.0 copy-start.4
  20.9 0.0 copy-start.2
  20.9 5.0 %all-to-all-start = ((bf16[4,6,128,256]{3,2,1,0:T(8,128)(2,1)}), bf16[4,6,128,256]{3,2,1,0:T(8,128)(2,1)}, u32[]{:S(2)}, u32[]{:S(2)}) async-start(bf16[4,6,128,256]{3,2,1,0:T(8,128)(2,1)} %bitcast.51), calls=%async_computation | async-start | bytes 3145728 | tf_op jit(solution)/shard_map/all_to_all | solution.py:22
  26.6 0.0 copy-done.4
  26.6 0.0 copy-done
  26.6 0.0 copy-done.2
  26.6 0.8 fusion.4
  27.4 1.9 %gather_fusion = bf16[24,128,256]{1,2,0:T(8,128)(2,1)} fusion(bf16[16,128,256]{1,2,0:T(8,128)(2,1)S(1)} %fusion.4, s32[1024]{0:T(1024)S(1)} %pad_clamp_fusion.3), kind=kCustom, calls=%fused_computation | custom fusion | bytes 3145824 | tf_op jit(solution)/shard_map/gather | solution.py:32
  29.4 34.1 %all-to-all-done = bf16[4,6,128,256]{3,2,1,0:T(8,128)(2,1)} async-done(((bf16[4,6,128,256]{3,2,1,0:T(8,128)(2,1)}), bf16[4,6,128,256]{3,2,1,0:T(8,128)(2,1)}, u32[]{:S(2)}, u32[]{:S(2)}) %all-to-all-start) | async-done | bytes 1572896 | tf_op jit(solution)/shard_map/all_to_all | solution.py:22
  63.5 3.3 %gather_fusion.2 = bf16[24,128,256]{2,1,0:T(8,128)(2,1)} fusion(bf16[24,128,256]{2,1,0:T(8,128)(2,1)} %bitcast.7, s32[1024]{0:T(1024)S(1)} %pad_clamp_fusion.1), kind=kCustom, calls=%fused_computation.2 | custom fusion | bytes 3145824 | tf_op jit(solution)/shard_map/gather | solution.py:27
  66.8 0.0 copy-start.1
  66.8 3.2 %multiply_convert_fusion = bf16[24,128,128]{2,1,0:T(8,128)(2,1)S(1)} fusion(s32[24,128,128]{2,1,0:T(8,128)} %param.8, bf16[24,128,256]{1,2,0:T(8,128)(2,1)} %gather_fusion, bf16[24,128,256]{2,1,0:T(8,128)(2,1)} %gather_fusion.2, f32[24]{0:T(128)S(1)} %compare_select_fusion.8), kind=kOutput, calls=%fused_computation.10 | convolution fusion | flops 202899456 | bytes 5505120 | tf_op jit(solution)/shard_map/ogj,omj->ogm/dot_general | solution.py:33
  69.9 0.0 copy-done.1
  70.0 1.8 %convolution_convert_fusion = bf16[24,128,256]{2,1,0:T(8,128)(2,1)} fusion(bf16[24,128,128]{2,1,0:T(8,128)(2,1)S(1)} %multiply_convert_fusion, bf16[24,128,256]{1,2,0:T(8,128)(2,1)S(1)} %copy-done.1), kind=kOutput, calls=%fused_computation.5 | convolution fusion | flops 202113024 | bytes 3932160 | tf_op jit(solution)/shard_map/yzj,yzh->yjh/dot_general | solution.py:47
  71.7 3.2 %gather_fusion.4 = bf16[24,128,256]{2,1,0:T(8,128)(2,1)} fusion(bf16[24,128,256]{2,1,0:T(8,128)(2,1)} %convolution_convert_fusion, s32[1024]{0:T(1024)S(1)} %pad_clamp_fusion), kind=kCustom, calls=%fused_computation.4 | custom fusion | bytes 3145824 | tf_op jit(solution)/shard_map/gather | solution.py:50
  75.0 0.0 copy-start.3
  75.0 4.5 %all-to-all-start.1 = ((bf16[4,6,128,256]{3,2,1,0:T(8,128)(2,1)}), bf16[4,6,128,256]{3,2,1,0:T(8,128)(2,1)}, u32[]{:S(2)}, u32[]{:S(2)}) async-start(bf16[4,6,128,256]{3,2,1,0:T(8,128)(2,1)} %bitcast.52), calls=%async_computation.1 | async-start | bytes 3145728 | tf_op jit(solution)/shard_map/all_to_all | solution.py:52
  79.5 0.0 reduce-scatter.2.cloned.1.call-start
  79.5 0.0 copy-done.3
  79.5 0.1 eq.19
  79.6 36.6 %all-to-all-done.1 = bf16[4,6,128,256]{3,2,1,0:T(8,128)(2,1)} async-done(((bf16[4,6,128,256]{3,2,1,0:T(8,128)(2,1)}), bf16[4,6,128,256]{3,2,1,0:T(8,128)(2,1)}, u32[]{:S(2)}, u32[]{:S(2)}) %all-to-all-start.1) | async-done | bytes 1572896 | tf_op jit(solution)/shard_map/all_to_all | solution.py:52
  116.2 2.6 %fusion = f32[8,128,256]{2,0,1:T(8,128)S(1)} fusion(s32[24]{0:T(128)S(1)} %eq.19, bf16[3,8,128,256]{3,2,1,0:T(8,128)(2,1)} %bitcast.19), kind=kOutput, calls=%fused_computation.7 | convolution fusion | flops 12583104 | bytes 2621536 | tf_op jit(solution)/shard_map/dot_general | solution.py:59
  118.8 1.3 copy.17
  120.2 0.0 reduce-scatter.2.cloned.1.call-update
  120.2 2.5 %gather_fusion.3 = bf16[24,256,256]{2,1,0:T(8,128)(2,1)} fusion(bf16[16,256,256]{2,1,0:T(8,128)(2,1)S(1)} %copy-done, s32[1024]{0:T(1024)S(1)} %pad_clamp_fusion.3), kind=kCustom, calls=%fused_computation.3 | custom fusion | bytes 6291552 | tf_op jit(solution)/shard_map/gather | solution.py:43
  122.7 31.8 %reduce-scatter.2.cloned.1.call-done = f32[1,128,256]{2,1,0:T(8,128)} async-done(((f32[8,128,256]{2,1,0:T(8,128)}), f32[1,128,256]{2,1,0:T(8,128)}) %reduce-scatter.2.cloned.1.call-update) | async-done | bytes 131088 | tf_op jit(solution)/shard_map/reduce_scatter | solution.py:65
  154.5 4.6 %fusion.6 = f32[128,256]{1,0:T(8,128)} fusion(bf16[24,256,256]{2,1,0:T(8,128)(2,1)} %gather_fusion.3, bf16[24,128,128]{2,1,0:T(8,128)(2,1)S(1)} %multiply_convert_fusion, bf16[24,128,256]{2,1,0:T(8,128)(2,1)} %gather_fusion.2, f32[1,128,256]{2,1,0:T(8,128)} %reduce-scatter.2.cloned.1.call-done), kind=kOutput, calls=%fused_computation.15 | convolution fusion | flops 604798976 | bytes 5767168 | tf_op jit(solution)/shard_map/tbs,trs->br/dot_general | solution.py:42
  (9 shorter events, 0.1 us)
Async XLA Ops:
  6.5 20.1 %copy-start = (bf16[16,256,256]{2,1,0:T(8,128)(2,1)S(1)}, bf16[16,256,256]{2,1,0:T(8,128)(2,1)}, u32[]{:S(2)}) copy-start(bf16[16,256,256]{2,1,0:T(8,128)(2,1)} %param.7) | copy-start | bytes 6291460
  20.9 5.7 %copy-start.4 = (s32[1,24]{1,0:T(1,128)S(1)}, s32[1,24]{1,0:T(1,128)}, u32[]{:S(2)}) copy-start(s32[1,24]{1,0:T(1,128)} %param.9) | copy-start | bytes 292
  20.9 5.7 %copy-start.2 = (bf16[128,256]{1,0:T(8,128)(2,1)S(1)}, bf16[128,256]{1,0:T(8,128)(2,1)}, u32[]{:S(2)}) copy-start(bf16[128,256]{1,0:T(8,128)(2,1)} %param.6) | copy-start | bytes 196612
  20.9 42.6 %all-to-all-start = ((bf16[4,6,128,256]{3,2,1,0:T(8,128)(2,1)}), bf16[4,6,128,256]{3,2,1,0:T(8,128)(2,1)}, u32[]{:S(2)}, u32[]{:S(2)}) async-start(bf16[4,6,128,256]{3,2,1,0:T(8,128)(2,1)} %bitcast.51), calls=%async_computation | async-start | bytes 3145728 | tf_op jit(solution)/shard_map/all_to_all | solution.py:22
  66.8 3.2 %copy-start.1 = (bf16[24,128,256]{1,2,0:T(8,128)(2,1)S(1)}, bf16[24,128,256]{1,2,0:T(8,128)(2,1)}, u32[]{:S(2)}) copy-start(bf16[24,128,256]{1,2,0:T(8,128)(2,1)} %gather_fusion) | copy-start | bytes 4718596
  75.0 4.5 %copy-start.3 = (s32[1,4,6]{2,1,0:T(4,128)S(1)}, s32[1,4,6]{2,1,0:T(4,128)}, u32[]{:S(2)}) copy-start(s32[1,4,6]{2,1,0:T(4,128)} %param.11) | copy-start | bytes 292
  75.0 41.2 %all-to-all-start.1 = ((bf16[4,6,128,256]{3,2,1,0:T(8,128)(2,1)}), bf16[4,6,128,256]{3,2,1,0:T(8,128)(2,1)}, u32[]{:S(2)}, u32[]{:S(2)}) async-start(bf16[4,6,128,256]{3,2,1,0:T(8,128)(2,1)} %bitcast.52), calls=%async_computation.1 | async-start | bytes 3145728 | tf_op jit(solution)/shard_map/all_to_all | solution.py:52
  79.5 75.0 %reduce-scatter.2.cloned.1.call-start = ((), (), s32[]{:S(2)}) async-start(), calls=%async_computation.3 | async-start | bytes 1179648 | tf_op jit(solution)/shard_map/reduce_scatter | solution.py:65
Sparse Core Ops, SparseCore 0:
  120.3 34.1 reduce-scatter.1
where the time goes:
time: 166 us
  waiting for transfers between devices  103 us (62%)
  local copies, waits for them, and re-layouts  15.2 us (9%)
  between operations  14.2 us (9%)
  matrix products  12.9 us (8%)
  blocking collectives  11.6 us (7%)
  starting transfers between devices  9.52 us (6%)
    all_to_all x1, waiting for transfers between devices, on_device(): lax.all_to_all(sent_terms, 'ent', split_axis=0, concat_axis=0, tiled=True)  36.6 us
    all_to_all x1, waiting for transfers between devices, on_device(): lax.all_to_all(outgoing, 'ent', split_axis=0, concat_axis=0, tiled=True)  34.1 us
    reduce_scatter x1, waiting for transfers between devices, on_device(): lax.psum_scatter(owner_terms.reshape(grp_count, block, width), 'grp', sca...  31.8 us
    all_gather x1, blocking collectives, on_device(): group_blocks = lax.all_gather(factor[None], 'grp', axis=0, tiled=True)  11.6 us
    all_to_all x1, starting transfers between devices, on_device(): lax.all_to_all(outgoing, 'ent', split_axis=0, concat_axis=0, tiled=True)  5 us
    dot_general x1, matrix products, on_device(): jnp.einsum('tbs,trs->br', relation_product, cores[relations], preferred_e...  4.58 us
    all_to_all x1, starting transfers between devices, on_device(): lax.all_to_all(sent_terms, 'ent', split_axis=0, concat_axis=0, tiled=True)  4.48 us
  transfers between devices with their start and end apart: 3, of which 3 were waited for; matrix products, arithmetic and copies ran while one was open for 3% of the time, Pallas kernels for 0%

commit v1 on v0

v1 whole, which is shorter than its diff:
```python
import jax
import jax.numpy as jnp
from jax import lax
from jax.sharding import PartitionSpec as P

LOSS_SCALE = 0.0625


def grp_reduce_scatter(parts, grp_count):
    if grp_count & (grp_count - 1):
        return lax.psum_scatter(parts, "grp", scatter_dimension=0, tiled=True)[0]
    me = lax.axis_index("grp")
    bit = 1
    while bit < grp_count:
        half = parts.reshape((parts.shape[0] // 2, 2) + parts.shape[1:])
        mine = (me // bit) % 2
        keep = jnp.where(mine == 0, half[:, 0], half[:, 1])
        send = jnp.where(mine == 0, half[:, 1], half[:, 0])
        got = lax.ppermute(send, "grp", [(i, i ^ bit) for i in range(grp_count)])
        parts = keep + got
        bit *= 2
    return parts[0]


def on_device(factor, cores, adjacency, tile_rels, tile_count, send_lists):
    ent_count = lax.axis_size("ent")
    grp_count = lax.axis_size("grp")
    my_ent = lax.axis_index("ent")
    tiles = tile_rels.shape[1]
    block = factor.shape[0]
    width = factor.shape[1]
    per_relay = tiles // ent_count
    lanes = block
    head_rows = 16

    tile_ids = jnp.arange(tiles, dtype=jnp.int32)
    live = (tile_ids < tile_count[0]).astype(jnp.float32)
    relay_ids = jnp.arange(ent_count, dtype=jnp.int32)
    slot_ids = jnp.arange(per_relay, dtype=jnp.int32)
    tile_of = slot_ids[None, :] * ent_count + (relay_ids[:, None] - my_ent) % ent_count
    adj_out = adjacency.astype(jnp.bfloat16)[tile_of].reshape(ent_count, per_relay * block, lanes)
    own_out = jnp.broadcast_to(
        factor.reshape(1, block * width // lanes, lanes), (ent_count, block * width // lanes, lanes)
    )
    head = jnp.concatenate(
        [tile_rels[0][tile_of].astype(jnp.float32), live[tile_of]], axis=1
    )
    head = jnp.pad(head, ((0, 0), (0, lanes - 2 * per_relay)))
    head = jnp.broadcast_to(head[:, None, :], (ent_count, head_rows, lanes)).astype(jnp.bfloat16)
    outgoing = jnp.concatenate([adj_out, own_out, head], axis=1)
    arrived = lax.all_to_all(outgoing, "ent", split_axis=0, concat_axis=0, tiled=True)

    adj_in = arrived[:, : per_relay * block].reshape(ent_count * per_relay, block, block)
    src_f = arrived[:, per_relay * block : per_relay * block + block * width // lanes].reshape(
        ent_count, block, width
    )
    head_in = arrived[:, -head_rows].astype(jnp.float32)
    rels = head_in[:, :per_relay].astype(jnp.int32).reshape(ent_count * per_relay)
    alive = head_in[:, per_relay : 2 * per_relay].reshape(ent_count * per_relay)
    groups = send_lists[0].reshape(ent_count * per_relay)

    group_blocks = lax.all_gather(factor, "grp", axis=0, tiled=False)
    panels = group_blocks[groups]
    core_tiles = cores[rels]
    src_tiles = jnp.repeat(src_f, per_relay, axis=0)
    mapped = jnp.einsum(
        "tbr,trs->tbs", src_tiles, core_tiles, preferred_element_type=jnp.float32
    ).astype(jnp.bfloat16)
    predicted = jnp.einsum("tgj,tmj->tgm", mapped, panels, preferred_element_type=jnp.float32)
    resid = (
        (predicted - adj_in.astype(jnp.float32)) * (LOSS_SCALE * alive)[:, None, None]
    ).astype(jnp.bfloat16)
    product = jnp.einsum(
        "tmw,twe->tme", resid, panels, preferred_element_type=jnp.float32
    ).astype(jnp.bfloat16)
    row_parts = jnp.einsum(
        "ejbs,ejrs->ebr",
        product.reshape(ent_count, per_relay, block, width),
        core_tiles.reshape(ent_count, per_relay, width, width),
        preferred_element_type=jnp.float32,
    )
    column_terms = jnp.einsum(
        "tzj,tzh->tjh", resid, mapped, preferred_element_type=jnp.float32
    ).astype(jnp.bfloat16)
    owner_onehot = (groups[:, None] == jnp.arange(grp_count, dtype=jnp.int32)[None, :]).astype(
        jnp.float32
    )
    owner_terms = jnp.dot(
        owner_onehot.T,
        column_terms.reshape(ent_count * per_relay, block * width).astype(jnp.float32),
        precision=lax.Precision.HIGHEST,
        preferred_element_type=jnp.float32,
    ).reshape(grp_count, block, width)

    rows_back = lax.all_to_all(row_parts, "ent", split_axis=0, concat_axis=0, tiled=True)
    owner_part = grp_reduce_scatter(owner_terms, grp_count)
    return rows_back.sum(axis=0) + owner_part


def solution(mesh):
    in_specs = (
        P(("grp", "ent"), None),
        P(),
        P(("grp", "ent"), None, None),
        P(("grp", "ent"), None),
        P(("grp", "ent")),
        P(("grp", "ent"), None, None),
    )
    out_specs = P(("grp", "ent"), None)
    return jax.shard_map(
        on_device, mesh=mesh, in_specs=in_specs, out_specs=out_specs, check_vma=False
    )
```

time: 166 us -> 86.1 us (0.52)
  waiting for transfers between devices: 103 us -> 26.7 us
  between operations: 14.2 us -> 1.03 us
  other arithmetic: 0.08 us -> 9.27 us
  starting transfers between devices: 9.52 us -> 13.1 us
  local copies, waits for them, and re-layouts: 15.2 us -> 13.2 us
  blocking collectives: 11.6 us -> 9.87 us
    reduce_scatter x1 -> x0, waiting for transfers between devices: 31.8 us -> none  [on_device(): lax.psum_scatter(owner_terms.reshape(grp_count, block, width), 'grp', sca...]
    all_to_all x1, waiting for transfers between devices: 36.6 us -> 12.5 us  [on_device(): lax.all_to_all(row_parts, 'ent', split_axis=0, concat_axis=0, tiled=True)]
    all_to_all x1, waiting for transfers between devices: 34.1 us -> 14.3 us  [on_device(): lax.all_to_all(outgoing, 'ent', split_axis=0, concat_axis=0, tiled=True)]
    gather x5, local copies, waits for them, and re-layouts: 12.8 us -> 7.58 us  [the longest x1 2.49 us: on_device(): core_tiles = cores[rels]]
    convert_element_type x0 -> x3, other arithmetic: none -> 3.18 us  [the longest x1 2.48 us: on_device(): adjacency.astype(jnp.bfloat16)[tile_of]]
    ppermute x0 -> x3, starting transfers between devices: none -> 3.13 us  [grp_reduce_scatter(): got = lax.ppermute(send, 'grp', [(i, i ^ bit) for i in range(grp_count)])]
    add x0 -> x2, other arithmetic: none -> 2.71 us  [the longest x1 2.02 us: grp_reduce_scatter(): parts = keep + got]
    slice x0 -> x3, local copies, waits for them, and re-layouts: none -> 2.68 us  [the longest x1 1.31 us: on_device(): arrived[:, :per_relay * block].reshape(ent_count * per_relay, block, block)]
  transfers between devices with their start and end apart: 3 -> 5, of which waited for: 3 -> 2; matrix products, arithmetic and copies ran while one was open for 3% -> 12% of each run, Pallas kernels for 0% -> 0%
where the time goes in v1:
time: 86.1 us; the launch traced here: 85.4 us
  waiting for transfers between devices  26.7 us (31%)
  local copies, waits for them, and re-layouts  13.2 us (15%)
  starting transfers between devices  13.1 us (15%)
  matrix products  12.2 us (14%)
  blocking collectives  9.87 us (11%)
  other arithmetic  9.27 us (11%)
  between operations  1.03 us (1%)
    all_to_all x1, waiting for transfers between devices, on_device(): lax.all_to_all(outgoing, 'ent', split_axis=0, concat_axis=0, tiled=True)  14.3 us
    all_to_all x1, waiting for transfers between devices, on_device(): lax.all_to_all(row_parts, 'ent', split_axis=0, concat_axis=0, tiled=True)  12.5 us
    all_gather x1, blocking collectives, on_device(): group_blocks = lax.all_gather(factor, 'grp', axis=0, tiled=False)  9.87 us
    all_to_all x1, starting transfers between devices, on_device(): lax.all_to_all(outgoing, 'ent', split_axis=0, concat_axis=0, tiled=True)  6.45 us
    dot_general x1, matrix products, on_device(): jnp.einsum('ejbs,ejrs->ebr', product.reshape(ent_count, per_relay, block,...  3.84 us
    all_to_all x1, starting transfers between devices, on_device(): lax.all_to_all(row_parts, 'ent', split_axis=0, concat_axis=0, tiled=True)  3.47 us
    dot_general x1, matrix products, on_device(): jnp.einsum('tmw,twe->tme', resid, panels, preferred_element_type=jnp.floa...  3.39 us
    ppermute x3, starting transfers between devices, grp_reduce_scatter(): got = lax.ppermute(send, 'grp', [(i, i ^ bit) for i in range(grp_count)])  3.13 us
  transfers between devices with their start and end apart: 5, of which 2 were waited for; matrix products, arithmetic and copies ran while one was open for 12% of the time, Pallas kernels for 0%

profile of v1, /device:TPU:0, one launch (start us, length us, event | category | flops | bytes accessed | tf_op | source)
XLA Modules:
  0.0 85.4 jit_solution(14765218693752632312)
XLA Ops:
  0.0 0.0 copy-start
  0.0 0.0 copy-start.1
  0.9 0.1 compare_select_fusion
  0.9 0.1 reshape.263
  1.0 0.0 copy-start.5
  1.0 0.7 gather_fusion.2
  1.7 0.1 reshape.307
  1.8 0.0 copy-done.1
  1.8 0.7 gather_fusion.1
  2.5 0.1 reshape.308
  2.6 0.0 copy-done.5
  2.7 2.5 %convert_element_type.42 = bf16[24,128,128]{2,1,0:T(8,128)(2,1)} convert(s32[24,128,128]{2,1,0:T(8,128)} %param.8) | non-fusion elementwise | flops 393216 | bytes 2359296 | tf_op jit(solution)/shard_map/convert_element_type | solution.py:41
  5.1 1.8 %gather_fusion = bf16[24,128,128]{2,1,0:T(8,128)(2,1)S(1)} fusion(bf16[24,128,128]{2,1,0:T(8,128)(2,1)} %convert_element_type.42, s32[1024]{0:T(1024)S(1)} %pad_clamp_fusion.2), kind=kCustom, calls=%fused_computation | custom fusion | bytes 1572960 | tf_op jit(solution)/shard_map/gather | solution.py:41
  7.0 0.1 fusion.11
  7.1 1.1 %pad_maximum_fusion = bf16[4,1040,128]{2,1,0:T(8,128)(2,1)} fusion(bf16[4,16,128]{2,1,0:T(8,128)(2,1)S(1)} %broadcast_in_dim.10, bf16[4,256,128]{2,1,0:T(8,128)(2,1)S(1)} %broadcast_in_dim.9, bf16[4,768,128]{2,1,0:T(8,128)(2,1)S(1)} %bitcast.78), kind=kLoop, calls=%fused_computation.15 | loop fusion | flops 3194880 | bytes 2129920 | tf_op jit(solution)/shard_map/concatenate | solution.py:50
  8.2 0.0 copy-start.6
  8.2 6.4 %all-to-all-start = ((bf16[4,1040,128]{2,1,0:T(8,128)(2,1)}), bf16[4,1040,128]{2,1,0:T(8,128)(2,1)}, u32[]{:S(2)}, u32[]{:S(2)}) async-start(bf16[4,1040,128]{2,1,0:T(8,128)(2,1)} %pad_maximum_fusion), calls=%async_computation | async-start | bytes 2129920 | tf_op jit(solution)/shard_map/all_to_all | solution.py:51
  14.6 0.0 copy-done.6
  14.6 0.1 reshape_squeeze.3
  14.7 0.1 eq.52
  14.8 9.9 %all-gather = bf16[1024,256]{1,0:T(8,128)(2,1)S(1)} all-gather(bf16[128,256]{1,0:T(8,128)(2,1)S(1)} %copy-done.5), channel_id=2, replica_groups=mesh['grp'=8,'ent'=4] {'grp'}, dimensions={0}, use_global_device_ids=true | all-gather | bytes 589824 | tf_op jit(solution)/shard_map/all_gather | solution.py:62
  24.7 1.9 %gather_fusion.4 = bf16[24,128,256]{2,1,0:T(8,128)(2,1)} fusion(bf16[8,128,256]{2,1,0:T(8,128)(2,1)S(1)} %bitcast.73, s32[1024]{0:T(1024)S(1)} %pad_clamp_fusion), kind=kCustom, calls=%fused_computation.4 | custom fusion | bytes 3145824 | tf_op jit(solution)/shard_map/gather | solution.py:63
  26.5 14.3 %all-to-all-done = bf16[4,1040,128]{2,1,0:T(8,128)(2,1)} async-done(((bf16[4,1040,128]{2,1,0:T(8,128)(2,1)}), bf16[4,1040,128]{2,1,0:T(8,128)(2,1)}, u32[]{:S(2)}, u32[]{:S(2)}) %all-to-all-start) | async-done | bytes 1064992 | tf_op jit(solution)/shard_map/all_to_all | solution.py:51
  40.8 1.0 %slice.60 = bf16[4,256,128]{2,1,0:T(8,128)(2,1)S(1)} slice(bf16[4,1040,128]{2,1,0:T(8,128)(2,1)} %all-to-all-done), slice={[0:4], [768:1024], [0:128]} | slice | bytes 524288 | tf_op jit(solution)/shard_map/slice | solution.py:54
  41.8 0.1 reshape.251
  41.9 0.7 slice_convert_fusion
  42.6 0.1 slice_multiply_fusion
  42.6 0.1 reshape.253
  42.7 0.1 mul.28
  42.8 0.0 copy-done
  42.8 2.5 %gather_fusion.3 = bf16[24,256,256]{2,1,0:T(8,128)(2,1)} fusion(bf16[16,256,256]{2,1,0:T(8,128)(2,1)S(1)} %copy-done, s32[1024]{0:T(1024)S(1)} %pad_clamp_fusion.1), kind=kCustom, calls=%fused_computation.3 | custom fusion | bytes 6291552 | tf_op jit(solution)/shard_map/gather | solution.py:64
  45.3 0.2 broadcast_in_dim.11
  45.5 2.5 %convolution_convert_fusion.2 = bf16[24,128,256]{2,1,0:T(8,128)(2,1)S(1)} fusion(bf16[24,128,256]{2,1,0:T(8,128)(2,1)S(1)} %bitcast.74, bf16[24,256,256]{2,1,0:T(8,128)(2,1)} %gather_fusion.3), kind=kOutput, calls=%fused_computation.7 | convolution fusion | flops 403439616 | bytes 6291456 | tf_op jit(solution)/shard_map/tbr,trs->tbs/dot_general | solution.py:66
  48.0 0.0 copy-start.2
  48.0 1.3 %slice.62 = bf16[4,768,128]{2,1,0:T(8,128)(2,1)S(1)} slice(bf16[4,1040,128]{2,1,0:T(8,128)(2,1)} %all-to-all-done), slice={[0:4], [0:768], [0:128]} | slice | bytes 1572864 | tf_op jit(solution)/shard_map/slice | solution.py:53
  49.3 0.3 copy-done.2
  49.6 0.6 fusion.3
  50.2 0.0 copy-start.3
  50.2 0.6 convolution_convert_fusion
  50.8 0.3 copy-done.3
  51.1 1.3 %fusion = f32[4,2,128,256]{3,0,2,1:T(4,128)S(1)} fusion(s32[4,2]{0,1:T(2,128)S(1)} %multiply_add_fusion, s32[24]{0:T(128)S(1)} %eq.52, bf16[3,8,128,256]{3,2,1,0:T(8,128)(2,1)S(1)} %bitcast.76), kind=kOutput, calls=%fused_computation.9 | convolution fusion | flops 12583104 | bytes 2621568 | tf_op jit(solution)/shard_map/dot_general | solution.py:88
  52.4 0.9 %select_bitcast_fusion = f32[4,128,256]{2,0,1:T(4,128)} fusion(f32[4,2,128,256]{3,0,2,1:T(4,128)S(1)} %fusion, pred[]{:T(512)S(6)} %eq.51), kind=kLoop, calls=%fused_computation.17 | loop fusion | flops 131072 | bytes 1572865 | tf_op jit(solution)/shard_map/jit(_where)/select_n | solution.py:18
  53.3 0.0 collective-permute-start
  53.3 3.4 %convolution_convert_fusion.1 = bf16[24,128,256]{2,1,0:T(8,128)(2,1)} fusion(bf16[24,128,128]{2,1,0:T(8,128)(2,1)} %copy-done.3, bf16[24,128,256]{2,1,0:T(8,128)(2,1)} %gather_fusion.4), kind=kOutput, calls=%fused_computation.6 | convolution fusion | flops 202113024 | bytes 3932160 | tf_op jit(solution)/shard_map/tmw,twe->tme/dot_general | solution.py:73
  56.7 0.0 collective-permute-done
  56.7 2.0 %bitcast_add_fusion = f32[4,128,256]{2,0,1:T(4,128)} fusion(f32[4,128,256]{2,0,1:T(4,128)} %collective-permute-done, f32[4,2,128,256]{3,0,2,1:T(4,128)S(1)} %fusion, pred[]{:T(512)S(6)} %eq.51), kind=kLoop, calls=%fused_computation.16 | loop fusion | flops 262144 | bytes 2097153 | tf_op jit(solution)/shard_map/add | solution.py:20
  58.7 1.4 %reshape.257 = f32[2,2,128,256]{3,1,0,2:T(2,128)S(1)} reshape(f32[4,128,256]{2,0,1:T(4,128)} %bitcast_add_fusion) | data formatting | bytes 1048576 | tf_op jit(solution)/shard_map/reshape | solution.py:15
  60.2 0.0 copy-start.4
  60.2 0.4 fusion.15
  60.6 1.6 %collective-permute-start.1 = (f32[2,128,256]{2,1,0:T(8,128)S(1)}, f32[2,128,256]{2,1,0:T(8,128)}, u32[]{:S(2)}, u32[]{:S(2)}) collective-permute-start(f32[2,128,256]{2,1,0:T(8,128)S(1)} %select_bitcast_fusion.1), channel_id=1, source_target_pairs={{0,8},{4,12},{8,0},{12,4},{16,24},{20,28},{24,16},{28,20},{1,9},{5... | collective-permute-start | bytes 786440 | tf_op jit(solution)/shard_map/ppermute | solution.py:19
  62.2 0.0 copy-done.4
  62.2 3.8 %convolution_bitcast_fusion = f32[4,128,256]{2,1,0:T(8,128)} fusion(bf16[4,6,128,256]{3,2,1,0:T(8,128)(2,1)S(1)} %bitcast.75, bf16[4,6,256,256]{3,2,1,0:T(8,128)(2,1)} %bitcast.72), kind=kOutput, calls=%fused_computation.14 | convolution fusion | flops 402653184 | bytes 5242880 | tf_op jit(solution)/shard_map/ejbs,ejrs->ebr/dot_general | solution.py:76
  66.0 3.5 %all-to-all-start.1 = ((f32[4,128,256]{2,1,0:T(8,128)}), f32[4,128,256]{2,1,0:T(8,128)S(1)}, u32[]{:S(2)}, u32[]{:S(2)}) async-start(f32[4,128,256]{2,1,0:T(8,128)} %convolution_bitcast_fusion), calls=%async_computation.1 | async-start | bytes 1048576 | tf_op jit(solution)/shard_map/all_to_all | solution.py:95
  69.5 0.0 collective-permute-done.1
  69.6 1.0 %fusion.4 = f32[1,2,128,256]{3,2,1,0:T(8,128)S(1)} fusion(f32[2,128,256]{2,1,0:T(8,128)} %collective-permute-done.1, f32[2,1,128,256]{3,1,0,2:T(1,128)S(1)} %get-tuple-element.6, f32[2,1,128,256]{3,1,0,2:T(1,128)S(1)} %get-tuple-element.5, pred[]{:T(512)S(6)} %eq.50), kind=kLoop, calls=%fused_computation.19 | loop fusion | flops 131072 | bytes 1048577 | tf_op jit(solution)/shard_map/reshape | solution.py:15
  70.6 1.6 %collective-permute-start.2 = (f32[1,128,256]{2,1,0:T(8,128)S(1)}, f32[1,128,256]{2,1,0:T(8,128)S(1)}, u32[]{:S(2)}, u32[]{:S(2)}) collective-permute-start(f32[1,128,256]{2,1,0:T(8,128)S(1)} %select_bitcast_fusion.2), channel_id=1, source_target_pairs={{0,16},{4,20},{8,24},{12,28},{16,0},{20,4},{24,8},{28,12},{1,17},{... | collective-permute-start | bytes 393224 | tf_op jit(solution)/shard_map/ppermute | solution.py:19
  72.2 12.5 %all-to-all-done.1 = f32[4,128,256]{2,1,0:T(8,128)S(1)} async-done(((f32[4,128,256]{2,1,0:T(8,128)}), f32[4,128,256]{2,1,0:T(8,128)S(1)}, u32[]{:S(2)}, u32[]{:S(2)}) %all-to-all-start.1) | async-done | bytes 524320 | tf_op jit(solution)/shard_map/all_to_all | solution.py:95
  84.7 0.0 collective-permute-done.2
  84.7 0.7 bitcast_add_fusion.2
  (16 shorter events, 0.2 us)
Async XLA Ops:
  0.0 42.8 %copy-start = (bf16[16,256,256]{2,1,0:T(8,128)(2,1)S(1)}, bf16[16,256,256]{2,1,0:T(8,128)(2,1)}, u32[]{:S(2)}) copy-start(bf16[16,256,256]{2,1,0:T(8,128)(2,1)} %param.7) | copy-start | bytes 6291460
  0.0 1.8 %copy-start.1 = (s32[1,24]{1,0:T(1,128)S(1)}, s32[1,24]{1,0:T(1,128)}, u32[]{:S(2)}) copy-start(s32[1,24]{1,0:T(1,128)} %param.9) | copy-start | bytes 292
  1.0 1.6 %copy-start.5 = (bf16[128,256]{1,0:T(8,128)(2,1)S(1)}, bf16[128,256]{1,0:T(8,128)(2,1)}, u32[]{:S(2)}) copy-start(bf16[128,256]{1,0:T(8,128)(2,1)} %param.6) | copy-start | bytes 196612
  8.2 6.5 %copy-start.6 = (s32[1,4,6]{2,1,0:T(4,128)S(1)}, s32[1,4,6]{2,1,0:T(4,128)}, u32[]{:S(2)}) copy-start(s32[1,4,6]{2,1,0:T(4,128)} %param.11) | copy-start | bytes 292
  8.2 32.6 %all-to-all-start = ((bf16[4,1040,128]{2,1,0:T(8,128)(2,1)}), bf16[4,1040,128]{2,1,0:T(8,128)(2,1)}, u32[]{:S(2)}, u32[]{:S(2)}) async-start(bf16[4,1040,128]{2,1,0:T(8,128)(2,1)} %pad_maximum_fusion), calls=%async_computation | async-start | bytes 2129920 | tf_op jit(solution)/shard_map/all_to_all | solution.py:51
  48.0 1.6 %copy-start.2 = (bf16[24,128,256]{2,1,0:T(8,128)(2,1)S(1)}, bf16[24,128,256]{2,1,0:T(8,128)(2,1)}, u32[]{:S(2)}) copy-start(bf16[24,128,256]{2,1,0:T(8,128)(2,1)} %gather_fusion.4) | copy-start | bytes 4718596
  50.2 0.9 %copy-start.3 = (bf16[24,128,128]{2,1,0:T(8,128)(2,1)}, bf16[24,128,128]{2,1,0:T(8,128)(2,1)S(1)}, u32[]{:S(2)}) copy-start(bf16[24,128,128]{2,1,0:T(8,128)(2,1)S(1)} %fusion.3) | copy-start | bytes 2359300
  53.3 3.4 %collective-permute-start = (f32[4,128,256]{2,0,1:T(4,128)}, f32[4,128,256]{2,0,1:T(4,128)}, u32[]{:S(2)}, u32[]{:S(2)}) collective-permute-start(f32[4,128,256]{2,0,1:T(4,128)} %select_bitcast_fusion), channel_id=1, source_target_pairs={{0,4},{4,0},{8,12},{12,8},{16,20},{20,16},{24,28},{28,24},{1,5},{5... | collective-permute-start | bytes 1572872 | tf_op jit(solution)/shard_map/ppermute | solution.py:19
  60.2 2.0 %copy-start.4 = (bf16[24,128,256]{2,1,0:T(8,128)(2,1)S(1)}, bf16[24,128,256]{2,1,0:T(8,128)(2,1)}, u32[]{:S(2)}) copy-start(bf16[24,128,256]{2,1,0:T(8,128)(2,1)} %convolution_convert_fusion.1) | copy-start | bytes 4718596
  60.6 8.9 %collective-permute-start.1 = (f32[2,128,256]{2,1,0:T(8,128)S(1)}, f32[2,128,256]{2,1,0:T(8,128)}, u32[]{:S(2)}, u32[]{:S(2)}) collective-permute-start(f32[2,128,256]{2,1,0:T(8,128)S(1)} %select_bitcast_fusion.1), channel_id=1, source_target_pairs={{0,8},{4,12},{8,0},{12,4},{16,24},{20,28},{24,16},{28,20},{1,9},{5... | collective-permute-start | bytes 786440 | tf_op jit(solution)/shard_map/ppermute | solution.py:19
  66.0 18.6 %all-to-all-start.1 = ((f32[4,128,256]{2,1,0:T(8,128)}), f32[4,128,256]{2,1,0:T(8,128)S(1)}, u32[]{:S(2)}, u32[]{:S(2)}) async-start(f32[4,128,256]{2,1,0:T(8,128)} %convolution_bitcast_fusion), calls=%async_computation.1 | async-start | bytes 1048576 | tf_op jit(solution)/shard_map/all_to_all | solution.py:95
  70.6 14.1 %collective-permute-start.2 = (f32[1,128,256]{2,1,0:T(8,128)S(1)}, f32[1,128,256]{2,1,0:T(8,128)S(1)}, u32[]{:S(2)}, u32[]{:S(2)}) collective-permute-start(f32[1,128,256]{2,1,0:T(8,128)S(1)} %select_bitcast_fusion.2), channel_id=1, source_target_pairs={{0,16},{4,20},{8,24},{12,28},{16,0},{20,4},{24,8},{28,12},{1,17},{... | collective-permute-start | bytes 393224 | tf_op jit(solution)/shard_map/ppermute | solution.py:19

commit v2 on v1

v2 whole, which is shorter than its diff:
```python
import jax
import jax.numpy as jnp
from jax import lax
from jax.sharding import PartitionSpec as P

LOSS_SCALE = 0.0625


def grp_reduce_scatter(parts, grp_count):
    if grp_count & (grp_count - 1):
        return lax.psum_scatter(parts, "grp", scatter_dimension=0, tiled=True)[0]
    me = lax.axis_index("grp")
    bit = 1
    while bit < grp_count:
        half = parts.reshape((parts.shape[0] // 2, 2) + parts.shape[1:])
        mine = (me // bit) % 2
        keep = jnp.where(mine == 0, half[:, 0], half[:, 1])
        send = jnp.where(mine == 0, half[:, 1], half[:, 0])
        got = lax.ppermute(send, "grp", [(i, i ^ bit) for i in range(grp_count)])
        parts = keep + got
        bit *= 2
    return parts[0]


def grp_gather(block, grp_count):
    if grp_count & (grp_count - 1):
        return lax.all_gather(block, "grp", axis=0, tiled=False)
    me = lax.axis_index("grp")
    held = block[None]
    bit = 1
    while bit < grp_count:
        got = lax.ppermute(held, "grp", [(i, i ^ bit) for i in range(grp_count)])
        low = (me // bit) % 2 == 0
        held = jnp.where(
            low, jnp.concatenate([held, got], axis=0), jnp.concatenate([got, held], axis=0)
        )
        bit *= 2
    return held


def shift_ent(x, shift, ent_count):
    if shift % ent_count == 0:
        return x
    return lax.ppermute(x, "ent", [(i, (i + shift) % ent_count) for i in range(ent_count)])


def on_device(factor, cores, adjacency, tile_rels, tile_count, send_lists):
    ent_count = lax.axis_size("ent")
    grp_count = lax.axis_size("grp")
    my_ent = lax.axis_index("ent")
    tiles = tile_rels.shape[1]
    block = factor.shape[0]
    width = factor.shape[1]
    per_relay = tiles // ent_count
    head_rows = 16
    chunks = 2 if per_relay % 2 == 0 else 1
    per_chunk = per_relay // chunks

    tile_ids = jnp.arange(tiles, dtype=jnp.int32)
    live = (tile_ids < tile_count[0]).astype(jnp.float32).reshape(per_relay, ent_count)
    rels_by_shift = tile_rels[0].reshape(per_relay, ent_count)
    adj_by_shift = adjacency.reshape(per_relay, ent_count, block, block)
    sent_heads = []
    sent_adj = []
    for k in range(ent_count):
        head = jnp.concatenate(
            [rels_by_shift[:, k].astype(jnp.float32), live[:, k]], axis=0
        )
        head = jnp.pad(head, (0, width - 2 * per_relay))
        head = jnp.broadcast_to(head[None, :], (head_rows, width)).astype(jnp.bfloat16)
        sent_heads.append(shift_ent(jnp.concatenate([factor, head], axis=0), k, ent_count))
        sent_adj.append(
            [
                shift_ent(
                    adj_by_shift[c * per_chunk : (c + 1) * per_chunk, k].astype(jnp.bfloat16),
                    k,
                    ent_count,
                )
                for c in range(chunks)
            ]
        )

    group_blocks = grp_gather(factor, grp_count)
    routes = send_lists[0]
    src_of = (my_ent - jnp.arange(ent_count, dtype=jnp.int32)) % ent_count
    groups_all = routes[src_of]
    src_f = jnp.stack([h[:block] for h in sent_heads])
    heads = jnp.stack([h[block].astype(jnp.float32) for h in sent_heads])
    rels_all = heads[:, :per_relay].astype(jnp.int32)
    alive_all = heads[:, per_relay : 2 * per_relay]

    row_parts = jnp.zeros((ent_count, block, width), jnp.float32)
    owner_terms = jnp.zeros((grp_count, block, width), jnp.float32)
    for c in range(chunks):
        sl = slice(c * per_chunk, (c + 1) * per_chunk)
        count = ent_count * per_chunk
        adj_in = jnp.stack([a[c] for a in sent_adj]).reshape(count, block, block)
        rels = rels_all[:, sl].reshape(count)
        alive = alive_all[:, sl].reshape(count)
        groups = groups_all[:, sl].reshape(count)
        panels = group_blocks[groups]
        core_tiles = cores[rels]
        src_tiles = jnp.repeat(src_f, per_chunk, axis=0)
        mapped = jnp.einsum(
            "tbr,trs->tbs", src_tiles, core_tiles, preferred_element_type=jnp.float32
        ).astype(jnp.bfloat16)
        predicted = jnp.einsum(
            "tgj,tmj->tgm", mapped, panels, preferred_element_type=jnp.float32
        )
        resid = (
            (predicted - adj_in.astype(jnp.float32)) * (LOSS_SCALE * alive)[:, None, None]
        ).astype(jnp.bfloat16)
        product = jnp.einsum(
            "tmw,twe->tme", resid, panels, preferred_element_type=jnp.float32
        ).astype(jnp.bfloat16)
        row_parts = row_parts + jnp.einsum(
            "ejbs,ejrs->ebr",
            product.reshape(ent_count, per_chunk, block, width),
            core_tiles.reshape(ent_count, per_chunk, width, width),
            preferred_element_type=jnp.float32,
        )
        column_terms = jnp.einsum(
            "tzj,tzh->tjh", resid, mapped, preferred_element_type=jnp.float32
        ).astype(jnp.bfloat16)
        owner_onehot = (
            groups[:, None] == jnp.arange(grp_count, dtype=jnp.int32)[None, :]
        ).astype(jnp.float32)
        owner_terms = owner_terms + jnp.dot(
            owner_onehot.T,
            column_terms.reshape(count, block * width).astype(jnp.float32),
            precision=lax.Precision.HIGHEST,
            preferred_element_type=jnp.float32,
        ).reshape(grp_count, block, width)

    rows = row_parts[0]
    for k in range(1, ent_count):
        rows = rows + shift_ent(row_parts[k], -k, ent_count)
    owner_part = grp_reduce_scatter(owner_terms, grp_count)
    return rows + owner_part


def solution(mesh):
    in_specs = (
        P(("grp", "ent"), None),
        P(),
        P(("grp", "ent"), None, None),
        P(("grp", "ent"), None),
        P(("grp", "ent")),
        P(("grp", "ent"), None, None),
    )
    out_specs = P(("grp", "ent"), None)
    return jax.shard_map(
        on_device, mesh=mesh, in_specs=in_specs, out_specs=out_specs, check_vma=False
    )
```

time: 86.1 us -> 80.5 us (0.935)
  waiting for transfers between devices: 26.7 us -> 13.6 us
  blocking collectives: 9.87 us -> 0 us
  starting transfers between devices: 13.1 us -> 22.7 us
  local copies, waits for them, and re-layouts: 13.2 us -> 21.6 us
  matrix products: 12.2 us -> 9.45 us
  other arithmetic: 9.27 us -> 11.2 us
    all_to_all x2 -> x0, waiting for transfers between devices: 26.7 us -> none  [the longest x1 14.3 us: on_device(): lax.all_to_all(outgoing, 'ent', split_axis=0, concat_axis=0, tiled=True)]
    ppermute x0 -> x15, starting transfers between devices: none -> 21.5 us  [the longest x12 18.4 us: shift_ent(): lax.ppermute(x, 'ent', [(i, (i + shift) % ent_count) for i in range(ent_c...]
    ppermute x0 -> x15, waiting for transfers between devices: none -> 11.1 us  [the longest x12 11.1 us: shift_ent(): lax.ppermute(x, 'ent', [(i, (i + shift) % ent_count) for i in range(ent_c...]
    all_to_all x2 -> x0, starting transfers between devices: 9.92 us -> none  [the longest x1 6.45 us: on_device(): lax.all_to_all(outgoing, 'ent', split_axis=0, concat_axis=0, tiled=True)]
    all_gather x1 -> x0, blocking collectives: 9.87 us -> none  [on_device(): group_blocks = lax.all_gather(factor, 'grp', axis=0, tiled=False)]
    another operation x1 -> x7, other arithmetic: 0.01 us -> 5.32 us  [the longest x2 3.45 us: on_device(): adj_in = jnp.stack([a[c] for a in sent_adj]).reshape(count, block, block)]
    unnamed x14 -> x31, local copies, waits for them, and re-layouts: 0.62 us -> 3.96 us
    convert_element_type x3 -> x1, other arithmetic: 3.18 us -> 0.01 us  [on_device(): rels_all = heads[:, :per_relay].astype(jnp.int32)]
  transfers between devices with their start and end apart: 5 -> 18, of which waited for: 2 -> 4; matrix products, arithmetic and copies ran while one was open for 12% -> 26% of each run, Pallas kernels for 0% -> 0%
where the time goes in v2:
time: 80.5 us; the launch traced here: 79.8 us
  starting transfers between devices  22.7 us (28%)
  local copies, waits for them, and re-layouts  21.6 us (27%)
  waiting for transfers between devices  13.6 us (17%)
  other arithmetic  11.2 us (14%)
  matrix products  9.45 us (12%)
  between operations  1.23 us (2%)
    ppermute x12, starting transfers between devices, shift_ent(): lax.ppermute(x, 'ent', [(i, (i + shift) % ent_count) for i in range(ent_c...  18.4 us
    ppermute x12, waiting for transfers between devices, shift_ent(): lax.ppermute(x, 'ent', [(i, (i + shift) % ent_count) for i in range(ent_c...  11.1 us
    unnamed x31, local copies, waits for them, and re-layouts  3.96 us
    gather x2, local copies, waits for them, and re-layouts, on_device(): core_tiles = cores[rels]  3.72 us
    another operation x2, other arithmetic, on_device(): adj_in = jnp.stack([a[c] for a in sent_adj]).reshape(count, block, block)  3.45 us
    ppermute x3, starting transfers between devices, grp_gather(): got = lax.ppermute(held, 'grp', [(i, i ^ bit) for i in range(grp_count)])  3.08 us
    reshape x1, local copies, waits for them, and re-layouts, grp_reduce_scatter(): half = parts.reshape((parts.shape[0] // 2, 2) + parts.shape[1:])  2.86 us
    another operation x3, local copies, waits for them, and re-layouts, on_device(): src_f = jnp.stack([h[:block] for h in sent_heads])  2.65 us
  transfers between devices with their start and end apart: 18, of which 4 were waited for; matrix products, arithmetic and copies ran while one was open for 26% of the time, Pallas kernels for 0%

profile of v2, /device:TPU:0, one launch (start us, length us, event | category | flops | bytes accessed | tf_op | source)
XLA Modules:
  0.0 79.8 jit_solution(12397381506533659932)
XLA Ops:
  0.8 0.5 broadcast.257
  1.3 1.3 %reduce.11 = s32[24]{0:T(128)S(1)} reduce(s32[1,24]{1,0:T(1,128)} %param.9, s32[]{:T(128)} %broadcast.257), dimensions={0}, to_apply=%param.9.reduce_sub_computation.3 | reduce | bytes 196 | tf_op args[3]
  2.7 0.2 fusion.20
  3.1 0.9 %pad_maximum_fusion.3 = (bf16[144,256]{1,0:T(8,128)(2,1)S(1)}, bf16[144,256]{1,0:T(8,128)(2,1)S(1)}, bf16[144,256]{1,0:T(8,128)(2,1)S(1)}) fusion(bf16[16,256]{1,0:T(8,128)(2,1)S(1)} %broadcast_in_dim.8, bf16[128,256]{1,0:T(8,128)(2,1)} %param.6, bf16[16,256]{1,0:T(8,128)(2,1)S(1)} %broadcast_in_dim.9, bf16[16,256]{1,0:T(8,128)(2,1)S(1)} %broadcast_in_dim.10), kind=kLoop, calls=%fused_computation.57 | loop fusion | flops 368640 | bytes 311296 | tf_op jit(solution)/shard_map/concatenate | solution.py:71
  4.0 5.1 %collective-permute-start.2 = (bf16[144,256]{1,0:T(8,128)(2,1)S(1)}, bf16[144,256]{1,0:T(8,128)(2,1)}, u32[]{:S(2)}, u32[]{:S(2)}) collective-permute-start(bf16[144,256]{1,0:T(8,128)(2,1)S(1)} %get-tuple-element.24), channel_id=1, source_target_pairs={{0,3},{1,0},{2,1},{3,2},{4,7},{5,4},{6,5},{7,6},{8,11},{9,8},{10,9... | collective-permute-start | bytes 221192 | tf_op jit(solution)/shard_map/ppermute | solution.py:44
  9.1 1.0 %collective-permute-start = (bf16[144,256]{1,0:T(8,128)(2,1)S(1)}, bf16[144,256]{1,0:T(8,128)(2,1)}, u32[]{:S(2)}, u32[]{:S(2)}) collective-permute-start(bf16[144,256]{1,0:T(8,128)(2,1)S(1)} %get-tuple-element.22), channel_id=1, source_target_pairs={{0,1},{1,2},{2,3},{3,0},{4,5},{5,6},{6,7},{7,4},{8,9},{9,10},{10,1... | collective-permute-start | bytes 221192 | tf_op jit(solution)/shard_map/ppermute | solution.py:44
  10.1 1.6 %convert.58 = bf16[24,128,128]{2,1,0:T(8,128)(2,1)S(1)} convert(s32[24,128,128]{2,1,0:T(8,128)} %param.8) | non-fusion elementwise | flops 393216 | bytes 2359296 | tf_op jit(solution)/shard_map/convert.11
  11.8 2.9 %collective-permute-start.11 = (bf16[3,128,128]{2,1,0:T(8,128)(2,1)S(1)}, bf16[3,128,128]{2,1,0:T(8,128)(2,1)S(1)}, u32[]{:S(2)}, u32[]{:S(2)}) collective-permute-start(bf16[3,128,128]{2,1,0:T(8,128)(2,1)S(1)} %get-tuple-element.18), channel_id=1, source_target_pairs={{0,3},{1,0},{2,1},{3,2},{4,7},{5,4},{6,5},{7,6},{8,11},{9,8},{10,9... | collective-permute-start | bytes 294920 | tf_op jit(solution)/shard_map/ppermute | solution.py:44
  14.7 0.6 gather_fusion.1
  15.3 0.1 reshape.334
  15.8 0.6 copy-done.14
  16.5 1.1 %collective-permute-start.10 = (bf16[3,128,128]{2,1,0:T(8,128)(2,1)S(1)}, bf16[3,128,128]{2,1,0:T(8,128)(2,1)}, u32[]{:S(2)}, u32[]{:S(2)}) collective-permute-start(bf16[3,128,128]{2,1,0:T(8,128)(2,1)S(1)} %get-tuple-element.12), channel_id=1, source_target_pairs={{0,2},{1,3},{2,0},{3,1},{4,6},{5,7},{6,4},{7,5},{8,10},{9,11},{10,... | collective-permute-start | bytes 294920 | tf_op jit(solution)/shard_map/ppermute | solution.py:44
  17.6 0.9 %maximum_select_fusion.2 = bf16[2,128,256]{2,1,0:T(8,128)(2,1)S(1)} fusion(bf16[1,128,256]{2,1,0:T(8,128)(2,1)} %copy-done.14, bf16[1,128,256]{2,1,0:T(8,128)(2,1)S(1)} %bitcast.197, pred[]{:T(512)S(6)} %eq.56), kind=kLoop, calls=%fused_computation.46 | loop fusion | flops 196608 | bytes 262145 | tf_op jit(solution)/shard_map/jit(_where)/select_n | solution.py:34
  18.6 0.7 slice.193
  19.3 3.8 %collective-permute-start.8 = (bf16[3,128,128]{2,1,0:T(8,128)(2,1)S(1)}, bf16[3,128,128]{2,1,0:T(8,128)(2,1)}, u32[]{:S(2)}, u32[]{:S(2)}) collective-permute-start(bf16[3,128,128]{2,1,0:T(8,128)(2,1)S(1)} %get-tuple-element.15), channel_id=1, source_target_pairs={{0,3},{1,0},{2,1},{3,2},{4,7},{5,4},{6,5},{7,6},{8,11},{9,8},{10,9... | collective-permute-start | bytes 294920 | tf_op jit(solution)/shard_map/ppermute | solution.py:44
  23.1 0.7 slice.192
  23.8 1.5 %collective-permute-start.4 = (bf16[2,128,256]{2,1,0:T(8,128)(2,1)S(1)}, bf16[2,128,256]{2,1,0:T(8,128)(2,1)S(1)}, u32[]{:S(2)}, u32[]{:S(2)}) collective-permute-start(bf16[2,128,256]{2,1,0:T(8,128)(2,1)S(1)} %maximum_select_fusion.2), channel_id=1, source_target_pairs={{0,8},{4,12},{8,0},{12,4},{16,24},{20,28},{24,16},{28,20},{1,9},{5... | collective-permute-start | bytes 393224 | tf_op jit(solution)/shard_map/ppermute | solution.py:32
  25.3 0.7 slice.191
  26.0 0.1 reshape.338
  26.2 1.9 %gather_fusion.3 = bf16[12,256,256]{2,1,0:T(8,128)(2,1)} fusion(bf16[16,256,256]{2,1,0:T(8,128)(2,1)S(1)} %copy-done, s32[1024]{0:T(1024)S(1)} %pad_clamp_fusion.1), kind=kCustom, calls=%fused_computation.3 | custom fusion | bytes 3145776 | tf_op jit(solution)/shard_map/gather | solution.py:102
  28.1 1.8 %gather_fusion = bf16[12,256,256]{2,1,0:T(8,128)(2,1)} fusion(bf16[16,256,256]{2,1,0:T(8,128)(2,1)S(1)} %copy-done, s32[1024]{0:T(1024)S(1)} %pad_clamp_fusion.4), kind=kCustom, calls=%fused_computation | custom fusion | bytes 3145776 | tf_op jit(solution)/shard_map/gather | solution.py:102
  30.0 1.0 %slice_bitcast_fusion.16 = bf16[1,128,256]{2,1,0:T(8,128)(2,1)S(1)} fusion(bf16[144,256]{1,0:T(8,128)(2,1)} %collective-permute-done.2), kind=kLoop, calls=%fused_computation.60 | loop fusion | bytes 131072 | tf_op jit(solution)/shard_map/stack | solution.py:87
  30.9 0.8 %slice_bitcast_fusion.17 = bf16[1,128,256]{2,1,0:T(8,128)(2,1)S(1)} fusion(bf16[144,256]{1,0:T(8,128)(2,1)} %collective-permute-done.1), kind=kLoop, calls=%fused_computation.61 | loop fusion | bytes 131072 | tf_op jit(solution)/shard_map/stack | solution.py:87
  31.8 0.8 %slice_bitcast_fusion.18 = bf16[1,128,256]{2,1,0:T(8,128)(2,1)S(1)} fusion(bf16[144,256]{1,0:T(8,128)(2,1)} %collective-permute-done), kind=kLoop, calls=%fused_computation.62 | loop fusion | bytes 131072 | tf_op jit(solution)/shard_map/stack | solution.py:87
  32.8 1.3 %convolution_convert_fusion.3 = bf16[12,128,256]{2,1,0:T(8,128)(2,1)} fusion(bf16[12,128,256]{2,1,0:T(8,128)(2,1)S(1)} %bitcast.187, bf16[12,256,256]{2,1,0:T(8,128)(2,1)S(1)} %copy-done.3), kind=kOutput, calls=%fused_computation.8 | convolution fusion | flops 201719808 | bytes 3145728 | tf_op jit(solution)/shard_map/tbr,trs->tbs/dot_general | solution.py:104
  34.0 0.3 copy-done.1
  34.3 1.3 %convolution_convert_fusion.5 = bf16[12,128,256]{2,1,0:T(8,128)(2,1)} fusion(bf16[12,128,256]{2,1,0:T(8,128)(2,1)S(1)} %bitcast.188, bf16[12,256,256]{2,1,0:T(8,128)(2,1)S(1)} %copy-done.1), kind=kOutput, calls=%fused_computation.10 | convolution fusion | flops 201719808 | bytes 3145728 | tf_op jit(solution)/shard_map/tbr,trs->tbs/dot_general | solution.py:104
  35.6 1.6 %collective-permute-start.5 = (bf16[4,128,256]{2,1,0:T(8,128)(2,1)S(1)}, bf16[4,128,256]{2,1,0:T(8,128)(2,1)}, u32[]{:S(2)}, u32[]{:S(2)}) collective-permute-start(bf16[4,128,256]{2,1,0:T(8,128)(2,1)S(1)} %maximum_select_fusion.1), channel_id=1, source_target_pairs={{0,16},{4,20},{8,24},{12,28},{16,0},{20,4},{24,8},{28,12},{1,17},{... | collective-permute-start | bytes 786440 | tf_op jit(solution)/shard_map/ppermute | solution.py:32
  37.3 0.1 mul.41
  37.5 0.6 collective-permute-start.6
  38.0 1.7 %pad_maximum_fusion.1 = bf16[4,3,128,128]{3,2,1,0:T(8,128)(2,1)} fusion(bf16[1,3,128,128]{3,2,1,0:T(8,128)(2,1)S(1)} %bitcast.200, bf16[1,3,128,128]{3,2,1,0:T(8,128)(2,1)} %bitcast.33, bf16[1,3,128,128]{3,2,1,0:T(8,128)(2,1)} %bitcast.31, bf16[1,3,128,128]{3,2,1,0:T(8,128)(2,1)S(1)} %get-tuple-element.14), kind=kLoop, calls=%fused_computation.30 | loop fusion | flops 589824 | bytes 786432 | tf_op jit(solution)/shard_map/stack | solution.py:97
  39.8 5.2 %collective-permute-done.7 = bf16[3,128,128]{2,1,0:T(8,128)(2,1)S(1)} collective-permute-done((bf16[3,128,128]{2,1,0:T(8,128)(2,1)S(1)}, bf16[3,128,128]{2,1,0:T(8,128)(2,1)S(1)}, u32[]{:S(2)}, u32[]{:S(2)}) %collective-permute-start.7) | collective-permute-done | bytes 98336 | tf_op jit(solution)/shard_map/ppermute | solution.py:44
  45.0 1.7 %pad_maximum_fusion = bf16[4,3,128,128]{3,2,1,0:T(8,128)(2,1)} fusion(bf16[1,3,128,128]{3,2,1,0:T(8,128)(2,1)} %bitcast.21, bf16[1,3,128,128]{3,2,1,0:T(8,128)(2,1)S(1)} %bitcast.201, bf16[1,3,128,128]{3,2,1,0:T(8,128)(2,1)S(1)} %bitcast.202, bf16[1,3,128,128]{3,2,1,0:T(8,128)(2,1)S(1)} %get-tuple-element.11), kind=kLoop, calls=%fused_computation.29 | loop fusion | flops 589824 | bytes 786432 | tf_op jit(solution)/shard_map/stack | solution.py:97
  46.7 1.1 %maximum_select_fusion = bf16[8,128,256]{2,1,0:T(8,128)(2,1)S(1)} fusion(bf16[4,128,256]{2,1,0:T(8,128)(2,1)} %collective-permute-done.5, bf16[4,128,256]{2,1,0:T(8,128)(2,1)S(1)} %maximum_select_fusion.1, pred[]{:T(512)S(6)} %eq.54), kind=kLoop, calls=%fused_computation.26 | loop fusion | flops 786432 | bytes 1048577 | tf_op jit(solution)/shard_map/jit(_where)/select_n | solution.py:34
  47.8 1.5 %gather_fusion.4 = bf16[12,128,256]{2,1,0:T(8,128)(2,1)} fusion(bf16[8,128,256]{2,1,0:T(8,128)(2,1)S(1)} %maximum_select_fusion, s32[1024]{0:T(1024)S(1)} %pad_clamp_fusion), kind=kCustom, calls=%fused_computation.4 | custom fusion | bytes 1572912 | tf_op jit(solution)/shard_map/gather | solution.py:101
  49.3 0.6 gather_fusion.2
  49.9 1.7 %fusion.2 = bf16[12,128,128]{2,1,0:T(8,128)(2,1)S(1)} fusion(bf16[12,128,256]{2,1,0:T(8,128)(2,1)} %convolution_convert_fusion.5, bf16[12,128,256]{2,1,0:T(8,128)(2,1)S(1)} %gather_fusion.2, bf16[12,128,128]{2,1,0:T(8,128)(2,1)} %bitcast.195, f32[12]{0:T(128)S(1)} %mul.37), kind=kOutput, calls=%fused_computation.16 | convolution fusion | flops 101449728 | bytes 2359344 | tf_op jit(solution)/shard_map/tgj,tmj->tgm/dot_general | solution.py:107
  51.7 0.4 convolution_convert_fusion.1
  52.2 0.6 copy-done.5
  52.8 0.2 copy-done.7
  53.0 0.1 copy-done.11
  53.1 0.4 fusion.3
  53.5 0.4 convolution_convert_fusion
  54.0 0.3 copy-done.9
  54.2 0.5 fusion.6
  54.8 1.5 %convolution_add_fusion = f32[8,128,256]{2,0,1:T(8,128)} fusion(f32[8,128,256]{2,0,1:T(8,128)S(1)} %fusion.6, bf16[128,256,12]{1,0,2:T(8,128)(2,1)S(1)} %slice_bitcast_fusion, s32[12]{0:T(128)S(1)} %eq.61), kind=kOutput, calls=%fused_computation.11 | convolution fusion | flops 6553696 | bytes 2883632 | tf_op jit(solution)/shard_map/dot_general | solution.py:128
  56.3 2.9 %reshape.344 = f32[4,2,128,256]{3,1,0,2:T(2,128)} reshape(f32[8,128,256]{2,0,1:T(8,128)} %convolution_add_fusion) | data formatting | bytes 2097152 | tf_op jit(solution)/shard_map/reshape | solution.py:15
  59.1 2.5 %fusion.41 = (f32[4,1,128,256]{3,1,0,2:T(1,128)S(1)}, f32[4,1,128,256]{3,1,0,2:T(1,128)S(1)}) fusion(f32[4,2,128,256]{3,1,0,2:T(2,128)} %reshape.344), kind=kLoop, calls=%fused_computation.119 | loop fusion | bytes 2097152 | tf_op jit(solution)/shard_map/slice | solution.py:17
  61.7 0.2 select_bitcast_fusion
  62.0 0.4 convolution_convert_fusion.2
  62.3 0.8 copy-done.4
  63.1 0.6 convolution_bitcast_fusion
  63.7 0.4 convolution_convert_fusion.4
  64.1 0.2 bitcast_add_fusion
  64.4 0.6 collective-permute-start.16
  65.0 0.5 copy-done.2
  65.5 0.6 fusion.4
  66.3 0.6 collective-permute-start.13
  66.8 3.2 %collective-permute-start.12 = (f32[128,256]{1,0:T(8,128)S(1)}, f32[128,256]{1,0:T(8,128)S(1)}, u32[]{:S(2)}, u32[]{:S(2)}) collective-permute-start(f32[128,256]{1,0:T(8,128)S(1)} %get-tuple-element.19), channel_id=1, source_target_pairs={{0,3},{1,0},{2,1},{3,2},{4,7},{5,4},{6,5},{7,6},{8,11},{9,8},{10,9... | collective-permute-start | bytes 393224 | tf_op jit(solution)/shard_map/ppermute | solution.py:44
  70.1 2.4 %collective-permute-done.16 = f32[2,128,256]{2,1,0:T(8,128)S(1)} collective-permute-done((f32[2,128,256]{2,1,0:T(8,128)S(1)}, f32[2,128,256]{2,1,0:T(8,128)S(1)}, u32[]{:S(2)}, u32[]{:S(2)}) %collective-permute-start.16) | collective-permute-done | bytes 262176 | tf_op jit(solution)/shard_map/ppermute | solution.py:19
  72.6 0.6 collective-permute-start.17
  73.2 1.3 %collective-permute-done.14 = f32[128,256]{1,0:T(8,128)S(1)} collective-permute-done((f32[128,256]{1,0:T(8,128)S(1)}, f32[128,256]{1,0:T(8,128)S(1)}, u32[]{:S(2)}, u32[]{:S(2)}) %collective-permute-start.14) | collective-permute-done | bytes 131104 | tf_op jit(solution)/shard_map/ppermute | solution.py:44
  74.5 4.6 %collective-permute-done.13 = f32[128,256]{1,0:T(8,128)S(1)} collective-permute-done((f32[128,256]{1,0:T(8,128)S(1)}, f32[128,256]{1,0:T(8,128)S(1)}, u32[]{:S(2)}, u32[]{:S(2)}) %collective-permute-start.13) | collective-permute-done | bytes 131104 | tf_op jit(solution)/shard_map/ppermute | solution.py:44
  79.0 0.7 fusion.12
  (82 shorter events, 1.8 us)
Async XLA Ops:
  0.0 26.2 %copy-start = (bf16[16,256,256]{2,1,0:T(8,128)(2,1)S(1)}, bf16[16,256,256]{2,1,0:T(8,128)(2,1)}, u32[]{:S(2)}) copy-start(bf16[16,256,256]{2,1,0:T(8,128)(2,1)} %param.7) | copy-start | bytes 6291460
  4.0 14.5 %collective-permute-start.2 = (bf16[144,256]{1,0:T(8,128)(2,1)S(1)}, bf16[144,256]{1,0:T(8,128)(2,1)}, u32[]{:S(2)}, u32[]{:S(2)}) collective-permute-start(bf16[144,256]{1,0:T(8,128)(2,1)S(1)} %get-tuple-element.24), channel_id=1, source_target_pairs={{0,3},{1,0},{2,1},{3,2},{4,7},{5,4},{6,5},{7,6},{8,11},{9,8},{10,9... | collective-permute-start | bytes 221192 | tf_op jit(solution)/shard_map/ppermute | solution.py:44
  9.1 10.2 %collective-permute-start.1 = (bf16[144,256]{1,0:T(8,128)(2,1)S(1)}, bf16[144,256]{1,0:T(8,128)(2,1)}, u32[]{:S(2)}, u32[]{:S(2)}) collective-permute-start(bf16[144,256]{1,0:T(8,128)(2,1)S(1)} %get-tuple-element.23), channel_id=1, source_target_pairs={{0,2},{1,3},{2,0},{3,1},{4,6},{5,7},{6,4},{7,5},{8,10},{9,11},{10,... | collective-permute-start | bytes 221192 | tf_op jit(solution)/shard_map/ppermute | solution.py:44
  9.1 14.7 %collective-permute-start = (bf16[144,256]{1,0:T(8,128)(2,1)S(1)}, bf16[144,256]{1,0:T(8,128)(2,1)}, u32[]{:S(2)}, u32[]{:S(2)}) collective-permute-start(bf16[144,256]{1,0:T(8,128)(2,1)S(1)} %get-tuple-element.22), channel_id=1, source_target_pairs={{0,1},{1,2},{2,3},{3,0},{4,5},{5,6},{6,7},{7,4},{8,9},{9,10},{10,1... | collective-permute-start | bytes 221192 | tf_op jit(solution)/shard_map/ppermute | solution.py:44
  10.1 4.6 %copy-start.13 = (s32[1,4,6]{2,1,0:T(4,128)S(1)}, s32[1,4,6]{2,1,0:T(4,128)}, u32[]{:S(2)}) copy-start(s32[1,4,6]{2,1,0:T(4,128)} %param.11) | copy-start | bytes 292
  10.1 7.5 %copy-start.12 = (bf16[128,256]{1,0:T(8,128)(2,1)S(1)}, bf16[128,256]{1,0:T(8,128)(2,1)}, u32[]{:S(2)}) copy-start(bf16[128,256]{1,0:T(8,128)(2,1)} %param.6) | copy-start | bytes 196612
  10.1 5.7 %collective-permute-start.3 = (bf16[1,128,256]{2,1,0:T(8,128)(2,1)}, bf16[1,128,256]{2,1,0:T(8,128)(2,1)S(1)}, u32[]{:S(2)}, u32[]{:S(2)}) collective-permute-start(bf16[1,128,256]{2,1,0:T(8,128)(2,1)} %bitcast.196), channel_id=1, source_target_pairs={{0,4},{4,0},{8,12},{12,8},{16,20},{20,16},{24,28},{28,24},{1,5},{5... | collective-permute-start | bytes 196616 | tf_op jit(solution)/shard_map/ppermute | solution.py:32
  11.8 25.6 %collective-permute-start.11 = (bf16[3,128,128]{2,1,0:T(8,128)(2,1)S(1)}, bf16[3,128,128]{2,1,0:T(8,128)(2,1)S(1)}, u32[]{:S(2)}, u32[]{:S(2)}) collective-permute-start(bf16[3,128,128]{2,1,0:T(8,128)(2,1)S(1)} %get-tuple-element.18), channel_id=1, source_target_pairs={{0,3},{1,0},{2,1},{3,2},{4,7},{5,4},{6,5},{7,6},{8,11},{9,8},{10,9... | collective-permute-start | bytes 294920 | tf_op jit(solution)/shard_map/ppermute | solution.py:44
  15.8 0.6 copy-start.14
  16.5 21.0 %collective-permute-start.10 = (bf16[3,128,128]{2,1,0:T(8,128)(2,1)S(1)}, bf16[3,128,128]{2,1,0:T(8,128)(2,1)}, u32[]{:S(2)}, u32[]{:S(2)}) collective-permute-start(bf16[3,128,128]{2,1,0:T(8,128)(2,1)S(1)} %get-tuple-element.12), channel_id=1, source_target_pairs={{0,2},{1,3},{2,0},{3,1},{4,6},{5,7},{6,4},{7,5},{8,10},{9,11},{10,... | collective-permute-start | bytes 294920 | tf_op jit(solution)/shard_map/ppermute | solution.py:44
  18.5 19.5 %collective-permute-start.9 = (bf16[3,128,128]{2,1,0:T(8,128)(2,1)S(1)}, bf16[3,128,128]{2,1,0:T(8,128)(2,1)}, u32[]{:S(2)}, u32[]{:S(2)}) collective-permute-start(bf16[3,128,128]{2,1,0:T(8,128)(2,1)S(1)} %get-tuple-element.13), channel_id=1, source_target_pairs={{0,1},{1,2},{2,3},{3,0},{4,5},{5,6},{6,7},{7,4},{8,9},{9,10},{10,1... | collective-permute-start | bytes 294920 | tf_op jit(solution)/shard_map/ppermute | solution.py:44
  19.3 20.5 %collective-permute-start.8 = (bf16[3,128,128]{2,1,0:T(8,128)(2,1)S(1)}, bf16[3,128,128]{2,1,0:T(8,128)(2,1)}, u32[]{:S(2)}, u32[]{:S(2)}) collective-permute-start(bf16[3,128,128]{2,1,0:T(8,128)(2,1)S(1)} %get-tuple-element.15), channel_id=1, source_target_pairs={{0,3},{1,0},{2,1},{3,2},{4,7},{5,4},{6,5},{7,6},{8,11},{9,8},{10,9... | collective-permute-start | bytes 294920 | tf_op jit(solution)/shard_map/ppermute | solution.py:44
  23.8 11.8 %collective-permute-start.4 = (bf16[2,128,256]{2,1,0:T(8,128)(2,1)S(1)}, bf16[2,128,256]{2,1,0:T(8,128)(2,1)S(1)}, u32[]{:S(2)}, u32[]{:S(2)}) collective-permute-start(bf16[2,128,256]{2,1,0:T(8,128)(2,1)S(1)} %maximum_select_fusion.2), channel_id=1, source_target_pairs={{0,8},{4,12},{8,0},{12,4},{16,24},{20,28},{24,16},{28,20},{1,9},{5... | collective-permute-start | bytes 393224 | tf_op jit(solution)/shard_map/ppermute | solution.py:32
  30.0 2.8 %copy-start.3 = (bf16[12,256,256]{2,1,0:T(8,128)(2,1)S(1)}, bf16[12,256,256]{2,1,0:T(8,128)(2,1)}, u32[]{:S(2)}) copy-start(bf16[12,256,256]{2,1,0:T(8,128)(2,1)} %gather_fusion.3) | copy-start | bytes 4718596
  32.7 1.6 %copy-start.1 = (bf16[12,256,256]{2,1,0:T(8,128)(2,1)S(1)}, bf16[12,256,256]{2,1,0:T(8,128)(2,1)}, u32[]{:S(2)}) copy-start(bf16[12,256,256]{2,1,0:T(8,128)(2,1)} %gather_fusion) | copy-start | bytes 4718596
  35.6 11.1 %collective-permute-start.5 = (bf16[4,128,256]{2,1,0:T(8,128)(2,1)S(1)}, bf16[4,128,256]{2,1,0:T(8,128)(2,1)}, u32[]{:S(2)}, u32[]{:S(2)}) collective-permute-start(bf16[4,128,256]{2,1,0:T(8,128)(2,1)S(1)} %maximum_select_fusion.1), channel_id=1, source_target_pairs={{0,16},{4,20},{8,24},{12,28},{16,0},{20,4},{24,8},{28,12},{1,17},{... | collective-permute-start | bytes 786440 | tf_op jit(solution)/shard_map/ppermute | solution.py:32
  37.4 7.6 %collective-permute-start.7 = (bf16[3,128,128]{2,1,0:T(8,128)(2,1)S(1)}, bf16[3,128,128]{2,1,0:T(8,128)(2,1)S(1)}, u32[]{:S(2)}, u32[]{:S(2)}) collective-permute-start(bf16[3,128,128]{2,1,0:T(8,128)(2,1)S(1)} %get-tuple-element.16), channel_id=1, source_target_pairs={{0,2},{1,3},{2,0},{3,1},{4,6},{5,7},{6,4},{7,5},{8,10},{9,11},{10,... | collective-permute-start | bytes 294920 | tf_op jit(solution)/shard_map/ppermute | solution.py:44
  37.5 7.5 %collective-permute-start.6 = (bf16[3,128,128]{2,1,0:T(8,128)(2,1)S(1)}, bf16[3,128,128]{2,1,0:T(8,128)(2,1)S(1)}, u32[]{:S(2)}, u32[]{:S(2)}) collective-permute-start(bf16[3,128,128]{2,1,0:T(8,128)(2,1)S(1)} %get-tuple-element.17), channel_id=1, source_target_pairs={{0,1},{1,2},{2,3},{3,0},{4,5},{5,6},{6,7},{7,4},{8,9},{9,10},{10,1... | collective-permute-start | bytes 294920 | tf_op jit(solution)/shard_map/ppermute | solution.py:44
  49.9 1.7 %copy-start.8 = (bf16[12,128,256]{2,1,0:T(8,128)(2,1)S(1)}, bf16[12,128,256]{2,1,0:T(8,128)(2,1)}, u32[]{:S(2)}) copy-start(bf16[12,128,256]{2,1,0:T(8,128)(2,1)} %convolution_convert_fusion.5) | copy-start | bytes 2359300
  51.6 1.1 %copy-start.5 = (bf16[12,128,256]{2,1,0:T(8,128)(2,1)S(1)}, bf16[12,128,256]{2,1,0:T(8,128)(2,1)}, u32[]{:S(2)}) copy-start(bf16[12,128,256]{2,1,0:T(8,128)(2,1)} %gather_fusion.4) | copy-start | bytes 2359300
  51.7 1.4 %copy-start.7 = (bf16[12,128,256]{2,1,0:T(8,128)(2,1)S(1)}, bf16[12,128,256]{2,1,0:T(8,128)(2,1)}, u32[]{:S(2)}) copy-start(bf16[12,128,256]{2,1,0:T(8,128)(2,1)} %convolution_convert_fusion.3) | copy-start | bytes 2359300
  51.7 1.4 %copy-start.11 = (bf16[4,3,128,128]{3,2,1,0:T(8,128)(2,1)S(1)}, bf16[4,3,128,128]{3,2,1,0:T(8,128)(2,1)}, u32[]{:S(2)}) copy-start(bf16[4,3,128,128]{3,2,1,0:T(8,128)(2,1)} %pad_maximum_fusion.1) | copy-start | bytes 1179652
  53.5 0.8 copy-start.9
  59.1 2.8 %copy-start.6 = (bf16[12,128,256]{2,1,0:T(8,128)(2,1)S(1)}, bf16[12,128,256]{2,1,0:T(8,128)(2,1)}, u32[]{:S(2)}) copy-start(bf16[12,128,256]{2,1,0:T(8,128)(2,1)} %gather_fusion.4) | copy-start | bytes 2359300
  59.1 2.8 %copy-start.10 = (bf16[12,128,128]{2,1,0:T(8,128)(2,1)S(1)}, bf16[12,128,128]{2,1,0:T(8,128)(2,1)}, u32[]{:S(2)}) copy-start(bf16[12,128,128]{2,1,0:T(8,128)(2,1)} %copy-done.9) | copy-start | bytes 1179652
  61.7 1.4 %copy-start.4 = (bf16[12,256,256]{2,1,0:T(8,128)(2,1)S(1)}, bf16[12,256,256]{2,1,0:T(8,128)(2,1)}, u32[]{:S(2)}) copy-start(bf16[12,256,256]{2,1,0:T(8,128)(2,1)} %gather_fusion.3) | copy-start | bytes 4718596
  61.9 2.2 %collective-permute-start.15 = (f32[4,128,256]{2,1,0:T(8,128)S(1)}, f32[4,128,256]{2,1,0:T(8,128)S(1)}, u32[]{:S(2)}, u32[]{:S(2)}) collective-permute-start(f32[4,128,256]{2,1,0:T(8,128)S(1)} %select_bitcast_fusion), channel_id=1, source_target_pairs={{0,4},{4,0},{8,12},{12,8},{16,20},{20,16},{24,28},{28,24},{1,5},{5... | collective-permute-start | bytes 1572872 | tf_op jit(solution)/shard_map/ppermute | solution.py:19
  64.1 1.4 %copy-start.2 = (bf16[12,256,256]{2,1,0:T(8,128)(2,1)S(1)}, bf16[12,256,256]{2,1,0:T(8,128)(2,1)}, u32[]{:S(2)}) copy-start(bf16[12,256,256]{2,1,0:T(8,128)(2,1)} %gather_fusion) | copy-start | bytes 4718596
  64.4 8.1 %collective-permute-start.16 = (f32[2,128,256]{2,1,0:T(8,128)S(1)}, f32[2,128,256]{2,1,0:T(8,128)S(1)}, u32[]{:S(2)}, u32[]{:S(2)}) collective-permute-start(f32[2,128,256]{2,1,0:T(8,128)S(1)} %select_bitcast_fusion.1), channel_id=1, source_target_pairs={{0,8},{4,12},{8,0},{12,4},{16,24},{20,28},{24,16},{28,20},{1,9},{5... | collective-permute-start | bytes 786440 | tf_op jit(solution)/shard_map/ppermute | solution.py:19
  66.2 8.3 %collective-permute-start.14 = (f32[128,256]{1,0:T(8,128)S(1)}, f32[128,256]{1,0:T(8,128)S(1)}, u32[]{:S(2)}, u32[]{:S(2)}) collective-permute-start(f32[128,256]{1,0:T(8,128)S(1)} %get-tuple-element.20), channel_id=1, source_target_pairs={{0,1},{1,2},{2,3},{3,0},{4,5},{5,6},{6,7},{7,4},{8,9},{9,10},{10,1... | collective-permute-start | bytes 393224 | tf_op jit(solution)/shard_map/ppermute | solution.py:44
  66.3 12.8 %collective-permute-start.13 = (f32[128,256]{1,0:T(8,128)S(1)}, f32[128,256]{1,0:T(8,128)S(1)}, u32[]{:S(2)}, u32[]{:S(2)}) collective-permute-start(f32[128,256]{1,0:T(8,128)S(1)} %get-tuple-element.21), channel_id=1, source_target_pairs={{0,2},{1,3},{2,0},{3,1},{4,6},{5,7},{6,4},{7,5},{8,10},{9,11},{10,... | collective-permute-start | bytes 393224 | tf_op jit(solution)/shard_map/ppermute | solution.py:44
  66.8 12.2 %collective-permute-start.12 = (f32[128,256]{1,0:T(8,128)S(1)}, f32[128,256]{1,0:T(8,128)S(1)}, u32[]{:S(2)}, u32[]{:S(2)}) collective-permute-start(f32[128,256]{1,0:T(8,128)S(1)} %get-tuple-element.19), channel_id=1, source_target_pairs={{0,3},{1,0},{2,1},{3,2},{4,7},{5,4},{6,5},{7,6},{8,11},{9,8},{10,9... | collective-permute-start | bytes 393224 | tf_op jit(solution)/shard_map/ppermute | solution.py:44
  72.6 6.4 %collective-permute-start.17 = (f32[1,128,256]{2,1,0:T(8,128)S(1)}, f32[1,128,256]{2,1,0:T(8,128)S(1)}, u32[]{:S(2)}, u32[]{:S(2)}) collective-permute-start(f32[1,128,256]{2,1,0:T(8,128)S(1)} %select_bitcast_fusion.2), channel_id=1, source_target_pairs={{0,16},{4,20},{8,24},{12,28},{16,0},{20,4},{24,8},{28,12},{1,17},{... | collective-permute-start | bytes 393224 | tf_op jit(solution)/shard_map/ppermute | solution.py:19

commit v3 on v1

v3 whole, which is shorter than its diff:
```python
import jax
import jax.numpy as jnp
from jax import lax
from jax.experimental import pallas as pl
from jax.experimental.pallas import tpu as pltpu
from jax.sharding import PartitionSpec as P

LOSS_SCALE = 0.0625


def bit_reverse(values, bits):
    out = jnp.zeros_like(values)
    for b in range(bits):
        out = out | (((values >> b) & 1) << (bits - 1 - b))
    return out


def grp_reduce_scatter(parts, grp_count):
    me = lax.axis_index("grp")
    bit = 1
    while bit < grp_count:
        half = parts.reshape((2, parts.shape[0] // 2) + parts.shape[1:])
        mine = (me // bit) % 2
        keep = half[mine]
        send = half[1 - mine]
        got = lax.ppermute(send, "grp", [(i, i ^ bit) for i in range(grp_count)])
        parts = keep + got
        bit *= 2
    return parts[0]


def grp_gather(block, grp_count):
    me = lax.axis_index("grp")
    held = block[None]
    bit = 1
    while bit < grp_count:
        got = lax.ppermute(held, "grp", [(i, i ^ bit) for i in range(grp_count)])
        low = (me // bit) % 2 == 0
        held = jnp.where(
            low, jnp.concatenate([held, got], axis=0), jnp.concatenate([got, held], axis=0)
        )
        bit *= 2
    return held


def shift_ent(x, shift, ent_count):
    return lax.ppermute(x, "ent", [(i, (i + shift) % ent_count) for i in range(ent_count)])


def tile_kernel(rels_ref, groups_ref, slots_ref, alive_ref, adj_ref, src_ref, panel_ref, core_ref,
                row_ref, owner_ref, *, per_relay):
    t = pl.program_id(0)

    @pl.when(t == 0)
    def _():
        owner_ref[...] = jnp.zeros_like(owner_ref)

    @pl.when(t % per_relay == 0)
    def _():
        row_ref[...] = jnp.zeros_like(row_ref)

    own = src_ref[0]
    core = core_ref[0]
    panel = panel_ref[0]
    nt = (((1,), (1,)), ((), ()))
    mapped = jnp.dot(own, core, preferred_element_type=jnp.float32).astype(jnp.bfloat16)
    predicted = lax.dot_general(mapped, panel, nt, preferred_element_type=jnp.float32)
    scale = LOSS_SCALE * alive_ref[t].astype(jnp.float32)
    resid = ((predicted - adj_ref[0].astype(jnp.float32)) * scale).astype(jnp.bfloat16)
    product = jnp.dot(resid, panel, preferred_element_type=jnp.float32).astype(jnp.bfloat16)
    row_ref[0] += lax.dot_general(product, core, nt, preferred_element_type=jnp.float32)
    resid_t = resid.astype(jnp.float32).T.astype(jnp.bfloat16)
    column = jnp.dot(resid_t, mapped, preferred_element_type=jnp.float32).astype(jnp.bfloat16)
    slot = slots_ref[t]
    owner_ref[slot] += column.astype(jnp.float32)


def on_device(factor, cores, adjacency, tile_rels, tile_count, send_lists):
    ent_count = lax.axis_size("ent")
    grp_count = lax.axis_size("grp")
    my_ent = lax.axis_index("ent")
    tiles = tile_rels.shape[1]
    block = factor.shape[0]
    width = factor.shape[1]
    per_relay = tiles // ent_count
    head_rows = 16
    count = ent_count * per_relay
    grp_bits = grp_count.bit_length() - 1

    tile_ids = jnp.arange(tiles, dtype=jnp.int32)
    live = (tile_ids < tile_count.reshape(())).astype(jnp.float32)
    relay_ids = jnp.arange(ent_count, dtype=jnp.int32)
    slot_ids = jnp.arange(per_relay, dtype=jnp.int32)
    tile_of = slot_ids[None, :] * ent_count + (relay_ids[:, None] - my_ent) % ent_count
    adj_out = adjacency[tile_of].astype(jnp.bfloat16)
    head = jnp.concatenate(
        [tile_rels.reshape(tiles)[tile_of].astype(jnp.float32), live[tile_of]], axis=1
    )
    head = jnp.pad(head, ((0, 0), (0, width - 2 * per_relay)))
    head = jnp.broadcast_to(head[:, None, :], (ent_count, head_rows, width)).astype(jnp.bfloat16)
    own_out = jnp.concatenate(
        [jnp.broadcast_to(factor[None], (ent_count, block, width)), head], axis=1
    )
    adj_in = lax.all_to_all(adj_out, "ent", split_axis=0, concat_axis=0, tiled=True)
    own_in = lax.all_to_all(own_out, "ent", split_axis=0, concat_axis=0, tiled=True)
    group_blocks = grp_gather(factor, grp_count)

    heads = own_in[:, block].astype(jnp.float32)
    rels = heads[:, :per_relay].astype(jnp.int32).reshape(count)
    alive = heads[:, per_relay : 2 * per_relay].astype(jnp.int32).reshape(count)
    groups = send_lists.reshape(count)
    slots = bit_reverse(groups, grp_bits)

    grid_spec = pltpu.PrefetchScalarGridSpec(
        num_scalar_prefetch=4,
        grid=(count,),
        in_specs=[
            pl.BlockSpec((1, block, block), lambda t, r, g, s, a: (t, 0, 0)),
            pl.BlockSpec((1, block, width), lambda t, r, g, s, a: (t // per_relay, 0, 0)),
            pl.BlockSpec((1, block, width), lambda t, r, g, s, a: (g[t], 0, 0)),
            pl.BlockSpec((1, width, width), lambda t, r, g, s, a: (r[t], 0, 0)),
        ],
        out_specs=[
            pl.BlockSpec((1, block, width), lambda t, r, g, s, a: (t // per_relay, 0, 0)),
            pl.BlockSpec((grp_count, block, width), lambda t, r, g, s, a: (0, 0, 0)),
        ],
    )
    row_parts, owner_terms = pl.pallas_call(
        lambda *refs: tile_kernel(*refs, per_relay=per_relay),
        grid_spec=grid_spec,
        out_shape=[
            jax.ShapeDtypeStruct((ent_count, block, width), jnp.float32),
            jax.ShapeDtypeStruct((grp_count, block, width), jnp.float32),
        ],
    )(
        rels,
        groups,
        slots,
        alive,
        adj_in.reshape(count, block, block),
        own_in,
        group_blocks,
        cores,
    )

    rows = row_parts[my_ent]
    for k in range(1, ent_count):
        rows = rows + shift_ent(row_parts[(my_ent - k) % ent_count], -k, ent_count)
    owner_part = grp_reduce_scatter(owner_terms, grp_count)
    return (rows + owner_part)


def solution(mesh):
    in_specs = (
        P(("grp", "ent"), None),
        P(),
        P(("grp", "ent"), None, None),
        P(("grp", "ent"), None),
        P(("grp", "ent")),
        P(("grp", "ent"), None, None),
    )
    out_specs = P(("grp", "ent"), None)
    return jax.shard_map(
        on_device, mesh=mesh, in_specs=in_specs, out_specs=out_specs, check_vma=False
    )
```

time: 86.1 us -> 85.4 us (level)
  Pallas kernels: 0 us -> 21.1 us
  matrix products: 12.2 us -> 0 us
  blocking collectives: 9.87 us -> 0 us
  local copies, waits for them, and re-layouts: 13.2 us -> 6.47 us
  starting transfers between devices: 13.1 us -> 18.2 us
  waiting for transfers between devices: 26.7 us -> 31.6 us
  other arithmetic: 9.27 us -> 6.26 us
    pallas_call x0 -> x1, Pallas kernels: none -> 21.1 us  [on_device(): pl.pallas_call(lambda *refs: tile_kernel(*refs, per_relay=per_relay), gri...]
    all_to_all x2, waiting for transfers between devices: 26.7 us -> 10.9 us  [the longest x1 7.9 us: on_device(): lax.all_to_all(own_out, 'ent', split_axis=0, concat_axis=0, tiled=True)]
    ppermute x0 -> x6, waiting for transfers between devices: none -> 14.8 us  [the longest x3 9.35 us: grp_gather(): got = lax.ppermute(held, 'grp', [(i, i ^ bit) for i in range(grp_count)])]
    dot_general x6 -> x0, matrix products: 12.2 us -> none  [the longest x1 3.84 us: on_device(): jnp.einsum('ejbs,ejrs->ebr', product.reshape(ent_count, per_relay, block,...]
    all_gather x1 -> x0, blocking collectives: 9.87 us -> none  [on_device(): group_blocks = lax.all_gather(factor, 'grp', axis=0, tiled=False)]
    ppermute x3, waiting for transfers between devices: 0.01 us -> 5.99 us  [grp_reduce_scatter(): got = lax.ppermute(send, 'grp', [(i, i ^ bit) for i in range(grp_count)])]
    gather x4 -> x2, local copies, waits for them, and re-layouts: 6.88 us -> 1.35 us  [the longest x1 0.71 us: on_device(): tile_rels.reshape(tiles)[tile_of].astype(jnp.float32)]
    ppermute x0 -> x6, starting transfers between devices: none -> 5.24 us  [the longest x3 3.21 us: grp_gather(): got = lax.ppermute(held, 'grp', [(i, i ^ bit) for i in range(grp_count)])]
  transfers between devices with their start and end apart: 5 -> 11, of which waited for: 2 -> 8; matrix products, arithmetic and copies ran while one was open for 12% -> 6% of each run, Pallas kernels for 0% -> 0%
where the time goes in v3:
time: 85.4 us; the launch traced here: 84.5 us
  waiting for transfers between devices  31.6 us (37%)
  Pallas kernels  21.1 us (25%)
  starting transfers between devices  18.2 us (21%)
  local copies, waits for them, and re-layouts  6.47 us (8%)
  other arithmetic  6.26 us (7%)
  between operations  0.87 us (1%)
    pallas_call x1, Pallas kernels, on_device(): pl.pallas_call(lambda *refs: tile_kernel(*refs, per_relay=per_relay), gri...  21.1 us
    ppermute x3, waiting for transfers between devices, grp_gather(): got = lax.ppermute(held, 'grp', [(i, i ^ bit) for i in range(grp_count)])  9.35 us
    all_to_all x1, waiting for transfers between devices, on_device(): lax.all_to_all(own_out, 'ent', split_axis=0, concat_axis=0, tiled=True)  7.9 us
    all_to_all x1, starting transfers between devices, on_device(): lax.all_to_all(own_out, 'ent', split_axis=0, concat_axis=0, tiled=True)  6.33 us
    ppermute x3, waiting for transfers between devices, grp_reduce_scatter(): got = lax.ppermute(send, 'grp', [(i, i ^ bit) for i in range(grp_count)])  5.99 us
    ppermute x3, waiting for transfers between devices, shift_ent(): lax.ppermute(x, 'ent', [(i, (i + shift) % ent_count) for i in range(ent_c...  5.4 us
    all_to_all x1, starting transfers between devices, on_device(): lax.all_to_all(adj_out, 'ent', split_axis=0, concat_axis=0, tiled=True)  3.49 us
    ppermute x3, starting transfers between devices, grp_gather(): got = lax.ppermute(held, 'grp', [(i, i ^ bit) for i in range(grp_count)])  3.21 us
  transfers between devices with their start and end apart: 11, of which 8 were waited for; matrix products, arithmetic and copies ran while one was open for 6% of the time, Pallas kernels for 0%

profile of v3, /device:TPU:0, one launch (start us, length us, event | category | flops | bytes accessed | tf_op | source)
XLA Modules:
  0.0 84.5 jit_solution(9851422933651448082)
XLA Ops:
  0.0 0.0 copy-start
  0.0 0.0 copy-start.1
  0.0 0.1 compare_select_fusion
  0.1 0.1 reshape.123
  0.9 0.0 copy-start.5
  0.9 0.7 gather_fusion.1
  1.6 0.1 reshape.149
  1.7 0.0 copy-done.1
  1.7 0.7 gather_fusion
  2.4 0.1 reshape.151
  2.5 0.1 fusion.4
  2.5 0.0 copy-done.5
  2.6 0.7 pad_maximum_fusion
  3.3 6.3 %all-to-all-start = ((bf16[4,144,256]{2,1,0:T(8,128)(2,1)}), bf16[4,144,256]{2,1,0:T(8,128)(2,1)S(1)}, u32[]{:S(2)}, u32[]{:S(2)}) async-start(bf16[4,144,256]{2,1,0:T(8,128)(2,1)} %pad_maximum_fusion), calls=%async_computation | async-start | bytes 589824 | tf_op jit(solution)/shard_map/all_to_all | solution.py:105
  9.7 0.0 copy-done
  9.7 0.6 gather_fusion.2
  10.3 0.0 copy-start.7
  10.3 1.1 %convert_element_type.34 = bf16[24,128,128]{2,1,0:T(8,128)(2,1)} convert(s32[24,128,128]{2,1,0:T(8,128)S(1)} %gather_fusion.2) | non-fusion elementwise | flops 393216 | bytes 2359296 | tf_op jit(solution)/shard_map/convert_element_type | solution.py:95
  11.4 7.9 %all-to-all-done.refs_5_ = bf16[4,144,256]{2,1,0:T(8,128)(2,1)S(1)} async-done(((bf16[4,144,256]{2,1,0:T(8,128)(2,1)}), bf16[4,144,256]{2,1,0:T(8,128)(2,1)S(1)}, u32[]{:S(2)}, u32[]{:S(2)}) %all-to-all-start) | async-done | bytes 294944 | tf_op jit(solution)/shard_map/all_to_all | solution.py:105
  19.3 0.0 copy-start.3
  19.3 3.5 %all-to-all-start.1 = ((bf16[4,6,128,128]{3,2,1,0:T(8,128)(2,1)}), bf16[4,6,128,128]{3,2,1,0:T(8,128)(2,1)S(1)}, u32[]{:S(2)}, u32[]{:S(2)}) async-start(bf16[4,6,128,128]{3,2,1,0:T(8,128)(2,1)} %bitcast.39), calls=%async_computation.1 | async-start | bytes 1572864 | tf_op jit(solution)/shard_map/all_to_all | solution.py:104
  22.8 0.1 collective-permute-start
  22.9 0.0 copy-done.7
  22.9 0.1 reshape.115.refs_1_
  23.0 0.0 copy-start.6
  23.0 1.1 %collective-permute-done = bf16[1,128,256]{2,1,0:T(8,128)(2,1)S(1)} collective-permute-done((bf16[1,128,256]{2,1,0:T(8,128)(2,1)S(1)}, bf16[1,128,256]{2,1,0:T(8,128)(2,1)S(1)}, u32[]{:S(2)}, u32[]{:S(2)}) %collective-permute-start) | collective-permute-done | bytes 65568 | tf_op jit(solution)/shard_map/ppermute | solution.py:37
  24.1 1.6 %collective-permute-start.1 = (bf16[2,128,256]{2,1,0:T(8,128)(2,1)S(1)}, bf16[2,128,256]{2,1,0:T(8,128)(2,1)S(1)}, u32[]{:S(2)}, u32[]{:S(2)}) collective-permute-start(bf16[2,128,256]{2,1,0:T(8,128)(2,1)S(1)} %maximum_select_fusion.2), channel_id=1, source_target_pairs={{0,8},{4,12},{8,0},{12,4},{16,24},{20,28},{24,16},{28,20},{1,9},{5... | collective-permute-start | bytes 393224 | tf_op jit(solution)/shard_map/ppermute | solution.py:37
  25.7 0.5 shift-left_or_fusion.refs_2_
  26.2 3.5 %collective-permute-done.1 = bf16[2,128,256]{2,1,0:T(8,128)(2,1)S(1)} collective-permute-done((bf16[2,128,256]{2,1,0:T(8,128)(2,1)S(1)}, bf16[2,128,256]{2,1,0:T(8,128)(2,1)S(1)}, u32[]{:S(2)}, u32[]{:S(2)}) %collective-permute-start.1) | collective-permute-done | bytes 131104 | tf_op jit(solution)/shard_map/ppermute | solution.py:37
  29.8 1.6 %collective-permute-start.2 = (bf16[4,128,256]{2,1,0:T(8,128)(2,1)S(1)}, bf16[4,128,256]{2,1,0:T(8,128)(2,1)S(1)}, u32[]{:S(2)}, u32[]{:S(2)}) collective-permute-start(bf16[4,128,256]{2,1,0:T(8,128)(2,1)S(1)} %maximum_select_fusion.1), channel_id=1, source_target_pairs={{0,16},{4,20},{8,24},{12,28},{16,0},{20,4},{24,8},{28,12},{1,17},{... | collective-permute-start | bytes 786440 | tf_op jit(solution)/shard_map/ppermute | solution.py:37
  31.4 0.1 slice_convert_fusion.1
  31.4 0.6 reshape.114.refs_0_
  32.0 0.6 reshape.116.refs_3_
  32.6 4.7 %collective-permute-done.2 = bf16[4,128,256]{2,1,0:T(8,128)(2,1)S(1)} collective-permute-done((bf16[4,128,256]{2,1,0:T(8,128)(2,1)S(1)}, bf16[4,128,256]{2,1,0:T(8,128)(2,1)S(1)}, u32[]{:S(2)}, u32[]{:S(2)}) %collective-permute-start.2) | collective-permute-done | bytes 262176 | tf_op jit(solution)/shard_map/ppermute | solution.py:37
  37.4 0.9 %maximum_select_fusion.refs_6_ = bf16[8,128,256]{2,1,0:T(8,128)(2,1)} fusion(bf16[4,128,256]{2,1,0:T(8,128)(2,1)S(1)} %collective-permute-done.2, bf16[4,128,256]{2,1,0:T(8,128)(2,1)S(1)} %maximum_select_fusion.1, pred[]{:T(512)S(6)} %eq.21), kind=kLoop, calls=%fused_computation.3 | loop fusion | flops 786432 | bytes 1048577 | tf_op jit(solution)/shard_map/jit(_where)/select_n | solution.py:39
  38.3 0.0 copy-done.3
  38.3 3.0 %all-to-all-done.1 = bf16[4,6,128,128]{3,2,1,0:T(8,128)(2,1)S(1)} async-done(((bf16[4,6,128,128]{3,2,1,0:T(8,128)(2,1)}), bf16[4,6,128,128]{3,2,1,0:T(8,128)(2,1)S(1)}, u32[]{:S(2)}, u32[]{:S(2)}) %all-to-all-start.1) | async-done | bytes 786464 | tf_op jit(solution)/shard_map/all_to_all | solution.py:104
  41.3 0.0 copy-start.2
  41.3 0.0 copy-done.6
  41.3 0.9 %copy-done.2 = bf16[4,6,128,128]{3,2,1,0:T(8,128)(2,1)} copy-done((bf16[4,6,128,128]{3,2,1,0:T(8,128)(2,1)}, bf16[4,6,128,128]{3,2,1,0:T(8,128)(2,1)S(1)}, u32[]{:S(2)}) %copy-start.2) | copy-done | bytes 786456
  42.2 21.1 %shard_map.64 = (f32[4,128,256]{2,1,0:T(8,128)}, f32[8,128,256]{2,1,0:T(8,128)}) custom-call(s32[24]{0:T(128)} %reshape.114.refs_0_, s32[24]{0:T(128)} %copy-done.6, s32[24]{0:T(128)} %shift-left_or_fusion.refs_2_, s32[24]{0:T(128)} %reshape.116.refs_3_, bf16[24,128,128]{2,1,0:T(8,128)(2,1)} %bitcast.38, bf16[4,144,256]{2,1,0:T(8,128)(2,1)} %copy-done.3, ...), custom_call_target="tpu_custom_call" | custom-call | tf_op jit(solution)/shard_map/pallas_call | solution.py:128
  63.3 0.0 copy-start.4
  63.3 1.1 %dynamic-slice_bitcast_fusion = f32[4,128,256]{2,1,0:T(8,128)S(1)} fusion(f32[2,4,128,256]{3,2,1,0:T(8,128)} %bitcast.42, s32[]{:T(128)S(6)} %select_n.142), kind=kLoop, calls=%fused_computation.5 | loop fusion | bytes 1048580 | tf_op jit(solution)/shard_map/squeeze | solution.py:25
  64.4 0.1 collective-permute-start.6
  64.5 1.9 %collective-permute-done.6 = f32[4,128,256]{2,1,0:T(8,128)S(1)} collective-permute-done((f32[4,128,256]{2,1,0:T(8,128)S(1)}, f32[4,128,256]{2,1,0:T(8,128)S(1)}, u32[]{:S(2)}, u32[]{:S(2)}) %collective-permute-start.6) | collective-permute-done | bytes 524320 | tf_op jit(solution)/shard_map/ppermute | solution.py:26
  66.4 1.1 %bitcast_add_fusion = f32[4,128,256]{2,1,0:T(8,128)S(1)} fusion(f32[4,128,256]{2,1,0:T(8,128)S(1)} %collective-permute-done.6, f32[2,4,128,256]{3,2,1,0:T(8,128)} %bitcast.43, s32[]{:T(128)S(6)} %select_n.141), kind=kLoop, calls=%fused_computation.4 | loop fusion | flops 131072 | bytes 1572868 | tf_op jit(solution)/shard_map/add | solution.py:27
  67.5 1.5 %collective-permute-start.7 = (f32[2,128,256]{2,1,0:T(8,128)S(1)}, f32[2,128,256]{2,1,0:T(8,128)S(1)}, u32[]{:S(2)}, u32[]{:S(2)}) collective-permute-start(f32[2,128,256]{2,1,0:T(8,128)S(1)} %dynamic-slice_bitcast_fusion.1), channel_id=1, source_target_pairs={{0,8},{4,12},{8,0},{12,4},{16,24},{20,28},{24,16},{28,20},{1,9},{5... | collective-permute-start | bytes 786440 | tf_op jit(solution)/shard_map/ppermute | solution.py:26
  69.1 0.0 copy-done.4
  69.1 0.7 dynamic-slice_bitcast_fusion.4
  69.8 1.4 %collective-permute-start.3 = (f32[128,256]{1,0:T(8,128)}, f32[128,256]{1,0:T(8,128)S(1)}, u32[]{:S(2)}, u32[]{:S(2)}) collective-permute-start(f32[128,256]{1,0:T(8,128)} %get-tuple-element.9), channel_id=1, source_target_pairs={{0,3},{1,0},{2,1},{3,2},{4,7},{5,4},{6,5},{7,6},{8,11},{9,8},{10,9... | collective-permute-start | bytes 393224 | tf_op jit(solution)/shard_map/ppermute | solution.py:47
  71.2 0.0 collective-permute-start.4
  71.2 0.6 collective-permute-start.5
  71.8 4.1 %collective-permute-done.7 = f32[2,128,256]{2,1,0:T(8,128)S(1)} collective-permute-done((f32[2,128,256]{2,1,0:T(8,128)S(1)}, f32[2,128,256]{2,1,0:T(8,128)S(1)}, u32[]{:S(2)}, u32[]{:S(2)}) %collective-permute-start.7) | collective-permute-done | bytes 262176 | tf_op jit(solution)/shard_map/ppermute | solution.py:26
  76.0 1.5 %collective-permute-start.8 = (f32[1,128,256]{2,1,0:T(8,128)S(1)}, f32[1,128,256]{2,1,0:T(8,128)S(1)}, u32[]{:S(2)}, u32[]{:S(2)}) collective-permute-start(f32[1,128,256]{2,1,0:T(8,128)S(1)} %constant_dynamic-slice_fusion), channel_id=1, source_target_pairs={{0,16},{4,20},{8,24},{12,28},{16,0},{20,4},{24,8},{28,12},{1,17},{... | collective-permute-start | bytes 393224 | tf_op jit(solution)/shard_map/ppermute | solution.py:26
  77.5 0.0 collective-permute-done.3
  77.5 5.4 %collective-permute-done.4 = f32[128,256]{1,0:T(8,128)S(1)} collective-permute-done((f32[128,256]{1,0:T(8,128)}, f32[128,256]{1,0:T(8,128)S(1)}, u32[]{:S(2)}, u32[]{:S(2)}) %collective-permute-start.4) | collective-permute-done | bytes 131104 | tf_op jit(solution)/shard_map/ppermute | solution.py:47
  82.9 0.0 collective-permute-done.5
  82.9 0.0 collective-permute-done.8
  82.9 1.6 %bitcast_add_fusion.2 = f32[128,256]{1,0:T(8,128)} fusion(f32[128,256]{1,0:T(8,128)} %collective-permute-done.5, f32[128,256]{1,0:T(8,128)S(1)} %collective-permute-done.4, f32[128,256]{1,0:T(8,128)S(1)} %collective-permute-done.3, f32[1,128,256]{2,1,0:T(8,128)S(1)} %collective-permute-done.8, f32[2,128,256]{2,1,0:T(8,128)S(1)} %bitcast_add_fusion.1, ...), kind=kLoop, calls=%fused_computation.11 | loop fusion | flops 163840 | bytes 917512 | tf_op jit(solution)/shard_map/add | solution.py:150
  (14 shorter events, 0.2 us)
Async XLA Ops:
  0.0 9.7 %copy-start = (s32[24,128,128]{2,1,0:T(8,128)S(1)}, s32[24,128,128]{2,1,0:T(8,128)}, u32[]{:S(2)}) copy-start(s32[24,128,128]{2,1,0:T(8,128)} %param.8) | copy-start | bytes 4718596
  0.0 1.7 %copy-start.1 = (s32[1,24]{1,0:T(1,128)S(1)}, s32[1,24]{1,0:T(1,128)}, u32[]{:S(2)}) copy-start(s32[1,24]{1,0:T(1,128)} %param.9) | copy-start | bytes 292
  0.9 1.7 %copy-start.5 = (bf16[128,256]{1,0:T(8,128)(2,1)S(1)}, bf16[128,256]{1,0:T(8,128)(2,1)}, u32[]{:S(2)}) copy-start(bf16[128,256]{1,0:T(8,128)(2,1)} %param.6) | copy-start | bytes 196612
  3.3 15.9 %all-to-all-start = ((bf16[4,144,256]{2,1,0:T(8,128)(2,1)}), bf16[4,144,256]{2,1,0:T(8,128)(2,1)S(1)}, u32[]{:S(2)}, u32[]{:S(2)}) async-start(bf16[4,144,256]{2,1,0:T(8,128)(2,1)} %pad_maximum_fusion), calls=%async_computation | async-start | bytes 589824 | tf_op jit(solution)/shard_map/all_to_all | solution.py:105
  10.3 12.6 %copy-start.7 = (s32[1,4,6]{2,1,0:T(4,128)S(1)}, s32[1,4,6]{2,1,0:T(4,128)}, u32[]{:S(2)}) copy-start(s32[1,4,6]{2,1,0:T(4,128)} %param.11) | copy-start | bytes 292
  19.3 19.0 %copy-start.3 = (bf16[4,144,256]{2,1,0:T(8,128)(2,1)}, bf16[4,144,256]{2,1,0:T(8,128)(2,1)S(1)}, u32[]{:S(2)}) copy-start(bf16[4,144,256]{2,1,0:T(8,128)(2,1)S(1)} %all-to-all-done.refs_5_) | copy-start | bytes 884740
  19.3 22.0 %all-to-all-start.1 = ((bf16[4,6,128,128]{3,2,1,0:T(8,128)(2,1)}), bf16[4,6,128,128]{3,2,1,0:T(8,128)(2,1)S(1)}, u32[]{:S(2)}, u32[]{:S(2)}) async-start(bf16[4,6,128,128]{3,2,1,0:T(8,128)(2,1)} %bitcast.39), calls=%async_computation.1 | async-start | bytes 1572864 | tf_op jit(solution)/shard_map/all_to_all | solution.py:104
  22.8 1.3 %collective-permute-start = (bf16[1,128,256]{2,1,0:T(8,128)(2,1)S(1)}, bf16[1,128,256]{2,1,0:T(8,128)(2,1)S(1)}, u32[]{:S(2)}, u32[]{:S(2)}) collective-permute-start(bf16[1,128,256]{2,1,0:T(8,128)(2,1)S(1)} %bitcast.44), channel_id=1, source_target_pairs={{0,4},{4,0},{8,12},{12,8},{16,20},{20,16},{24,28},{28,24},{1,5},{5... | collective-permute-start | bytes 196616 | tf_op jit(solution)/shard_map/ppermute | solution.py:37
  23.0 18.3 %copy-start.6 = (s32[24]{0:T(128)}, s32[24]{0:T(128)S(1)}, u32[]{:S(2)}) copy-start(s32[24]{0:T(128)S(1)} %reshape.115.refs_1_) | copy-start | bytes 292
  24.1 5.6 %collective-permute-start.1 = (bf16[2,128,256]{2,1,0:T(8,128)(2,1)S(1)}, bf16[2,128,256]{2,1,0:T(8,128)(2,1)S(1)}, u32[]{:S(2)}, u32[]{:S(2)}) collective-permute-start(bf16[2,128,256]{2,1,0:T(8,128)(2,1)S(1)} %maximum_select_fusion.2), channel_id=1, source_target_pairs={{0,8},{4,12},{8,0},{12,4},{16,24},{20,28},{24,16},{28,20},{1,9},{5... | collective-permute-start | bytes 393224 | tf_op jit(solution)/shard_map/ppermute | solution.py:37
  29.8 7.6 %collective-permute-start.2 = (bf16[4,128,256]{2,1,0:T(8,128)(2,1)S(1)}, bf16[4,128,256]{2,1,0:T(8,128)(2,1)S(1)}, u32[]{:S(2)}, u32[]{:S(2)}) collective-permute-start(bf16[4,128,256]{2,1,0:T(8,128)(2,1)S(1)} %maximum_select_fusion.1), channel_id=1, source_target_pairs={{0,16},{4,20},{8,24},{12,28},{16,0},{20,4},{24,8},{28,12},{1,17},{... | collective-permute-start | bytes 786440 | tf_op jit(solution)/shard_map/ppermute | solution.py:37
  41.3 0.9 %copy-start.2 = (bf16[4,6,128,128]{3,2,1,0:T(8,128)(2,1)}, bf16[4,6,128,128]{3,2,1,0:T(8,128)(2,1)S(1)}, u32[]{:S(2)}) copy-start(bf16[4,6,128,128]{3,2,1,0:T(8,128)(2,1)S(1)} %all-to-all-done.1) | copy-start | bytes 2359300
  63.3 5.8 %copy-start.4 = (f32[4,128,256]{2,1,0:T(8,128)S(1)}, f32[4,128,256]{2,1,0:T(8,128)}, u32[]{:S(2)}) copy-start(f32[4,128,256]{2,1,0:T(8,128)} %get-tuple-element.7) | copy-start | bytes 1572868
  64.4 2.0 %collective-permute-start.6 = (f32[4,128,256]{2,1,0:T(8,128)S(1)}, f32[4,128,256]{2,1,0:T(8,128)S(1)}, u32[]{:S(2)}, u32[]{:S(2)}) collective-permute-start(f32[4,128,256]{2,1,0:T(8,128)S(1)} %dynamic-slice_bitcast_fusion), channel_id=1, source_target_pairs={{0,4},{4,0},{8,12},{12,8},{16,20},{20,16},{24,28},{28,24},{1,5},{5... | collective-permute-start | bytes 1572872 | tf_op jit(solution)/shard_map/ppermute | solution.py:26
  67.5 8.4 %collective-permute-start.7 = (f32[2,128,256]{2,1,0:T(8,128)S(1)}, f32[2,128,256]{2,1,0:T(8,128)S(1)}, u32[]{:S(2)}, u32[]{:S(2)}) collective-permute-start(f32[2,128,256]{2,1,0:T(8,128)S(1)} %dynamic-slice_bitcast_fusion.1), channel_id=1, source_target_pairs={{0,8},{4,12},{8,0},{12,4},{16,24},{20,28},{24,16},{28,20},{1,9},{5... | collective-permute-start | bytes 786440 | tf_op jit(solution)/shard_map/ppermute | solution.py:26
  69.8 7.7 %collective-permute-start.3 = (f32[128,256]{1,0:T(8,128)}, f32[128,256]{1,0:T(8,128)S(1)}, u32[]{:S(2)}, u32[]{:S(2)}) collective-permute-start(f32[128,256]{1,0:T(8,128)} %get-tuple-element.9), channel_id=1, source_target_pairs={{0,3},{1,0},{2,1},{3,2},{4,7},{5,4},{6,5},{7,6},{8,11},{9,8},{10,9... | collective-permute-start | bytes 393224 | tf_op jit(solution)/shard_map/ppermute | solution.py:47
  71.2 11.7 %collective-permute-start.4 = (f32[128,256]{1,0:T(8,128)}, f32[128,256]{1,0:T(8,128)S(1)}, u32[]{:S(2)}, u32[]{:S(2)}) collective-permute-start(f32[128,256]{1,0:T(8,128)} %get-tuple-element.11), channel_id=1, source_target_pairs={{0,2},{1,3},{2,0},{3,1},{4,6},{5,7},{6,4},{7,5},{8,10},{9,11},{10,... | collective-permute-start | bytes 393224 | tf_op jit(solution)/shard_map/ppermute | solution.py:47
  71.2 11.7 %collective-permute-start.5 = (f32[128,256]{1,0:T(8,128)S(1)}, f32[128,256]{1,0:T(8,128)}, u32[]{:S(2)}, u32[]{:S(2)}) collective-permute-start(f32[128,256]{1,0:T(8,128)S(1)} %get-tuple-element.10), channel_id=1, source_target_pairs={{0,1},{1,2},{2,3},{3,0},{4,5},{5,6},{6,7},{7,4},{8,9},{9,10},{10,1... | collective-permute-start | bytes 393224 | tf_op jit(solution)/shard_map/ppermute | solution.py:47
  76.0 6.9 %collective-permute-start.8 = (f32[1,128,256]{2,1,0:T(8,128)S(1)}, f32[1,128,256]{2,1,0:T(8,128)S(1)}, u32[]{:S(2)}, u32[]{:S(2)}) collective-permute-start(f32[1,128,256]{2,1,0:T(8,128)S(1)} %constant_dynamic-slice_fusion), channel_id=1, source_target_pairs={{0,16},{4,20},{8,24},{12,28},{16,0},{20,4},{24,8},{28,12},{1,17},{... | collective-permute-start | bytes 393224 | tf_op jit(solution)/shard_map/ppermute | solution.py:26

commit v4 on v3

v4 whole, which is shorter than its diff:
```python
import jax
import jax.numpy as jnp
from jax import lax
from jax.experimental import pallas as pl
from jax.experimental.pallas import tpu as pltpu
from jax.sharding import PartitionSpec as P

LOSS_SCALE = 0.0625


def bit_reverse(values, bits):
    out = jnp.zeros_like(values)
    for b in range(bits):
        out = out | (((values >> b) & 1) << (bits - 1 - b))
    return out


def grp_reduce_scatter(parts, grp_count):
    me = lax.axis_index("grp")
    bit = 1
    while bit < grp_count:
        half = parts.reshape((2, parts.shape[0] // 2) + parts.shape[1:])
        mine = (me // bit) % 2
        keep = half[mine]
        send = half[1 - mine]
        got = lax.ppermute(send, "grp", [(i, i ^ bit) for i in range(grp_count)])
        parts = keep + got
        bit *= 2
    return parts[0]


def grp_gather(block, grp_count):
    me = lax.axis_index("grp")
    held = block[None]
    bit = 1
    while bit < grp_count:
        got = lax.ppermute(held, "grp", [(i, i ^ bit) for i in range(grp_count)])
        low = (me // bit) % 2 == 0
        held = jnp.where(
            low, jnp.concatenate([held, got], axis=0), jnp.concatenate([got, held], axis=0)
        )
        bit *= 2
    return held


def shift_ent(x, shift, ent_count):
    return lax.ppermute(x, "ent", [(i, (i + shift) % ent_count) for i in range(ent_count)])


def tile_kernel(rels_ref, groups_ref, slots_ref, alive_ref, in_ref, core_ref, panel_ref,
                row_ref, owner_ref, *, per_relay, block):
    e = pl.program_id(0)

    @pl.when(e == 0)
    def _():
        owner_ref[...] = jnp.zeros_like(owner_ref)

    nt = (((1,), (1,)), ((), ()))
    base = per_relay * block
    own_lo = in_ref[0, base : base + block, :]
    own_hi = in_ref[0, base + block : base + 2 * block, :]
    acc = None
    for j in range(per_relay):
        t = e * per_relay + j
        r = rels_ref[t]
        core = core_ref[r]
        panel = panel_ref[groups_ref[t]]
        mapped = (
            jnp.dot(own_lo, core[:block], preferred_element_type=jnp.float32)
            + jnp.dot(own_hi, core[block:], preferred_element_type=jnp.float32)
        ).astype(jnp.bfloat16)
        predicted = lax.dot_general(mapped, panel, nt, preferred_element_type=jnp.float32)
        scale = LOSS_SCALE * alive_ref[t].astype(jnp.float32)
        adj = in_ref[0, j * block : (j + 1) * block, :].astype(jnp.float32)
        resid = ((predicted - adj) * scale).astype(jnp.bfloat16)
        product = jnp.dot(resid, panel, preferred_element_type=jnp.float32).astype(jnp.bfloat16)
        part = lax.dot_general(product, core, nt, preferred_element_type=jnp.float32)
        acc = part if acc is None else acc + part
        resid_t = resid.astype(jnp.float32).T.astype(jnp.bfloat16)
        column = jnp.dot(resid_t, mapped, preferred_element_type=jnp.float32).astype(jnp.bfloat16)
        slot = slots_ref[t]
        owner_ref[slot] += column.astype(jnp.float32)
    row_ref[0] = acc


def on_device(factor, cores, adjacency, tile_rels, tile_count, send_lists):
    ent_count = lax.axis_size("ent")
    grp_count = lax.axis_size("grp")
    my_ent = lax.axis_index("ent")
    tiles = tile_rels.shape[1]
    block = factor.shape[0]
    width = factor.shape[1]
    per_relay = tiles // ent_count
    head_rows = 16
    count = ent_count * per_relay
    grp_bits = grp_count.bit_length() - 1
    relations = cores.shape[0]

    tile_ids = jnp.arange(tiles, dtype=jnp.int32)
    live = (tile_ids < tile_count.reshape(())).astype(jnp.float32)
    relay_ids = jnp.arange(ent_count, dtype=jnp.int32)
    slot_ids = jnp.arange(per_relay, dtype=jnp.int32)
    tile_of = slot_ids[None, :] * ent_count + (relay_ids[:, None] - my_ent) % ent_count
    adj_out = adjacency[tile_of].astype(jnp.bfloat16).reshape(ent_count, per_relay * block, block)
    halves = jnp.concatenate([factor[:, :block], factor[:, block:]], axis=0)
    head = jnp.concatenate(
        [tile_rels.reshape(tiles)[tile_of].astype(jnp.float32), live[tile_of]], axis=1
    )
    head = jnp.pad(head, ((0, 0), (0, block - 2 * per_relay)))
    head = jnp.broadcast_to(head[:, None, :], (ent_count, head_rows, block)).astype(jnp.bfloat16)
    outgoing = jnp.concatenate(
        [adj_out, jnp.broadcast_to(halves[None], (ent_count,) + halves.shape), head], axis=1
    )
    arrived = lax.all_to_all(outgoing, "ent", split_axis=0, concat_axis=0, tiled=True)
    group_blocks = grp_gather(factor, grp_count)

    heads = arrived[:, -head_rows].astype(jnp.float32)
    rels = heads[:, :per_relay].astype(jnp.int32).reshape(count)
    alive = heads[:, per_relay : 2 * per_relay].astype(jnp.int32).reshape(count)
    groups = send_lists.reshape(count)
    slots = bit_reverse(groups, grp_bits)
    rows_in = arrived.shape[1]

    grid_spec = pltpu.PrefetchScalarGridSpec(
        num_scalar_prefetch=4,
        grid=(ent_count,),
        in_specs=[
            pl.BlockSpec((1, rows_in, block), lambda e, r, g, s, a: (e, 0, 0)),
            pl.BlockSpec((relations, width, width), lambda e, r, g, s, a: (0, 0, 0)),
            pl.BlockSpec((grp_count, block, width), lambda e, r, g, s, a: (0, 0, 0)),
        ],
        out_specs=[
            pl.BlockSpec((1, block, width), lambda e, r, g, s, a: (e, 0, 0)),
            pl.BlockSpec((grp_count, block, width), lambda e, r, g, s, a: (0, 0, 0)),
        ],
    )
    row_parts, owner_terms = pl.pallas_call(
        lambda *refs: tile_kernel(*refs, per_relay=per_relay, block=block),
        grid_spec=grid_spec,
        out_shape=[
            jax.ShapeDtypeStruct((ent_count, block, width), jnp.float32),
            jax.ShapeDtypeStruct((grp_count, block, width), jnp.float32),
        ],
    )(rels, groups, slots, alive, arrived, cores, group_blocks)

    rows = row_parts[my_ent]
    for k in range(1, ent_count):
        rows = rows + shift_ent(row_parts[(my_ent - k) % ent_count], -k, ent_count)
    owner_part = grp_reduce_scatter(owner_terms, grp_count)
    return rows + owner_part


def solution(mesh):
    in_specs = (
        P(("grp", "ent"), None),
        P(),
        P(("grp", "ent"), None, None),
        P(("grp", "ent"), None),
        P(("grp", "ent")),
        P(("grp", "ent"), None, None),
    )
    out_specs = P(("grp", "ent"), None)
    return jax.shard_map(
        on_device, mesh=mesh, in_specs=in_specs, out_specs=out_specs, check_vma=False
    )
```

time: 85.4 us -> 74 us (0.87)
  Pallas kernels: 21.1 us -> 13.2 us
  starting transfers between devices: 18.2 us -> 14.8 us
  waiting for transfers between devices: 31.6 us -> 32.8 us
    pallas_call x1, Pallas kernels: 21.1 us -> 13.2 us  [on_device(): pl.pallas_call(lambda *refs: tile_kernel(*refs, per_relay=per_relay, bloc...]
    all_to_all x2 -> x1, starting transfers between devices: 9.82 us -> 6.46 us  [on_device(): lax.all_to_all(outgoing, 'ent', split_axis=0, concat_axis=0, tiled=True)]
    ppermute x3, waiting for transfers between devices: 9.35 us -> 10.7 us  [grp_gather(): got = lax.ppermute(held, 'grp', [(i, i ^ bit) for i in range(grp_count)])]
    convert_element_type x2, other arithmetic: 1.05 us -> 0.16 us  [the longest x1 0.16 us: on_device(): adjacency[tile_of].astype(jnp.bfloat16)]
    all_to_all x2 -> x1, waiting for transfers between devices: 10.9 us -> 10.7 us  [on_device(): lax.all_to_all(outgoing, 'ent', split_axis=0, concat_axis=0, tiled=True)]
  transfers between devices with their start and end apart: 11 -> 10, of which waited for: 8 -> 7; matrix products, arithmetic and copies ran while one was open for 6% -> 3% of each run, Pallas kernels for 0% -> 0%
where the time goes in v4:
time: 74 us; the launch traced here: 73.7 us
  waiting for transfers between devices  32.8 us (44%)
  starting transfers between devices  14.8 us (20%)
  Pallas kernels  13.2 us (18%)
  local copies, waits for them, and re-layouts  6.33 us (9%)
  other arithmetic  5.68 us (8%)
  between operations  0.78 us (1%)
    pallas_call x1, Pallas kernels, on_device(): pl.pallas_call(lambda *refs: tile_kernel(*refs, per_relay=per_relay, bloc...  13.2 us
    ppermute x3, waiting for transfers between devices, grp_gather(): got = lax.ppermute(held, 'grp', [(i, i ^ bit) for i in range(grp_count)])  10.7 us
    all_to_all x1, waiting for transfers between devices, on_device(): lax.all_to_all(outgoing, 'ent', split_axis=0, concat_axis=0, tiled=True)  10.7 us
    all_to_all x1, starting transfers between devices, on_device(): lax.all_to_all(outgoing, 'ent', split_axis=0, concat_axis=0, tiled=True)  6.46 us
    ppermute x3, waiting for transfers between devices, grp_reduce_scatter(): got = lax.ppermute(send, 'grp', [(i, i ^ bit) for i in range(grp_count)])  5.99 us
    ppermute x3, waiting for transfers between devices, shift_ent(): lax.ppermute(x, 'ent', [(i, (i + shift) % ent_count) for i in range(ent_c...  5.39 us
    ppermute x3, starting transfers between devices, grp_reduce_scatter(): got = lax.ppermute(send, 'grp', [(i, i ^ bit) for i in range(grp_count)])  3.21 us
    ppermute x3, starting transfers between devices, grp_gather(): got = lax.ppermute(held, 'grp', [(i, i ^ bit) for i in range(grp_count)])  3.14 us
  transfers between devices with their start and end apart: 10, of which 7 were waited for; matrix products, arithmetic and copies ran while one was open for 3% of the time, Pallas kernels for 0%

profile of v4, /device:TPU:0, one launch (start us, length us, event | category | flops | bytes accessed | tf_op | source)
XLA Modules:
  0.0 73.7 jit_solution(10009589726984725547)
XLA Ops:
  0.0 0.0 copy-start
  0.0 0.0 copy-start.1
  0.0 0.1 compare_select_fusion
  0.1 0.1 reshape.122
  0.9 0.7 gather_fusion.2
  1.6 0.1 reshape.149
  1.6 0.0 copy-done.1
  1.6 0.7 gather_fusion.1
  2.4 0.1 reshape.151
  2.4 0.0 copy-done
  2.5 0.7 gather_fusion
  3.1 0.0 copy-start.4
  3.1 0.2 convert_element_type.38
  3.3 0.7 copy-done.4
  4.0 0.1 fusion.4
  4.1 1.1 %pad_maximum_fusion = bf16[4,1040,128]{2,1,0:T(8,128)(2,1)} fusion(bf16[4,16,128]{2,1,0:T(8,128)(2,1)S(1)} %broadcast_in_dim.7, bf16[4,256,128]{2,1,0:T(8,128)(2,1)S(1)} %broadcast_in_dim.6, bf16[4,768,128]{2,1,0:T(8,128)(2,1)S(1)} %bitcast.35), kind=kLoop, calls=%fused_computation.3 | loop fusion | flops 3194880 | bytes 2129920 | tf_op jit(solution)/shard_map/concatenate | solution.py:111
  5.2 0.0 copy-start.6
  5.2 6.5 %all-to-all-start = ((bf16[4,1040,128]{2,1,0:T(8,128)(2,1)}), bf16[4,1040,128]{2,1,0:T(8,128)(2,1)S(1)}, u32[]{:S(2)}, u32[]{:S(2)}) async-start(bf16[4,1040,128]{2,1,0:T(8,128)(2,1)} %pad_maximum_fusion), calls=%async_computation | async-start | bytes 2129920 | tf_op jit(solution)/shard_map/all_to_all | solution.py:114
  11.6 0.0 collective-permute-start
  11.6 1.3 %collective-permute-done = bf16[1,128,256]{2,1,0:T(8,128)(2,1)S(1)} collective-permute-done((bf16[1,128,256]{2,1,0:T(8,128)(2,1)S(1)}, bf16[1,128,256]{2,1,0:T(8,128)(2,1)S(1)}, u32[]{:S(2)}, u32[]{:S(2)}) %collective-permute-start) | collective-permute-done | bytes 65568 | tf_op jit(solution)/shard_map/ppermute | solution.py:37
  12.9 1.6 %collective-permute-start.1 = (bf16[2,128,256]{2,1,0:T(8,128)(2,1)S(1)}, bf16[2,128,256]{2,1,0:T(8,128)(2,1)S(1)}, u32[]{:S(2)}, u32[]{:S(2)}) collective-permute-start(bf16[2,128,256]{2,1,0:T(8,128)(2,1)S(1)} %maximum_select_fusion.2), channel_id=1, source_target_pairs={{0,8},{4,12},{8,0},{12,4},{16,24},{20,28},{24,16},{28,20},{1,9},{5... | collective-permute-start | bytes 393224 | tf_op jit(solution)/shard_map/ppermute | solution.py:37
  14.5 4.1 %collective-permute-done.1 = bf16[2,128,256]{2,1,0:T(8,128)(2,1)S(1)} collective-permute-done((bf16[2,128,256]{2,1,0:T(8,128)(2,1)S(1)}, bf16[2,128,256]{2,1,0:T(8,128)(2,1)S(1)}, u32[]{:S(2)}, u32[]{:S(2)}) %collective-permute-start.1) | collective-permute-done | bytes 131104 | tf_op jit(solution)/shard_map/ppermute | solution.py:37
  18.6 1.6 %collective-permute-start.2 = (bf16[4,128,256]{2,1,0:T(8,128)(2,1)S(1)}, bf16[4,128,256]{2,1,0:T(8,128)(2,1)S(1)}, u32[]{:S(2)}, u32[]{:S(2)}) collective-permute-start(bf16[4,128,256]{2,1,0:T(8,128)(2,1)S(1)} %maximum_select_fusion.1), channel_id=1, source_target_pairs={{0,16},{4,20},{8,24},{12,28},{16,0},{20,4},{24,8},{28,12},{1,17},{... | collective-permute-start | bytes 786440 | tf_op jit(solution)/shard_map/ppermute | solution.py:37
  20.1 0.0 copy-done.6
  20.2 0.1 reshape.115.refs_1_
  20.2 0.0 copy-start.5
  20.2 0.5 shift-left_or_fusion.refs_2_
  20.7 5.4 %collective-permute-done.2 = bf16[4,128,256]{2,1,0:T(8,128)(2,1)S(1)} collective-permute-done((bf16[4,128,256]{2,1,0:T(8,128)(2,1)S(1)}, bf16[4,128,256]{2,1,0:T(8,128)(2,1)S(1)}, u32[]{:S(2)}, u32[]{:S(2)}) %collective-permute-start.2) | collective-permute-done | bytes 262176 | tf_op jit(solution)/shard_map/ppermute | solution.py:37
  26.2 0.9 %maximum_select_fusion.refs_6_ = bf16[8,128,256]{2,1,0:T(8,128)(2,1)} fusion(bf16[4,128,256]{2,1,0:T(8,128)(2,1)S(1)} %collective-permute-done.2, bf16[4,128,256]{2,1,0:T(8,128)(2,1)S(1)} %maximum_select_fusion.1, pred[]{:T(512)S(6)} %eq.21), kind=kLoop, calls=%fused_computation.4 | loop fusion | flops 786432 | bytes 1048577 | tf_op jit(solution)/shard_map/jit(_where)/select_n | solution.py:39
  27.0 10.7 %all-to-all-done.refs_4_ = bf16[4,1040,128]{2,1,0:T(8,128)(2,1)S(1)} async-done(((bf16[4,1040,128]{2,1,0:T(8,128)(2,1)}), bf16[4,1040,128]{2,1,0:T(8,128)(2,1)S(1)}, u32[]{:S(2)}, u32[]{:S(2)}) %all-to-all-start) | async-done | bytes 1064992 | tf_op jit(solution)/shard_map/all_to_all | solution.py:114
  37.7 0.0 copy-start.2
  37.7 0.1 slice_convert_fusion.1
  37.8 0.7 reshape.114.refs_0_
  38.5 0.6 reshape.116.refs_3_
  39.1 0.0 copy-done.5
  39.1 0.0 copy-done.2
  39.1 13.2 %shard_map.64 = (f32[4,128,256]{2,1,0:T(8,128)}, f32[8,128,256]{2,1,0:T(8,128)}) custom-call(s32[24]{0:T(128)} %reshape.114.refs_0_, s32[24]{0:T(128)} %copy-done.5, s32[24]{0:T(128)} %shift-left_or_fusion.refs_2_, s32[24]{0:T(128)} %reshape.116.refs_3_, bf16[4,1040,128]{2,1,0:T(8,128)(2,1)} %copy-done.2, bf16[16,256,256]{2,1,0:T(8,128)(2,1)} %refs_5_.1, ...), custom_call_target="tpu_custom_call" | custom-call | tf_op jit(solution)/shard_map/pallas_call | solution.py:137
  52.3 0.0 copy-start.3
  52.3 1.1 %dynamic-slice_bitcast_fusion = f32[4,128,256]{2,1,0:T(8,128)S(1)} fusion(f32[2,4,128,256]{3,2,1,0:T(8,128)} %bitcast.38, s32[]{:T(128)S(6)} %select_n.142), kind=kLoop, calls=%fused_computation.6 | loop fusion | bytes 1048580 | tf_op jit(solution)/shard_map/squeeze | solution.py:25
  53.5 0.1 collective-permute-start.6
  53.6 1.9 %collective-permute-done.6 = f32[4,128,256]{2,1,0:T(8,128)S(1)} collective-permute-done((f32[4,128,256]{2,1,0:T(8,128)S(1)}, f32[4,128,256]{2,1,0:T(8,128)S(1)}, u32[]{:S(2)}, u32[]{:S(2)}) %collective-permute-start.6) | collective-permute-done | bytes 524320 | tf_op jit(solution)/shard_map/ppermute | solution.py:26
  55.4 1.1 %bitcast_add_fusion = f32[4,128,256]{2,1,0:T(8,128)S(1)} fusion(f32[4,128,256]{2,1,0:T(8,128)S(1)} %collective-permute-done.6, f32[2,4,128,256]{3,2,1,0:T(8,128)} %bitcast.39, s32[]{:T(128)S(6)} %select_n.141), kind=kLoop, calls=%fused_computation.5 | loop fusion | flops 131072 | bytes 1572868 | tf_op jit(solution)/shard_map/add | solution.py:27
  56.6 1.6 %collective-permute-start.7 = (f32[2,128,256]{2,1,0:T(8,128)S(1)}, f32[2,128,256]{2,1,0:T(8,128)S(1)}, u32[]{:S(2)}, u32[]{:S(2)}) collective-permute-start(f32[2,128,256]{2,1,0:T(8,128)S(1)} %dynamic-slice_bitcast_fusion.1), channel_id=1, source_target_pairs={{0,8},{4,12},{8,0},{12,4},{16,24},{20,28},{24,16},{28,20},{1,9},{5... | collective-permute-start | bytes 786440 | tf_op jit(solution)/shard_map/ppermute | solution.py:26
  58.1 0.0 copy-done.3
  58.1 0.7 dynamic-slice_bitcast_fusion.4
  58.9 1.5 %collective-permute-start.3 = (f32[128,256]{1,0:T(8,128)}, f32[128,256]{1,0:T(8,128)S(1)}, u32[]{:S(2)}, u32[]{:S(2)}) collective-permute-start(f32[128,256]{1,0:T(8,128)} %get-tuple-element.9), channel_id=1, source_target_pairs={{0,3},{1,0},{2,1},{3,2},{4,7},{5,4},{6,5},{7,6},{8,11},{9,8},{10,9... | collective-permute-start | bytes 393224 | tf_op jit(solution)/shard_map/ppermute | solution.py:47
  60.3 0.0 collective-permute-start.4
  60.3 0.6 collective-permute-start.5
  60.9 4.1 %collective-permute-done.7 = f32[2,128,256]{2,1,0:T(8,128)S(1)} collective-permute-done((f32[2,128,256]{2,1,0:T(8,128)S(1)}, f32[2,128,256]{2,1,0:T(8,128)S(1)}, u32[]{:S(2)}, u32[]{:S(2)}) %collective-permute-start.7) | collective-permute-done | bytes 262176 | tf_op jit(solution)/shard_map/ppermute | solution.py:26
  65.1 1.6 %collective-permute-start.8 = (f32[1,128,256]{2,1,0:T(8,128)S(1)}, f32[1,128,256]{2,1,0:T(8,128)S(1)}, u32[]{:S(2)}, u32[]{:S(2)}) collective-permute-start(f32[1,128,256]{2,1,0:T(8,128)S(1)} %constant_dynamic-slice_fusion), channel_id=1, source_target_pairs={{0,16},{4,20},{8,24},{12,28},{16,0},{20,4},{24,8},{28,12},{1,17},{... | collective-permute-start | bytes 393224 | tf_op jit(solution)/shard_map/ppermute | solution.py:26
  66.6 0.0 collective-permute-done.3
  66.7 5.4 %collective-permute-done.4 = f32[128,256]{1,0:T(8,128)S(1)} collective-permute-done((f32[128,256]{1,0:T(8,128)}, f32[128,256]{1,0:T(8,128)S(1)}, u32[]{:S(2)}, u32[]{:S(2)}) %collective-permute-start.4) | collective-permute-done | bytes 131104 | tf_op jit(solution)/shard_map/ppermute | solution.py:47
  72.0 0.0 collective-permute-done.5
  72.0 0.0 collective-permute-done.8
  72.0 1.6 %bitcast_add_fusion.2 = f32[128,256]{1,0:T(8,128)} fusion(f32[128,256]{1,0:T(8,128)} %collective-permute-done.5, f32[128,256]{1,0:T(8,128)S(1)} %collective-permute-done.4, f32[128,256]{1,0:T(8,128)S(1)} %collective-permute-done.3, f32[1,128,256]{2,1,0:T(8,128)S(1)} %collective-permute-done.8, f32[2,128,256]{2,1,0:T(8,128)S(1)} %bitcast_add_fusion.1, ...), kind=kLoop, calls=%fused_computation.11 | loop fusion | flops 163840 | bytes 917512 | tf_op jit(solution)/shard_map/add | solution.py:150
  (15 shorter events, 0.2 us)
Async XLA Ops:
  0.0 2.4 %copy-start = (s32[24,128,128]{2,1,0:T(8,128)S(1)}, s32[24,128,128]{2,1,0:T(8,128)}, u32[]{:S(2)}) copy-start(s32[24,128,128]{2,1,0:T(8,128)} %param.8) | copy-start | bytes 4718596
  0.0 1.6 %copy-start.1 = (s32[1,24]{1,0:T(1,128)S(1)}, s32[1,24]{1,0:T(1,128)}, u32[]{:S(2)}) copy-start(s32[1,24]{1,0:T(1,128)} %param.9) | copy-start | bytes 292
  3.1 0.8 %copy-start.4 = (bf16[128,256]{1,0:T(8,128)(2,1)S(1)}, bf16[128,256]{1,0:T(8,128)(2,1)}, u32[]{:S(2)}) copy-start(bf16[128,256]{1,0:T(8,128)(2,1)} %param.6) | copy-start | bytes 196612
  5.2 15.0 %copy-start.6 = (s32[1,4,6]{2,1,0:T(4,128)S(1)}, s32[1,4,6]{2,1,0:T(4,128)}, u32[]{:S(2)}) copy-start(s32[1,4,6]{2,1,0:T(4,128)} %param.11) | copy-start | bytes 292
  5.2 32.5 %all-to-all-start = ((bf16[4,1040,128]{2,1,0:T(8,128)(2,1)}), bf16[4,1040,128]{2,1,0:T(8,128)(2,1)S(1)}, u32[]{:S(2)}, u32[]{:S(2)}) async-start(bf16[4,1040,128]{2,1,0:T(8,128)(2,1)} %pad_maximum_fusion), calls=%async_computation | async-start | bytes 2129920 | tf_op jit(solution)/shard_map/all_to_all | solution.py:114
  11.6 1.3 %collective-permute-start = (bf16[1,128,256]{2,1,0:T(8,128)(2,1)S(1)}, bf16[1,128,256]{2,1,0:T(8,128)(2,1)S(1)}, u32[]{:S(2)}, u32[]{:S(2)}) collective-permute-start(bf16[1,128,256]{2,1,0:T(8,128)(2,1)S(1)} %bitcast.40), channel_id=1, source_target_pairs={{0,4},{4,0},{8,12},{12,8},{16,20},{20,16},{24,28},{28,24},{1,5},{5... | collective-permute-start | bytes 196616 | tf_op jit(solution)/shard_map/ppermute | solution.py:37
  12.9 5.6 %collective-permute-start.1 = (bf16[2,128,256]{2,1,0:T(8,128)(2,1)S(1)}, bf16[2,128,256]{2,1,0:T(8,128)(2,1)S(1)}, u32[]{:S(2)}, u32[]{:S(2)}) collective-permute-start(bf16[2,128,256]{2,1,0:T(8,128)(2,1)S(1)} %maximum_select_fusion.2), channel_id=1, source_target_pairs={{0,8},{4,12},{8,0},{12,4},{16,24},{20,28},{24,16},{28,20},{1,9},{5... | collective-permute-start | bytes 393224 | tf_op jit(solution)/shard_map/ppermute | solution.py:37
  18.6 7.6 %collective-permute-start.2 = (bf16[4,128,256]{2,1,0:T(8,128)(2,1)S(1)}, bf16[4,128,256]{2,1,0:T(8,128)(2,1)S(1)}, u32[]{:S(2)}, u32[]{:S(2)}) collective-permute-start(bf16[4,128,256]{2,1,0:T(8,128)(2,1)S(1)} %maximum_select_fusion.1), channel_id=1, source_target_pairs={{0,16},{4,20},{8,24},{12,28},{16,0},{20,4},{24,8},{28,12},{1,17},{... | collective-permute-start | bytes 786440 | tf_op jit(solution)/shard_map/ppermute | solution.py:37
  20.2 18.9 %copy-start.5 = (s32[24]{0:T(128)}, s32[24]{0:T(128)S(1)}, u32[]{:S(2)}) copy-start(s32[24]{0:T(128)S(1)} %reshape.115.refs_1_) | copy-start | bytes 292
  37.7 1.4 %copy-start.2 = (bf16[4,1040,128]{2,1,0:T(8,128)(2,1)}, bf16[4,1040,128]{2,1,0:T(8,128)(2,1)S(1)}, u32[]{:S(2)}) copy-start(bf16[4,1040,128]{2,1,0:T(8,128)(2,1)S(1)} %all-to-all-done.refs_4_) | copy-start | bytes 3194884
  52.3 5.8 %copy-start.3 = (f32[4,128,256]{2,1,0:T(8,128)S(1)}, f32[4,128,256]{2,1,0:T(8,128)}, u32[]{:S(2)}) copy-start(f32[4,128,256]{2,1,0:T(8,128)} %get-tuple-element.7) | copy-start | bytes 1572868
  53.5 2.0 %collective-permute-start.6 = (f32[4,128,256]{2,1,0:T(8,128)S(1)}, f32[4,128,256]{2,1,0:T(8,128)S(1)}, u32[]{:S(2)}, u32[]{:S(2)}) collective-permute-start(f32[4,128,256]{2,1,0:T(8,128)S(1)} %dynamic-slice_bitcast_fusion), channel_id=1, source_target_pairs={{0,4},{4,0},{8,12},{12,8},{16,20},{20,16},{24,28},{28,24},{1,5},{5... | collective-permute-start | bytes 1572872 | tf_op jit(solution)/shard_map/ppermute | solution.py:26
  56.6 8.4 %collective-permute-start.7 = (f32[2,128,256]{2,1,0:T(8,128)S(1)}, f32[2,128,256]{2,1,0:T(8,128)S(1)}, u32[]{:S(2)}, u32[]{:S(2)}) collective-permute-start(f32[2,128,256]{2,1,0:T(8,128)S(1)} %dynamic-slice_bitcast_fusion.1), channel_id=1, source_target_pairs={{0,8},{4,12},{8,0},{12,4},{16,24},{20,28},{24,16},{28,20},{1,9},{5... | collective-permute-start | bytes 786440 | tf_op jit(solution)/shard_map/ppermute | solution.py:26
  58.9 7.8 %collective-permute-start.3 = (f32[128,256]{1,0:T(8,128)}, f32[128,256]{1,0:T(8,128)S(1)}, u32[]{:S(2)}, u32[]{:S(2)}) collective-permute-start(f32[128,256]{1,0:T(8,128)} %get-tuple-element.9), channel_id=1, source_target_pairs={{0,3},{1,0},{2,1},{3,2},{4,7},{5,4},{6,5},{7,6},{8,11},{9,8},{10,9... | collective-permute-start | bytes 393224 | tf_op jit(solution)/shard_map/ppermute | solution.py:47
  60.3 11.7 %collective-permute-start.4 = (f32[128,256]{1,0:T(8,128)}, f32[128,256]{1,0:T(8,128)S(1)}, u32[]{:S(2)}, u32[]{:S(2)}) collective-permute-start(f32[128,256]{1,0:T(8,128)} %get-tuple-element.11), channel_id=1, source_target_pairs={{0,2},{1,3},{2,0},{3,1},{4,6},{5,7},{6,4},{7,5},{8,10},{9,11},{10,... | collective-permute-start | bytes 393224 | tf_op jit(solution)/shard_map/ppermute | solution.py:47
  60.3 11.7 %collective-permute-start.5 = (f32[128,256]{1,0:T(8,128)S(1)}, f32[128,256]{1,0:T(8,128)}, u32[]{:S(2)}, u32[]{:S(2)}) collective-permute-start(f32[128,256]{1,0:T(8,128)S(1)} %get-tuple-element.10), channel_id=1, source_target_pairs={{0,1},{1,2},{2,3},{3,0},{4,5},{5,6},{6,7},{7,4},{8,9},{9,10},{10,1... | collective-permute-start | bytes 393224 | tf_op jit(solution)/shard_map/ppermute | solution.py:47
  65.1 7.0 %collective-permute-start.8 = (f32[1,128,256]{2,1,0:T(8,128)S(1)}, f32[1,128,256]{2,1,0:T(8,128)S(1)}, u32[]{:S(2)}, u32[]{:S(2)}) collective-permute-start(f32[1,128,256]{2,1,0:T(8,128)S(1)} %constant_dynamic-slice_fusion), channel_id=1, source_target_pairs={{0,16},{4,20},{8,24},{12,28},{16,0},{20,4},{24,8},{28,12},{1,17},{... | collective-permute-start | bytes 393224 | tf_op jit(solution)/shard_map/ppermute | solution.py:26

commit v5 on v4

--- a/solution.py
+++ b/solution.py
@@ -57,29 +57,41 @@
 
     nt = (((1,), (1,)), ((), ()))
     base = per_relay * block
-    own_lo = in_ref[0, base : base + block, :]
-    own_hi = in_ref[0, base + block : base + 2 * block, :]
-    acc = None
-    for j in range(per_relay):
-        t = e * per_relay + j
-        r = rels_ref[t]
-        core = core_ref[r]
-        panel = panel_ref[groups_ref[t]]
-        mapped = (
-            jnp.dot(own_lo, core[:block], preferred_element_type=jnp.float32)
-            + jnp.dot(own_hi, core[block:], preferred_element_type=jnp.float32)
-        ).astype(jnp.bfloat16)
-        predicted = lax.dot_general(mapped, panel, nt, preferred_element_type=jnp.float32)
+    own = jnp.concatenate(
+        [in_ref[0, base : base + block, :], in_ref[0, base + block : base + 2 * block, :]], axis=1
+    )
+    ts = [e * per_relay + j for j in range(per_relay)]
+    rels = [rels_ref[t] for t in ts]
+    groups = [groups_ref[t] for t in ts]
+    mapped = [
+        jnp.dot(own, core_ref[r], preferred_element_type=jnp.float32).astype(jnp.bfloat16)
+        for r in rels
+    ]
+    predicted = [
+        lax.dot_general(m, panel_ref[g], nt, preferred_element_type=jnp.float32)
+        for m, g in zip(mapped, groups)
+    ]
+    resids = []
+    for j, t in enumerate(ts):
         scale = LOSS_SCALE * alive_ref[t].astype(jnp.float32)
         adj = in_ref[0, j * block : (j + 1) * block, :].astype(jnp.float32)
-        resid = ((predicted - adj) * scale).astype(jnp.bfloat16)
-        product = jnp.dot(resid, panel, preferred_element_type=jnp.float32).astype(jnp.bfloat16)
-        part = lax.dot_general(product, core, nt, preferred_element_type=jnp.float32)
+        resids.append(((predicted[j] - adj) * scale).astype(jnp.bfloat16))
+    products = [
+        jnp.dot(r, panel_ref[g], preferred_element_type=jnp.float32).astype(jnp.bfloat16)
+        for r, g in zip(resids, groups)
+    ]
+    columns = [
+        jnp.dot(
+            r.astype(jnp.float32).T.astype(jnp.bfloat16), m, preferred_element_type=jnp.float32
+        ).astype(jnp.bfloat16)
+        for r, m in zip(resids, mapped)
+    ]
+    acc = None
+    for p, r in zip(products, rels):
+        part = lax.dot_general(p, core_ref[r], nt, preferred_element_type=jnp.float32)
         acc = part if acc is None else acc + part
-        resid_t = resid.astype(jnp.float32).T.astype(jnp.bfloat16)
-        column = jnp.dot(resid_t, mapped, preferred_element_type=jnp.float32).astype(jnp.bfloat16)
-        slot = slots_ref[t]
-        owner_ref[slot] += column.astype(jnp.float32)
+    for c, t in zip(columns, ts):
+        owner_ref[slots_ref[t]] += c.astype(jnp.float32)
     row_ref[0] = acc
 
 

time: 74 us -> 67.9 us (0.918)
  Pallas kernels: 13.2 us -> 7.07 us
    pallas_call x1, Pallas kernels: 13.2 us -> 7.07 us  [on_device(): pl.pallas_call(lambda *refs: tile_kernel(*refs, per_relay=per_relay, bloc...]
where the time goes in v5:
time: 67.9 us; the launch traced here: 67.5 us
  waiting for transfers between devices  32.8 us (48%)
  starting transfers between devices  14.8 us (22%)
  Pallas kernels  7.07 us (10%)
  local copies, waits for them, and re-layouts  6.33 us (9%)
  other arithmetic  5.68 us (8%)
  between operations  0.78 us (1%)
    ppermute x3, waiting for transfers between devices, grp_gather(): got = lax.ppermute(held, 'grp', [(i, i ^ bit) for i in range(grp_count)])  10.7 us
    all_to_all x1, waiting for transfers between devices, on_device(): lax.all_to_all(outgoing, 'ent', split_axis=0, concat_axis=0, tiled=True)  10.7 us
    pallas_call x1, Pallas kernels, on_device(): pl.pallas_call(lambda *refs: tile_kernel(*refs, per_relay=per_relay, bloc...  7.07 us
    all_to_all x1, starting transfers between devices, on_device(): lax.all_to_all(outgoing, 'ent', split_axis=0, concat_axis=0, tiled=True)  6.46 us
    ppermute x3, waiting for transfers between devices, grp_reduce_scatter(): got = lax.ppermute(send, 'grp', [(i, i ^ bit) for i in range(grp_count)])  5.99 us
    ppermute x3, waiting for transfers between devices, shift_ent(): lax.ppermute(x, 'ent', [(i, (i + shift) % ent_count) for i in range(ent_c...  5.39 us
    ppermute x3, starting transfers between devices, grp_reduce_scatter(): got = lax.ppermute(send, 'grp', [(i, i ^ bit) for i in range(grp_count)])  3.21 us
    ppermute x3, starting transfers between devices, grp_gather(): got = lax.ppermute(held, 'grp', [(i, i ^ bit) for i in range(grp_count)])  3.14 us
  transfers between devices with their start and end apart: 10, of which 7 were waited for; matrix products, arithmetic and copies ran while one was open for 3% of the time, Pallas kernels for 0%

profile of v5, /device:TPU:0, one launch (start us, length us, event | category | flops | bytes accessed | tf_op | source)
XLA Modules:
  0.0 67.5 jit_solution(16875046129791256876)
XLA Ops:
  0.0 0.0 copy-start
  0.0 0.0 copy-start.1
  0.0 0.1 compare_select_fusion
  0.1 0.1 reshape.122
  0.9 0.7 %gather_fusion.2 = bf16[24]{0:T(256)(128)(2,1)S(1)} fusion(bf16[24]{0:T(256)(128)(2,1)S(1)} %compare_convert_fusion, s32[1024]{0:T(1024)S(1)} %pad_clamp_fusion), kind=kCustom, calls=%fused_computation.2 | custom fusion | bytes 192 | tf_op jit(solution)/shard_map/gather | solution.py:119
  1.6 0.1 reshape.149
  1.6 0.0 copy-done.1
  1.6 0.7 %gather_fusion.1 = s32[24]{0:T(128)S(1)} fusion(s32[24]{0:T(128)S(1)} %bitcast.34, s32[1024]{0:T(1024)S(1)} %pad_clamp_fusion), kind=kCustom, calls=%fused_computation.1 | custom fusion | bytes 288 | tf_op jit(solution)/shard_map/gather | solution.py:119
  2.4 0.1 reshape.151
  2.4 0.0 copy-done
  2.5 0.7 gather_fusion
  3.1 0.0 copy-start.4
  3.1 0.2 convert_element_type.38
  3.3 0.7 copy-done.4
  4.0 0.1 fusion.4
  4.1 1.1 %pad_maximum_fusion = bf16[4,1040,128]{2,1,0:T(8,128)(2,1)} fusion(bf16[4,16,128]{2,1,0:T(8,128)(2,1)S(1)} %broadcast_in_dim.7, bf16[4,256,128]{2,1,0:T(8,128)(2,1)S(1)} %broadcast_in_dim.6, bf16[4,768,128]{2,1,0:T(8,128)(2,1)S(1)} %bitcast.35), kind=kLoop, calls=%fused_computation.3 | loop fusion | flops 3194880 | bytes 2129920 | tf_op jit(solution)/shard_map/concatenate | solution.py:123
  5.2 0.0 copy-start.6
  5.2 6.5 %all-to-all-start = ((bf16[4,1040,128]{2,1,0:T(8,128)(2,1)}), bf16[4,1040,128]{2,1,0:T(8,128)(2,1)S(1)}, u32[]{:S(2)}, u32[]{:S(2)}) async-start(bf16[4,1040,128]{2,1,0:T(8,128)(2,1)} %pad_maximum_fusion), calls=%async_computation | async-start | bytes 2129920 | tf_op jit(solution)/shard_map/all_to_all | solution.py:126
  11.6 0.0 collective-permute-start
  11.6 1.3 %collective-permute-done = bf16[1,128,256]{2,1,0:T(8,128)(2,1)S(1)} collective-permute-done((bf16[1,128,256]{2,1,0:T(8,128)(2,1)S(1)}, bf16[1,128,256]{2,1,0:T(8,128)(2,1)S(1)}, u32[]{:S(2)}, u32[]{:S(2)}) %collective-permute-start) | collective-permute-done | bytes 65568 | tf_op jit(solution)/shard_map/ppermute | solution.py:37
  12.9 1.6 %collective-permute-start.1 = (bf16[2,128,256]{2,1,0:T(8,128)(2,1)S(1)}, bf16[2,128,256]{2,1,0:T(8,128)(2,1)S(1)}, u32[]{:S(2)}, u32[]{:S(2)}) collective-permute-start(bf16[2,128,256]{2,1,0:T(8,128)(2,1)S(1)} %maximum_select_fusion.2), channel_id=1, source_target_pairs={{0,8},{4,12},{8,0},{12,4},{16,24},{20,28},{24,16},{28,20},{1,9},{5... | collective-permute-start | bytes 393224 | tf_op jit(solution)/shard_map/ppermute | solution.py:37
  14.5 4.1 %collective-permute-done.1 = bf16[2,128,256]{2,1,0:T(8,128)(2,1)S(1)} collective-permute-done((bf16[2,128,256]{2,1,0:T(8,128)(2,1)S(1)}, bf16[2,128,256]{2,1,0:T(8,128)(2,1)S(1)}, u32[]{:S(2)}, u32[]{:S(2)}) %collective-permute-start.1) | collective-permute-done | bytes 131104 | tf_op jit(solution)/shard_map/ppermute | solution.py:37
  18.6 1.6 %collective-permute-start.2 = (bf16[4,128,256]{2,1,0:T(8,128)(2,1)S(1)}, bf16[4,128,256]{2,1,0:T(8,128)(2,1)S(1)}, u32[]{:S(2)}, u32[]{:S(2)}) collective-permute-start(bf16[4,128,256]{2,1,0:T(8,128)(2,1)S(1)} %maximum_select_fusion.1), channel_id=1, source_target_pairs={{0,16},{4,20},{8,24},{12,28},{16,0},{20,4},{24,8},{28,12},{1,17},{... | collective-permute-start | bytes 786440 | tf_op jit(solution)/shard_map/ppermute | solution.py:37
  20.1 0.0 copy-done.6
  20.2 0.1 reshape.115.refs_1_
  20.2 0.0 copy-start.5
  20.2 0.5 shift-left_or_fusion.refs_2_
  20.7 5.4 %collective-permute-done.2 = bf16[4,128,256]{2,1,0:T(8,128)(2,1)S(1)} collective-permute-done((bf16[4,128,256]{2,1,0:T(8,128)(2,1)S(1)}, bf16[4,128,256]{2,1,0:T(8,128)(2,1)S(1)}, u32[]{:S(2)}, u32[]{:S(2)}) %collective-permute-start.2) | collective-permute-done | bytes 262176 | tf_op jit(solution)/shard_map/ppermute | solution.py:37
  26.2 0.9 %maximum_select_fusion.refs_6_ = bf16[8,128,256]{2,1,0:T(8,128)(2,1)} fusion(bf16[4,128,256]{2,1,0:T(8,128)(2,1)S(1)} %collective-permute-done.2, bf16[4,128,256]{2,1,0:T(8,128)(2,1)S(1)} %maximum_select_fusion.1, pred[]{:T(512)S(6)} %eq.21), kind=kLoop, calls=%fused_computation.4 | loop fusion | flops 786432 | bytes 1048577 | tf_op jit(solution)/shard_map/jit(_where)/select_n | solution.py:39
  27.0 10.7 %all-to-all-done.refs_4_ = bf16[4,1040,128]{2,1,0:T(8,128)(2,1)S(1)} async-done(((bf16[4,1040,128]{2,1,0:T(8,128)(2,1)}), bf16[4,1040,128]{2,1,0:T(8,128)(2,1)S(1)}, u32[]{:S(2)}, u32[]{:S(2)}) %all-to-all-start) | async-done | bytes 1064992 | tf_op jit(solution)/shard_map/all_to_all | solution.py:126
  37.7 0.0 copy-start.2
  37.7 0.1 slice_convert_fusion.1
  37.8 0.7 %reshape.114.refs_0_ = s32[24]{0:T(128)} reshape(s32[4,6]{1,0:T(4,128)S(1)} %get-tuple-element.15) | data formatting | bytes 192 | tf_op jit(solution)/shard_map/reshape | solution.py:130
  38.5 0.6 reshape.116.refs_3_
  39.1 0.0 copy-done.5
  39.1 0.0 copy-done.2
  39.1 7.1 %shard_map.64 = (f32[4,128,256]{2,1,0:T(8,128)}, f32[8,128,256]{2,1,0:T(8,128)}) custom-call(s32[24]{0:T(128)} %reshape.114.refs_0_, s32[24]{0:T(128)} %copy-done.5, s32[24]{0:T(128)} %shift-left_or_fusion.refs_2_, s32[24]{0:T(128)} %reshape.116.refs_3_, bf16[4,1040,128]{2,1,0:T(8,128)(2,1)} %copy-done.2, bf16[16,256,256]{2,1,0:T(8,128)(2,1)} %refs_5_.1, ...), custom_call_target="tpu_custom_call" | custom-call | tf_op jit(solution)/shard_map/pallas_call | solution.py:149
  46.2 0.0 copy-start.3
  46.2 1.1 %dynamic-slice_bitcast_fusion = f32[4,128,256]{2,1,0:T(8,128)S(1)} fusion(f32[2,4,128,256]{3,2,1,0:T(8,128)} %bitcast.38, s32[]{:T(128)S(6)} %select_n.142), kind=kLoop, calls=%fused_computation.6 | loop fusion | bytes 1048580 | tf_op jit(solution)/shard_map/squeeze | solution.py:25
  47.3 0.1 collective-permute-start.6
  47.4 1.9 %collective-permute-done.6 = f32[4,128,256]{2,1,0:T(8,128)S(1)} collective-permute-done((f32[4,128,256]{2,1,0:T(8,128)S(1)}, f32[4,128,256]{2,1,0:T(8,128)S(1)}, u32[]{:S(2)}, u32[]{:S(2)}) %collective-permute-start.6) | collective-permute-done | bytes 524320 | tf_op jit(solution)/shard_map/ppermute | solution.py:26
  49.3 1.1 %bitcast_add_fusion = f32[4,128,256]{2,1,0:T(8,128)S(1)} fusion(f32[4,128,256]{2,1,0:T(8,128)S(1)} %collective-permute-done.6, f32[2,4,128,256]{3,2,1,0:T(8,128)} %bitcast.39, s32[]{:T(128)S(6)} %select_n.141), kind=kLoop, calls=%fused_computation.5 | loop fusion | flops 131072 | bytes 1572868 | tf_op jit(solution)/shard_map/add | solution.py:27
  50.4 1.6 %collective-permute-start.7 = (f32[2,128,256]{2,1,0:T(8,128)S(1)}, f32[2,128,256]{2,1,0:T(8,128)S(1)}, u32[]{:S(2)}, u32[]{:S(2)}) collective-permute-start(f32[2,128,256]{2,1,0:T(8,128)S(1)} %dynamic-slice_bitcast_fusion.1), channel_id=1, source_target_pairs={{0,8},{4,12},{8,0},{12,4},{16,24},{20,28},{24,16},{28,20},{1,9},{5... | collective-permute-start | bytes 786440 | tf_op jit(solution)/shard_map/ppermute | solution.py:26
  52.0 0.0 copy-done.3
  52.0 0.7 %dynamic-slice_bitcast_fusion.4 = (f32[128,256]{1,0:T(8,128)}, f32[128,256]{1,0:T(8,128)S(1)}, f32[128,256]{1,0:T(8,128)}) fusion(f32[4,128,256]{2,1,0:T(8,128)S(1)} %copy-done.3, s32[]{:T(128)S(6)} %select_n.136, s32[]{:T(128)S(6)} %select_n.140, s32[]{:T(128)S(6)} %select_n.138), kind=kLoop, calls=%fused_computation.17 | loop fusion | bytes 786444 | tf_op jit(solution)/shard_map/squeeze | solution.py:160
  52.7 1.5 %collective-permute-start.3 = (f32[128,256]{1,0:T(8,128)}, f32[128,256]{1,0:T(8,128)S(1)}, u32[]{:S(2)}, u32[]{:S(2)}) collective-permute-start(f32[128,256]{1,0:T(8,128)} %get-tuple-element.9), channel_id=1, source_target_pairs={{0,3},{1,0},{2,1},{3,2},{4,7},{5,4},{6,5},{7,6},{8,11},{9,8},{10,9... | collective-permute-start | bytes 393224 | tf_op jit(solution)/shard_map/ppermute | solution.py:47
  54.2 0.0 collective-permute-start.4
  54.2 0.6 collective-permute-start.5
  54.7 4.1 %collective-permute-done.7 = f32[2,128,256]{2,1,0:T(8,128)S(1)} collective-permute-done((f32[2,128,256]{2,1,0:T(8,128)S(1)}, f32[2,128,256]{2,1,0:T(8,128)S(1)}, u32[]{:S(2)}, u32[]{:S(2)}) %collective-permute-start.7) | collective-permute-done | bytes 262176 | tf_op jit(solution)/shard_map/ppermute | solution.py:26
  58.9 1.6 %collective-permute-start.8 = (f32[1,128,256]{2,1,0:T(8,128)S(1)}, f32[1,128,256]{2,1,0:T(8,128)S(1)}, u32[]{:S(2)}, u32[]{:S(2)}) collective-permute-start(f32[1,128,256]{2,1,0:T(8,128)S(1)} %constant_dynamic-slice_fusion), channel_id=1, source_target_pairs={{0,16},{4,20},{8,24},{12,28},{16,0},{20,4},{24,8},{28,12},{1,17},{... | collective-permute-start | bytes 393224 | tf_op jit(solution)/shard_map/ppermute | solution.py:26
  60.5 0.0 collective-permute-done.3
  60.5 5.4 %collective-permute-done.4 = f32[128,256]{1,0:T(8,128)S(1)} collective-permute-done((f32[128,256]{1,0:T(8,128)}, f32[128,256]{1,0:T(8,128)S(1)}, u32[]{:S(2)}, u32[]{:S(2)}) %collective-permute-start.4) | collective-permute-done | bytes 131104 | tf_op jit(solution)/shard_map/ppermute | solution.py:47
  65.9 0.0 collective-permute-done.5
  65.9 0.0 collective-permute-done.8
  65.9 1.6 %bitcast_add_fusion.2 = f32[128,256]{1,0:T(8,128)} fusion(f32[128,256]{1,0:T(8,128)} %collective-permute-done.5, f32[128,256]{1,0:T(8,128)S(1)} %collective-permute-done.4, f32[128,256]{1,0:T(8,128)S(1)} %collective-permute-done.3, f32[1,128,256]{2,1,0:T(8,128)S(1)} %collective-permute-done.8, f32[2,128,256]{2,1,0:T(8,128)S(1)} %bitcast_add_fusion.1, ...), kind=kLoop, calls=%fused_computation.11 | loop fusion | flops 163840 | bytes 917512 | tf_op jit(solution)/shard_map/add | solution.py:162
  (15 shorter events, 0.2 us)
Async XLA Ops:
  0.0 2.4 %copy-start = (s32[24,128,128]{2,1,0:T(8,128)S(1)}, s32[24,128,128]{2,1,0:T(8,128)}, u32[]{:S(2)}) copy-start(s32[24,128,128]{2,1,0:T(8,128)} %param.8) | copy-start | bytes 4718596
  0.0 1.6 %copy-start.1 = (s32[1,24]{1,0:T(1,128)S(1)}, s32[1,24]{1,0:T(1,128)}, u32[]{:S(2)}) copy-start(s32[1,24]{1,0:T(1,128)} %param.9) | copy-start | bytes 292
  3.1 0.8 %copy-start.4 = (bf16[128,256]{1,0:T(8,128)(2,1)S(1)}, bf16[128,256]{1,0:T(8,128)(2,1)}, u32[]{:S(2)}) copy-start(bf16[128,256]{1,0:T(8,128)(2,1)} %param.6) | copy-start | bytes 196612
  5.2 15.0 %copy-start.6 = (s32[1,4,6]{2,1,0:T(4,128)S(1)}, s32[1,4,6]{2,1,0:T(4,128)}, u32[]{:S(2)}) copy-start(s32[1,4,6]{2,1,0:T(4,128)} %param.11) | copy-start | bytes 292
  5.2 32.5 %all-to-all-start = ((bf16[4,1040,128]{2,1,0:T(8,128)(2,1)}), bf16[4,1040,128]{2,1,0:T(8,128)(2,1)S(1)}, u32[]{:S(2)}, u32[]{:S(2)}) async-start(bf16[4,1040,128]{2,1,0:T(8,128)(2,1)} %pad_maximum_fusion), calls=%async_computation | async-start | bytes 2129920 | tf_op jit(solution)/shard_map/all_to_all | solution.py:126
  11.6 1.3 %collective-permute-start = (bf16[1,128,256]{2,1,0:T(8,128)(2,1)S(1)}, bf16[1,128,256]{2,1,0:T(8,128)(2,1)S(1)}, u32[]{:S(2)}, u32[]{:S(2)}) collective-permute-start(bf16[1,128,256]{2,1,0:T(8,128)(2,1)S(1)} %bitcast.40), channel_id=1, source_target_pairs={{0,4},{4,0},{8,12},{12,8},{16,20},{20,16},{24,28},{28,24},{1,5},{5... | collective-permute-start | bytes 196616 | tf_op jit(solution)/shard_map/ppermute | solution.py:37
  12.9 5.6 %collective-permute-start.1 = (bf16[2,128,256]{2,1,0:T(8,128)(2,1)S(1)}, bf16[2,128,256]{2,1,0:T(8,128)(2,1)S(1)}, u32[]{:S(2)}, u32[]{:S(2)}) collective-permute-start(bf16[2,128,256]{2,1,0:T(8,128)(2,1)S(1)} %maximum_select_fusion.2), channel_id=1, source_target_pairs={{0,8},{4,12},{8,0},{12,4},{16,24},{20,28},{24,16},{28,20},{1,9},{5... | collective-permute-start | bytes 393224 | tf_op jit(solution)/shard_map/ppermute | solution.py:37
  18.6 7.6 %collective-permute-start.2 = (bf16[4,128,256]{2,1,0:T(8,128)(2,1)S(1)}, bf16[4,128,256]{2,1,0:T(8,128)(2,1)S(1)}, u32[]{:S(2)}, u32[]{:S(2)}) collective-permute-start(bf16[4,128,256]{2,1,0:T(8,128)(2,1)S(1)} %maximum_select_fusion.1), channel_id=1, source_target_pairs={{0,16},{4,20},{8,24},{12,28},{16,0},{20,4},{24,8},{28,12},{1,17},{... | collective-permute-start | bytes 786440 | tf_op jit(solution)/shard_map/ppermute | solution.py:37
  20.2 18.9 %copy-start.5 = (s32[24]{0:T(128)}, s32[24]{0:T(128)S(1)}, u32[]{:S(2)}) copy-start(s32[24]{0:T(128)S(1)} %reshape.115.refs_1_) | copy-start | bytes 292
  37.7 1.4 %copy-start.2 = (bf16[4,1040,128]{2,1,0:T(8,128)(2,1)}, bf16[4,1040,128]{2,1,0:T(8,128)(2,1)S(1)}, u32[]{:S(2)}) copy-start(bf16[4,1040,128]{2,1,0:T(8,128)(2,1)S(1)} %all-to-all-done.refs_4_) | copy-start | bytes 3194884
  46.2 5.8 %copy-start.3 = (f32[4,128,256]{2,1,0:T(8,128)S(1)}, f32[4,128,256]{2,1,0:T(8,128)}, u32[]{:S(2)}) copy-start(f32[4,128,256]{2,1,0:T(8,128)} %get-tuple-element.7) | copy-start | bytes 1572868
  47.3 2.0 %collective-permute-start.6 = (f32[4,128,256]{2,1,0:T(8,128)S(1)}, f32[4,128,256]{2,1,0:T(8,128)S(1)}, u32[]{:S(2)}, u32[]{:S(2)}) collective-permute-start(f32[4,128,256]{2,1,0:T(8,128)S(1)} %dynamic-slice_bitcast_fusion), channel_id=1, source_target_pairs={{0,4},{4,0},{8,12},{12,8},{16,20},{20,16},{24,28},{28,24},{1,5},{5... | collective-permute-start | bytes 1572872 | tf_op jit(solution)/shard_map/ppermute | solution.py:26
  50.4 8.4 %collective-permute-start.7 = (f32[2,128,256]{2,1,0:T(8,128)S(1)}, f32[2,128,256]{2,1,0:T(8,128)S(1)}, u32[]{:S(2)}, u32[]{:S(2)}) collective-permute-start(f32[2,128,256]{2,1,0:T(8,128)S(1)} %dynamic-slice_bitcast_fusion.1), channel_id=1, source_target_pairs={{0,8},{4,12},{8,0},{12,4},{16,24},{20,28},{24,16},{28,20},{1,9},{5... | collective-permute-start | bytes 786440 | tf_op jit(solution)/shard_map/ppermute | solution.py:26
  52.7 7.8 %collective-permute-start.3 = (f32[128,256]{1,0:T(8,128)}, f32[128,256]{1,0:T(8,128)S(1)}, u32[]{:S(2)}, u32[]{:S(2)}) collective-permute-start(f32[128,256]{1,0:T(8,128)} %get-tuple-element.9), channel_id=1, source_target_pairs={{0,3},{1,0},{2,1},{3,2},{4,7},{5,4},{6,5},{7,6},{8,11},{9,8},{10,9... | collective-permute-start | bytes 393224 | tf_op jit(solution)/shard_map/ppermute | solution.py:47
  54.2 11.7 %collective-permute-start.4 = (f32[128,256]{1,0:T(8,128)}, f32[128,256]{1,0:T(8,128)S(1)}, u32[]{:S(2)}, u32[]{:S(2)}) collective-permute-start(f32[128,256]{1,0:T(8,128)} %get-tuple-element.11), channel_id=1, source_target_pairs={{0,2},{1,3},{2,0},{3,1},{4,6},{5,7},{6,4},{7,5},{8,10},{9,11},{10,... | collective-permute-start | bytes 393224 | tf_op jit(solution)/shard_map/ppermute | solution.py:47
  54.2 11.7 %collective-permute-start.5 = (f32[128,256]{1,0:T(8,128)S(1)}, f32[128,256]{1,0:T(8,128)}, u32[]{:S(2)}, u32[]{:S(2)}) collective-permute-start(f32[128,256]{1,0:T(8,128)S(1)} %get-tuple-element.10), channel_id=1, source_target_pairs={{0,1},{1,2},{2,3},{3,0},{4,5},{5,6},{6,7},{7,4},{8,9},{9,10},{10,1... | collective-permute-start | bytes 393224 | tf_op jit(solution)/shard_map/ppermute | solution.py:47
  58.9 7.0 %collective-permute-start.8 = (f32[1,128,256]{2,1,0:T(8,128)S(1)}, f32[1,128,256]{2,1,0:T(8,128)S(1)}, u32[]{:S(2)}, u32[]{:S(2)}) collective-permute-start(f32[1,128,256]{2,1,0:T(8,128)S(1)} %constant_dynamic-slice_fusion), channel_id=1, source_target_pairs={{0,16},{4,20},{8,24},{12,28},{16,0},{20,4},{24,8},{28,12},{1,17},{... | collective-permute-start | bytes 393224 | tf_op jit(solution)/shard_map/ppermute | solution.py:26

commit v6 on v5

--- a/solution.py
+++ b/solution.py
@@ -16,15 +16,11 @@
 
 
 def grp_reduce_scatter(parts, grp_count):
-    me = lax.axis_index("grp")
     bit = 1
     while bit < grp_count:
-        half = parts.reshape((2, parts.shape[0] // 2) + parts.shape[1:])
-        mine = (me // bit) % 2
-        keep = half[mine]
-        send = half[1 - mine]
-        got = lax.ppermute(send, "grp", [(i, i ^ bit) for i in range(grp_count)])
-        parts = keep + got
+        half = parts.shape[0] // 2
+        got = lax.ppermute(parts[half:], "grp", [(i, i ^ bit) for i in range(grp_count)])
+        parts = parts[:half] + got
         bit *= 2
     return parts[0]
 
@@ -47,7 +43,7 @@
     return lax.ppermute(x, "ent", [(i, (i + shift) % ent_count) for i in range(ent_count)])
 
 
-def tile_kernel(rels_ref, groups_ref, slots_ref, alive_ref, in_ref, core_ref, panel_ref,
+def tile_kernel(rels_ref, groups_ref, slots_ref, alive_ref, shift_ref, in_ref, core_ref, panel_ref,
                 row_ref, owner_ref, *, per_relay, block):
     e = pl.program_id(0)
 
@@ -130,20 +126,21 @@
     rels = heads[:, :per_relay].astype(jnp.int32).reshape(count)
     alive = heads[:, per_relay : 2 * per_relay].astype(jnp.int32).reshape(count)
     groups = send_lists.reshape(count)
-    slots = bit_reverse(groups, grp_bits)
+    slots = bit_reverse(groups ^ lax.axis_index("grp"), grp_bits)
+    shifts = (my_ent - jnp.arange(ent_count, dtype=jnp.int32)) % ent_count
     rows_in = arrived.shape[1]
 
     grid_spec = pltpu.PrefetchScalarGridSpec(
-        num_scalar_prefetch=4,
+        num_scalar_prefetch=5,
         grid=(ent_count,),
         in_specs=[
-            pl.BlockSpec((1, rows_in, block), lambda e, r, g, s, a: (e, 0, 0)),
-            pl.BlockSpec((relations, width, width), lambda e, r, g, s, a: (0, 0, 0)),
-            pl.BlockSpec((grp_count, block, width), lambda e, r, g, s, a: (0, 0, 0)),
+            pl.BlockSpec((1, rows_in, block), lambda e, r, g, s, a, k: (e, 0, 0)),
+            pl.BlockSpec((relations, width, width), lambda e, r, g, s, a, k: (0, 0, 0)),
+            pl.BlockSpec((grp_count, block, width), lambda e, r, g, s, a, k: (0, 0, 0)),
         ],
         out_specs=[
-            pl.BlockSpec((1, block, width), lambda e, r, g, s, a: (e, 0, 0)),
-            pl.BlockSpec((grp_count, block, width), lambda e, r, g, s, a: (0, 0, 0)),
+            pl.BlockSpec((1, block, width), lambda e, r, g, s, a, k: (k[e], 0, 0)),
+            pl.BlockSpec((grp_count, block, width), lambda e, r, g, s, a, k: (0, 0, 0)),
         ],
     )
     row_parts, owner_terms = pl.pallas_call(
@@ -153,11 +150,11 @@
             jax.ShapeDtypeStruct((ent_count, block, width), jnp.float32),
             jax.ShapeDtypeStruct((grp_count, block, width), jnp.float32),
         ],
-    )(rels, groups, slots, alive, arrived, cores, group_blocks)
+    )(rels, groups, slots, alive, shifts, arrived, cores, group_blocks)
 
-    rows = row_parts[my_ent]
+    rows = row_parts[0]
     for k in range(1, ent_count):
-        rows = rows + shift_ent(row_parts[(my_ent - k) % ent_count], -k, ent_count)
+        rows = rows + shift_ent(row_parts[k], -k, ent_count)
     owner_part = grp_reduce_scatter(owner_terms, grp_count)
     return rows + owner_part
 

time: 67.9 us -> 65.9 us (0.971)
  local copies, waits for them, and re-layouts: 6.33 us -> 4.93 us
    squeeze x4 -> x1, local copies, waits for them, and re-layouts: 1.9 us -> 0.03 us  [on_device(): rows = rows + shift_ent(row_parts[k], -k, ent_count)]
    slice x0 -> x3, local copies, waits for them, and re-layouts: none -> 1.16 us  [grp_reduce_scatter(): parts[half:]]
    add x1, other arithmetic: 1.61 us -> 0.71 us  [on_device(): return rows + owner_part]
  transfers between devices with their start and end apart: 10 -> 10, of which waited for: 7 -> 8; matrix products, arithmetic and copies ran while one was open for 3% -> 3% of each run, Pallas kernels for 0% -> 0%
where the time goes in v6:
time: 65.9 us; the launch traced here: 65.5 us
  waiting for transfers between devices  32.4 us (49%)
  starting transfers between devices  15 us (23%)
  Pallas kernels  7.08 us (11%)
  other arithmetic  5.27 us (8%)
  local copies, waits for them, and re-layouts  4.93 us (7%)
  between operations  0.91 us (1%)
    all_to_all x1, waiting for transfers between devices, on_device(): lax.all_to_all(outgoing, 'ent', split_axis=0, concat_axis=0, tiled=True)  10.7 us
    ppermute x3, waiting for transfers between devices, grp_gather(): got = lax.ppermute(held, 'grp', [(i, i ^ bit) for i in range(grp_count)])  10.2 us
    pallas_call x1, Pallas kernels, on_device(): pl.pallas_call(lambda *refs: tile_kernel(*refs, per_relay=per_relay, bloc...  7.08 us
    ppermute x3, waiting for transfers between devices, grp_reduce_scatter(): lax.ppermute(parts[half:], 'grp', [(i, i ^ bit) for i in range(grp_count)])  6.56 us
    all_to_all x1, starting transfers between devices, on_device(): lax.all_to_all(outgoing, 'ent', split_axis=0, concat_axis=0, tiled=True)  6.45 us
    ppermute x3, waiting for transfers between devices, shift_ent(): lax.ppermute(x, 'ent', [(i, (i + shift) % ent_count) for i in range(ent_c...  4.88 us
    ppermute x3, starting transfers between devices, grp_reduce_scatter(): lax.ppermute(parts[half:], 'grp', [(i, i ^ bit) for i in range(grp_count)])  3.22 us
    ppermute x3, starting transfers between devices, grp_gather(): got = lax.ppermute(held, 'grp', [(i, i ^ bit) for i in range(grp_count)])  3.14 us
  transfers between devices with their start and end apart: 10, of which 8 were waited for; matrix products, arithmetic and copies ran while one was open for 3% of the time, Pallas kernels for 0%

profile of v6, /device:TPU:0, one launch (start us, length us, event | category | flops | bytes accessed | tf_op | source)
XLA Modules:
  0.0 65.5 jit_solution(12547973607961564430)
XLA Ops:
  0.0 0.0 copy-start
  0.0 0.0 copy-start.1
  0.8 0.1 compare_select_fusion
  0.9 0.1 reshape.109
  1.0 0.0 copy-start.4
  1.0 0.7 %gather_fusion.2 = bf16[24]{0:T(256)(128)(2,1)S(1)} fusion(bf16[24]{0:T(256)(128)(2,1)S(1)} %compare_convert_fusion, s32[1024]{0:T(1024)S(1)} %pad_clamp_fusion), kind=kCustom, calls=%fused_computation.2 | custom fusion | bytes 192 | tf_op jit(solution)/shard_map/gather | solution.py:115
  1.7 0.1 reshape.136
  1.8 0.0 copy-done.1
  1.8 0.7 %gather_fusion.1 = s32[24]{0:T(128)S(1)} fusion(s32[24]{0:T(128)S(1)} %bitcast.26, s32[1024]{0:T(1024)S(1)} %pad_clamp_fusion), kind=kCustom, calls=%fused_computation.1 | custom fusion | bytes 288 | tf_op jit(solution)/shard_map/gather | solution.py:115
  2.5 0.1 reshape.138
  2.6 0.0 copy-done.4
  2.6 0.0 copy-done
  2.6 0.6 gather_fusion
  3.3 0.2 convert_element_type.38
  3.4 0.1 fusion.6
  3.6 1.1 %pad_maximum_fusion = bf16[4,1040,128]{2,1,0:T(8,128)(2,1)} fusion(bf16[4,16,128]{2,1,0:T(8,128)(2,1)S(1)} %broadcast_in_dim.7, bf16[4,256,128]{2,1,0:T(8,128)(2,1)S(1)} %broadcast_in_dim.6, bf16[4,768,128]{2,1,0:T(8,128)(2,1)S(1)} %bitcast.27), kind=kLoop, calls=%fused_computation.3 | loop fusion | flops 3194880 | bytes 2129920 | tf_op jit(solution)/shard_map/concatenate | solution.py:119
  4.7 0.0 copy-start.6
  4.7 6.4 %all-to-all-start = ((bf16[4,1040,128]{2,1,0:T(8,128)(2,1)}), bf16[4,1040,128]{2,1,0:T(8,128)(2,1)S(1)}, u32[]{:S(2)}, u32[]{:S(2)}) async-start(bf16[4,1040,128]{2,1,0:T(8,128)(2,1)} %pad_maximum_fusion), calls=%async_computation | async-start | bytes 2129920 | tf_op jit(solution)/shard_map/all_to_all | solution.py:122
  11.1 0.0 collective-permute-start
  11.1 1.3 %collective-permute-done = bf16[1,128,256]{2,1,0:T(8,128)(2,1)S(1)} collective-permute-done((bf16[1,128,256]{2,1,0:T(8,128)(2,1)S(1)}, bf16[1,128,256]{2,1,0:T(8,128)(2,1)S(1)}, u32[]{:S(2)}, u32[]{:S(2)}) %collective-permute-start) | collective-permute-done | bytes 65568 | tf_op jit(solution)/shard_map/ppermute | solution.py:33
  12.4 1.6 %collective-permute-start.1 = (bf16[2,128,256]{2,1,0:T(8,128)(2,1)S(1)}, bf16[2,128,256]{2,1,0:T(8,128)(2,1)S(1)}, u32[]{:S(2)}, u32[]{:S(2)}) collective-permute-start(bf16[2,128,256]{2,1,0:T(8,128)(2,1)S(1)} %maximum_select_fusion.2), channel_id=1, source_target_pairs={{0,8},{4,12},{8,0},{12,4},{16,24},{20,28},{24,16},{28,20},{1,9},{5... | collective-permute-start | bytes 393224 | tf_op jit(solution)/shard_map/ppermute | solution.py:33
  13.9 4.1 %collective-permute-done.1 = bf16[2,128,256]{2,1,0:T(8,128)(2,1)S(1)} collective-permute-done((bf16[2,128,256]{2,1,0:T(8,128)(2,1)S(1)}, bf16[2,128,256]{2,1,0:T(8,128)(2,1)S(1)}, u32[]{:S(2)}, u32[]{:S(2)}) %collective-permute-start.1) | collective-permute-done | bytes 131104 | tf_op jit(solution)/shard_map/ppermute | solution.py:33
  18.0 1.6 %collective-permute-start.2 = (bf16[4,128,256]{2,1,0:T(8,128)(2,1)S(1)}, bf16[4,128,256]{2,1,0:T(8,128)(2,1)S(1)}, u32[]{:S(2)}, u32[]{:S(2)}) collective-permute-start(bf16[4,128,256]{2,1,0:T(8,128)(2,1)S(1)} %maximum_select_fusion.1), channel_id=1, source_target_pairs={{0,16},{4,20},{8,24},{12,28},{16,0},{20,4},{24,8},{28,12},{1,17},{... | collective-permute-start | bytes 786440 | tf_op jit(solution)/shard_map/ppermute | solution.py:33
  19.6 0.5 and_select_fusion.refs_4_
  20.1 0.0 copy-done.6
  20.1 0.1 reshape.104.refs_1_
  20.2 0.0 copy-start.5
  20.2 0.5 shift-left_or_fusion.refs_2_
  20.7 4.9 %collective-permute-done.2 = bf16[4,128,256]{2,1,0:T(8,128)(2,1)S(1)} collective-permute-done((bf16[4,128,256]{2,1,0:T(8,128)(2,1)S(1)}, bf16[4,128,256]{2,1,0:T(8,128)(2,1)S(1)}, u32[]{:S(2)}, u32[]{:S(2)}) %collective-permute-start.2) | collective-permute-done | bytes 262176 | tf_op jit(solution)/shard_map/ppermute | solution.py:33
  25.6 0.9 %maximum_select_fusion.refs_7_ = bf16[8,128,256]{2,1,0:T(8,128)(2,1)} fusion(bf16[4,128,256]{2,1,0:T(8,128)(2,1)S(1)} %collective-permute-done.2, bf16[4,128,256]{2,1,0:T(8,128)(2,1)S(1)} %maximum_select_fusion.1, pred[]{:T(512)S(6)} %eq.17), kind=kLoop, calls=%fused_computation.4 | loop fusion | flops 786432 | bytes 1048577 | tf_op jit(solution)/shard_map/jit(_where)/select_n | solution.py:35
  26.5 10.7 %all-to-all-done.refs_5_ = bf16[4,1040,128]{2,1,0:T(8,128)(2,1)S(1)} async-done(((bf16[4,1040,128]{2,1,0:T(8,128)(2,1)}), bf16[4,1040,128]{2,1,0:T(8,128)(2,1)S(1)}, u32[]{:S(2)}, u32[]{:S(2)}) %all-to-all-start) | async-done | bytes 1064992 | tf_op jit(solution)/shard_map/all_to_all | solution.py:122
  37.2 0.0 copy-start.2
  37.2 0.1 slice_convert_fusion.1
  37.3 0.7 %reshape.105.refs_3_ = s32[24]{0:T(128)} reshape(s32[4,6]{1,0:T(4,128)S(1)} %get-tuple-element.14) | data formatting | bytes 192 | tf_op jit(solution)/shard_map/reshape | solution.py:127
  37.9 0.6 reshape.103.refs_0_
  38.5 0.0 copy-done.5
  38.5 0.0 copy-done.2
  38.5 7.1 %shard_map.64 = (f32[4,128,256]{2,1,0:T(8,128)}, f32[8,128,256]{2,1,0:T(8,128)}) custom-call(s32[24]{0:T(128)} %reshape.103.refs_0_, s32[24]{0:T(128)} %copy-done.5, s32[24]{0:T(128)} %shift-left_or_fusion.refs_2_, s32[24]{0:T(128)} %reshape.105.refs_3_, s32[4]{0:T(128)} %and_select_fusion.refs_4_, bf16[4,1040,128]{2,1,0:T(8,128)(2,1)} %copy-done.2, ...), custom_call_target="tpu_custom_call" | custom-call | tf_op jit(solution)/shard_map/pallas_call | solution.py:146
  45.6 0.0 copy-start.3
  45.6 1.1 %slice.55 = f32[4,128,256]{2,1,0:T(8,128)S(1)} slice(f32[8,128,256]{2,1,0:T(8,128)} %get-tuple-element.8), slice={[4:8], [0:128], [0:256]} | slice | bytes 1048576 | tf_op jit(solution)/shard_map/slice | solution.py:22
  46.8 0.1 collective-permute-start.6
  46.8 1.9 %collective-permute-done.6 = f32[4,128,256]{2,1,0:T(8,128)S(1)} collective-permute-done((f32[4,128,256]{2,1,0:T(8,128)S(1)}, f32[4,128,256]{2,1,0:T(8,128)S(1)}, u32[]{:S(2)}, u32[]{:S(2)}) %collective-permute-start.6) | collective-permute-done | bytes 524320 | tf_op jit(solution)/shard_map/ppermute | solution.py:22
  48.7 1.1 %slice_add_fusion = f32[4,128,256]{2,1,0:T(8,128)S(1)} fusion(f32[4,128,256]{2,1,0:T(8,128)S(1)} %collective-permute-done.6, f32[8,128,256]{2,1,0:T(8,128)} %get-tuple-element.8), kind=kLoop, calls=%fused_computation.5 | loop fusion | flops 131072 | bytes 1572864 | tf_op jit(solution)/shard_map/add | solution.py:23
  49.9 1.6 %collective-permute-start.7 = (f32[2,128,256]{2,1,0:T(8,128)S(1)}, f32[2,128,256]{2,1,0:T(8,128)S(1)}, u32[]{:S(2)}, u32[]{:S(2)}) collective-permute-start(f32[2,128,256]{2,1,0:T(8,128)S(1)} %slice.68), channel_id=1, source_target_pairs={{0,8},{4,12},{8,0},{12,4},{16,24},{20,28},{24,16},{28,20},{1,9},{5... | collective-permute-start | bytes 786440 | tf_op jit(solution)/shard_map/ppermute | solution.py:22
  51.4 0.0 copy-done.3
  51.5 1.5 %collective-permute-start.3 = (f32[128,256]{1,0:T(8,128)S(1)}, f32[128,256]{1,0:T(8,128)S(1)}, u32[]{:S(2)}, u32[]{:S(2)}) collective-permute-start(f32[128,256]{1,0:T(8,128)S(1)} %get-tuple-element.9), channel_id=1, source_target_pairs={{0,3},{1,0},{2,1},{3,2},{4,7},{5,4},{6,5},{7,6},{8,11},{9,8},{10,9... | collective-permute-start | bytes 393224 | tf_op jit(solution)/shard_map/ppermute | solution.py:43
  53.0 0.6 collective-permute-start.5
  53.5 0.1 collective-permute-start.4
  53.6 4.7 %collective-permute-done.7 = f32[2,128,256]{2,1,0:T(8,128)S(1)} collective-permute-done((f32[2,128,256]{2,1,0:T(8,128)S(1)}, f32[2,128,256]{2,1,0:T(8,128)S(1)}, u32[]{:S(2)}, u32[]{:S(2)}) %collective-permute-start.7) | collective-permute-done | bytes 262176 | tf_op jit(solution)/shard_map/ppermute | solution.py:22
  58.3 1.6 %collective-permute-start.8 = (f32[1,128,256]{2,1,0:T(8,128)S(1)}, f32[1,128,256]{2,1,0:T(8,128)S(1)}, u32[]{:S(2)}, u32[]{:S(2)}) collective-permute-start(f32[1,128,256]{2,1,0:T(8,128)S(1)} %slice.70), channel_id=1, source_target_pairs={{0,16},{4,20},{8,24},{12,28},{16,0},{20,4},{24,8},{28,12},{1,17},{... | collective-permute-start | bytes 393224 | tf_op jit(solution)/shard_map/ppermute | solution.py:22
  59.9 0.0 collective-permute-done.3
  59.9 1.3 %collective-permute-done.5 = f32[128,256]{1,0:T(8,128)S(1)} collective-permute-done((f32[128,256]{1,0:T(8,128)S(1)}, f32[128,256]{1,0:T(8,128)S(1)}, u32[]{:S(2)}, u32[]{:S(2)}) %collective-permute-start.5) | collective-permute-done | bytes 131104 | tf_op jit(solution)/shard_map/ppermute | solution.py:43
  61.3 3.5 %collective-permute-done.4 = f32[128,256]{1,0:T(8,128)S(1)} collective-permute-done((f32[128,256]{1,0:T(8,128)S(1)}, f32[128,256]{1,0:T(8,128)S(1)}, u32[]{:S(2)}, u32[]{:S(2)}) %collective-permute-start.4) | collective-permute-done | bytes 131104 | tf_op jit(solution)/shard_map/ppermute | solution.py:43
  64.8 0.0 collective-permute-done.8
  64.8 0.7 %fusion.1 = f32[128,256]{1,0:T(8,128)} fusion(f32[1,128,256]{2,1,0:T(8,128)S(1)} %collective-permute-done.8, f32[2,128,256]{2,1,0:T(8,128)S(1)} %slice_add_fusion.1, f32[128,256]{1,0:T(8,128)S(1)} %collective-permute-done.5, f32[128,256]{1,0:T(8,128)S(1)} %collective-permute-done.4, f32[128,256]{1,0:T(8,128)S(1)} %collective-permute-done.3, ...), kind=kLoop, calls=%fused_computation.10 | loop fusion | flops 163840 | bytes 917504 | tf_op jit(solution)/shard_map/add | solution.py:159
  (16 shorter events, 0.2 us)
Async XLA Ops:
  0.0 2.6 %copy-start = (s32[24,128,128]{2,1,0:T(8,128)S(1)}, s32[24,128,128]{2,1,0:T(8,128)}, u32[]{:S(2)}) copy-start(s32[24,128,128]{2,1,0:T(8,128)} %param.8) | copy-start | bytes 4718596
  0.0 1.8 %copy-start.1 = (s32[1,24]{1,0:T(1,128)S(1)}, s32[1,24]{1,0:T(1,128)}, u32[]{:S(2)}) copy-start(s32[1,24]{1,0:T(1,128)} %param.9) | copy-start | bytes 292
  1.0 1.6 %copy-start.4 = (bf16[128,256]{1,0:T(8,128)(2,1)S(1)}, bf16[128,256]{1,0:T(8,128)(2,1)}, u32[]{:S(2)}) copy-start(bf16[128,256]{1,0:T(8,128)(2,1)} %param.6) | copy-start | bytes 196612
  4.7 15.5 %copy-start.6 = (s32[1,4,6]{2,1,0:T(4,128)S(1)}, s32[1,4,6]{2,1,0:T(4,128)}, u32[]{:S(2)}) copy-start(s32[1,4,6]{2,1,0:T(4,128)} %param.11) | copy-start | bytes 292
  4.7 32.5 %all-to-all-start = ((bf16[4,1040,128]{2,1,0:T(8,128)(2,1)}), bf16[4,1040,128]{2,1,0:T(8,128)(2,1)S(1)}, u32[]{:S(2)}, u32[]{:S(2)}) async-start(bf16[4,1040,128]{2,1,0:T(8,128)(2,1)} %pad_maximum_fusion), calls=%async_computation | async-start | bytes 2129920 | tf_op jit(solution)/shard_map/all_to_all | solution.py:122
  11.1 1.3 %collective-permute-start = (bf16[1,128,256]{2,1,0:T(8,128)(2,1)S(1)}, bf16[1,128,256]{2,1,0:T(8,128)(2,1)S(1)}, u32[]{:S(2)}, u32[]{:S(2)}) collective-permute-start(bf16[1,128,256]{2,1,0:T(8,128)(2,1)S(1)} %bitcast.28), channel_id=1, source_target_pairs={{0,4},{4,0},{8,12},{12,8},{16,20},{20,16},{24,28},{28,24},{1,5},{5... | collective-permute-start | bytes 196616 | tf_op jit(solution)/shard_map/ppermute | solution.py:33
  12.4 5.6 %collective-permute-start.1 = (bf16[2,128,256]{2,1,0:T(8,128)(2,1)S(1)}, bf16[2,128,256]{2,1,0:T(8,128)(2,1)S(1)}, u32[]{:S(2)}, u32[]{:S(2)}) collective-permute-start(bf16[2,128,256]{2,1,0:T(8,128)(2,1)S(1)} %maximum_select_fusion.2), channel_id=1, source_target_pairs={{0,8},{4,12},{8,0},{12,4},{16,24},{20,28},{24,16},{28,20},{1,9},{5... | collective-permute-start | bytes 393224 | tf_op jit(solution)/shard_map/ppermute | solution.py:33
  18.0 7.6 %collective-permute-start.2 = (bf16[4,128,256]{2,1,0:T(8,128)(2,1)S(1)}, bf16[4,128,256]{2,1,0:T(8,128)(2,1)S(1)}, u32[]{:S(2)}, u32[]{:S(2)}) collective-permute-start(bf16[4,128,256]{2,1,0:T(8,128)(2,1)S(1)} %maximum_select_fusion.1), channel_id=1, source_target_pairs={{0,16},{4,20},{8,24},{12,28},{16,0},{20,4},{24,8},{28,12},{1,17},{... | collective-permute-start | bytes 786440 | tf_op jit(solution)/shard_map/ppermute | solution.py:33
  20.2 18.3 %copy-start.5 = (s32[24]{0:T(128)}, s32[24]{0:T(128)S(1)}, u32[]{:S(2)}) copy-start(s32[24]{0:T(128)S(1)} %reshape.104.refs_1_) | copy-start | bytes 292
  37.2 1.4 %copy-start.2 = (bf16[4,1040,128]{2,1,0:T(8,128)(2,1)}, bf16[4,1040,128]{2,1,0:T(8,128)(2,1)S(1)}, u32[]{:S(2)}) copy-start(bf16[4,1040,128]{2,1,0:T(8,128)(2,1)S(1)} %all-to-all-done.refs_5_) | copy-start | bytes 3194884
  45.6 5.8 %copy-start.3 = (f32[4,128,256]{2,1,0:T(8,128)S(1)}, f32[4,128,256]{2,1,0:T(8,128)}, u32[]{:S(2)}) copy-start(f32[4,128,256]{2,1,0:T(8,128)} %get-tuple-element.7) | copy-start | bytes 1572868
  46.8 2.0 %collective-permute-start.6 = (f32[4,128,256]{2,1,0:T(8,128)S(1)}, f32[4,128,256]{2,1,0:T(8,128)S(1)}, u32[]{:S(2)}, u32[]{:S(2)}) collective-permute-start(f32[4,128,256]{2,1,0:T(8,128)S(1)} %slice.55), channel_id=1, source_target_pairs={{0,4},{4,0},{8,12},{12,8},{16,20},{20,16},{24,28},{28,24},{1,5},{5... | collective-permute-start | bytes 1572872 | tf_op jit(solution)/shard_map/ppermute | solution.py:22
  49.9 8.4 %collective-permute-start.7 = (f32[2,128,256]{2,1,0:T(8,128)S(1)}, f32[2,128,256]{2,1,0:T(8,128)S(1)}, u32[]{:S(2)}, u32[]{:S(2)}) collective-permute-start(f32[2,128,256]{2,1,0:T(8,128)S(1)} %slice.68), channel_id=1, source_target_pairs={{0,8},{4,12},{8,0},{12,4},{16,24},{20,28},{24,16},{28,20},{1,9},{5... | collective-permute-start | bytes 786440 | tf_op jit(solution)/shard_map/ppermute | solution.py:22
  51.5 8.5 %collective-permute-start.3 = (f32[128,256]{1,0:T(8,128)S(1)}, f32[128,256]{1,0:T(8,128)S(1)}, u32[]{:S(2)}, u32[]{:S(2)}) collective-permute-start(f32[128,256]{1,0:T(8,128)S(1)} %get-tuple-element.9), channel_id=1, source_target_pairs={{0,3},{1,0},{2,1},{3,2},{4,7},{5,4},{6,5},{7,6},{8,11},{9,8},{10,9... | collective-permute-start | bytes 393224 | tf_op jit(solution)/shard_map/ppermute | solution.py:43
  53.0 8.3 %collective-permute-start.5 = (f32[128,256]{1,0:T(8,128)S(1)}, f32[128,256]{1,0:T(8,128)S(1)}, u32[]{:S(2)}, u32[]{:S(2)}) collective-permute-start(f32[128,256]{1,0:T(8,128)S(1)} %get-tuple-element.10), channel_id=1, source_target_pairs={{0,1},{1,2},{2,3},{3,0},{4,5},{5,6},{6,7},{7,4},{8,9},{9,10},{10,1... | collective-permute-start | bytes 393224 | tf_op jit(solution)/shard_map/ppermute | solution.py:43
  53.5 11.3 %collective-permute-start.4 = (f32[128,256]{1,0:T(8,128)S(1)}, f32[128,256]{1,0:T(8,128)S(1)}, u32[]{:S(2)}, u32[]{:S(2)}) collective-permute-start(f32[128,256]{1,0:T(8,128)S(1)} %get-tuple-element.11), channel_id=1, source_target_pairs={{0,2},{1,3},{2,0},{3,1},{4,6},{5,7},{6,4},{7,5},{8,10},{9,11},{10,... | collective-permute-start | bytes 393224 | tf_op jit(solution)/shard_map/ppermute | solution.py:43
  58.3 6.5 %collective-permute-start.8 = (f32[1,128,256]{2,1,0:T(8,128)S(1)}, f32[1,128,256]{2,1,0:T(8,128)S(1)}, u32[]{:S(2)}, u32[]{:S(2)}) collective-permute-start(f32[1,128,256]{2,1,0:T(8,128)S(1)} %slice.70), channel_id=1, source_target_pairs={{0,16},{4,20},{8,24},{12,28},{16,0},{20,4},{24,8},{28,12},{1,17},{... | collective-permute-start | bytes 393224 | tf_op jit(solution)/shard_map/ppermute | solution.py:22

commit v7 on v6

--- a/solution.py
+++ b/solution.py
@@ -104,15 +104,22 @@
     grp_bits = grp_count.bit_length() - 1
     relations = cores.shape[0]
 
-    tile_ids = jnp.arange(tiles, dtype=jnp.int32)
-    live = (tile_ids < tile_count.reshape(())).astype(jnp.float32)
     relay_ids = jnp.arange(ent_count, dtype=jnp.int32)
     slot_ids = jnp.arange(per_relay, dtype=jnp.int32)
     tile_of = slot_ids[None, :] * ent_count + (relay_ids[:, None] - my_ent) % ent_count
-    adj_out = adjacency[tile_of].astype(jnp.bfloat16).reshape(ent_count, per_relay * block, block)
+    live = (tile_of < tile_count.reshape(())).astype(jnp.float32)
+    start = (ent_count - my_ent) % ent_count
+
+    def by_relay(x):
+        doubled = jnp.concatenate([x, x], axis=1)
+        return jnp.swapaxes(lax.dynamic_slice_in_dim(doubled, start, ent_count, axis=1), 0, 1)
+
+    adj_out = by_relay(adjacency.reshape(per_relay, ent_count, block, block)).astype(
+        jnp.bfloat16
+    ).reshape(ent_count, per_relay * block, block)
     halves = jnp.concatenate([factor[:, :block], factor[:, block:]], axis=0)
     head = jnp.concatenate(
-        [tile_rels.reshape(tiles)[tile_of].astype(jnp.float32), live[tile_of]], axis=1
+        [by_relay(tile_rels.reshape(per_relay, ent_count)).astype(jnp.float32), live], axis=1
     )
     head = jnp.pad(head, ((0, 0), (0, block - 2 * per_relay)))
     head = jnp.broadcast_to(head[:, None, :], (ent_count, head_rows, block)).astype(jnp.bfloat16)

time: 65.9 us -> 67.9 us (1.030)
  other arithmetic: 5.27 us -> 8.22 us
  local copies, waits for them, and re-layouts: 4.93 us -> 4.24 us
    gather x3 -> x0, local copies, waits for them, and re-layouts: 2.06 us -> none  [the longest x1 0.71 us: on_device(): tile_rels.reshape(tiles)[tile_of].astype(jnp.float32)]
    convert_element_type x2, other arithmetic: 0.16 us -> 1.72 us  [the longest x1 1.64 us: on_device(): by_relay(adjacency.reshape(per_relay, ent_count, block, block))]
    unnamed x0 -> x1, other arithmetic: none -> 1.22 us
    slice x1, local copies, waits for them, and re-layouts: 0.01 us -> 0.78 us  [on_device(): halves = jnp.concatenate([factor[:, :block], factor[:, block:]], axis=0)]
where the time goes in v7:
time: 67.9 us; the launch traced here: 67.4 us
  waiting for transfers between devices  32.2 us (47%)
  starting transfers between devices  14.9 us (22%)
  other arithmetic  8.22 us (12%)
  Pallas kernels  7.1 us (10%)
  local copies, waits for them, and re-layouts  4.24 us (6%)
  between operations  0.76 us (1%)
    all_to_all x1, waiting for transfers between devices, on_device(): lax.all_to_all(outgoing, 'ent', split_axis=0, concat_axis=0, tiled=True)  10.7 us
    ppermute x3, waiting for transfers between devices, grp_gather(): got = lax.ppermute(held, 'grp', [(i, i ^ bit) for i in range(grp_count)])  10.1 us
    pallas_call x1, Pallas kernels, on_device(): pl.pallas_call(lambda *refs: tile_kernel(*refs, per_relay=per_relay, bloc...  7.1 us
    ppermute x3, waiting for transfers between devices, grp_reduce_scatter(): lax.ppermute(parts[half:], 'grp', [(i, i ^ bit) for i in range(grp_count)])  6.56 us
    all_to_all x1, starting transfers between devices, on_device(): lax.all_to_all(outgoing, 'ent', split_axis=0, concat_axis=0, tiled=True)  6.4 us
    ppermute x3, waiting for transfers between devices, shift_ent(): lax.ppermute(x, 'ent', [(i, (i + shift) % ent_count) for i in range(ent_c...  4.88 us
    ppermute x3, starting transfers between devices, grp_reduce_scatter(): lax.ppermute(parts[half:], 'grp', [(i, i ^ bit) for i in range(grp_count)])  3.23 us
    ppermute x3, starting transfers between devices, grp_gather(): got = lax.ppermute(held, 'grp', [(i, i ^ bit) for i in range(grp_count)])  3.14 us
  transfers between devices with their start and end apart: 10, of which 8 were waited for; matrix products, arithmetic and copies ran while one was open for 3% of the time, Pallas kernels for 0%

profile of v7, /device:TPU:0, one launch (start us, length us, event | category | flops | bytes accessed | tf_op | source)
XLA Modules:
  0.0 67.4 jit_solution(17042657100541640750)
XLA Ops:
  0.7 0.5 broadcast.86
  1.2 1.2 %reduce.3 = s32[24]{0:T(128)S(1)} reduce(s32[1,24]{1,0:T(1,128)} %param.9, s32[]{:T(128)} %broadcast.86), dimensions={0}, to_apply=%param.9.reduce_sub_computation.3 | reduce | bytes 196 | tf_op args[3]
  2.4 0.1 reshape.54
  2.5 0.1 pad_add_fusion
  2.5 0.1 fusion.5
  2.6 0.1 copy.15
  2.7 0.8 %fusion.11 = (bf16[128,128]{1,0:T(8,128)(2,1)S(1)}, bf16[128,128]{1,0:T(8,128)(2,1)S(1)}) fusion(bf16[128,256]{1,0:T(8,128)(2,1)} %param.6), kind=kLoop, calls=%fused_computation.42 | loop fusion | bytes 131072 | tf_op jit(solution)/shard_map/slice | solution.py:120
  3.5 1.6 %copy_convert_fusion = bf16[6,4,128,128]{3,2,0,1:T(8,128)(2,1)S(1)} fusion(s32[]{:T(128)S(6)} %select_n.73, s32[6,4,128,128]{3,2,1,0:T(8,128)} %bitcast.29), kind=kLoop, calls=%fused_computation.3 | loop fusion | flops 786432 | bytes 2359300 | tf_op jit(solution)/shard_map/convert_element_type | solution.py:117
  5.1 0.1 convert_convert_fusion.1
  5.2 0.1 fusion.8
  5.4 1.1 %pad_maximum_fusion = bf16[4,1040,128]{2,1,0:T(8,128)(2,1)} fusion(bf16[4,16,128]{2,1,0:T(8,128)(2,1)S(1)} %broadcast_in_dim.7, bf16[4,256,128]{2,1,0:T(8,128)(2,1)S(1)} %broadcast_in_dim.6, bf16[4,768,128]{2,1,0:T(8,128)(2,1)S(1)} %bitcast.28), kind=kLoop, calls=%fused_computation.4 | loop fusion | flops 3194880 | bytes 2129920 | tf_op jit(solution)/shard_map/concatenate | solution.py:126
  6.4 0.0 copy-start.2
  6.4 0.0 copy-start.4
  6.4 6.4 %all-to-all-start = ((bf16[4,1040,128]{2,1,0:T(8,128)(2,1)}), bf16[4,1040,128]{2,1,0:T(8,128)(2,1)S(1)}, u32[]{:S(2)}, u32[]{:S(2)}) async-start(bf16[4,1040,128]{2,1,0:T(8,128)(2,1)} %pad_maximum_fusion), calls=%async_computation | async-start | bytes 2129920 | tf_op jit(solution)/shard_map/all_to_all | solution.py:129
  12.8 0.0 copy-done.2
  12.8 0.0 collective-permute-start
  12.8 1.2 %collective-permute-done = bf16[1,128,256]{2,1,0:T(8,128)(2,1)S(1)} collective-permute-done((bf16[1,128,256]{2,1,0:T(8,128)(2,1)S(1)}, bf16[1,128,256]{2,1,0:T(8,128)(2,1)S(1)}, u32[]{:S(2)}, u32[]{:S(2)}) %collective-permute-start) | collective-permute-done | bytes 65568 | tf_op jit(solution)/shard_map/ppermute | solution.py:33
  14.1 1.6 %collective-permute-start.1 = (bf16[2,128,256]{2,1,0:T(8,128)(2,1)S(1)}, bf16[2,128,256]{2,1,0:T(8,128)(2,1)S(1)}, u32[]{:S(2)}, u32[]{:S(2)}) collective-permute-start(bf16[2,128,256]{2,1,0:T(8,128)(2,1)S(1)} %maximum_select_fusion.2), channel_id=1, source_target_pairs={{0,8},{4,12},{8,0},{12,4},{16,24},{20,28},{24,16},{28,20},{1,9},{5... | collective-permute-start | bytes 393224 | tf_op jit(solution)/shard_map/ppermute | solution.py:33
  15.7 4.1 %collective-permute-done.1 = bf16[2,128,256]{2,1,0:T(8,128)(2,1)S(1)} collective-permute-done((bf16[2,128,256]{2,1,0:T(8,128)(2,1)S(1)}, bf16[2,128,256]{2,1,0:T(8,128)(2,1)S(1)}, u32[]{:S(2)}, u32[]{:S(2)}) %collective-permute-start.1) | collective-permute-done | bytes 131104 | tf_op jit(solution)/shard_map/ppermute | solution.py:33
  19.8 1.6 %collective-permute-start.2 = (bf16[4,128,256]{2,1,0:T(8,128)(2,1)S(1)}, bf16[4,128,256]{2,1,0:T(8,128)(2,1)S(1)}, u32[]{:S(2)}, u32[]{:S(2)}) collective-permute-start(bf16[4,128,256]{2,1,0:T(8,128)(2,1)S(1)} %maximum_select_fusion.1), channel_id=1, source_target_pairs={{0,16},{4,20},{8,24},{12,28},{16,0},{20,4},{24,8},{28,12},{1,17},{... | collective-permute-start | bytes 786440 | tf_op jit(solution)/shard_map/ppermute | solution.py:33
  21.3 0.6 and_select_fusion.refs_4_
  21.9 0.0 copy-done.4
  21.9 0.1 reshape.57.refs_1_
  22.0 0.0 copy-start.3
  22.0 0.5 shift-left_or_fusion.refs_2_
  22.5 4.8 %collective-permute-done.2 = bf16[4,128,256]{2,1,0:T(8,128)(2,1)S(1)} collective-permute-done((bf16[4,128,256]{2,1,0:T(8,128)(2,1)S(1)}, bf16[4,128,256]{2,1,0:T(8,128)(2,1)S(1)}, u32[]{:S(2)}, u32[]{:S(2)}) %collective-permute-start.2) | collective-permute-done | bytes 262176 | tf_op jit(solution)/shard_map/ppermute | solution.py:33
  27.4 0.9 %maximum_select_fusion.refs_7_ = bf16[8,128,256]{2,1,0:T(8,128)(2,1)} fusion(bf16[4,128,256]{2,1,0:T(8,128)(2,1)S(1)} %collective-permute-done.2, bf16[4,128,256]{2,1,0:T(8,128)(2,1)S(1)} %maximum_select_fusion.1, pred[]{:T(512)S(6)} %eq.18), kind=kLoop, calls=%fused_computation.5 | loop fusion | flops 786432 | bytes 1048577 | tf_op jit(solution)/shard_map/jit(_where)/select_n | solution.py:35
  28.2 10.7 %all-to-all-done.refs_5_ = bf16[4,1040,128]{2,1,0:T(8,128)(2,1)S(1)} async-done(((bf16[4,1040,128]{2,1,0:T(8,128)(2,1)}), bf16[4,1040,128]{2,1,0:T(8,128)(2,1)S(1)}, u32[]{:S(2)}, u32[]{:S(2)}) %all-to-all-start) | async-done | bytes 1064992 | tf_op jit(solution)/shard_map/all_to_all | solution.py:129
  38.9 0.0 copy-start
  38.9 0.1 slice_convert_fusion.1
  39.0 0.9 %reshape.58.refs_3_ = s32[24]{0:T(128)} reshape(s32[4,6]{1,0:T(4,128)S(1)} %get-tuple-element.14) | data formatting | bytes 192 | tf_op jit(solution)/shard_map/reshape | solution.py:134
  39.8 0.6 reshape.56.refs_0_
  40.4 0.0 copy-done.3
  40.4 0.0 copy-done
  40.4 7.1 %shard_map.64 = (f32[4,128,256]{2,1,0:T(8,128)}, f32[8,128,256]{2,1,0:T(8,128)}) custom-call(s32[24]{0:T(128)} %reshape.56.refs_0_, s32[24]{0:T(128)} %copy-done.3, s32[24]{0:T(128)} %shift-left_or_fusion.refs_2_, s32[24]{0:T(128)} %reshape.58.refs_3_, s32[4]{0:T(128)} %and_select_fusion.refs_4_, bf16[4,1040,128]{2,1,0:T(8,128)(2,1)} %copy-done, ...), custom_call_target="tpu_custom_call" | custom-call | tf_op jit(solution)/shard_map/pallas_call | solution.py:153
  47.5 0.0 copy-start.1
  47.5 1.1 %slice.55 = f32[4,128,256]{2,1,0:T(8,128)S(1)} slice(f32[8,128,256]{2,1,0:T(8,128)} %get-tuple-element.8), slice={[4:8], [0:128], [0:256]} | slice | bytes 1048576 | tf_op jit(solution)/shard_map/slice | solution.py:22
  48.7 0.1 collective-permute-start.6
  48.8 1.9 %collective-permute-done.6 = f32[4,128,256]{2,1,0:T(8,128)S(1)} collective-permute-done((f32[4,128,256]{2,1,0:T(8,128)S(1)}, f32[4,128,256]{2,1,0:T(8,128)S(1)}, u32[]{:S(2)}, u32[]{:S(2)}) %collective-permute-start.6) | collective-permute-done | bytes 524320 | tf_op jit(solution)/shard_map/ppermute | solution.py:22
  50.7 1.1 %slice_add_fusion = f32[4,128,256]{2,1,0:T(8,128)S(1)} fusion(f32[4,128,256]{2,1,0:T(8,128)S(1)} %collective-permute-done.6, f32[8,128,256]{2,1,0:T(8,128)} %get-tuple-element.8), kind=kLoop, calls=%fused_computation.6 | loop fusion | flops 131072 | bytes 1572864 | tf_op jit(solution)/shard_map/add | solution.py:23
  51.8 1.6 %collective-permute-start.7 = (f32[2,128,256]{2,1,0:T(8,128)S(1)}, f32[2,128,256]{2,1,0:T(8,128)S(1)}, u32[]{:S(2)}, u32[]{:S(2)}) collective-permute-start(f32[2,128,256]{2,1,0:T(8,128)S(1)} %slice.62), channel_id=1, source_target_pairs={{0,8},{4,12},{8,0},{12,4},{16,24},{20,28},{24,16},{28,20},{1,9},{5... | collective-permute-start | bytes 786440 | tf_op jit(solution)/shard_map/ppermute | solution.py:22
  53.4 0.0 copy-done.1
  53.4 1.5 %collective-permute-start.3 = (f32[128,256]{1,0:T(8,128)S(1)}, f32[128,256]{1,0:T(8,128)S(1)}, u32[]{:S(2)}, u32[]{:S(2)}) collective-permute-start(f32[128,256]{1,0:T(8,128)S(1)} %get-tuple-element.9), channel_id=1, source_target_pairs={{0,3},{1,0},{2,1},{3,2},{4,7},{5,4},{6,5},{7,6},{8,11},{9,8},{10,9... | collective-permute-start | bytes 393224 | tf_op jit(solution)/shard_map/ppermute | solution.py:43
  54.9 0.5 collective-permute-start.5
  55.5 0.1 collective-permute-start.4
  55.6 4.7 %collective-permute-done.7 = f32[2,128,256]{2,1,0:T(8,128)S(1)} collective-permute-done((f32[2,128,256]{2,1,0:T(8,128)S(1)}, f32[2,128,256]{2,1,0:T(8,128)S(1)}, u32[]{:S(2)}, u32[]{:S(2)}) %collective-permute-start.7) | collective-permute-done | bytes 262176 | tf_op jit(solution)/shard_map/ppermute | solution.py:22
  60.3 1.6 %collective-permute-start.8 = (f32[1,128,256]{2,1,0:T(8,128)S(1)}, f32[1,128,256]{2,1,0:T(8,128)S(1)}, u32[]{:S(2)}, u32[]{:S(2)}) collective-permute-start(f32[1,128,256]{2,1,0:T(8,128)S(1)} %slice.64), channel_id=1, source_target_pairs={{0,16},{4,20},{8,24},{12,28},{16,0},{20,4},{24,8},{28,12},{1,17},{... | collective-permute-start | bytes 393224 | tf_op jit(solution)/shard_map/ppermute | solution.py:22
  61.9 0.0 collective-permute-done.3
  61.9 1.3 %collective-permute-done.5 = f32[128,256]{1,0:T(8,128)S(1)} collective-permute-done((f32[128,256]{1,0:T(8,128)S(1)}, f32[128,256]{1,0:T(8,128)S(1)}, u32[]{:S(2)}, u32[]{:S(2)}) %collective-permute-start.5) | collective-permute-done | bytes 131104 | tf_op jit(solution)/shard_map/ppermute | solution.py:43
  63.2 3.5 %collective-permute-done.4 = f32[128,256]{1,0:T(8,128)S(1)} collective-permute-done((f32[128,256]{1,0:T(8,128)S(1)}, f32[128,256]{1,0:T(8,128)S(1)}, u32[]{:S(2)}, u32[]{:S(2)}) %collective-permute-start.4) | collective-permute-done | bytes 131104 | tf_op jit(solution)/shard_map/ppermute | solution.py:43
  66.7 0.0 collective-permute-done.8
  66.7 0.7 %fusion.2 = f32[128,256]{1,0:T(8,128)} fusion(f32[1,128,256]{2,1,0:T(8,128)S(1)} %collective-permute-done.8, f32[2,128,256]{2,1,0:T(8,128)S(1)} %slice_add_fusion.1, f32[128,256]{1,0:T(8,128)S(1)} %collective-permute-done.5, f32[128,256]{1,0:T(8,128)S(1)} %collective-permute-done.4, f32[128,256]{1,0:T(8,128)S(1)} %collective-permute-done.3, ...), kind=kLoop, calls=%fused_computation.11 | loop fusion | flops 163840 | bytes 917504 | tf_op jit(solution)/shard_map/add | solution.py:166
  (12 shorter events, 0.2 us)
Async XLA Ops:
  6.4 6.4 %copy-start.2 = (bf16[128,256]{1,0:T(8,128)(2,1)S(1)}, bf16[128,256]{1,0:T(8,128)(2,1)}, u32[]{:S(2)}) copy-start(bf16[128,256]{1,0:T(8,128)(2,1)} %param.6) | copy-start | bytes 196612
  6.4 15.5 %copy-start.4 = (s32[1,4,6]{2,1,0:T(4,128)S(1)}, s32[1,4,6]{2,1,0:T(4,128)}, u32[]{:S(2)}) copy-start(s32[1,4,6]{2,1,0:T(4,128)} %param.11) | copy-start | bytes 292
  6.4 32.5 %all-to-all-start = ((bf16[4,1040,128]{2,1,0:T(8,128)(2,1)}), bf16[4,1040,128]{2,1,0:T(8,128)(2,1)S(1)}, u32[]{:S(2)}, u32[]{:S(2)}) async-start(bf16[4,1040,128]{2,1,0:T(8,128)(2,1)} %pad_maximum_fusion), calls=%async_computation | async-start | bytes 2129920 | tf_op jit(solution)/shard_map/all_to_all | solution.py:129
  12.8 1.3 %collective-permute-start = (bf16[1,128,256]{2,1,0:T(8,128)(2,1)S(1)}, bf16[1,128,256]{2,1,0:T(8,128)(2,1)S(1)}, u32[]{:S(2)}, u32[]{:S(2)}) collective-permute-start(bf16[1,128,256]{2,1,0:T(8,128)(2,1)S(1)} %bitcast.30), channel_id=1, source_target_pairs={{0,4},{4,0},{8,12},{12,8},{16,20},{20,16},{24,28},{28,24},{1,5},{5... | collective-permute-start | bytes 196616 | tf_op jit(solution)/shard_map/ppermute | solution.py:33
  14.1 5.6 %collective-permute-start.1 = (bf16[2,128,256]{2,1,0:T(8,128)(2,1)S(1)}, bf16[2,128,256]{2,1,0:T(8,128)(2,1)S(1)}, u32[]{:S(2)}, u32[]{:S(2)}) collective-permute-start(bf16[2,128,256]{2,1,0:T(8,128)(2,1)S(1)} %maximum_select_fusion.2), channel_id=1, source_target_pairs={{0,8},{4,12},{8,0},{12,4},{16,24},{20,28},{24,16},{28,20},{1,9},{5... | collective-permute-start | bytes 393224 | tf_op jit(solution)/shard_map/ppermute | solution.py:33
  19.8 7.6 %collective-permute-start.2 = (bf16[4,128,256]{2,1,0:T(8,128)(2,1)S(1)}, bf16[4,128,256]{2,1,0:T(8,128)(2,1)S(1)}, u32[]{:S(2)}, u32[]{:S(2)}) collective-permute-start(bf16[4,128,256]{2,1,0:T(8,128)(2,1)S(1)} %maximum_select_fusion.1), channel_id=1, source_target_pairs={{0,16},{4,20},{8,24},{12,28},{16,0},{20,4},{24,8},{28,12},{1,17},{... | collective-permute-start | bytes 786440 | tf_op jit(solution)/shard_map/ppermute | solution.py:33
  22.0 18.4 %copy-start.3 = (s32[24]{0:T(128)}, s32[24]{0:T(128)S(1)}, u32[]{:S(2)}) copy-start(s32[24]{0:T(128)S(1)} %reshape.57.refs_1_) | copy-start | bytes 292
  38.9 1.5 %copy-start = (bf16[4,1040,128]{2,1,0:T(8,128)(2,1)}, bf16[4,1040,128]{2,1,0:T(8,128)(2,1)S(1)}, u32[]{:S(2)}) copy-start(bf16[4,1040,128]{2,1,0:T(8,128)(2,1)S(1)} %all-to-all-done.refs_5_) | copy-start | bytes 3194884
  47.5 5.8 %copy-start.1 = (f32[4,128,256]{2,1,0:T(8,128)S(1)}, f32[4,128,256]{2,1,0:T(8,128)}, u32[]{:S(2)}) copy-start(f32[4,128,256]{2,1,0:T(8,128)} %get-tuple-element.7) | copy-start | bytes 1572868
  48.7 2.0 %collective-permute-start.6 = (f32[4,128,256]{2,1,0:T(8,128)S(1)}, f32[4,128,256]{2,1,0:T(8,128)S(1)}, u32[]{:S(2)}, u32[]{:S(2)}) collective-permute-start(f32[4,128,256]{2,1,0:T(8,128)S(1)} %slice.55), channel_id=1, source_target_pairs={{0,4},{4,0},{8,12},{12,8},{16,20},{20,16},{24,28},{28,24},{1,5},{5... | collective-permute-start | bytes 1572872 | tf_op jit(solution)/shard_map/ppermute | solution.py:22
  51.8 8.4 %collective-permute-start.7 = (f32[2,128,256]{2,1,0:T(8,128)S(1)}, f32[2,128,256]{2,1,0:T(8,128)S(1)}, u32[]{:S(2)}, u32[]{:S(2)}) collective-permute-start(f32[2,128,256]{2,1,0:T(8,128)S(1)} %slice.62), channel_id=1, source_target_pairs={{0,8},{4,12},{8,0},{12,4},{16,24},{20,28},{24,16},{28,20},{1,9},{5... | collective-permute-start | bytes 786440 | tf_op jit(solution)/shard_map/ppermute | solution.py:22
  53.4 8.5 %collective-permute-start.3 = (f32[128,256]{1,0:T(8,128)S(1)}, f32[128,256]{1,0:T(8,128)S(1)}, u32[]{:S(2)}, u32[]{:S(2)}) collective-permute-start(f32[128,256]{1,0:T(8,128)S(1)} %get-tuple-element.9), channel_id=1, source_target_pairs={{0,3},{1,0},{2,1},{3,2},{4,7},{5,4},{6,5},{7,6},{8,11},{9,8},{10,9... | collective-permute-start | bytes 393224 | tf_op jit(solution)/shard_map/ppermute | solution.py:43
  54.9 8.3 %collective-permute-start.5 = (f32[128,256]{1,0:T(8,128)S(1)}, f32[128,256]{1,0:T(8,128)S(1)}, u32[]{:S(2)}, u32[]{:S(2)}) collective-permute-start(f32[128,256]{1,0:T(8,128)S(1)} %get-tuple-element.10), channel_id=1, source_target_pairs={{0,1},{1,2},{2,3},{3,0},{4,5},{5,6},{6,7},{7,4},{8,9},{9,10},{10,1... | collective-permute-start | bytes 393224 | tf_op jit(solution)/shard_map/ppermute | solution.py:43
  55.5 11.3 %collective-permute-start.4 = (f32[128,256]{1,0:T(8,128)S(1)}, f32[128,256]{1,0:T(8,128)S(1)}, u32[]{:S(2)}, u32[]{:S(2)}) collective-permute-start(f32[128,256]{1,0:T(8,128)S(1)} %get-tuple-element.11), channel_id=1, source_target_pairs={{0,2},{1,3},{2,0},{3,1},{4,6},{5,7},{6,4},{7,5},{8,10},{9,11},{10,... | collective-permute-start | bytes 393224 | tf_op jit(solution)/shard_map/ppermute | solution.py:43
  60.3 6.5 %collective-permute-start.8 = (f32[1,128,256]{2,1,0:T(8,128)S(1)}, f32[1,128,256]{2,1,0:T(8,128)S(1)}, u32[]{:S(2)}, u32[]{:S(2)}) collective-permute-start(f32[1,128,256]{2,1,0:T(8,128)S(1)} %slice.64), channel_id=1, source_target_pairs={{0,16},{4,20},{8,24},{12,28},{16,0},{20,4},{24,8},{28,12},{1,17},{... | collective-permute-start | bytes 393224 | tf_op jit(solution)/shard_map/ppermute | solution.py:22

commit v8 on v6

--- a/solution.py
+++ b/solution.py
@@ -135,8 +135,8 @@
         grid=(ent_count,),
         in_specs=[
             pl.BlockSpec((1, rows_in, block), lambda e, r, g, s, a, k: (e, 0, 0)),
-            pl.BlockSpec((relations, width, width), lambda e, r, g, s, a, k: (0, 0, 0)),
-            pl.BlockSpec((grp_count, block, width), lambda e, r, g, s, a, k: (0, 0, 0)),
+            pl.BlockSpec(memory_space=pltpu.VMEM),
+            pl.BlockSpec(memory_space=pltpu.VMEM),
         ],
         out_specs=[
             pl.BlockSpec((1, block, width), lambda e, r, g, s, a, k: (k[e], 0, 0)),

time: 65.9 us -> 65.9 us (level)
  no operation moved by 1% of the time
where the time goes in v8:
time: 65.9 us; the launch traced here: 65.5 us
  waiting for transfers between devices  32.4 us (49%)
  starting transfers between devices  15 us (23%)
  Pallas kernels  7.08 us (11%)
  other arithmetic  5.27 us (8%)
  local copies, waits for them, and re-layouts  4.93 us (7%)
  between operations  0.91 us (1%)
    all_to_all x1, waiting for transfers between devices, on_device(): lax.all_to_all(outgoing, 'ent', split_axis=0, concat_axis=0, tiled=True)  10.7 us
    ppermute x3, waiting for transfers between devices, grp_gather(): got = lax.ppermute(held, 'grp', [(i, i ^ bit) for i in range(grp_count)])  10.2 us
    pallas_call x1, Pallas kernels, on_device(): pl.pallas_call(lambda *refs: tile_kernel(*refs, per_relay=per_relay, bloc...  7.08 us
    ppermute x3, waiting for transfers between devices, grp_reduce_scatter(): lax.ppermute(parts[half:], 'grp', [(i, i ^ bit) for i in range(grp_count)])  6.57 us
    all_to_all x1, starting transfers between devices, on_device(): lax.all_to_all(outgoing, 'ent', split_axis=0, concat_axis=0, tiled=True)  6.45 us
    ppermute x3, waiting for transfers between devices, shift_ent(): lax.ppermute(x, 'ent', [(i, (i + shift) % ent_count) for i in range(ent_c...  4.88 us
    ppermute x3, starting transfers between devices, grp_reduce_scatter(): lax.ppermute(parts[half:], 'grp', [(i, i ^ bit) for i in range(grp_count)])  3.23 us
    ppermute x3, starting transfers between devices, grp_gather(): got = lax.ppermute(held, 'grp', [(i, i ^ bit) for i in range(grp_count)])  3.14 us
  transfers between devices with their start and end apart: 10, of which 8 were waited for; matrix products, arithmetic and copies ran while one was open for 3% of the time, Pallas kernels for 0%

profile of v8, /device:TPU:0, one launch (start us, length us, event | category | flops | bytes accessed | tf_op | source)
XLA Modules:
  0.0 65.5 jit_solution(12547973607961564430)
XLA Ops:
  0.0 0.0 copy-start
  0.0 0.0 copy-start.1
  0.8 0.1 compare_select_fusion
  0.9 0.1 reshape.109
  1.0 0.0 copy-start.4
  1.0 0.7 %gather_fusion.2 = bf16[24]{0:T(256)(128)(2,1)S(1)} fusion(bf16[24]{0:T(256)(128)(2,1)S(1)} %compare_convert_fusion, s32[1024]{0:T(1024)S(1)} %pad_clamp_fusion), kind=kCustom, calls=%fused_computation.2 | custom fusion | bytes 192 | tf_op jit(solution)/shard_map/gather | solution.py:115
  1.7 0.1 reshape.136
  1.8 0.0 copy-done.1
  1.8 0.7 %gather_fusion.1 = s32[24]{0:T(128)S(1)} fusion(s32[24]{0:T(128)S(1)} %bitcast.26, s32[1024]{0:T(1024)S(1)} %pad_clamp_fusion), kind=kCustom, calls=%fused_computation.1 | custom fusion | bytes 288 | tf_op jit(solution)/shard_map/gather | solution.py:115
  2.5 0.1 reshape.138
  2.6 0.0 copy-done.4
  2.6 0.0 copy-done
  2.6 0.6 gather_fusion
  3.3 0.2 convert_element_type.38
  3.4 0.1 fusion.6
  3.6 1.1 %pad_maximum_fusion = bf16[4,1040,128]{2,1,0:T(8,128)(2,1)} fusion(bf16[4,16,128]{2,1,0:T(8,128)(2,1)S(1)} %broadcast_in_dim.7, bf16[4,256,128]{2,1,0:T(8,128)(2,1)S(1)} %broadcast_in_dim.6, bf16[4,768,128]{2,1,0:T(8,128)(2,1)S(1)} %bitcast.27), kind=kLoop, calls=%fused_computation.3 | loop fusion | flops 3194880 | bytes 2129920 | tf_op jit(solution)/shard_map/concatenate | solution.py:119
  4.7 0.0 copy-start.6
  4.7 6.4 %all-to-all-start = ((bf16[4,1040,128]{2,1,0:T(8,128)(2,1)}), bf16[4,1040,128]{2,1,0:T(8,128)(2,1)S(1)}, u32[]{:S(2)}, u32[]{:S(2)}) async-start(bf16[4,1040,128]{2,1,0:T(8,128)(2,1)} %pad_maximum_fusion), calls=%async_computation | async-start | bytes 2129920 | tf_op jit(solution)/shard_map/all_to_all | solution.py:122
  11.1 0.0 collective-permute-start
  11.1 1.3 %collective-permute-done = bf16[1,128,256]{2,1,0:T(8,128)(2,1)S(1)} collective-permute-done((bf16[1,128,256]{2,1,0:T(8,128)(2,1)S(1)}, bf16[1,128,256]{2,1,0:T(8,128)(2,1)S(1)}, u32[]{:S(2)}, u32[]{:S(2)}) %collective-permute-start) | collective-permute-done | bytes 65568 | tf_op jit(solution)/shard_map/ppermute | solution.py:33
  12.4 1.6 %collective-permute-start.1 = (bf16[2,128,256]{2,1,0:T(8,128)(2,1)S(1)}, bf16[2,128,256]{2,1,0:T(8,128)(2,1)S(1)}, u32[]{:S(2)}, u32[]{:S(2)}) collective-permute-start(bf16[2,128,256]{2,1,0:T(8,128)(2,1)S(1)} %maximum_select_fusion.2), channel_id=1, source_target_pairs={{0,8},{4,12},{8,0},{12,4},{16,24},{20,28},{24,16},{28,20},{1,9},{5... | collective-permute-start | bytes 393224 | tf_op jit(solution)/shard_map/ppermute | solution.py:33
  13.9 4.1 %collective-permute-done.1 = bf16[2,128,256]{2,1,0:T(8,128)(2,1)S(1)} collective-permute-done((bf16[2,128,256]{2,1,0:T(8,128)(2,1)S(1)}, bf16[2,128,256]{2,1,0:T(8,128)(2,1)S(1)}, u32[]{:S(2)}, u32[]{:S(2)}) %collective-permute-start.1) | collective-permute-done | bytes 131104 | tf_op jit(solution)/shard_map/ppermute | solution.py:33
  18.0 1.6 %collective-permute-start.2 = (bf16[4,128,256]{2,1,0:T(8,128)(2,1)S(1)}, bf16[4,128,256]{2,1,0:T(8,128)(2,1)S(1)}, u32[]{:S(2)}, u32[]{:S(2)}) collective-permute-start(bf16[4,128,256]{2,1,0:T(8,128)(2,1)S(1)} %maximum_select_fusion.1), channel_id=1, source_target_pairs={{0,16},{4,20},{8,24},{12,28},{16,0},{20,4},{24,8},{28,12},{1,17},{... | collective-permute-start | bytes 786440 | tf_op jit(solution)/shard_map/ppermute | solution.py:33
  19.6 0.5 and_select_fusion.refs_4_
  20.1 0.0 copy-done.6
  20.1 0.1 reshape.104.refs_1_
  20.2 0.0 copy-start.5
  20.2 0.5 shift-left_or_fusion.refs_2_
  20.7 4.9 %collective-permute-done.2 = bf16[4,128,256]{2,1,0:T(8,128)(2,1)S(1)} collective-permute-done((bf16[4,128,256]{2,1,0:T(8,128)(2,1)S(1)}, bf16[4,128,256]{2,1,0:T(8,128)(2,1)S(1)}, u32[]{:S(2)}, u32[]{:S(2)}) %collective-permute-start.2) | collective-permute-done | bytes 262176 | tf_op jit(solution)/shard_map/ppermute | solution.py:33
  25.6 0.9 %maximum_select_fusion.refs_7_ = bf16[8,128,256]{2,1,0:T(8,128)(2,1)} fusion(bf16[4,128,256]{2,1,0:T(8,128)(2,1)S(1)} %collective-permute-done.2, bf16[4,128,256]{2,1,0:T(8,128)(2,1)S(1)} %maximum_select_fusion.1, pred[]{:T(512)S(6)} %eq.17), kind=kLoop, calls=%fused_computation.4 | loop fusion | flops 786432 | bytes 1048577 | tf_op jit(solution)/shard_map/jit(_where)/select_n | solution.py:35
  26.5 10.7 %all-to-all-done.refs_5_ = bf16[4,1040,128]{2,1,0:T(8,128)(2,1)S(1)} async-done(((bf16[4,1040,128]{2,1,0:T(8,128)(2,1)}), bf16[4,1040,128]{2,1,0:T(8,128)(2,1)S(1)}, u32[]{:S(2)}, u32[]{:S(2)}) %all-to-all-start) | async-done | bytes 1064992 | tf_op jit(solution)/shard_map/all_to_all | solution.py:122
  37.2 0.0 copy-start.2
  37.2 0.1 slice_convert_fusion.1
  37.3 0.7 %reshape.105.refs_3_ = s32[24]{0:T(128)} reshape(s32[4,6]{1,0:T(4,128)S(1)} %get-tuple-element.14) | data formatting | bytes 192 | tf_op jit(solution)/shard_map/reshape | solution.py:127
  37.9 0.6 reshape.103.refs_0_
  38.5 0.0 copy-done.5
  38.5 0.0 copy-done.2
  38.5 7.1 %shard_map.64 = (f32[4,128,256]{2,1,0:T(8,128)}, f32[8,128,256]{2,1,0:T(8,128)}) custom-call(s32[24]{0:T(128)} %reshape.103.refs_0_, s32[24]{0:T(128)} %copy-done.5, s32[24]{0:T(128)} %shift-left_or_fusion.refs_2_, s32[24]{0:T(128)} %reshape.105.refs_3_, s32[4]{0:T(128)} %and_select_fusion.refs_4_, bf16[4,1040,128]{2,1,0:T(8,128)(2,1)} %copy-done.2, ...), custom_call_target="tpu_custom_call" | custom-call | tf_op jit(solution)/shard_map/pallas_call | solution.py:146
  45.6 0.0 copy-start.3
  45.6 1.1 %slice.55 = f32[4,128,256]{2,1,0:T(8,128)S(1)} slice(f32[8,128,256]{2,1,0:T(8,128)} %get-tuple-element.8), slice={[4:8], [0:128], [0:256]} | slice | bytes 1048576 | tf_op jit(solution)/shard_map/slice | solution.py:22
  46.8 0.1 collective-permute-start.6
  46.8 1.9 %collective-permute-done.6 = f32[4,128,256]{2,1,0:T(8,128)S(1)} collective-permute-done((f32[4,128,256]{2,1,0:T(8,128)S(1)}, f32[4,128,256]{2,1,0:T(8,128)S(1)}, u32[]{:S(2)}, u32[]{:S(2)}) %collective-permute-start.6) | collective-permute-done | bytes 524320 | tf_op jit(solution)/shard_map/ppermute | solution.py:22
  48.7 1.1 %slice_add_fusion = f32[4,128,256]{2,1,0:T(8,128)S(1)} fusion(f32[4,128,256]{2,1,0:T(8,128)S(1)} %collective-permute-done.6, f32[8,128,256]{2,1,0:T(8,128)} %get-tuple-element.8), kind=kLoop, calls=%fused_computation.5 | loop fusion | flops 131072 | bytes 1572864 | tf_op jit(solution)/shard_map/add | solution.py:23
  49.9 1.6 %collective-permute-start.7 = (f32[2,128,256]{2,1,0:T(8,128)S(1)}, f32[2,128,256]{2,1,0:T(8,128)S(1)}, u32[]{:S(2)}, u32[]{:S(2)}) collective-permute-start(f32[2,128,256]{2,1,0:T(8,128)S(1)} %slice.68), channel_id=1, source_target_pairs={{0,8},{4,12},{8,0},{12,4},{16,24},{20,28},{24,16},{28,20},{1,9},{5... | collective-permute-start | bytes 786440 | tf_op jit(solution)/shard_map/ppermute | solution.py:22
  51.4 0.0 copy-done.3
  51.5 1.5 %collective-permute-start.3 = (f32[128,256]{1,0:T(8,128)S(1)}, f32[128,256]{1,0:T(8,128)S(1)}, u32[]{:S(2)}, u32[]{:S(2)}) collective-permute-start(f32[128,256]{1,0:T(8,128)S(1)} %get-tuple-element.9), channel_id=1, source_target_pairs={{0,3},{1,0},{2,1},{3,2},{4,7},{5,4},{6,5},{7,6},{8,11},{9,8},{10,9... | collective-permute-start | bytes 393224 | tf_op jit(solution)/shard_map/ppermute | solution.py:43
  53.0 0.6 collective-permute-start.5
  53.5 0.1 collective-permute-start.4
  53.6 4.7 %collective-permute-done.7 = f32[2,128,256]{2,1,0:T(8,128)S(1)} collective-permute-done((f32[2,128,256]{2,1,0:T(8,128)S(1)}, f32[2,128,256]{2,1,0:T(8,128)S(1)}, u32[]{:S(2)}, u32[]{:S(2)}) %collective-permute-start.7) | collective-permute-done | bytes 262176 | tf_op jit(solution)/shard_map/ppermute | solution.py:22
  58.3 1.6 %collective-permute-start.8 = (f32[1,128,256]{2,1,0:T(8,128)S(1)}, f32[1,128,256]{2,1,0:T(8,128)S(1)}, u32[]{:S(2)}, u32[]{:S(2)}) collective-permute-start(f32[1,128,256]{2,1,0:T(8,128)S(1)} %slice.70), channel_id=1, source_target_pairs={{0,16},{4,20},{8,24},{12,28},{16,0},{20,4},{24,8},{28,12},{1,17},{... | collective-permute-start | bytes 393224 | tf_op jit(solution)/shard_map/ppermute | solution.py:22
  59.9 0.0 collective-permute-done.3
  59.9 1.3 %collective-permute-done.5 = f32[128,256]{1,0:T(8,128)S(1)} collective-permute-done((f32[128,256]{1,0:T(8,128)S(1)}, f32[128,256]{1,0:T(8,128)S(1)}, u32[]{:S(2)}, u32[]{:S(2)}) %collective-permute-start.5) | collective-permute-done | bytes 131104 | tf_op jit(solution)/shard_map/ppermute | solution.py:43
  61.3 3.5 %collective-permute-done.4 = f32[128,256]{1,0:T(8,128)S(1)} collective-permute-done((f32[128,256]{1,0:T(8,128)S(1)}, f32[128,256]{1,0:T(8,128)S(1)}, u32[]{:S(2)}, u32[]{:S(2)}) %collective-permute-start.4) | collective-permute-done | bytes 131104 | tf_op jit(solution)/shard_map/ppermute | solution.py:43
  64.8 0.0 collective-permute-done.8
  64.8 0.7 %fusion.1 = f32[128,256]{1,0:T(8,128)} fusion(f32[1,128,256]{2,1,0:T(8,128)S(1)} %collective-permute-done.8, f32[2,128,256]{2,1,0:T(8,128)S(1)} %slice_add_fusion.1, f32[128,256]{1,0:T(8,128)S(1)} %collective-permute-done.5, f32[128,256]{1,0:T(8,128)S(1)} %collective-permute-done.4, f32[128,256]{1,0:T(8,128)S(1)} %collective-permute-done.3, ...), kind=kLoop, calls=%fused_computation.10 | loop fusion | flops 163840 | bytes 917504 | tf_op jit(solution)/shard_map/add | solution.py:159
  (16 shorter events, 0.2 us)
Async XLA Ops:
  0.0 2.6 %copy-start = (s32[24,128,128]{2,1,0:T(8,128)S(1)}, s32[24,128,128]{2,1,0:T(8,128)}, u32[]{:S(2)}) copy-start(s32[24,128,128]{2,1,0:T(8,128)} %param.8) | copy-start | bytes 4718596
  0.0 1.8 %copy-start.1 = (s32[1,24]{1,0:T(1,128)S(1)}, s32[1,24]{1,0:T(1,128)}, u32[]{:S(2)}) copy-start(s32[1,24]{1,0:T(1,128)} %param.9) | copy-start | bytes 292
  1.0 1.6 %copy-start.4 = (bf16[128,256]{1,0:T(8,128)(2,1)S(1)}, bf16[128,256]{1,0:T(8,128)(2,1)}, u32[]{:S(2)}) copy-start(bf16[128,256]{1,0:T(8,128)(2,1)} %param.6) | copy-start | bytes 196612
  4.7 15.5 %copy-start.6 = (s32[1,4,6]{2,1,0:T(4,128)S(1)}, s32[1,4,6]{2,1,0:T(4,128)}, u32[]{:S(2)}) copy-start(s32[1,4,6]{2,1,0:T(4,128)} %param.11) | copy-start | bytes 292
  4.7 32.5 %all-to-all-start = ((bf16[4,1040,128]{2,1,0:T(8,128)(2,1)}), bf16[4,1040,128]{2,1,0:T(8,128)(2,1)S(1)}, u32[]{:S(2)}, u32[]{:S(2)}) async-start(bf16[4,1040,128]{2,1,0:T(8,128)(2,1)} %pad_maximum_fusion), calls=%async_computation | async-start | bytes 2129920 | tf_op jit(solution)/shard_map/all_to_all | solution.py:122
  11.1 1.3 %collective-permute-start = (bf16[1,128,256]{2,1,0:T(8,128)(2,1)S(1)}, bf16[1,128,256]{2,1,0:T(8,128)(2,1)S(1)}, u32[]{:S(2)}, u32[]{:S(2)}) collective-permute-start(bf16[1,128,256]{2,1,0:T(8,128)(2,1)S(1)} %bitcast.28), channel_id=1, source_target_pairs={{0,4},{4,0},{8,12},{12,8},{16,20},{20,16},{24,28},{28,24},{1,5},{5... | collective-permute-start | bytes 196616 | tf_op jit(solution)/shard_map/ppermute | solution.py:33
  12.4 5.6 %collective-permute-start.1 = (bf16[2,128,256]{2,1,0:T(8,128)(2,1)S(1)}, bf16[2,128,256]{2,1,0:T(8,128)(2,1)S(1)}, u32[]{:S(2)}, u32[]{:S(2)}) collective-permute-start(bf16[2,128,256]{2,1,0:T(8,128)(2,1)S(1)} %maximum_select_fusion.2), channel_id=1, source_target_pairs={{0,8},{4,12},{8,0},{12,4},{16,24},{20,28},{24,16},{28,20},{1,9},{5... | collective-permute-start | bytes 393224 | tf_op jit(solution)/shard_map/ppermute | solution.py:33
  18.0 7.6 %collective-permute-start.2 = (bf16[4,128,256]{2,1,0:T(8,128)(2,1)S(1)}, bf16[4,128,256]{2,1,0:T(8,128)(2,1)S(1)}, u32[]{:S(2)}, u32[]{:S(2)}) collective-permute-start(bf16[4,128,256]{2,1,0:T(8,128)(2,1)S(1)} %maximum_select_fusion.1), channel_id=1, source_target_pairs={{0,16},{4,20},{8,24},{12,28},{16,0},{20,4},{24,8},{28,12},{1,17},{... | collective-permute-start | bytes 786440 | tf_op jit(solution)/shard_map/ppermute | solution.py:33
  20.2 18.3 %copy-start.5 = (s32[24]{0:T(128)}, s32[24]{0:T(128)S(1)}, u32[]{:S(2)}) copy-start(s32[24]{0:T(128)S(1)} %reshape.104.refs_1_) | copy-start | bytes 292
  37.2 1.4 %copy-start.2 = (bf16[4,1040,128]{2,1,0:T(8,128)(2,1)}, bf16[4,1040,128]{2,1,0:T(8,128)(2,1)S(1)}, u32[]{:S(2)}) copy-start(bf16[4,1040,128]{2,1,0:T(8,128)(2,1)S(1)} %all-to-all-done.refs_5_) | copy-start | bytes 3194884
  45.6 5.8 %copy-start.3 = (f32[4,128,256]{2,1,0:T(8,128)S(1)}, f32[4,128,256]{2,1,0:T(8,128)}, u32[]{:S(2)}) copy-start(f32[4,128,256]{2,1,0:T(8,128)} %get-tuple-element.7) | copy-start | bytes 1572868
  46.8 2.0 %collective-permute-start.6 = (f32[4,128,256]{2,1,0:T(8,128)S(1)}, f32[4,128,256]{2,1,0:T(8,128)S(1)}, u32[]{:S(2)}, u32[]{:S(2)}) collective-permute-start(f32[4,128,256]{2,1,0:T(8,128)S(1)} %slice.55), channel_id=1, source_target_pairs={{0,4},{4,0},{8,12},{12,8},{16,20},{20,16},{24,28},{28,24},{1,5},{5... | collective-permute-start | bytes 1572872 | tf_op jit(solution)/shard_map/ppermute | solution.py:22
  49.9 8.4 %collective-permute-start.7 = (f32[2,128,256]{2,1,0:T(8,128)S(1)}, f32[2,128,256]{2,1,0:T(8,128)S(1)}, u32[]{:S(2)}, u32[]{:S(2)}) collective-permute-start(f32[2,128,256]{2,1,0:T(8,128)S(1)} %slice.68), channel_id=1, source_target_pairs={{0,8},{4,12},{8,0},{12,4},{16,24},{20,28},{24,16},{28,20},{1,9},{5... | collective-permute-start | bytes 786440 | tf_op jit(solution)/shard_map/ppermute | solution.py:22
  51.5 8.5 %collective-permute-start.3 = (f32[128,256]{1,0:T(8,128)S(1)}, f32[128,256]{1,0:T(8,128)S(1)}, u32[]{:S(2)}, u32[]{:S(2)}) collective-permute-start(f32[128,256]{1,0:T(8,128)S(1)} %get-tuple-element.9), channel_id=1, source_target_pairs={{0,3},{1,0},{2,1},{3,2},{4,7},{5,4},{6,5},{7,6},{8,11},{9,8},{10,9... | collective-permute-start | bytes 393224 | tf_op jit(solution)/shard_map/ppermute | solution.py:43
  53.0 8.3 %collective-permute-start.5 = (f32[128,256]{1,0:T(8,128)S(1)}, f32[128,256]{1,0:T(8,128)S(1)}, u32[]{:S(2)}, u32[]{:S(2)}) collective-permute-start(f32[128,256]{1,0:T(8,128)S(1)} %get-tuple-element.10), channel_id=1, source_target_pairs={{0,1},{1,2},{2,3},{3,0},{4,5},{5,6},{6,7},{7,4},{8,9},{9,10},{10,1... | collective-permute-start | bytes 393224 | tf_op jit(solution)/shard_map/ppermute | solution.py:43
  53.5 11.3 %collective-permute-start.4 = (f32[128,256]{1,0:T(8,128)S(1)}, f32[128,256]{1,0:T(8,128)S(1)}, u32[]{:S(2)}, u32[]{:S(2)}) collective-permute-start(f32[128,256]{1,0:T(8,128)S(1)} %get-tuple-element.11), channel_id=1, source_target_pairs={{0,2},{1,3},{2,0},{3,1},{4,6},{5,7},{6,4},{7,5},{8,10},{9,11},{10,... | collective-permute-start | bytes 393224 | tf_op jit(solution)/shard_map/ppermute | solution.py:43
  58.3 6.5 %collective-permute-start.8 = (f32[1,128,256]{2,1,0:T(8,128)S(1)}, f32[1,128,256]{2,1,0:T(8,128)S(1)}, u32[]{:S(2)}, u32[]{:S(2)}) collective-permute-start(f32[1,128,256]{2,1,0:T(8,128)S(1)} %slice.70), channel_id=1, source_target_pairs={{0,16},{4,20},{8,24},{12,28},{16,0},{20,4},{24,8},{28,12},{1,17},{... | collective-permute-start | bytes 393224 | tf_op jit(solution)/shard_map/ppermute | solution.py:22

commit v9 on v8

--- a/solution.py
+++ b/solution.py
@@ -15,8 +15,9 @@
     return out
 
 
-def grp_reduce_scatter(parts, grp_count):
-    bit = 1
+def grp_reduce_scatter(keep, send, grp_count):
+    parts = keep + lax.ppermute(send, "grp", [(i, i ^ 1) for i in range(grp_count)])
+    bit = 2
     while bit < grp_count:
         half = parts.shape[0] // 2
         got = lax.ppermute(parts[half:], "grp", [(i, i ^ bit) for i in range(grp_count)])
@@ -43,22 +44,24 @@
     return lax.ppermute(x, "ent", [(i, (i + shift) % ent_count) for i in range(ent_count)])
 
 
-def tile_kernel(rels_ref, groups_ref, slots_ref, alive_ref, shift_ref, in_ref, core_ref, panel_ref,
-                row_ref, owner_ref, *, per_relay, block):
+def tile_kernel(codes_ref, groups_ref, slots_ref, shift_ref, in_ref, core_ref, panel_ref,
+                row_ref, keep_ref, send_ref, *, per_relay, block):
     e = pl.program_id(0)
 
     @pl.when(e == 0)
     def _():
-        owner_ref[...] = jnp.zeros_like(owner_ref)
+        keep_ref[...] = jnp.zeros_like(keep_ref)
+        send_ref[...] = jnp.zeros_like(send_ref)
 
     nt = (((1,), (1,)), ((), ()))
     base = per_relay * block
     own = jnp.concatenate(
         [in_ref[0, base : base + block, :], in_ref[0, base + block : base + 2 * block, :]], axis=1
     )
-    ts = [e * per_relay + j for j in range(per_relay)]
-    rels = [rels_ref[t] for t in ts]
-    groups = [groups_ref[t] for t in ts]
+    half = keep_ref.shape[0]
+    codes = [codes_ref[e, j] for j in range(per_relay)]
+    rels = [c // 2 for c in codes]
+    groups = [groups_ref[e, j] for j in range(per_relay)]
     mapped = [
         jnp.dot(own, core_ref[r], preferred_element_type=jnp.float32).astype(jnp.bfloat16)
         for r in rels
@@ -68,8 +71,8 @@
         for m, g in zip(mapped, groups)
     ]
     resids = []
-    for j, t in enumerate(ts):
-        scale = LOSS_SCALE * alive_ref[t].astype(jnp.float32)
+    for j in range(per_relay):
+        scale = LOSS_SCALE * (codes[j] % 2).astype(jnp.float32)
         adj = in_ref[0, j * block : (j + 1) * block, :].astype(jnp.float32)
         resids.append(((predicted[j] - adj) * scale).astype(jnp.bfloat16))
     products = [
@@ -86,8 +89,18 @@
     for p, r in zip(products, rels):
         part = lax.dot_general(p, core_ref[r], nt, preferred_element_type=jnp.float32)
         acc = part if acc is None else acc + part
-    for c, t in zip(columns, ts):
-        owner_ref[slots_ref[t]] += c.astype(jnp.float32)
+    for j, c in enumerate(columns):
+        slot = slots_ref[e, j]
+        column = c.astype(jnp.float32)
+
+        @pl.when(slot < half)
+        def _():
+            keep_ref[jnp.minimum(slot, half - 1)] += column
+
+        @pl.when(slot >= half)
+        def _():
+            send_ref[jnp.maximum(slot - half, 0)] += column
+
     row_ref[0] = acc
 
 
@@ -123,39 +136,40 @@
     group_blocks = grp_gather(factor, grp_count)
 
     heads = arrived[:, -head_rows].astype(jnp.float32)
-    rels = heads[:, :per_relay].astype(jnp.int32).reshape(count)
-    alive = heads[:, per_relay : 2 * per_relay].astype(jnp.int32).reshape(count)
-    groups = send_lists.reshape(count)
+    codes = (heads[:, :per_relay] * 2 + heads[:, per_relay : 2 * per_relay]).astype(jnp.int32)
+    groups = send_lists.reshape(ent_count, per_relay)
     slots = bit_reverse(groups ^ lax.axis_index("grp"), grp_bits)
     shifts = (my_ent - jnp.arange(ent_count, dtype=jnp.int32)) % ent_count
     rows_in = arrived.shape[1]
 
     grid_spec = pltpu.PrefetchScalarGridSpec(
-        num_scalar_prefetch=5,
+        num_scalar_prefetch=4,
         grid=(ent_count,),
         in_specs=[
-            pl.BlockSpec((1, rows_in, block), lambda e, r, g, s, a, k: (e, 0, 0)),
+            pl.BlockSpec((1, rows_in, block), lambda e, c, g, s, k: (e, 0, 0)),
             pl.BlockSpec(memory_space=pltpu.VMEM),
             pl.BlockSpec(memory_space=pltpu.VMEM),
         ],
         out_specs=[
-            pl.BlockSpec((1, block, width), lambda e, r, g, s, a, k: (k[e], 0, 0)),
-            pl.BlockSpec((grp_count, block, width), lambda e, r, g, s, a, k: (0, 0, 0)),
+            pl.BlockSpec((1, block, width), lambda e, c, g, s, k: (k[e], 0, 0)),
+            pl.BlockSpec((grp_count // 2, block, width), lambda e, c, g, s, k: (0, 0, 0)),
+            pl.BlockSpec((grp_count // 2, block, width), lambda e, c, g, s, k: (0, 0, 0)),
         ],
     )
-    row_parts, owner_terms = pl.pallas_call(
+    row_parts, owner_keep, owner_send = pl.pallas_call(
         lambda *refs: tile_kernel(*refs, per_relay=per_relay, block=block),
         grid_spec=grid_spec,
         out_shape=[
             jax.ShapeDtypeStruct((ent_count, block, width), jnp.float32),
-            jax.ShapeDtypeStruct((grp_count, block, width), jnp.float32),
+            jax.ShapeDtypeStruct((grp_count // 2, block, width), jnp.float32),
+            jax.ShapeDtypeStruct((grp_count // 2, block, width), jnp.float32),
         ],
-    )(rels, groups, slots, alive, shifts, arrived, cores, group_blocks)
+    )(codes, groups, slots, shifts, arrived, cores, group_blocks)
 
     rows = row_parts[0]
     for k in range(1, ent_count):
         rows = rows + shift_ent(row_parts[k], -k, ent_count)
-    owner_part = grp_reduce_scatter(owner_terms, grp_count)
+    owner_part = grp_reduce_scatter(owner_keep, owner_send, grp_count)
     return rows + owner_part
 
 

time: 65.9 us -> 65.3 us (level)
  local copies, waits for them, and re-layouts: 4.93 us -> 2.69 us
  other arithmetic: 5.27 us -> 6.14 us
  Pallas kernels: 7.08 us -> 7.87 us
    ppermute x0 -> x1, waiting for transfers between devices: none -> 2.11 us  [grp_reduce_scatter(): lax.ppermute(send, 'grp', [(i, i ^ 1) for i in range(grp_count)])]
    ppermute x3 -> x2, waiting for transfers between devices: 6.57 us -> 4.68 us  [grp_reduce_scatter(): lax.ppermute(parts[half:], 'grp', [(i, i ^ bit) for i in range(grp_count)])]
    reshape x3 -> x0, local copies, waits for them, and re-layouts: 1.35 us -> none  [the longest x1 0.68 us: on_device(): alive = heads[:, per_relay:2 * per_relay].astype(jnp.int32).reshape(count)]
    slice x3 -> x2, local copies, waits for them, and re-layouts: 1.16 us -> 0.03 us  [grp_reduce_scatter(): parts[half:]]
    add x0 -> x1, other arithmetic: none -> 1.11 us  [grp_reduce_scatter(): keep + lax.ppermute(send, 'grp', [(i, i ^ 1) for i in range(grp_count)])]
    add x2 -> x1, other arithmetic: 1.15 us -> 0.03 us  [grp_reduce_scatter(): parts = parts[:half] + got]
    pallas_call x1, Pallas kernels: 7.08 us -> 7.87 us  [on_device(): pl.pallas_call(lambda *refs: tile_kernel(*refs, per_relay=per_relay, bloc...]
    convert_element_type x1, other arithmetic: 0.08 us -> 0.74 us  [on_device(): (heads[:, :per_relay] * 2 + heads[:, per_relay:2 * per_relay]).astype(jnp...]
where the time goes in v9:
time: 65.3 us; the launch traced here: 65 us
  waiting for transfers between devices  32.5 us (50%)
  starting transfers between devices  14.9 us (23%)
  Pallas kernels  7.87 us (12%)
  other arithmetic  6.14 us (9%)
  local copies, waits for them, and re-layouts  2.69 us (4%)
  between operations  0.9 us (1%)
    all_to_all x1, waiting for transfers between devices, on_device(): lax.all_to_all(outgoing, 'ent', split_axis=0, concat_axis=0, tiled=True)  10.6 us
    ppermute x3, waiting for transfers between devices, grp_gather(): got = lax.ppermute(held, 'grp', [(i, i ^ bit) for i in range(grp_count)])  10.1 us
    pallas_call x1, Pallas kernels, on_device(): pl.pallas_call(lambda *refs: tile_kernel(*refs, per_relay=per_relay, bloc...  7.87 us
    all_to_all x1, starting transfers between devices, on_device(): lax.all_to_all(outgoing, 'ent', split_axis=0, concat_axis=0, tiled=True)  6.45 us
    ppermute x3, waiting for transfers between devices, shift_ent(): lax.ppermute(x, 'ent', [(i, (i + shift) % ent_count) for i in range(ent_c...  4.88 us
    ppermute x2, waiting for transfers between devices, grp_reduce_scatter(): lax.ppermute(parts[half:], 'grp', [(i, i ^ bit) for i in range(grp_count)])  4.68 us
    ppermute x3, starting transfers between devices, grp_gather(): got = lax.ppermute(held, 'grp', [(i, i ^ bit) for i in range(grp_count)])  3.14 us
    ppermute x2, starting transfers between devices, grp_reduce_scatter(): lax.ppermute(parts[half:], 'grp', [(i, i ^ bit) for i in range(grp_count)])  3.13 us
  transfers between devices with their start and end apart: 10, of which 8 were waited for; matrix products, arithmetic and copies ran while one was open for 3% of the time, Pallas kernels for 0%

profile of v9, /device:TPU:0, one launch (start us, length us, event | category | flops | bytes accessed | tf_op | source)
XLA Modules:
  0.0 65.0 jit_solution(15486870965781972615)
XLA Ops:
  0.0 0.0 copy-start
  0.0 0.0 copy-start.1
  0.8 0.1 compare_select_fusion
  0.9 0.1 reshape.101
  1.0 0.0 copy-start.4
  1.0 0.7 %gather_fusion.2 = bf16[24]{0:T(256)(128)(2,1)S(1)} fusion(bf16[24]{0:T(256)(128)(2,1)S(1)} %compare_convert_fusion, s32[1024]{0:T(1024)S(1)} %pad_clamp_fusion), kind=kCustom, calls=%fused_computation.2 | custom fusion | bytes 192 | tf_op jit(solution)/shard_map/gather | solution.py:128
  1.7 0.1 reshape.128
  1.8 0.0 copy-done.1
  1.8 0.7 %gather_fusion.1 = s32[24]{0:T(128)S(1)} fusion(s32[24]{0:T(128)S(1)} %bitcast.28, s32[1024]{0:T(1024)S(1)} %pad_clamp_fusion), kind=kCustom, calls=%fused_computation.1 | custom fusion | bytes 288 | tf_op jit(solution)/shard_map/gather | solution.py:128
  2.5 0.1 reshape.130
  2.6 0.0 copy-done.4
  2.6 0.0 copy-done
  2.6 0.6 gather_fusion
  3.3 0.2 convert_element_type.34
  3.4 0.1 fusion.6
  3.6 1.1 %pad_maximum_fusion = bf16[4,1040,128]{2,1,0:T(8,128)(2,1)} fusion(bf16[4,16,128]{2,1,0:T(8,128)(2,1)S(1)} %broadcast_in_dim.7, bf16[4,256,128]{2,1,0:T(8,128)(2,1)S(1)} %broadcast_in_dim.6, bf16[4,768,128]{2,1,0:T(8,128)(2,1)S(1)} %bitcast.29), kind=kLoop, calls=%fused_computation.3 | loop fusion | flops 3194880 | bytes 2129920 | tf_op jit(solution)/shard_map/concatenate | solution.py:132
  4.6 0.0 copy-start.5
  4.6 6.4 %all-to-all-start = ((bf16[4,1040,128]{2,1,0:T(8,128)(2,1)}), bf16[4,1040,128]{2,1,0:T(8,128)(2,1)S(1)}, u32[]{:S(2)}, u32[]{:S(2)}) async-start(bf16[4,1040,128]{2,1,0:T(8,128)(2,1)} %pad_maximum_fusion), calls=%async_computation | async-start | bytes 2129920 | tf_op jit(solution)/shard_map/all_to_all | solution.py:135
  11.1 0.0 collective-permute-start
  11.1 1.3 %collective-permute-done = bf16[1,128,256]{2,1,0:T(8,128)(2,1)S(1)} collective-permute-done((bf16[1,128,256]{2,1,0:T(8,128)(2,1)S(1)}, bf16[1,128,256]{2,1,0:T(8,128)(2,1)S(1)}, u32[]{:S(2)}, u32[]{:S(2)}) %collective-permute-start) | collective-permute-done | bytes 65568 | tf_op jit(solution)/shard_map/ppermute | solution.py:34
  12.4 1.6 %collective-permute-start.1 = (bf16[2,128,256]{2,1,0:T(8,128)(2,1)S(1)}, bf16[2,128,256]{2,1,0:T(8,128)(2,1)S(1)}, u32[]{:S(2)}, u32[]{:S(2)}) collective-permute-start(bf16[2,128,256]{2,1,0:T(8,128)(2,1)S(1)} %maximum_select_fusion.2), channel_id=1, source_target_pairs={{0,8},{4,12},{8,0},{12,4},{16,24},{20,28},{24,16},{28,20},{1,9},{5... | collective-permute-start | bytes 393224 | tf_op jit(solution)/shard_map/ppermute | solution.py:34
  13.9 4.1 %collective-permute-done.1 = bf16[2,128,256]{2,1,0:T(8,128)(2,1)S(1)} collective-permute-done((bf16[2,128,256]{2,1,0:T(8,128)(2,1)S(1)}, bf16[2,128,256]{2,1,0:T(8,128)(2,1)S(1)}, u32[]{:S(2)}, u32[]{:S(2)}) %collective-permute-start.1) | collective-permute-done | bytes 131104 | tf_op jit(solution)/shard_map/ppermute | solution.py:34
  18.0 1.6 %collective-permute-start.2 = (bf16[4,128,256]{2,1,0:T(8,128)(2,1)S(1)}, bf16[4,128,256]{2,1,0:T(8,128)(2,1)S(1)}, u32[]{:S(2)}, u32[]{:S(2)}) collective-permute-start(bf16[4,128,256]{2,1,0:T(8,128)(2,1)S(1)} %maximum_select_fusion.1), channel_id=1, source_target_pairs={{0,16},{4,20},{8,24},{12,28},{16,0},{20,4},{24,8},{28,12},{1,17},{... | collective-permute-start | bytes 786440 | tf_op jit(solution)/shard_map/ppermute | solution.py:34
  19.6 0.6 and_select_fusion.refs_3_
  20.2 0.0 copy-done.5
  20.2 0.6 shift-left_or_fusion.refs_2_
  20.8 4.8 %collective-permute-done.2 = bf16[4,128,256]{2,1,0:T(8,128)(2,1)S(1)} collective-permute-done((bf16[4,128,256]{2,1,0:T(8,128)(2,1)S(1)}, bf16[4,128,256]{2,1,0:T(8,128)(2,1)S(1)}, u32[]{:S(2)}, u32[]{:S(2)}) %collective-permute-start.2) | collective-permute-done | bytes 262176 | tf_op jit(solution)/shard_map/ppermute | solution.py:34
  25.6 0.9 %maximum_select_fusion.refs_6_ = bf16[8,128,256]{2,1,0:T(8,128)(2,1)} fusion(bf16[4,128,256]{2,1,0:T(8,128)(2,1)S(1)} %collective-permute-done.2, bf16[4,128,256]{2,1,0:T(8,128)(2,1)S(1)} %maximum_select_fusion.1, pred[]{:T(512)S(6)} %eq.17), kind=kLoop, calls=%fused_computation.4 | loop fusion | flops 786432 | bytes 1048577 | tf_op jit(solution)/shard_map/jit(_where)/select_n | solution.py:36
  26.5 10.6 %all-to-all-done.refs_4_ = bf16[4,1040,128]{2,1,0:T(8,128)(2,1)S(1)} async-done(((bf16[4,1040,128]{2,1,0:T(8,128)(2,1)}), bf16[4,1040,128]{2,1,0:T(8,128)(2,1)S(1)}, u32[]{:S(2)}, u32[]{:S(2)}) %all-to-all-start) | async-done | bytes 1064992 | tf_op jit(solution)/shard_map/all_to_all | solution.py:135
  37.2 0.0 copy-start.2
  37.2 0.7 %add_convert_fusion.refs_0_ = s32[4,6]{1,0:T(4,128)} fusion(f32[4,128]{1,0:T(4,128)S(1)} %bitcast.32), kind=kLoop, calls=%fused_computation.29 | loop fusion | flops 72 | bytes 288 | tf_op jit(solution)/shard_map/convert_element_type | solution.py:139
  37.9 0.2 copy-done.2
  38.2 7.9 %shard_map.64 = (f32[4,128,256]{2,1,0:T(8,128)}, f32[4,128,256]{2,1,0:T(8,128)}, f32[4,128,256]{2,1,0:T(8,128)}) custom-call(s32[4,6]{1,0:T(4,128)} %add_convert_fusion.refs_0_, s32[4,6]{1,0:T(4,128)} %bitcast.33, s32[4,6]{1,0:T(4,128)} %shift-left_or_fusion.refs_2_, s32[4]{0:T(128)} %and_select_fusion.refs_3_, bf16[4,1040,128]{2,1,0:T(8,128)(2,1)} %copy-done.2, ...), custom_call_target="tpu_custom_call" | custom-call | tf_op jit(solution)/shard_map/pallas_call | solution.py:159
  46.0 0.0 copy-start.3
  46.0 0.0 collective-permute-start.6
  46.1 2.1 %collective-permute-done.6 = f32[4,128,256]{2,1,0:T(8,128)S(1)} collective-permute-done((f32[4,128,256]{2,1,0:T(8,128)}, f32[4,128,256]{2,1,0:T(8,128)S(1)}, u32[]{:S(2)}, u32[]{:S(2)}) %collective-permute-start.6) | collective-permute-done | bytes 524320 | tf_op jit(solution)/shard_map/ppermute | solution.py:19
  48.2 1.1 %add.101 = f32[4,128,256]{2,1,0:T(8,128)S(1)} add(f32[4,128,256]{2,1,0:T(8,128)} %get-tuple-element.9, f32[4,128,256]{2,1,0:T(8,128)S(1)} %collective-permute-done.6) | non-fusion elementwise | flops 131072 | bytes 1572864 | tf_op jit(solution)/shard_map/add | solution.py:19
  49.3 1.6 %collective-permute-start.7 = (f32[2,128,256]{2,1,0:T(8,128)S(1)}, f32[2,128,256]{2,1,0:T(8,128)S(1)}, u32[]{:S(2)}, u32[]{:S(2)}) collective-permute-start(f32[2,128,256]{2,1,0:T(8,128)S(1)} %slice.60), channel_id=1, source_target_pairs={{0,8},{4,12},{8,0},{12,4},{16,24},{20,28},{24,16},{28,20},{1,9},{5... | collective-permute-start | bytes 786440 | tf_op jit(solution)/shard_map/ppermute | solution.py:23
  50.9 0.0 copy-done.3
  50.9 1.5 %collective-permute-start.3 = (f32[128,256]{1,0:T(8,128)S(1)}, f32[128,256]{1,0:T(8,128)S(1)}, u32[]{:S(2)}, u32[]{:S(2)}) collective-permute-start(f32[128,256]{1,0:T(8,128)S(1)} %get-tuple-element.11), channel_id=1, source_target_pairs={{0,3},{1,0},{2,1},{3,2},{4,7},{5,4},{6,5},{7,6},{8,11},{9,8},{10,9... | collective-permute-start | bytes 393224 | tf_op jit(solution)/shard_map/ppermute | solution.py:44
  52.4 0.6 collective-permute-start.5
  53.0 0.1 collective-permute-start.4
  53.1 4.7 %collective-permute-done.7 = f32[2,128,256]{2,1,0:T(8,128)S(1)} collective-permute-done((f32[2,128,256]{2,1,0:T(8,128)S(1)}, f32[2,128,256]{2,1,0:T(8,128)S(1)}, u32[]{:S(2)}, u32[]{:S(2)}) %collective-permute-start.7) | collective-permute-done | bytes 262176 | tf_op jit(solution)/shard_map/ppermute | solution.py:23
  57.8 1.6 %collective-permute-start.8 = (f32[1,128,256]{2,1,0:T(8,128)S(1)}, f32[1,128,256]{2,1,0:T(8,128)S(1)}, u32[]{:S(2)}, u32[]{:S(2)}) collective-permute-start(f32[1,128,256]{2,1,0:T(8,128)S(1)} %slice.62), channel_id=1, source_target_pairs={{0,16},{4,20},{8,24},{12,28},{16,0},{20,4},{24,8},{28,12},{1,17},{... | collective-permute-start | bytes 393224 | tf_op jit(solution)/shard_map/ppermute | solution.py:23
  59.4 0.0 collective-permute-done.3
  59.4 1.3 %collective-permute-done.5 = f32[128,256]{1,0:T(8,128)S(1)} collective-permute-done((f32[128,256]{1,0:T(8,128)S(1)}, f32[128,256]{1,0:T(8,128)S(1)}, u32[]{:S(2)}, u32[]{:S(2)}) %collective-permute-start.5) | collective-permute-done | bytes 131104 | tf_op jit(solution)/shard_map/ppermute | solution.py:44
  60.7 3.5 %collective-permute-done.4 = f32[128,256]{1,0:T(8,128)S(1)} collective-permute-done((f32[128,256]{1,0:T(8,128)S(1)}, f32[128,256]{1,0:T(8,128)S(1)}, u32[]{:S(2)}, u32[]{:S(2)}) %collective-permute-start.4) | collective-permute-done | bytes 131104 | tf_op jit(solution)/shard_map/ppermute | solution.py:44
  64.3 0.0 collective-permute-done.8
  64.3 0.7 %fusion.1 = f32[128,256]{1,0:T(8,128)} fusion(f32[1,128,256]{2,1,0:T(8,128)S(1)} %collective-permute-done.8, f32[2,128,256]{2,1,0:T(8,128)S(1)} %slice_add_fusion, f32[128,256]{1,0:T(8,128)S(1)} %collective-permute-done.5, f32[128,256]{1,0:T(8,128)S(1)} %collective-permute-done.4, f32[128,256]{1,0:T(8,128)S(1)} %collective-permute-done.3, ...), kind=kLoop, calls=%fused_computation.9 | loop fusion | flops 163840 | bytes 917504 | tf_op jit(solution)/shard_map/add | solution.py:173
  (16 shorter events, 0.2 us)
Async XLA Ops:
  0.0 2.6 %copy-start = (s32[24,128,128]{2,1,0:T(8,128)S(1)}, s32[24,128,128]{2,1,0:T(8,128)}, u32[]{:S(2)}) copy-start(s32[24,128,128]{2,1,0:T(8,128)} %param.8) | copy-start | bytes 4718596
  0.0 1.8 %copy-start.1 = (s32[1,24]{1,0:T(1,128)S(1)}, s32[1,24]{1,0:T(1,128)}, u32[]{:S(2)}) copy-start(s32[1,24]{1,0:T(1,128)} %param.9) | copy-start | bytes 292
  1.0 1.6 %copy-start.4 = (bf16[128,256]{1,0:T(8,128)(2,1)S(1)}, bf16[128,256]{1,0:T(8,128)(2,1)}, u32[]{:S(2)}) copy-start(bf16[128,256]{1,0:T(8,128)(2,1)} %param.6) | copy-start | bytes 196612
  4.6 15.6 %copy-start.5 = (s32[1,4,6]{2,1,0:T(4,128)S(1)}, s32[1,4,6]{2,1,0:T(4,128)}, u32[]{:S(2)}) copy-start(s32[1,4,6]{2,1,0:T(4,128)} %param.11) | copy-start | bytes 292
  4.6 32.5 %all-to-all-start = ((bf16[4,1040,128]{2,1,0:T(8,128)(2,1)}), bf16[4,1040,128]{2,1,0:T(8,128)(2,1)S(1)}, u32[]{:S(2)}, u32[]{:S(2)}) async-start(bf16[4,1040,128]{2,1,0:T(8,128)(2,1)} %pad_maximum_fusion), calls=%async_computation | async-start | bytes 2129920 | tf_op jit(solution)/shard_map/all_to_all | solution.py:135
  11.1 1.3 %collective-permute-start = (bf16[1,128,256]{2,1,0:T(8,128)(2,1)S(1)}, bf16[1,128,256]{2,1,0:T(8,128)(2,1)S(1)}, u32[]{:S(2)}, u32[]{:S(2)}) collective-permute-start(bf16[1,128,256]{2,1,0:T(8,128)(2,1)S(1)} %bitcast.30), channel_id=1, source_target_pairs={{0,4},{4,0},{8,12},{12,8},{16,20},{20,16},{24,28},{28,24},{1,5},{5... | collective-permute-start | bytes 196616 | tf_op jit(solution)/shard_map/ppermute | solution.py:34
  12.4 5.6 %collective-permute-start.1 = (bf16[2,128,256]{2,1,0:T(8,128)(2,1)S(1)}, bf16[2,128,256]{2,1,0:T(8,128)(2,1)S(1)}, u32[]{:S(2)}, u32[]{:S(2)}) collective-permute-start(bf16[2,128,256]{2,1,0:T(8,128)(2,1)S(1)} %maximum_select_fusion.2), channel_id=1, source_target_pairs={{0,8},{4,12},{8,0},{12,4},{16,24},{20,28},{24,16},{28,20},{1,9},{5... | collective-permute-start | bytes 393224 | tf_op jit(solution)/shard_map/ppermute | solution.py:34
  18.0 7.6 %collective-permute-start.2 = (bf16[4,128,256]{2,1,0:T(8,128)(2,1)S(1)}, bf16[4,128,256]{2,1,0:T(8,128)(2,1)S(1)}, u32[]{:S(2)}, u32[]{:S(2)}) collective-permute-start(bf16[4,128,256]{2,1,0:T(8,128)(2,1)S(1)} %maximum_select_fusion.1), channel_id=1, source_target_pairs={{0,16},{4,20},{8,24},{12,28},{16,0},{20,4},{24,8},{28,12},{1,17},{... | collective-permute-start | bytes 786440 | tf_op jit(solution)/shard_map/ppermute | solution.py:34
  37.2 1.0 %copy-start.2 = (bf16[4,1040,128]{2,1,0:T(8,128)(2,1)}, bf16[4,1040,128]{2,1,0:T(8,128)(2,1)S(1)}, u32[]{:S(2)}) copy-start(bf16[4,1040,128]{2,1,0:T(8,128)(2,1)S(1)} %all-to-all-done.refs_4_) | copy-start | bytes 3194884
  46.0 4.8 %copy-start.3 = (f32[4,128,256]{2,1,0:T(8,128)S(1)}, f32[4,128,256]{2,1,0:T(8,128)}, u32[]{:S(2)}) copy-start(f32[4,128,256]{2,1,0:T(8,128)} %get-tuple-element.8) | copy-start | bytes 1572868
  46.0 2.1 %collective-permute-start.6 = (f32[4,128,256]{2,1,0:T(8,128)}, f32[4,128,256]{2,1,0:T(8,128)S(1)}, u32[]{:S(2)}, u32[]{:S(2)}) collective-permute-start(f32[4,128,256]{2,1,0:T(8,128)} %get-tuple-element.10), channel_id=1, source_target_pairs={{0,4},{4,0},{8,12},{12,8},{16,20},{20,16},{24,28},{28,24},{1,5},{5... | collective-permute-start | bytes 1572872 | tf_op jit(solution)/shard_map/ppermute | solution.py:19
  49.3 8.4 %collective-permute-start.7 = (f32[2,128,256]{2,1,0:T(8,128)S(1)}, f32[2,128,256]{2,1,0:T(8,128)S(1)}, u32[]{:S(2)}, u32[]{:S(2)}) collective-permute-start(f32[2,128,256]{2,1,0:T(8,128)S(1)} %slice.60), channel_id=1, source_target_pairs={{0,8},{4,12},{8,0},{12,4},{16,24},{20,28},{24,16},{28,20},{1,9},{5... | collective-permute-start | bytes 786440 | tf_op jit(solution)/shard_map/ppermute | solution.py:23
  50.9 8.5 %collective-permute-start.3 = (f32[128,256]{1,0:T(8,128)S(1)}, f32[128,256]{1,0:T(8,128)S(1)}, u32[]{:S(2)}, u32[]{:S(2)}) collective-permute-start(f32[128,256]{1,0:T(8,128)S(1)} %get-tuple-element.11), channel_id=1, source_target_pairs={{0,3},{1,0},{2,1},{3,2},{4,7},{5,4},{6,5},{7,6},{8,11},{9,8},{10,9... | collective-permute-start | bytes 393224 | tf_op jit(solution)/shard_map/ppermute | solution.py:44
  52.4 8.3 %collective-permute-start.5 = (f32[128,256]{1,0:T(8,128)S(1)}, f32[128,256]{1,0:T(8,128)S(1)}, u32[]{:S(2)}, u32[]{:S(2)}) collective-permute-start(f32[128,256]{1,0:T(8,128)S(1)} %get-tuple-element.12), channel_id=1, source_target_pairs={{0,1},{1,2},{2,3},{3,0},{4,5},{5,6},{6,7},{7,4},{8,9},{9,10},{10,1... | collective-permute-start | bytes 393224 | tf_op jit(solution)/shard_map/ppermute | solution.py:44
  53.0 11.3 %collective-permute-start.4 = (f32[128,256]{1,0:T(8,128)S(1)}, f32[128,256]{1,0:T(8,128)S(1)}, u32[]{:S(2)}, u32[]{:S(2)}) collective-permute-start(f32[128,256]{1,0:T(8,128)S(1)} %get-tuple-element.13), channel_id=1, source_target_pairs={{0,2},{1,3},{2,0},{3,1},{4,6},{5,7},{6,4},{7,5},{8,10},{9,11},{10,... | collective-permute-start | bytes 393224 | tf_op jit(solution)/shard_map/ppermute | solution.py:44
  57.8 6.5 %collective-permute-start.8 = (f32[1,128,256]{2,1,0:T(8,128)S(1)}, f32[1,128,256]{2,1,0:T(8,128)S(1)}, u32[]{:S(2)}, u32[]{:S(2)}) collective-permute-start(f32[1,128,256]{2,1,0:T(8,128)S(1)} %slice.62), channel_id=1, source_target_pairs={{0,16},{4,20},{8,24},{12,28},{16,0},{20,4},{24,8},{28,12},{1,17},{... | collective-permute-start | bytes 393224 | tf_op jit(solution)/shard_map/ppermute | solution.py:23

commit v10 on v9

--- a/solution.py
+++ b/solution.py
@@ -117,15 +117,15 @@
     grp_bits = grp_count.bit_length() - 1
     relations = cores.shape[0]
 
-    tile_ids = jnp.arange(tiles, dtype=jnp.int32)
-    live = (tile_ids < tile_count.reshape(())).astype(jnp.float32)
     relay_ids = jnp.arange(ent_count, dtype=jnp.int32)
     slot_ids = jnp.arange(per_relay, dtype=jnp.int32)
     tile_of = slot_ids[None, :] * ent_count + (relay_ids[:, None] - my_ent) % ent_count
     adj_out = adjacency[tile_of].astype(jnp.bfloat16).reshape(ent_count, per_relay * block, block)
     halves = jnp.concatenate([factor[:, :block], factor[:, block:]], axis=0)
     head = jnp.concatenate(
-        [tile_rels.reshape(tiles)[tile_of].astype(jnp.float32), live[tile_of]], axis=1
+        [tile_rels.reshape(tiles)[tile_of].astype(jnp.float32),
+         (tile_of < tile_count.reshape(())).astype(jnp.float32)],
+        axis=1,
     )
     head = jnp.pad(head, ((0, 0), (0, block - 2 * per_relay)))
     head = jnp.broadcast_to(head[:, None, :], (ent_count, head_rows, block)).astype(jnp.bfloat16)

time: 65.3 us -> 65.2 us (level)
    gather x1 -> x0, local copies, waits for them, and re-layouts: 0.7 us -> none  [on_device(): live[tile_of]]
where the time goes in v10:
time: 65.2 us; the launch traced here: 64.9 us
  waiting for transfers between devices  32.5 us (50%)
  starting transfers between devices  14.9 us (23%)
  Pallas kernels  7.88 us (12%)
  other arithmetic  6.2 us (10%)
  local copies, waits for them, and re-layouts  2.53 us (4%)
  between operations  0.9 us (1%)
    all_to_all x1, waiting for transfers between devices, on_device(): lax.all_to_all(outgoing, 'ent', split_axis=0, concat_axis=0, tiled=True)  10.6 us
    ppermute x3, waiting for transfers between devices, grp_gather(): got = lax.ppermute(held, 'grp', [(i, i ^ bit) for i in range(grp_count)])  10.1 us
    pallas_call x1, Pallas kernels, on_device(): pl.pallas_call(lambda *refs: tile_kernel(*refs, per_relay=per_relay, bloc...  7.88 us
    all_to_all x1, starting transfers between devices, on_device(): lax.all_to_all(outgoing, 'ent', split_axis=0, concat_axis=0, tiled=True)  6.45 us
    ppermute x3, waiting for transfers between devices, shift_ent(): lax.ppermute(x, 'ent', [(i, (i + shift) % ent_count) for i in range(ent_c...  4.89 us
    ppermute x2, waiting for transfers between devices, grp_reduce_scatter(): lax.ppermute(parts[half:], 'grp', [(i, i ^ bit) for i in range(grp_count)])  4.67 us
    ppermute x3, starting transfers between devices, grp_gather(): got = lax.ppermute(held, 'grp', [(i, i ^ bit) for i in range(grp_count)])  3.14 us
    ppermute x2, starting transfers between devices, grp_reduce_scatter(): lax.ppermute(parts[half:], 'grp', [(i, i ^ bit) for i in range(grp_count)])  3.13 us
  transfers between devices with their start and end apart: 10, of which 8 were waited for; matrix products, arithmetic and copies ran while one was open for 3% of the time, Pallas kernels for 0%

profile of v10, /device:TPU:0, one launch (start us, length us, event | category | flops | bytes accessed | tf_op | source)
XLA Modules:
  0.0 64.9 jit_solution(10939396896906254854)
XLA Ops:
  0.0 0.0 copy-start
  0.0 0.0 copy-start.3
  0.8 0.1 compare_select_fusion
  0.9 0.1 convert_convert_fusion
  1.0 0.1 reshape.101
  1.0 1.4 %gather_fusion.1 = s32[24]{0:T(128)S(1)} fusion(s32[24]{0:T(128)} %bitcast.28, s32[1024]{0:T(1024)S(1)} %pad_clamp_fusion), kind=kCustom, calls=%fused_computation.1 | custom fusion | bytes 288 | tf_op jit(solution)/shard_map/gather | solution.py:126
  2.4 0.1 reshape.120
  2.5 0.0 copy-done.3
  2.5 0.0 copy-done
  2.5 0.6 %gather_fusion = s32[24,128,128]{2,1,0:T(8,128)S(1)} fusion(s32[24,128,128]{2,1,0:T(8,128)S(1)} %copy-done, s32[1024]{0:T(1024)S(1)} %pad_clamp_fusion), kind=kCustom, calls=%fused_computation | custom fusion | bytes 3145824 | tf_op jit(solution)/shard_map/gather | solution.py:123
  3.2 0.2 convert_element_type.34
  3.4 0.1 fusion.6
  3.5 1.1 %pad_maximum_fusion = bf16[4,1040,128]{2,1,0:T(8,128)(2,1)} fusion(bf16[4,16,128]{2,1,0:T(8,128)(2,1)S(1)} %broadcast_in_dim.7, bf16[4,256,128]{2,1,0:T(8,128)(2,1)S(1)} %broadcast_in_dim.6, bf16[4,768,128]{2,1,0:T(8,128)(2,1)S(1)} %bitcast.29), kind=kLoop, calls=%fused_computation.2 | loop fusion | flops 3194880 | bytes 2129920 | tf_op jit(solution)/shard_map/concatenate | solution.py:132
  4.5 0.0 copy-start.4
  4.5 6.4 %all-to-all-start = ((bf16[4,1040,128]{2,1,0:T(8,128)(2,1)}), bf16[4,1040,128]{2,1,0:T(8,128)(2,1)S(1)}, u32[]{:S(2)}, u32[]{:S(2)}) async-start(bf16[4,1040,128]{2,1,0:T(8,128)(2,1)} %pad_maximum_fusion), calls=%async_computation | async-start | bytes 2129920 | tf_op jit(solution)/shard_map/all_to_all | solution.py:135
  11.0 0.0 collective-permute-start
  11.0 1.3 %collective-permute-done = bf16[1,128,256]{2,1,0:T(8,128)(2,1)S(1)} collective-permute-done((bf16[1,128,256]{2,1,0:T(8,128)(2,1)S(1)}, bf16[1,128,256]{2,1,0:T(8,128)(2,1)S(1)}, u32[]{:S(2)}, u32[]{:S(2)}) %collective-permute-start) | collective-permute-done | bytes 65568 | tf_op jit(solution)/shard_map/ppermute | solution.py:34
  12.3 1.6 %collective-permute-start.1 = (bf16[2,128,256]{2,1,0:T(8,128)(2,1)S(1)}, bf16[2,128,256]{2,1,0:T(8,128)(2,1)S(1)}, u32[]{:S(2)}, u32[]{:S(2)}) collective-permute-start(bf16[2,128,256]{2,1,0:T(8,128)(2,1)S(1)} %maximum_select_fusion.2), channel_id=1, source_target_pairs={{0,8},{4,12},{8,0},{12,4},{16,24},{20,28},{24,16},{28,20},{1,9},{5... | collective-permute-start | bytes 393224 | tf_op jit(solution)/shard_map/ppermute | solution.py:34
  13.8 4.1 %collective-permute-done.1 = bf16[2,128,256]{2,1,0:T(8,128)(2,1)S(1)} collective-permute-done((bf16[2,128,256]{2,1,0:T(8,128)(2,1)S(1)}, bf16[2,128,256]{2,1,0:T(8,128)(2,1)S(1)}, u32[]{:S(2)}, u32[]{:S(2)}) %collective-permute-start.1) | collective-permute-done | bytes 131104 | tf_op jit(solution)/shard_map/ppermute | solution.py:34
  17.9 1.6 %collective-permute-start.2 = (bf16[4,128,256]{2,1,0:T(8,128)(2,1)S(1)}, bf16[4,128,256]{2,1,0:T(8,128)(2,1)S(1)}, u32[]{:S(2)}, u32[]{:S(2)}) collective-permute-start(bf16[4,128,256]{2,1,0:T(8,128)(2,1)S(1)} %maximum_select_fusion.1), channel_id=1, source_target_pairs={{0,16},{4,20},{8,24},{12,28},{16,0},{20,4},{24,8},{28,12},{1,17},{... | collective-permute-start | bytes 786440 | tf_op jit(solution)/shard_map/ppermute | solution.py:34
  19.5 0.6 and_select_fusion.refs_3_
  20.1 0.0 copy-done.4
  20.1 0.6 shift-left_or_fusion.refs_2_
  20.7 4.8 %collective-permute-done.2 = bf16[4,128,256]{2,1,0:T(8,128)(2,1)S(1)} collective-permute-done((bf16[4,128,256]{2,1,0:T(8,128)(2,1)S(1)}, bf16[4,128,256]{2,1,0:T(8,128)(2,1)S(1)}, u32[]{:S(2)}, u32[]{:S(2)}) %collective-permute-start.2) | collective-permute-done | bytes 262176 | tf_op jit(solution)/shard_map/ppermute | solution.py:34
  25.5 0.9 %maximum_select_fusion.refs_6_ = bf16[8,128,256]{2,1,0:T(8,128)(2,1)} fusion(bf16[4,128,256]{2,1,0:T(8,128)(2,1)S(1)} %collective-permute-done.2, bf16[4,128,256]{2,1,0:T(8,128)(2,1)S(1)} %maximum_select_fusion.1, pred[]{:T(512)S(6)} %eq.17), kind=kLoop, calls=%fused_computation.3 | loop fusion | flops 786432 | bytes 1048577 | tf_op jit(solution)/shard_map/jit(_where)/select_n | solution.py:36
  26.4 10.6 %all-to-all-done.refs_4_ = bf16[4,1040,128]{2,1,0:T(8,128)(2,1)S(1)} async-done(((bf16[4,1040,128]{2,1,0:T(8,128)(2,1)}), bf16[4,1040,128]{2,1,0:T(8,128)(2,1)S(1)}, u32[]{:S(2)}, u32[]{:S(2)}) %all-to-all-start) | async-done | bytes 1064992 | tf_op jit(solution)/shard_map/all_to_all | solution.py:135
  37.1 0.0 copy-start.1
  37.1 0.7 %add_convert_fusion.refs_0_ = s32[4,6]{1,0:T(4,128)} fusion(f32[4,128]{1,0:T(4,128)S(1)} %bitcast.32), kind=kLoop, calls=%fused_computation.28 | loop fusion | flops 72 | bytes 288 | tf_op jit(solution)/shard_map/convert_element_type | solution.py:139
  37.8 0.2 copy-done.1
  38.1 7.9 %shard_map.64 = (f32[4,128,256]{2,1,0:T(8,128)}, f32[4,128,256]{2,1,0:T(8,128)}, f32[4,128,256]{2,1,0:T(8,128)}) custom-call(s32[4,6]{1,0:T(4,128)} %add_convert_fusion.refs_0_, s32[4,6]{1,0:T(4,128)} %bitcast.33, s32[4,6]{1,0:T(4,128)} %shift-left_or_fusion.refs_2_, s32[4]{0:T(128)} %and_select_fusion.refs_3_, bf16[4,1040,128]{2,1,0:T(8,128)(2,1)} %copy-done.1, ...), custom_call_target="tpu_custom_call" | custom-call | tf_op jit(solution)/shard_map/pallas_call | solution.py:159
  45.9 0.0 copy-start.2
  45.9 0.0 collective-permute-start.6
  46.0 2.1 %collective-permute-done.6 = f32[4,128,256]{2,1,0:T(8,128)S(1)} collective-permute-done((f32[4,128,256]{2,1,0:T(8,128)}, f32[4,128,256]{2,1,0:T(8,128)S(1)}, u32[]{:S(2)}, u32[]{:S(2)}) %collective-permute-start.6) | collective-permute-done | bytes 524320 | tf_op jit(solution)/shard_map/ppermute | solution.py:19
  48.1 1.1 %add.109 = f32[4,128,256]{2,1,0:T(8,128)S(1)} add(f32[4,128,256]{2,1,0:T(8,128)} %get-tuple-element.9, f32[4,128,256]{2,1,0:T(8,128)S(1)} %collective-permute-done.6) | non-fusion elementwise | flops 131072 | bytes 1572864 | tf_op jit(solution)/shard_map/add | solution.py:19
  49.2 1.6 %collective-permute-start.7 = (f32[2,128,256]{2,1,0:T(8,128)S(1)}, f32[2,128,256]{2,1,0:T(8,128)S(1)}, u32[]{:S(2)}, u32[]{:S(2)}) collective-permute-start(f32[2,128,256]{2,1,0:T(8,128)S(1)} %slice.58), channel_id=1, source_target_pairs={{0,8},{4,12},{8,0},{12,4},{16,24},{20,28},{24,16},{28,20},{1,9},{5... | collective-permute-start | bytes 786440 | tf_op jit(solution)/shard_map/ppermute | solution.py:23
  50.8 0.0 copy-done.2
  50.8 1.5 %collective-permute-start.3 = (f32[128,256]{1,0:T(8,128)S(1)}, f32[128,256]{1,0:T(8,128)S(1)}, u32[]{:S(2)}, u32[]{:S(2)}) collective-permute-start(f32[128,256]{1,0:T(8,128)S(1)} %get-tuple-element.11), channel_id=1, source_target_pairs={{0,3},{1,0},{2,1},{3,2},{4,7},{5,4},{6,5},{7,6},{8,11},{9,8},{10,9... | collective-permute-start | bytes 393224 | tf_op jit(solution)/shard_map/ppermute | solution.py:44
  52.3 0.6 collective-permute-start.5
  52.9 0.1 collective-permute-start.4
  53.0 4.7 %collective-permute-done.7 = f32[2,128,256]{2,1,0:T(8,128)S(1)} collective-permute-done((f32[2,128,256]{2,1,0:T(8,128)S(1)}, f32[2,128,256]{2,1,0:T(8,128)S(1)}, u32[]{:S(2)}, u32[]{:S(2)}) %collective-permute-start.7) | collective-permute-done | bytes 262176 | tf_op jit(solution)/shard_map/ppermute | solution.py:23
  57.7 1.6 %collective-permute-start.8 = (f32[1,128,256]{2,1,0:T(8,128)S(1)}, f32[1,128,256]{2,1,0:T(8,128)S(1)}, u32[]{:S(2)}, u32[]{:S(2)}) collective-permute-start(f32[1,128,256]{2,1,0:T(8,128)S(1)} %slice.60), channel_id=1, source_target_pairs={{0,16},{4,20},{8,24},{12,28},{16,0},{20,4},{24,8},{28,12},{1,17},{... | collective-permute-start | bytes 393224 | tf_op jit(solution)/shard_map/ppermute | solution.py:23
  59.3 0.0 collective-permute-done.3
  59.3 1.3 %collective-permute-done.5 = f32[128,256]{1,0:T(8,128)S(1)} collective-permute-done((f32[128,256]{1,0:T(8,128)S(1)}, f32[128,256]{1,0:T(8,128)S(1)}, u32[]{:S(2)}, u32[]{:S(2)}) %collective-permute-start.5) | collective-permute-done | bytes 131104 | tf_op jit(solution)/shard_map/ppermute | solution.py:44
  60.6 3.5 %collective-permute-done.4 = f32[128,256]{1,0:T(8,128)S(1)} collective-permute-done((f32[128,256]{1,0:T(8,128)S(1)}, f32[128,256]{1,0:T(8,128)S(1)}, u32[]{:S(2)}, u32[]{:S(2)}) %collective-permute-start.4) | collective-permute-done | bytes 131104 | tf_op jit(solution)/shard_map/ppermute | solution.py:44
  64.1 0.0 collective-permute-done.8
  64.1 0.7 %fusion.1 = f32[128,256]{1,0:T(8,128)} fusion(f32[1,128,256]{2,1,0:T(8,128)S(1)} %collective-permute-done.8, f32[2,128,256]{2,1,0:T(8,128)S(1)} %slice_add_fusion, f32[128,256]{1,0:T(8,128)S(1)} %collective-permute-done.5, f32[128,256]{1,0:T(8,128)S(1)} %collective-permute-done.4, f32[128,256]{1,0:T(8,128)S(1)} %collective-permute-done.3, ...), kind=kLoop, calls=%fused_computation.8 | loop fusion | flops 163840 | bytes 917504 | tf_op jit(solution)/shard_map/add | solution.py:173
  (15 shorter events, 0.2 us)
Async XLA Ops:
  0.0 2.5 %copy-start = (s32[24,128,128]{2,1,0:T(8,128)S(1)}, s32[24,128,128]{2,1,0:T(8,128)}, u32[]{:S(2)}) copy-start(s32[24,128,128]{2,1,0:T(8,128)} %param.8) | copy-start | bytes 4718596
  0.0 2.5 %copy-start.3 = (bf16[128,256]{1,0:T(8,128)(2,1)S(1)}, bf16[128,256]{1,0:T(8,128)(2,1)}, u32[]{:S(2)}) copy-start(bf16[128,256]{1,0:T(8,128)(2,1)} %param.6) | copy-start | bytes 196612
  4.5 15.6 %copy-start.4 = (s32[1,4,6]{2,1,0:T(4,128)S(1)}, s32[1,4,6]{2,1,0:T(4,128)}, u32[]{:S(2)}) copy-start(s32[1,4,6]{2,1,0:T(4,128)} %param.11) | copy-start | bytes 292
  4.5 32.5 %all-to-all-start = ((bf16[4,1040,128]{2,1,0:T(8,128)(2,1)}), bf16[4,1040,128]{2,1,0:T(8,128)(2,1)S(1)}, u32[]{:S(2)}, u32[]{:S(2)}) async-start(bf16[4,1040,128]{2,1,0:T(8,128)(2,1)} %pad_maximum_fusion), calls=%async_computation | async-start | bytes 2129920 | tf_op jit(solution)/shard_map/all_to_all | solution.py:135
  11.0 1.3 %collective-permute-start = (bf16[1,128,256]{2,1,0:T(8,128)(2,1)S(1)}, bf16[1,128,256]{2,1,0:T(8,128)(2,1)S(1)}, u32[]{:S(2)}, u32[]{:S(2)}) collective-permute-start(bf16[1,128,256]{2,1,0:T(8,128)(2,1)S(1)} %bitcast.30), channel_id=1, source_target_pairs={{0,4},{4,0},{8,12},{12,8},{16,20},{20,16},{24,28},{28,24},{1,5},{5... | collective-permute-start | bytes 196616 | tf_op jit(solution)/shard_map/ppermute | solution.py:34
  12.3 5.6 %collective-permute-start.1 = (bf16[2,128,256]{2,1,0:T(8,128)(2,1)S(1)}, bf16[2,128,256]{2,1,0:T(8,128)(2,1)S(1)}, u32[]{:S(2)}, u32[]{:S(2)}) collective-permute-start(bf16[2,128,256]{2,1,0:T(8,128)(2,1)S(1)} %maximum_select_fusion.2), channel_id=1, source_target_pairs={{0,8},{4,12},{8,0},{12,4},{16,24},{20,28},{24,16},{28,20},{1,9},{5... | collective-permute-start | bytes 393224 | tf_op jit(solution)/shard_map/ppermute | solution.py:34
  17.9 7.6 %collective-permute-start.2 = (bf16[4,128,256]{2,1,0:T(8,128)(2,1)S(1)}, bf16[4,128,256]{2,1,0:T(8,128)(2,1)S(1)}, u32[]{:S(2)}, u32[]{:S(2)}) collective-permute-start(bf16[4,128,256]{2,1,0:T(8,128)(2,1)S(1)} %maximum_select_fusion.1), channel_id=1, source_target_pairs={{0,16},{4,20},{8,24},{12,28},{16,0},{20,4},{24,8},{28,12},{1,17},{... | collective-permute-start | bytes 786440 | tf_op jit(solution)/shard_map/ppermute | solution.py:34
  37.1 1.0 %copy-start.1 = (bf16[4,1040,128]{2,1,0:T(8,128)(2,1)}, bf16[4,1040,128]{2,1,0:T(8,128)(2,1)S(1)}, u32[]{:S(2)}) copy-start(bf16[4,1040,128]{2,1,0:T(8,128)(2,1)S(1)} %all-to-all-done.refs_4_) | copy-start | bytes 3194884
  45.9 4.8 %copy-start.2 = (f32[4,128,256]{2,1,0:T(8,128)S(1)}, f32[4,128,256]{2,1,0:T(8,128)}, u32[]{:S(2)}) copy-start(f32[4,128,256]{2,1,0:T(8,128)} %get-tuple-element.8) | copy-start | bytes 1572868
  45.9 2.1 %collective-permute-start.6 = (f32[4,128,256]{2,1,0:T(8,128)}, f32[4,128,256]{2,1,0:T(8,128)S(1)}, u32[]{:S(2)}, u32[]{:S(2)}) collective-permute-start(f32[4,128,256]{2,1,0:T(8,128)} %get-tuple-element.10), channel_id=1, source_target_pairs={{0,4},{4,0},{8,12},{12,8},{16,20},{20,16},{24,28},{28,24},{1,5},{5... | collective-permute-start | bytes 1572872 | tf_op jit(solution)/shard_map/ppermute | solution.py:19
  49.2 8.4 %collective-permute-start.7 = (f32[2,128,256]{2,1,0:T(8,128)S(1)}, f32[2,128,256]{2,1,0:T(8,128)S(1)}, u32[]{:S(2)}, u32[]{:S(2)}) collective-permute-start(f32[2,128,256]{2,1,0:T(8,128)S(1)} %slice.58), channel_id=1, source_target_pairs={{0,8},{4,12},{8,0},{12,4},{16,24},{20,28},{24,16},{28,20},{1,9},{5... | collective-permute-start | bytes 786440 | tf_op jit(solution)/shard_map/ppermute | solution.py:23
  50.8 8.5 %collective-permute-start.3 = (f32[128,256]{1,0:T(8,128)S(1)}, f32[128,256]{1,0:T(8,128)S(1)}, u32[]{:S(2)}, u32[]{:S(2)}) collective-permute-start(f32[128,256]{1,0:T(8,128)S(1)} %get-tuple-element.11), channel_id=1, source_target_pairs={{0,3},{1,0},{2,1},{3,2},{4,7},{5,4},{6,5},{7,6},{8,11},{9,8},{10,9... | collective-permute-start | bytes 393224 | tf_op jit(solution)/shard_map/ppermute | solution.py:44
  52.3 8.3 %collective-permute-start.5 = (f32[128,256]{1,0:T(8,128)S(1)}, f32[128,256]{1,0:T(8,128)S(1)}, u32[]{:S(2)}, u32[]{:S(2)}) collective-permute-start(f32[128,256]{1,0:T(8,128)S(1)} %get-tuple-element.12), channel_id=1, source_target_pairs={{0,1},{1,2},{2,3},{3,0},{4,5},{5,6},{6,7},{7,4},{8,9},{9,10},{10,1... | collective-permute-start | bytes 393224 | tf_op jit(solution)/shard_map/ppermute | solution.py:44
  52.9 11.3 %collective-permute-start.4 = (f32[128,256]{1,0:T(8,128)S(1)}, f32[128,256]{1,0:T(8,128)S(1)}, u32[]{:S(2)}, u32[]{:S(2)}) collective-permute-start(f32[128,256]{1,0:T(8,128)S(1)} %get-tuple-element.13), channel_id=1, source_target_pairs={{0,2},{1,3},{2,0},{3,1},{4,6},{5,7},{6,4},{7,5},{8,10},{9,11},{10,... | collective-permute-start | bytes 393224 | tf_op jit(solution)/shard_map/ppermute | solution.py:44
  57.7 6.5 %collective-permute-start.8 = (f32[1,128,256]{2,1,0:T(8,128)S(1)}, f32[1,128,256]{2,1,0:T(8,128)S(1)}, u32[]{:S(2)}, u32[]{:S(2)}) collective-permute-start(f32[1,128,256]{2,1,0:T(8,128)S(1)} %slice.60), channel_id=1, source_target_pairs={{0,16},{4,20},{8,24},{12,28},{16,0},{20,4},{24,8},{28,12},{1,17},{... | collective-permute-start | bytes 393224 | tf_op jit(solution)/shard_map/ppermute | solution.py:23

commit v11 on v10

--- a/solution.py
+++ b/solution.py
@@ -44,14 +44,14 @@
     return lax.ppermute(x, "ent", [(i, (i + shift) % ent_count) for i in range(ent_count)])
 
 
-def tile_kernel(codes_ref, groups_ref, slots_ref, shift_ref, in_ref, core_ref, panel_ref,
-                row_ref, keep_ref, send_ref, *, per_relay, block):
-    e = pl.program_id(0)
-
-    @pl.when(e == 0)
+def tile_kernel(srcs_ref, codes_ref, groups_ref, slots_ref, in_ref, core_ref, panel_ref,
+                keep_in_ref, send_in_ref, row_ref, keep_ref, send_ref, *, per_relay, block):
+    e = srcs_ref[pl.program_id(0)]
+
+    @pl.when(pl.program_id(0) == 0)
     def _():
-        keep_ref[...] = jnp.zeros_like(keep_ref)
-        send_ref[...] = jnp.zeros_like(send_ref)
+        keep_ref[...] = keep_in_ref[...]
+        send_ref[...] = send_in_ref[...]
 
     nt = (((1,), (1,)), ((), ()))
     base = per_relay * block
@@ -135,41 +135,54 @@
     arrived = lax.all_to_all(outgoing, "ent", split_axis=0, concat_axis=0, tiled=True)
     group_blocks = grp_gather(factor, grp_count)
 
-    heads = arrived[:, -head_rows].astype(jnp.float32)
-    codes = (heads[:, :per_relay] * 2 + heads[:, per_relay : 2 * per_relay]).astype(jnp.int32)
+    def codes_of(buf):
+        heads = buf[:, -head_rows].astype(jnp.float32)
+        return (heads[:, :per_relay] * 2 + heads[:, per_relay : 2 * per_relay]).astype(jnp.int32)
+
     groups = send_lists.reshape(ent_count, per_relay)
     slots = bit_reverse(groups ^ lax.axis_index("grp"), grp_bits)
-    shifts = (my_ent - jnp.arange(ent_count, dtype=jnp.int32)) % ent_count
-    rows_in = arrived.shape[1]
-
-    grid_spec = pltpu.PrefetchScalarGridSpec(
-        num_scalar_prefetch=4,
-        grid=(ent_count,),
-        in_specs=[
-            pl.BlockSpec((1, rows_in, block), lambda e, c, g, s, k: (e, 0, 0)),
-            pl.BlockSpec(memory_space=pltpu.VMEM),
-            pl.BlockSpec(memory_space=pltpu.VMEM),
-        ],
-        out_specs=[
-            pl.BlockSpec((1, block, width), lambda e, c, g, s, k: (k[e], 0, 0)),
-            pl.BlockSpec((grp_count // 2, block, width), lambda e, c, g, s, k: (0, 0, 0)),
-            pl.BlockSpec((grp_count // 2, block, width), lambda e, c, g, s, k: (0, 0, 0)),
-        ],
-    )
-    row_parts, owner_keep, owner_send = pl.pallas_call(
-        lambda *refs: tile_kernel(*refs, per_relay=per_relay, block=block),
-        grid_spec=grid_spec,
-        out_shape=[
-            jax.ShapeDtypeStruct((ent_count, block, width), jnp.float32),
-            jax.ShapeDtypeStruct((grp_count // 2, block, width), jnp.float32),
-            jax.ShapeDtypeStruct((grp_count // 2, block, width), jnp.float32),
-        ],
-    )(codes, groups, slots, shifts, arrived, cores, group_blocks)
-
-    rows = row_parts[0]
+    rows_in = outgoing.shape[1]
+    half = grp_count // 2
+
+    def relay_tiles(srcs, codes, buf, keep, send):
+        steps = srcs.shape[0]
+        any_map = lambda i, *refs: (0, 0, 0)
+        return pl.pallas_call(
+            lambda *refs: tile_kernel(*refs, per_relay=per_relay, block=block),
+            grid_spec=pltpu.PrefetchScalarGridSpec(
+                num_scalar_prefetch=4,
+                grid=(steps,),
+                in_specs=[
+                    pl.BlockSpec((1, rows_in, block), lambda i, e, c, g, s: (e[i], 0, 0)),
+                    pl.BlockSpec(memory_space=pltpu.VMEM),
+                    pl.BlockSpec(memory_space=pltpu.VMEM),
+                    pl.BlockSpec((half, block, width), any_map),
+                    pl.BlockSpec((half, block, width), any_map),
+                ],
+                out_specs=[
+                    pl.BlockSpec((1, block, width), lambda i, *refs: (i, 0, 0)),
+                    pl.BlockSpec((half, block, width), any_map),
+                    pl.BlockSpec((half, block, width), any_map),
+                ],
+            ),
+            out_shape=[
+                jax.ShapeDtypeStruct((steps, block, width), jnp.float32),
+                jax.ShapeDtypeStruct((half, block, width), jnp.float32),
+                jax.ShapeDtypeStruct((half, block, width), jnp.float32),
+            ],
+        )(srcs, codes, groups, slots, buf, cores, group_blocks, keep, send)
+
+    empty = jnp.zeros((half, block, width), jnp.float32)
+    own_row, keep, send = relay_tiles(
+        my_ent.reshape(1).astype(jnp.int32), codes_of(outgoing), outgoing, empty, empty
+    )
+    remote_srcs = (my_ent - jnp.arange(1, ent_count, dtype=jnp.int32)) % ent_count
+    row_parts, keep, send = relay_tiles(remote_srcs, codes_of(arrived), arrived, keep, send)
+
+    rows = own_row[0]
     for k in range(1, ent_count):
-        rows = rows + shift_ent(row_parts[k], -k, ent_count)
-    owner_part = grp_reduce_scatter(owner_keep, owner_send, grp_count)
+        rows = rows + shift_ent(row_parts[k - 1], -k, ent_count)
+    owner_part = grp_reduce_scatter(keep, send, grp_count)
     return rows + owner_part
 
 

time: 65.2 us -> 64.9 us (level)
  waiting for transfers between devices: 32.5 us -> 25.8 us
  Pallas kernels: 7.88 us -> 12.1 us
  local copies, waits for them, and re-layouts: 2.53 us -> 4.14 us
  other arithmetic: 6.2 us -> 6.86 us
    all_to_all x1, waiting for transfers between devices: 10.6 us -> 4.93 us  [on_device(): lax.all_to_all(outgoing, 'ent', split_axis=0, concat_axis=0, tiled=True)]
    pallas_call x1 -> x2, Pallas kernels: 7.88 us -> 12.1 us  [relay_tiles(): pl.pallas_call(lambda *refs: tile_kernel(*refs, per_relay=per_relay, bloc...]
    broadcast_in_dim x0 -> x1, local copies, waits for them, and re-layouts: none -> 0.84 us  [on_device(): empty = jnp.zeros((half, block, width), jnp.float32)]
    convert_element_type x2 -> x4, other arithmetic: 0.75 us -> 1.48 us  [the longest x2 1.41 us: codes_of(): (heads[:, :per_relay] * 2 + heads[:, per_relay:2 * per_relay]).astype(jnp...]
    unnamed x10 -> x12, local copies, waits for them, and re-layouts: 0.25 us -> 0.93 us
  transfers between devices with their start and end apart: 10 -> 10, of which waited for: 8 -> 7; matrix products, arithmetic and copies ran while one was open for 3% -> 6% of each run, Pallas kernels for 0% -> 8%
where the time goes in v11:
time: 64.9 us; the launch traced here: 64.5 us
  waiting for transfers between devices  25.8 us (40%)
  starting transfers between devices  14.9 us (23%)
  Pallas kernels  12.1 us (19%)
  other arithmetic  6.86 us (11%)
  local copies, waits for them, and re-layouts  4.14 us (6%)
  between operations  0.78 us (1%)
    pallas_call x2, Pallas kernels, relay_tiles(): pl.pallas_call(lambda *refs: tile_kernel(*refs, per_relay=per_relay, bloc...  12.1 us
    ppermute x3, waiting for transfers between devices, grp_gather(): got = lax.ppermute(held, 'grp', [(i, i ^ bit) for i in range(grp_count)])  9.5 us
    all_to_all x1, starting transfers between devices, on_device(): lax.all_to_all(outgoing, 'ent', split_axis=0, concat_axis=0, tiled=True)  6.45 us
    all_to_all x1, waiting for transfers between devices, on_device(): lax.all_to_all(outgoing, 'ent', split_axis=0, concat_axis=0, tiled=True)  4.93 us
    ppermute x2, waiting for transfers between devices, grp_reduce_scatter(): lax.ppermute(parts[half:], 'grp', [(i, i ^ bit) for i in range(grp_count)])  4.69 us
    ppermute x3, waiting for transfers between devices, shift_ent(): lax.ppermute(x, 'ent', [(i, (i + shift) % ent_count) for i in range(ent_c...  4.53 us
    ppermute x3, starting transfers between devices, grp_gather(): got = lax.ppermute(held, 'grp', [(i, i ^ bit) for i in range(grp_count)])  3.14 us
    ppermute x2, starting transfers between devices, grp_reduce_scatter(): lax.ppermute(parts[half:], 'grp', [(i, i ^ bit) for i in range(grp_count)])  3.12 us
  transfers between devices with their start and end apart: 10, of which 7 were waited for; matrix products, arithmetic and copies ran while one was open for 6% of the time, Pallas kernels for 8%

profile of v11, /device:TPU:0, one launch (start us, length us, event | category | flops | bytes accessed | tf_op | source)
XLA Modules:
  0.0 64.5 jit_solution(10087993470854919253)
XLA Ops:
  0.0 0.0 copy-start
  0.0 0.1 compare_select_fusion
  0.1 0.1 reshape.105
  0.2 1.4 %gather_fusion = s32[24]{0:T(128)S(1)} fusion(s32[24]{0:T(128)} %bitcast.29, s32[1024]{0:T(1024)S(1)} %pad_clamp_fusion), kind=kCustom, calls=%fused_computation | custom fusion | bytes 288 | tf_op jit(solution)/shard_map/gather | solution.py:126
  1.6 0.1 reshape.124
  2.4 0.1 convert_convert_fusion
  2.5 0.0 copy-done
  2.5 0.6 %gather_fusion.1 = s32[24,128,128]{2,1,0:T(8,128)S(1)} fusion(s32[24,128,128]{2,1,0:T(8,128)S(1)} %copy-done, s32[1024]{0:T(1024)S(1)} %pad_clamp_fusion), kind=kCustom, calls=%fused_computation.1 | custom fusion | bytes 3145824 | tf_op jit(solution)/shard_map/gather | solution.py:123
  3.1 0.0 copy-start.3
  3.1 0.2 convert_element_type.43
  3.3 0.7 %copy-done.3 = bf16[128,256]{1,0:T(8,128)(2,1)S(1)} copy-done((bf16[128,256]{1,0:T(8,128)(2,1)S(1)}, bf16[128,256]{1,0:T(8,128)(2,1)}, u32[]{:S(2)}) %copy-start.3) | copy-done | bytes 65560
  4.0 0.1 fusion.9
  4.1 1.1 %pad_maximum_fusion.refs_4_ = bf16[4,1040,128]{2,1,0:T(8,128)(2,1)} fusion(bf16[4,16,128]{2,1,0:T(8,128)(2,1)S(1)} %broadcast_in_dim.9, bf16[4,256,128]{2,1,0:T(8,128)(2,1)S(1)} %broadcast_in_dim.8, bf16[4,768,128]{2,1,0:T(8,128)(2,1)S(1)} %bitcast.30), kind=kLoop, calls=%fused_computation.2 | loop fusion | flops 3194880 | bytes 2129920 | tf_op jit(solution)/shard_map/concatenate | solution.py:132
  5.2 0.0 copy-start.5
  5.2 6.4 %all-to-all-start = ((bf16[4,1040,128]{2,1,0:T(8,128)(2,1)}), bf16[4,1040,128]{2,1,0:T(8,128)(2,1)S(1)}, u32[]{:S(2)}, u32[]{:S(2)}) async-start(bf16[4,1040,128]{2,1,0:T(8,128)(2,1)} %pad_maximum_fusion.refs_4_), calls=%async_computation | async-start | bytes 2129920 | tf_op jit(solution)/shard_map/all_to_all | solution.py:135
  11.6 0.0 collective-permute-start
  11.6 1.3 %collective-permute-done = bf16[1,128,256]{2,1,0:T(8,128)(2,1)S(1)} collective-permute-done((bf16[1,128,256]{2,1,0:T(8,128)(2,1)S(1)}, bf16[1,128,256]{2,1,0:T(8,128)(2,1)S(1)}, u32[]{:S(2)}, u32[]{:S(2)}) %collective-permute-start) | collective-permute-done | bytes 65568 | tf_op jit(solution)/shard_map/ppermute | solution.py:34
  12.9 1.6 %collective-permute-start.1 = (bf16[2,128,256]{2,1,0:T(8,128)(2,1)S(1)}, bf16[2,128,256]{2,1,0:T(8,128)(2,1)S(1)}, u32[]{:S(2)}, u32[]{:S(2)}) collective-permute-start(bf16[2,128,256]{2,1,0:T(8,128)(2,1)S(1)} %maximum_select_fusion.2), channel_id=1, source_target_pairs={{0,8},{4,12},{8,0},{12,4},{16,24},{20,28},{24,16},{28,20},{1,9},{5... | collective-permute-start | bytes 393224 | tf_op jit(solution)/shard_map/ppermute | solution.py:34
  14.5 0.6 %add_convert_fusion.1.refs_1_ = s32[4,6]{1,0:T(4,128)} fusion(f32[4,128]{1,0:T(4,128)S(1)} %get-tuple-element.17), kind=kLoop, calls=%fused_computation.29 | loop fusion | flops 72 | bytes 288 | tf_op jit(solution)/shard_map/convert_element_type | solution.py:140
  15.1 3.4 %collective-permute-done.1 = bf16[2,128,256]{2,1,0:T(8,128)(2,1)S(1)} collective-permute-done((bf16[2,128,256]{2,1,0:T(8,128)(2,1)S(1)}, bf16[2,128,256]{2,1,0:T(8,128)(2,1)S(1)}, u32[]{:S(2)}, u32[]{:S(2)}) %collective-permute-start.1) | collective-permute-done | bytes 131104 | tf_op jit(solution)/shard_map/ppermute | solution.py:34
  18.6 1.6 %collective-permute-start.2 = (bf16[4,128,256]{2,1,0:T(8,128)(2,1)S(1)}, bf16[4,128,256]{2,1,0:T(8,128)(2,1)S(1)}, u32[]{:S(2)}, u32[]{:S(2)}) collective-permute-start(bf16[4,128,256]{2,1,0:T(8,128)(2,1)S(1)} %maximum_select_fusion.1), channel_id=1, source_target_pairs={{0,16},{4,20},{8,24},{12,28},{16,0},{20,4},{24,8},{28,12},{1,17},{... | collective-permute-start | bytes 786440 | tf_op jit(solution)/shard_map/ppermute | solution.py:34
  20.1 0.6 and_select_fusion.refs_0_
  20.8 0.0 copy-done.5
  20.8 0.6 shift-left_or_fusion.refs_3_
  21.3 4.8 %collective-permute-done.2 = bf16[4,128,256]{2,1,0:T(8,128)(2,1)S(1)} collective-permute-done((bf16[4,128,256]{2,1,0:T(8,128)(2,1)S(1)}, bf16[4,128,256]{2,1,0:T(8,128)(2,1)S(1)}, u32[]{:S(2)}, u32[]{:S(2)}) %collective-permute-start.2) | collective-permute-done | bytes 262176 | tf_op jit(solution)/shard_map/ppermute | solution.py:34
  26.2 0.9 %maximum_select_fusion.refs_6_ = bf16[8,128,256]{2,1,0:T(8,128)(2,1)} fusion(bf16[4,128,256]{2,1,0:T(8,128)(2,1)S(1)} %collective-permute-done.2, bf16[4,128,256]{2,1,0:T(8,128)(2,1)S(1)} %maximum_select_fusion.1, pred[]{:T(512)S(6)} %eq.17), kind=kLoop, calls=%fused_computation.3 | loop fusion | flops 786432 | bytes 1048577 | tf_op jit(solution)/shard_map/jit(_where)/select_n | solution.py:36
  27.0 0.8 %broadcast_in_dim.11.refs_7_.refs_8_ = f32[4,128,256]{2,1,0:T(8,128)} broadcast(f32[]{:T(128)} %constant.94.clone.1), dimensions={} | broadcast | bytes 524292 | tf_op jit(solution)/shard_map/broadcast_in_dim | solution.py:175
  27.9 4.9 %shard_map.64 = (f32[1,128,256]{2,1,0:T(8,128)}, f32[4,128,256]{2,1,0:T(8,128)}, f32[4,128,256]{2,1,0:T(8,128)}) custom-call(s32[1]{0:T(128)} %bitcast.refs_0_, s32[4,6]{1,0:T(4,128)} %add_convert_fusion.1.refs_1_, s32[4,6]{1,0:T(4,128)} %bitcast.33, s32[4,6]{1,0:T(4,128)} %shift-left_or_fusion.refs_3_, bf16[4,1040,128]{2,1,0:T(8,128)(2,1)} %pad_maximum_fusion.refs_4_, ...), custom_call_target="tpu_custom_call" | custom-call | tf_op jit(solution)/shard_map/pallas_call | solution.py:150
  32.8 4.9 %all-to-all-done.refs_4_ = bf16[4,1040,128]{2,1,0:T(8,128)(2,1)S(1)} async-done(((bf16[4,1040,128]{2,1,0:T(8,128)(2,1)}), bf16[4,1040,128]{2,1,0:T(8,128)(2,1)S(1)}, u32[]{:S(2)}, u32[]{:S(2)}) %all-to-all-start) | async-done | bytes 1064992 | tf_op jit(solution)/shard_map/all_to_all | solution.py:135
  37.7 0.0 copy-start.1
  37.7 0.8 %add_convert_fusion.refs_1_ = s32[4,6]{1,0:T(4,128)} fusion(f32[4,128]{1,0:T(4,128)S(1)} %bitcast.35), kind=kLoop, calls=%fused_computation.27 | loop fusion | flops 72 | bytes 288 | tf_op jit(solution)/shard_map/convert_element_type | solution.py:140
  38.5 0.2 copy-done.1
  38.7 7.2 %shard_map.65 = (f32[3,128,256]{2,1,0:T(8,128)}, f32[4,128,256]{2,1,0:T(8,128)}, f32[4,128,256]{2,1,0:T(8,128)}) custom-call(s32[3]{0:T(128)} %and_select_fusion.refs_0_, s32[4,6]{1,0:T(4,128)} %add_convert_fusion.refs_1_, s32[4,6]{1,0:T(4,128)} %bitcast.34, s32[4,6]{1,0:T(4,128)} %shift-left_or_fusion.refs_3_, bf16[4,1040,128]{2,1,0:T(8,128)(2,1)} %copy-done.1, ...), custom_call_target="tpu_custom_call" | custom-call | tf_op jit(solution)/shard_map/pallas_call | solution.py:150
  45.9 0.0 copy-start.2
  45.9 0.1 collective-permute-start.6
  46.0 2.1 %collective-permute-done.6 = f32[4,128,256]{2,1,0:T(8,128)S(1)} collective-permute-done((f32[4,128,256]{2,1,0:T(8,128)}, f32[4,128,256]{2,1,0:T(8,128)S(1)}, u32[]{:S(2)}, u32[]{:S(2)}) %collective-permute-start.6) | collective-permute-done | bytes 524320 | tf_op jit(solution)/shard_map/ppermute | solution.py:19
  48.1 1.1 %add.117 = f32[4,128,256]{2,1,0:T(8,128)S(1)} add(f32[4,128,256]{2,1,0:T(8,128)} %get-tuple-element.15, f32[4,128,256]{2,1,0:T(8,128)S(1)} %collective-permute-done.6) | non-fusion elementwise | flops 131072 | bytes 1572864 | tf_op jit(solution)/shard_map/add | solution.py:19
  49.2 0.0 copy-start.4
  49.2 1.5 %collective-permute-start.7 = (f32[2,128,256]{2,1,0:T(8,128)S(1)}, f32[2,128,256]{2,1,0:T(8,128)S(1)}, u32[]{:S(2)}, u32[]{:S(2)}) collective-permute-start(f32[2,128,256]{2,1,0:T(8,128)S(1)} %slice.63), channel_id=1, source_target_pairs={{0,8},{4,12},{8,0},{12,4},{16,24},{20,28},{24,16},{28,20},{1,9},{5... | collective-permute-start | bytes 786440 | tf_op jit(solution)/shard_map/ppermute | solution.py:23
  50.8 0.0 copy-done.2
  50.8 1.5 %collective-permute-start.3 = (f32[128,256]{1,0:T(8,128)S(1)}, f32[128,256]{1,0:T(8,128)S(1)}, u32[]{:S(2)}, u32[]{:S(2)}) collective-permute-start(f32[128,256]{1,0:T(8,128)S(1)} %get-tuple-element.19), channel_id=1, source_target_pairs={{0,3},{1,0},{2,1},{3,2},{4,7},{5,4},{6,5},{7,6},{8,11},{9,8},{10,9... | collective-permute-start | bytes 393224 | tf_op jit(solution)/shard_map/ppermute | solution.py:44
  52.3 0.0 collective-permute-start.4
  52.3 0.6 collective-permute-start.5
  53.0 4.7 %collective-permute-done.7 = f32[2,128,256]{2,1,0:T(8,128)S(1)} collective-permute-done((f32[2,128,256]{2,1,0:T(8,128)S(1)}, f32[2,128,256]{2,1,0:T(8,128)S(1)}, u32[]{:S(2)}, u32[]{:S(2)}) %collective-permute-start.7) | collective-permute-done | bytes 262176 | tf_op jit(solution)/shard_map/ppermute | solution.py:23
  57.7 1.6 %collective-permute-start.8 = (f32[1,128,256]{2,1,0:T(8,128)S(1)}, f32[1,128,256]{2,1,0:T(8,128)S(1)}, u32[]{:S(2)}, u32[]{:S(2)}) collective-permute-start(f32[1,128,256]{2,1,0:T(8,128)S(1)} %slice.65), channel_id=1, source_target_pairs={{0,16},{4,20},{8,24},{12,28},{16,0},{20,4},{24,8},{28,12},{1,17},{... | collective-permute-start | bytes 393224 | tf_op jit(solution)/shard_map/ppermute | solution.py:23
  59.3 0.0 collective-permute-done.3
  59.3 4.5 %collective-permute-done.4 = f32[128,256]{1,0:T(8,128)S(1)} collective-permute-done((f32[128,256]{1,0:T(8,128)S(1)}, f32[128,256]{1,0:T(8,128)S(1)}, u32[]{:S(2)}, u32[]{:S(2)}) %collective-permute-start.4) | collective-permute-done | bytes 131104 | tf_op jit(solution)/shard_map/ppermute | solution.py:44
  63.8 0.0 collective-permute-done.5
  63.8 0.0 collective-permute-done.8
  63.8 0.0 copy-done.4
  63.8 0.7 %fusion.1 = f32[128,256]{1,0:T(8,128)} fusion(f32[1,128,256]{2,1,0:T(8,128)S(1)} %collective-permute-done.8, f32[2,128,256]{2,1,0:T(8,128)S(1)} %slice_add_fusion, f32[128,256]{1,0:T(8,128)S(1)} %collective-permute-done.5, f32[128,256]{1,0:T(8,128)S(1)} %collective-permute-done.4, f32[128,256]{1,0:T(8,128)S(1)} %collective-permute-done.3, ...), kind=kLoop, calls=%fused_computation.8 | loop fusion | flops 163840 | bytes 917504 | tf_op jit(solution)/shard_map/add | solution.py:186
  (15 shorter events, 0.2 us)
Async XLA Ops:
  0.0 2.5 %copy-start = (s32[24,128,128]{2,1,0:T(8,128)S(1)}, s32[24,128,128]{2,1,0:T(8,128)}, u32[]{:S(2)}) copy-start(s32[24,128,128]{2,1,0:T(8,128)} %param.8) | copy-start | bytes 4718596
  3.1 0.8 %copy-start.3 = (bf16[128,256]{1,0:T(8,128)(2,1)S(1)}, bf16[128,256]{1,0:T(8,128)(2,1)}, u32[]{:S(2)}) copy-start(bf16[128,256]{1,0:T(8,128)(2,1)} %param.6) | copy-start | bytes 196612
  5.2 15.6 %copy-start.5 = (s32[1,4,6]{2,1,0:T(4,128)S(1)}, s32[1,4,6]{2,1,0:T(4,128)}, u32[]{:S(2)}) copy-start(s32[1,4,6]{2,1,0:T(4,128)} %param.11) | copy-start | bytes 292
  5.2 32.5 %all-to-all-start = ((bf16[4,1040,128]{2,1,0:T(8,128)(2,1)}), bf16[4,1040,128]{2,1,0:T(8,128)(2,1)S(1)}, u32[]{:S(2)}, u32[]{:S(2)}) async-start(bf16[4,1040,128]{2,1,0:T(8,128)(2,1)} %pad_maximum_fusion.refs_4_), calls=%async_computation | async-start | bytes 2129920 | tf_op jit(solution)/shard_map/all_to_all | solution.py:135
  11.6 1.3 %collective-permute-start = (bf16[1,128,256]{2,1,0:T(8,128)(2,1)S(1)}, bf16[1,128,256]{2,1,0:T(8,128)(2,1)S(1)}, u32[]{:S(2)}, u32[]{:S(2)}) collective-permute-start(bf16[1,128,256]{2,1,0:T(8,128)(2,1)S(1)} %bitcast.31), channel_id=1, source_target_pairs={{0,4},{4,0},{8,12},{12,8},{16,20},{20,16},{24,28},{28,24},{1,5},{5... | collective-permute-start | bytes 196616 | tf_op jit(solution)/shard_map/ppermute | solution.py:34
  12.9 5.6 %collective-permute-start.1 = (bf16[2,128,256]{2,1,0:T(8,128)(2,1)S(1)}, bf16[2,128,256]{2,1,0:T(8,128)(2,1)S(1)}, u32[]{:S(2)}, u32[]{:S(2)}) collective-permute-start(bf16[2,128,256]{2,1,0:T(8,128)(2,1)S(1)} %maximum_select_fusion.2), channel_id=1, source_target_pairs={{0,8},{4,12},{8,0},{12,4},{16,24},{20,28},{24,16},{28,20},{1,9},{5... | collective-permute-start | bytes 393224 | tf_op jit(solution)/shard_map/ppermute | solution.py:34
  18.6 7.6 %collective-permute-start.2 = (bf16[4,128,256]{2,1,0:T(8,128)(2,1)S(1)}, bf16[4,128,256]{2,1,0:T(8,128)(2,1)S(1)}, u32[]{:S(2)}, u32[]{:S(2)}) collective-permute-start(bf16[4,128,256]{2,1,0:T(8,128)(2,1)S(1)} %maximum_select_fusion.1), channel_id=1, source_target_pairs={{0,16},{4,20},{8,24},{12,28},{16,0},{20,4},{24,8},{28,12},{1,17},{... | collective-permute-start | bytes 786440 | tf_op jit(solution)/shard_map/ppermute | solution.py:34
  37.7 1.0 %copy-start.1 = (bf16[4,1040,128]{2,1,0:T(8,128)(2,1)}, bf16[4,1040,128]{2,1,0:T(8,128)(2,1)S(1)}, u32[]{:S(2)}) copy-start(bf16[4,1040,128]{2,1,0:T(8,128)(2,1)S(1)} %all-to-all-done.refs_4_) | copy-start | bytes 3194884
  45.9 4.9 %copy-start.2 = (f32[3,128,256]{2,1,0:T(8,128)S(1)}, f32[3,128,256]{2,1,0:T(8,128)}, u32[]{:S(2)}) copy-start(f32[3,128,256]{2,1,0:T(8,128)} %get-tuple-element.14) | copy-start | bytes 1179652
  45.9 2.2 %collective-permute-start.6 = (f32[4,128,256]{2,1,0:T(8,128)}, f32[4,128,256]{2,1,0:T(8,128)S(1)}, u32[]{:S(2)}, u32[]{:S(2)}) collective-permute-start(f32[4,128,256]{2,1,0:T(8,128)} %get-tuple-element.16), channel_id=1, source_target_pairs={{0,4},{4,0},{8,12},{12,8},{16,20},{20,16},{24,28},{28,24},{1,5},{5... | collective-permute-start | bytes 1572872 | tf_op jit(solution)/shard_map/ppermute | solution.py:19
  49.2 14.6 %copy-start.4 = (f32[1,128,256]{2,1,0:T(8,128)S(1)}, f32[1,128,256]{2,1,0:T(8,128)}, u32[]{:S(2)}) copy-start(f32[1,128,256]{2,1,0:T(8,128)} %get-tuple-element.11) | copy-start | bytes 393220
  49.2 8.4 %collective-permute-start.7 = (f32[2,128,256]{2,1,0:T(8,128)S(1)}, f32[2,128,256]{2,1,0:T(8,128)S(1)}, u32[]{:S(2)}, u32[]{:S(2)}) collective-permute-start(f32[2,128,256]{2,1,0:T(8,128)S(1)} %slice.63), channel_id=1, source_target_pairs={{0,8},{4,12},{8,0},{12,4},{16,24},{20,28},{24,16},{28,20},{1,9},{5... | collective-permute-start | bytes 786440 | tf_op jit(solution)/shard_map/ppermute | solution.py:23
  50.8 8.5 %collective-permute-start.3 = (f32[128,256]{1,0:T(8,128)S(1)}, f32[128,256]{1,0:T(8,128)S(1)}, u32[]{:S(2)}, u32[]{:S(2)}) collective-permute-start(f32[128,256]{1,0:T(8,128)S(1)} %get-tuple-element.19), channel_id=1, source_target_pairs={{0,3},{1,0},{2,1},{3,2},{4,7},{5,4},{6,5},{7,6},{8,11},{9,8},{10,9... | collective-permute-start | bytes 393224 | tf_op jit(solution)/shard_map/ppermute | solution.py:44
  52.3 11.5 %collective-permute-start.4 = (f32[128,256]{1,0:T(8,128)S(1)}, f32[128,256]{1,0:T(8,128)S(1)}, u32[]{:S(2)}, u32[]{:S(2)}) collective-permute-start(f32[128,256]{1,0:T(8,128)S(1)} %get-tuple-element.21), channel_id=1, source_target_pairs={{0,2},{1,3},{2,0},{3,1},{4,6},{5,7},{6,4},{7,5},{8,10},{9,11},{10,... | collective-permute-start | bytes 393224 | tf_op jit(solution)/shard_map/ppermute | solution.py:44
  52.3 11.5 %collective-permute-start.5 = (f32[128,256]{1,0:T(8,128)S(1)}, f32[128,256]{1,0:T(8,128)S(1)}, u32[]{:S(2)}, u32[]{:S(2)}) collective-permute-start(f32[128,256]{1,0:T(8,128)S(1)} %get-tuple-element.20), channel_id=1, source_target_pairs={{0,1},{1,2},{2,3},{3,0},{4,5},{5,6},{6,7},{7,4},{8,9},{9,10},{10,1... | collective-permute-start | bytes 393224 | tf_op jit(solution)/shard_map/ppermute | solution.py:44
  57.7 6.1 %collective-permute-start.8 = (f32[1,128,256]{2,1,0:T(8,128)S(1)}, f32[1,128,256]{2,1,0:T(8,128)S(1)}, u32[]{:S(2)}, u32[]{:S(2)}) collective-permute-start(f32[1,128,256]{2,1,0:T(8,128)S(1)} %slice.65), channel_id=1, source_target_pairs={{0,16},{4,20},{8,24},{12,28},{16,0},{20,4},{24,8},{28,12},{1,17},{... | collective-permute-start | bytes 393224 | tf_op jit(solution)/shard_map/ppermute | solution.py:23

commit v12 on v11

--- a/solution.py
+++ b/solution.py
@@ -123,7 +123,15 @@
     adj_out = adjacency[tile_of].astype(jnp.bfloat16).reshape(ent_count, per_relay * block, block)
     halves = jnp.concatenate([factor[:, :block], factor[:, block:]], axis=0)
     head = jnp.concatenate(
-        [tile_rels.reshape(tiles)[tile_of].astype(jnp.float32),
+        [
+            jnp.sum(
+                jnp.where(
+                    jnp.arange(tiles, dtype=jnp.int32) == tile_of[:, :, None],
+                    tile_rels.reshape(1, 1, tiles),
+                    0,
+                ),
+                axis=2,
+            ).astype(jnp.float32),
          (tile_of < tile_count.reshape(())).astype(jnp.float32)],
         axis=1,
     )

time: 64.9 us -> 64.6 us (level)
  local copies, waits for them, and re-layouts: 4.14 us -> 2.79 us
  other arithmetic: 6.86 us -> 7.88 us
    gather x1 -> x0, local copies, waits for them, and re-layouts: 1.45 us -> none  [on_device(): tile_rels.reshape(tiles)[tile_of].astype(jnp.float32)]
    reduce_sum x0 -> x1, other arithmetic: none -> 1.03 us  [on_device(): jnp.sum(jnp.where(jnp.arange(tiles, dtype=jnp.int32) == tile_of[:, :, Non...]
where the time goes in v12:
time: 64.6 us; the launch traced here: 64.3 us
  waiting for transfers between devices  25.8 us (40%)
  starting transfers between devices  15 us (23%)
  Pallas kernels  12 us (19%)
  other arithmetic  7.88 us (12%)
  local copies, waits for them, and re-layouts  2.79 us (4%)
  between operations  0.78 us (1%)
    pallas_call x2, Pallas kernels, relay_tiles(): pl.pallas_call(lambda *refs: tile_kernel(*refs, per_relay=per_relay, bloc...  12 us
    ppermute x3, waiting for transfers between devices, grp_gather(): got = lax.ppermute(held, 'grp', [(i, i ^ bit) for i in range(grp_count)])  9.57 us
    all_to_all x1, starting transfers between devices, on_device(): lax.all_to_all(outgoing, 'ent', split_axis=0, concat_axis=0, tiled=True)  6.45 us
    all_to_all x1, waiting for transfers between devices, on_device(): lax.all_to_all(outgoing, 'ent', split_axis=0, concat_axis=0, tiled=True)  4.92 us
    ppermute x2, waiting for transfers between devices, grp_reduce_scatter(): lax.ppermute(parts[half:], 'grp', [(i, i ^ bit) for i in range(grp_count)])  4.66 us
    ppermute x3, waiting for transfers between devices, shift_ent(): lax.ppermute(x, 'ent', [(i, (i + shift) % ent_count) for i in range(ent_c...  4.55 us
    ppermute x2, starting transfers between devices, grp_reduce_scatter(): lax.ppermute(parts[half:], 'grp', [(i, i ^ bit) for i in range(grp_count)])  3.14 us
    ppermute x3, starting transfers between devices, grp_gather(): got = lax.ppermute(held, 'grp', [(i, i ^ bit) for i in range(grp_count)])  3.14 us
  transfers between devices with their start and end apart: 10, of which 7 were waited for; matrix products, arithmetic and copies ran while one was open for 6% of the time, Pallas kernels for 8%

profile of v12, /device:TPU:0, one launch (start us, length us, event | category | flops | bytes accessed | tf_op | source)
XLA Modules:
  0.0 64.3 jit_solution(8766984562883300382)
XLA Ops:
  0.0 0.0 copy-start
  0.0 0.1 broadcast_add_fusion
  0.1 0.1 compare_select_fusion
  0.2 0.1 copy.7
  0.3 1.0 %select_reduce_fusion = s32[4,6]{0,1:T(8,128)S(1)} fusion(s32[24]{0:T(128)} %bitcast.35, s32[4,6]{0,1:T(8,128)S(1)} %copy.7), kind=kLoop, calls=%fused_computation.16 | loop fusion | flops 1704 | bytes 288 | tf_op jit(solution)/shard_map/reduce_sum | solution.py:127
  1.3 0.1 copy.8
  2.0 0.1 convert_convert_fusion
  2.1 0.1 reshape.129
  2.2 0.0 copy-done
  2.2 0.7 %gather_fusion = s32[24,128,128]{2,1,0:T(8,128)S(1)} fusion(s32[24,128,128]{2,1,0:T(8,128)S(1)} %copy-done, s32[1024]{0:T(1024)S(1)} %pad_clamp_fusion), kind=kCustom, calls=%fused_computation | custom fusion | bytes 3145824 | tf_op jit(solution)/shard_map/gather | solution.py:123
  2.9 0.0 copy-start.3
  2.9 0.2 convert_element_type.42
  3.1 0.7 %copy-done.3 = bf16[128,256]{1,0:T(8,128)(2,1)S(1)} copy-done((bf16[128,256]{1,0:T(8,128)(2,1)S(1)}, bf16[128,256]{1,0:T(8,128)(2,1)}, u32[]{:S(2)}) %copy-start.3) | copy-done | bytes 65560
  3.7 0.1 fusion.9
  3.9 1.1 %pad_maximum_fusion.refs_4_ = bf16[4,1040,128]{2,1,0:T(8,128)(2,1)} fusion(bf16[4,16,128]{2,1,0:T(8,128)(2,1)S(1)} %broadcast_in_dim.41, bf16[4,256,128]{2,1,0:T(8,128)(2,1)S(1)} %broadcast_in_dim.40, bf16[4,768,128]{2,1,0:T(8,128)(2,1)S(1)} %bitcast.29), kind=kLoop, calls=%fused_computation.1 | loop fusion | flops 3194880 | bytes 2129920 | tf_op jit(solution)/shard_map/concatenate | solution.py:140
  4.9 0.0 copy-start.5
  4.9 6.4 %all-to-all-start = ((bf16[4,1040,128]{2,1,0:T(8,128)(2,1)}), bf16[4,1040,128]{2,1,0:T(8,128)(2,1)S(1)}, u32[]{:S(2)}, u32[]{:S(2)}) async-start(bf16[4,1040,128]{2,1,0:T(8,128)(2,1)} %pad_maximum_fusion.refs_4_), calls=%async_computation | async-start | bytes 2129920 | tf_op jit(solution)/shard_map/all_to_all | solution.py:143
  11.4 0.0 collective-permute-start
  11.4 1.3 %collective-permute-done = bf16[1,128,256]{2,1,0:T(8,128)(2,1)S(1)} collective-permute-done((bf16[1,128,256]{2,1,0:T(8,128)(2,1)S(1)}, bf16[1,128,256]{2,1,0:T(8,128)(2,1)S(1)}, u32[]{:S(2)}, u32[]{:S(2)}) %collective-permute-start) | collective-permute-done | bytes 65568 | tf_op jit(solution)/shard_map/ppermute | solution.py:34
  12.7 1.6 %collective-permute-start.1 = (bf16[2,128,256]{2,1,0:T(8,128)(2,1)S(1)}, bf16[2,128,256]{2,1,0:T(8,128)(2,1)S(1)}, u32[]{:S(2)}, u32[]{:S(2)}) collective-permute-start(bf16[2,128,256]{2,1,0:T(8,128)(2,1)S(1)} %maximum_select_fusion.2), channel_id=1, source_target_pairs={{0,8},{4,12},{8,0},{12,4},{16,24},{20,28},{24,16},{28,20},{1,9},{5... | collective-permute-start | bytes 393224 | tf_op jit(solution)/shard_map/ppermute | solution.py:34
  14.2 0.7 %add_convert_fusion.1.refs_1_ = s32[4,6]{1,0:T(4,128)} fusion(f32[4,128]{1,0:T(4,128)S(1)} %get-tuple-element.17), kind=kLoop, calls=%fused_computation.30 | loop fusion | flops 72 | bytes 288 | tf_op jit(solution)/shard_map/convert_element_type | solution.py:148
  14.9 3.4 %collective-permute-done.1 = bf16[2,128,256]{2,1,0:T(8,128)(2,1)S(1)} collective-permute-done((bf16[2,128,256]{2,1,0:T(8,128)(2,1)S(1)}, bf16[2,128,256]{2,1,0:T(8,128)(2,1)S(1)}, u32[]{:S(2)}, u32[]{:S(2)}) %collective-permute-start.1) | collective-permute-done | bytes 131104 | tf_op jit(solution)/shard_map/ppermute | solution.py:34
  18.3 1.6 %collective-permute-start.2 = (bf16[4,128,256]{2,1,0:T(8,128)(2,1)S(1)}, bf16[4,128,256]{2,1,0:T(8,128)(2,1)S(1)}, u32[]{:S(2)}, u32[]{:S(2)}) collective-permute-start(bf16[4,128,256]{2,1,0:T(8,128)(2,1)S(1)} %maximum_select_fusion.1), channel_id=1, source_target_pairs={{0,16},{4,20},{8,24},{12,28},{16,0},{20,4},{24,8},{28,12},{1,17},{... | collective-permute-start | bytes 786440 | tf_op jit(solution)/shard_map/ppermute | solution.py:34
  19.9 0.5 and_select_fusion.refs_0_
  20.4 0.0 copy-done.5
  20.4 0.6 shift-left_or_fusion.refs_3_
  21.0 4.9 %collective-permute-done.2 = bf16[4,128,256]{2,1,0:T(8,128)(2,1)S(1)} collective-permute-done((bf16[4,128,256]{2,1,0:T(8,128)(2,1)S(1)}, bf16[4,128,256]{2,1,0:T(8,128)(2,1)S(1)}, u32[]{:S(2)}, u32[]{:S(2)}) %collective-permute-start.2) | collective-permute-done | bytes 262176 | tf_op jit(solution)/shard_map/ppermute | solution.py:34
  25.9 0.9 %maximum_select_fusion.refs_6_ = bf16[8,128,256]{2,1,0:T(8,128)(2,1)} fusion(bf16[4,128,256]{2,1,0:T(8,128)(2,1)S(1)} %collective-permute-done.2, bf16[4,128,256]{2,1,0:T(8,128)(2,1)S(1)} %maximum_select_fusion.1, pred[]{:T(512)S(6)} %eq.33), kind=kLoop, calls=%fused_computation.2 | loop fusion | flops 786432 | bytes 1048577 | tf_op jit(solution)/shard_map/jit(_where)/select_n | solution.py:36
  26.8 0.8 %broadcast_in_dim.43.refs_7_.refs_8_ = f32[4,128,256]{2,1,0:T(8,128)} broadcast(f32[]{:T(128)} %constant.94.clone.1), dimensions={} | broadcast | bytes 524292 | tf_op jit(solution)/shard_map/broadcast_in_dim | solution.py:183
  27.6 4.9 %shard_map.64 = (f32[1,128,256]{2,1,0:T(8,128)}, f32[4,128,256]{2,1,0:T(8,128)}, f32[4,128,256]{2,1,0:T(8,128)}) custom-call(s32[1]{0:T(128)} %bitcast.refs_0_, s32[4,6]{1,0:T(4,128)} %add_convert_fusion.1.refs_1_, s32[4,6]{1,0:T(4,128)} %bitcast.32, s32[4,6]{1,0:T(4,128)} %shift-left_or_fusion.refs_3_, bf16[4,1040,128]{2,1,0:T(8,128)(2,1)} %pad_maximum_fusion.refs_4_, ...), custom_call_target="tpu_custom_call" | custom-call | tf_op jit(solution)/shard_map/pallas_call | solution.py:158
  32.5 4.9 %all-to-all-done.refs_4_ = bf16[4,1040,128]{2,1,0:T(8,128)(2,1)S(1)} async-done(((bf16[4,1040,128]{2,1,0:T(8,128)(2,1)}), bf16[4,1040,128]{2,1,0:T(8,128)(2,1)S(1)}, u32[]{:S(2)}, u32[]{:S(2)}) %all-to-all-start) | async-done | bytes 1064992 | tf_op jit(solution)/shard_map/all_to_all | solution.py:143
  37.5 0.0 copy-start.1
  37.5 0.7 %add_convert_fusion.refs_1_ = s32[4,6]{1,0:T(4,128)} fusion(f32[4,128]{1,0:T(4,128)S(1)} %bitcast.34), kind=kLoop, calls=%fused_computation.28 | loop fusion | flops 72 | bytes 288 | tf_op jit(solution)/shard_map/convert_element_type | solution.py:148
  38.2 0.2 copy-done.1
  38.5 7.1 %shard_map.65 = (f32[3,128,256]{2,1,0:T(8,128)}, f32[4,128,256]{2,1,0:T(8,128)}, f32[4,128,256]{2,1,0:T(8,128)}) custom-call(s32[3]{0:T(128)} %and_select_fusion.refs_0_, s32[4,6]{1,0:T(4,128)} %add_convert_fusion.refs_1_, s32[4,6]{1,0:T(4,128)} %bitcast.33, s32[4,6]{1,0:T(4,128)} %shift-left_or_fusion.refs_3_, bf16[4,1040,128]{2,1,0:T(8,128)(2,1)} %copy-done.1, ...), custom_call_target="tpu_custom_call" | custom-call | tf_op jit(solution)/shard_map/pallas_call | solution.py:158
  45.6 0.0 copy-start.2
  45.6 0.1 collective-permute-start.6
  45.7 2.1 %collective-permute-done.6 = f32[4,128,256]{2,1,0:T(8,128)S(1)} collective-permute-done((f32[4,128,256]{2,1,0:T(8,128)}, f32[4,128,256]{2,1,0:T(8,128)S(1)}, u32[]{:S(2)}, u32[]{:S(2)}) %collective-permute-start.6) | collective-permute-done | bytes 524320 | tf_op jit(solution)/shard_map/ppermute | solution.py:19
  47.8 1.1 %add.119 = f32[4,128,256]{2,1,0:T(8,128)S(1)} add(f32[4,128,256]{2,1,0:T(8,128)} %get-tuple-element.15, f32[4,128,256]{2,1,0:T(8,128)S(1)} %collective-permute-done.6) | non-fusion elementwise | flops 131072 | bytes 1572864 | tf_op jit(solution)/shard_map/add | solution.py:19
  48.9 0.0 copy-start.4
  48.9 1.6 %collective-permute-start.7 = (f32[2,128,256]{2,1,0:T(8,128)S(1)}, f32[2,128,256]{2,1,0:T(8,128)S(1)}, u32[]{:S(2)}, u32[]{:S(2)}) collective-permute-start(f32[2,128,256]{2,1,0:T(8,128)S(1)} %slice.61), channel_id=1, source_target_pairs={{0,8},{4,12},{8,0},{12,4},{16,24},{20,28},{24,16},{28,20},{1,9},{5... | collective-permute-start | bytes 786440 | tf_op jit(solution)/shard_map/ppermute | solution.py:23
  50.5 0.0 copy-done.2
  50.5 1.5 %collective-permute-start.3 = (f32[128,256]{1,0:T(8,128)S(1)}, f32[128,256]{1,0:T(8,128)S(1)}, u32[]{:S(2)}, u32[]{:S(2)}) collective-permute-start(f32[128,256]{1,0:T(8,128)S(1)} %get-tuple-element.19), channel_id=1, source_target_pairs={{0,3},{1,0},{2,1},{3,2},{4,7},{5,4},{6,5},{7,6},{8,11},{9,8},{10,9... | collective-permute-start | bytes 393224 | tf_op jit(solution)/shard_map/ppermute | solution.py:44
  52.0 0.0 collective-permute-start.4
  52.0 0.6 collective-permute-start.5
  52.7 4.7 %collective-permute-done.7 = f32[2,128,256]{2,1,0:T(8,128)S(1)} collective-permute-done((f32[2,128,256]{2,1,0:T(8,128)S(1)}, f32[2,128,256]{2,1,0:T(8,128)S(1)}, u32[]{:S(2)}, u32[]{:S(2)}) %collective-permute-start.7) | collective-permute-done | bytes 262176 | tf_op jit(solution)/shard_map/ppermute | solution.py:23
  57.4 1.6 %collective-permute-start.8 = (f32[1,128,256]{2,1,0:T(8,128)S(1)}, f32[1,128,256]{2,1,0:T(8,128)S(1)}, u32[]{:S(2)}, u32[]{:S(2)}) collective-permute-start(f32[1,128,256]{2,1,0:T(8,128)S(1)} %slice.63), channel_id=1, source_target_pairs={{0,16},{4,20},{8,24},{12,28},{16,0},{20,4},{24,8},{28,12},{1,17},{... | collective-permute-start | bytes 393224 | tf_op jit(solution)/shard_map/ppermute | solution.py:23
  59.0 0.0 collective-permute-done.3
  59.0 4.5 %collective-permute-done.4 = f32[128,256]{1,0:T(8,128)S(1)} collective-permute-done((f32[128,256]{1,0:T(8,128)S(1)}, f32[128,256]{1,0:T(8,128)S(1)}, u32[]{:S(2)}, u32[]{:S(2)}) %collective-permute-start.4) | collective-permute-done | bytes 131104 | tf_op jit(solution)/shard_map/ppermute | solution.py:44
  63.5 0.0 collective-permute-done.5
  63.5 0.0 collective-permute-done.8
  63.5 0.0 copy-done.4
  63.6 0.7 %fusion.1 = f32[128,256]{1,0:T(8,128)} fusion(f32[1,128,256]{2,1,0:T(8,128)S(1)} %collective-permute-done.8, f32[2,128,256]{2,1,0:T(8,128)S(1)} %slice_add_fusion, f32[128,256]{1,0:T(8,128)S(1)} %collective-permute-done.5, f32[128,256]{1,0:T(8,128)S(1)} %collective-permute-done.4, f32[128,256]{1,0:T(8,128)S(1)} %collective-permute-done.3, ...), kind=kLoop, calls=%fused_computation.7 | loop fusion | flops 163840 | bytes 917504 | tf_op jit(solution)/shard_map/add | solution.py:194
  (15 shorter events, 0.2 us)
Async XLA Ops:
  0.0 2.2 %copy-start = (s32[24,128,128]{2,1,0:T(8,128)S(1)}, s32[24,128,128]{2,1,0:T(8,128)}, u32[]{:S(2)}) copy-start(s32[24,128,128]{2,1,0:T(8,128)} %param.8) | copy-start | bytes 4718596
  2.9 0.8 %copy-start.3 = (bf16[128,256]{1,0:T(8,128)(2,1)S(1)}, bf16[128,256]{1,0:T(8,128)(2,1)}, u32[]{:S(2)}) copy-start(bf16[128,256]{1,0:T(8,128)(2,1)} %param.6) | copy-start | bytes 196612
  4.9 15.5 %copy-start.5 = (s32[1,4,6]{2,1,0:T(4,128)S(1)}, s32[1,4,6]{2,1,0:T(4,128)}, u32[]{:S(2)}) copy-start(s32[1,4,6]{2,1,0:T(4,128)} %param.11) | copy-start | bytes 292
  4.9 32.5 %all-to-all-start = ((bf16[4,1040,128]{2,1,0:T(8,128)(2,1)}), bf16[4,1040,128]{2,1,0:T(8,128)(2,1)S(1)}, u32[]{:S(2)}, u32[]{:S(2)}) async-start(bf16[4,1040,128]{2,1,0:T(8,128)(2,1)} %pad_maximum_fusion.refs_4_), calls=%async_computation | async-start | bytes 2129920 | tf_op jit(solution)/shard_map/all_to_all | solution.py:143
  11.4 1.3 %collective-permute-start = (bf16[1,128,256]{2,1,0:T(8,128)(2,1)S(1)}, bf16[1,128,256]{2,1,0:T(8,128)(2,1)S(1)}, u32[]{:S(2)}, u32[]{:S(2)}) collective-permute-start(bf16[1,128,256]{2,1,0:T(8,128)(2,1)S(1)} %bitcast.30), channel_id=1, source_target_pairs={{0,4},{4,0},{8,12},{12,8},{16,20},{20,16},{24,28},{28,24},{1,5},{5... | collective-permute-start | bytes 196616 | tf_op jit(solution)/shard_map/ppermute | solution.py:34
  12.7 5.6 %collective-permute-start.1 = (bf16[2,128,256]{2,1,0:T(8,128)(2,1)S(1)}, bf16[2,128,256]{2,1,0:T(8,128)(2,1)S(1)}, u32[]{:S(2)}, u32[]{:S(2)}) collective-permute-start(bf16[2,128,256]{2,1,0:T(8,128)(2,1)S(1)} %maximum_select_fusion.2), channel_id=1, source_target_pairs={{0,8},{4,12},{8,0},{12,4},{16,24},{20,28},{24,16},{28,20},{1,9},{5... | collective-permute-start | bytes 393224 | tf_op jit(solution)/shard_map/ppermute | solution.py:34
  18.3 7.6 %collective-permute-start.2 = (bf16[4,128,256]{2,1,0:T(8,128)(2,1)S(1)}, bf16[4,128,256]{2,1,0:T(8,128)(2,1)S(1)}, u32[]{:S(2)}, u32[]{:S(2)}) collective-permute-start(bf16[4,128,256]{2,1,0:T(8,128)(2,1)S(1)} %maximum_select_fusion.1), channel_id=1, source_target_pairs={{0,16},{4,20},{8,24},{12,28},{16,0},{20,4},{24,8},{28,12},{1,17},{... | collective-permute-start | bytes 786440 | tf_op jit(solution)/shard_map/ppermute | solution.py:34
  37.5 1.0 %copy-start.1 = (bf16[4,1040,128]{2,1,0:T(8,128)(2,1)}, bf16[4,1040,128]{2,1,0:T(8,128)(2,1)S(1)}, u32[]{:S(2)}) copy-start(bf16[4,1040,128]{2,1,0:T(8,128)(2,1)S(1)} %all-to-all-done.refs_4_) | copy-start | bytes 3194884
  45.6 4.9 %copy-start.2 = (f32[3,128,256]{2,1,0:T(8,128)S(1)}, f32[3,128,256]{2,1,0:T(8,128)}, u32[]{:S(2)}) copy-start(f32[3,128,256]{2,1,0:T(8,128)} %get-tuple-element.14) | copy-start | bytes 1179652
  45.6 2.2 %collective-permute-start.6 = (f32[4,128,256]{2,1,0:T(8,128)}, f32[4,128,256]{2,1,0:T(8,128)S(1)}, u32[]{:S(2)}, u32[]{:S(2)}) collective-permute-start(f32[4,128,256]{2,1,0:T(8,128)} %get-tuple-element.16), channel_id=1, source_target_pairs={{0,4},{4,0},{8,12},{12,8},{16,20},{20,16},{24,28},{28,24},{1,5},{5... | collective-permute-start | bytes 1572872 | tf_op jit(solution)/shard_map/ppermute | solution.py:19
  48.9 14.7 %copy-start.4 = (f32[1,128,256]{2,1,0:T(8,128)S(1)}, f32[1,128,256]{2,1,0:T(8,128)}, u32[]{:S(2)}) copy-start(f32[1,128,256]{2,1,0:T(8,128)} %get-tuple-element.11) | copy-start | bytes 393220
  48.9 8.4 %collective-permute-start.7 = (f32[2,128,256]{2,1,0:T(8,128)S(1)}, f32[2,128,256]{2,1,0:T(8,128)S(1)}, u32[]{:S(2)}, u32[]{:S(2)}) collective-permute-start(f32[2,128,256]{2,1,0:T(8,128)S(1)} %slice.61), channel_id=1, source_target_pairs={{0,8},{4,12},{8,0},{12,4},{16,24},{20,28},{24,16},{28,20},{1,9},{5... | collective-permute-start | bytes 786440 | tf_op jit(solution)/shard_map/ppermute | solution.py:23
  50.5 8.5 %collective-permute-start.3 = (f32[128,256]{1,0:T(8,128)S(1)}, f32[128,256]{1,0:T(8,128)S(1)}, u32[]{:S(2)}, u32[]{:S(2)}) collective-permute-start(f32[128,256]{1,0:T(8,128)S(1)} %get-tuple-element.19), channel_id=1, source_target_pairs={{0,3},{1,0},{2,1},{3,2},{4,7},{5,4},{6,5},{7,6},{8,11},{9,8},{10,9... | collective-permute-start | bytes 393224 | tf_op jit(solution)/shard_map/ppermute | solution.py:44
  52.0 11.5 %collective-permute-start.4 = (f32[128,256]{1,0:T(8,128)S(1)}, f32[128,256]{1,0:T(8,128)S(1)}, u32[]{:S(2)}, u32[]{:S(2)}) collective-permute-start(f32[128,256]{1,0:T(8,128)S(1)} %get-tuple-element.21), channel_id=1, source_target_pairs={{0,2},{1,3},{2,0},{3,1},{4,6},{5,7},{6,4},{7,5},{8,10},{9,11},{10,... | collective-permute-start | bytes 393224 | tf_op jit(solution)/shard_map/ppermute | solution.py:44
  52.0 11.5 %collective-permute-start.5 = (f32[128,256]{1,0:T(8,128)S(1)}, f32[128,256]{1,0:T(8,128)S(1)}, u32[]{:S(2)}, u32[]{:S(2)}) collective-permute-start(f32[128,256]{1,0:T(8,128)S(1)} %get-tuple-element.20), channel_id=1, source_target_pairs={{0,1},{1,2},{2,3},{3,0},{4,5},{5,6},{6,7},{7,4},{8,9},{9,10},{10,1... | collective-permute-start | bytes 393224 | tf_op jit(solution)/shard_map/ppermute | solution.py:44
  57.4 6.1 %collective-permute-start.8 = (f32[1,128,256]{2,1,0:T(8,128)S(1)}, f32[1,128,256]{2,1,0:T(8,128)S(1)}, u32[]{:S(2)}, u32[]{:S(2)}) collective-permute-start(f32[1,128,256]{2,1,0:T(8,128)S(1)} %slice.63), channel_id=1, source_target_pairs={{0,16},{4,20},{8,24},{12,28},{16,0},{20,4},{24,8},{28,12},{1,17},{... | collective-permute-start | bytes 393224 | tf_op jit(solution)/shard_map/ppermute | solution.py:23

commit v13 on v11

--- a/solution.py
+++ b/solution.py
@@ -59,7 +59,7 @@
         [in_ref[0, base : base + block, :], in_ref[0, base + block : base + 2 * block, :]], axis=1
     )
     half = keep_ref.shape[0]
-    codes = [codes_ref[e, j] for j in range(per_relay)]
+    codes = [codes_ref[pl.program_id(0), j] for j in range(per_relay)]
     rels = [c // 2 for c in codes]
     groups = [groups_ref[e, j] for j in range(per_relay)]
     mapped = [
@@ -112,7 +112,6 @@
     block = factor.shape[0]
     width = factor.shape[1]
     per_relay = tiles // ent_count
-    head_rows = 16
     count = ent_count * per_relay
     grp_bits = grp_count.bit_length() - 1
     relations = cores.shape[0]
@@ -122,22 +121,26 @@
     tile_of = slot_ids[None, :] * ent_count + (relay_ids[:, None] - my_ent) % ent_count
     adj_out = adjacency[tile_of].astype(jnp.bfloat16).reshape(ent_count, per_relay * block, block)
     halves = jnp.concatenate([factor[:, :block], factor[:, block:]], axis=0)
-    head = jnp.concatenate(
-        [tile_rels.reshape(tiles)[tile_of].astype(jnp.float32),
-         (tile_of < tile_count.reshape(())).astype(jnp.float32)],
-        axis=1,
-    )
-    head = jnp.pad(head, ((0, 0), (0, block - 2 * per_relay)))
-    head = jnp.broadcast_to(head[:, None, :], (ent_count, head_rows, block)).astype(jnp.bfloat16)
     outgoing = jnp.concatenate(
-        [adj_out, jnp.broadcast_to(halves[None], (ent_count,) + halves.shape), head], axis=1
+        [adj_out, jnp.broadcast_to(halves[None], (ent_count,) + halves.shape)], axis=1
     )
     arrived = lax.all_to_all(outgoing, "ent", split_axis=0, concat_axis=0, tiled=True)
     group_blocks = grp_gather(factor, grp_count)
-
-    def codes_of(buf):
-        heads = buf[:, -head_rows].astype(jnp.float32)
-        return (heads[:, :per_relay] * 2 + heads[:, per_relay : 2 * per_relay]).astype(jnp.int32)
+    picked = jnp.sum(
+        jnp.where(
+            jnp.arange(tiles, dtype=jnp.int32) == tile_of[:, :, None],
+            tile_rels.reshape(1, 1, tiles),
+            0,
+        ),
+        axis=2,
+    )
+    codes_out = picked * 2 + (tile_of < tile_count.reshape(())).astype(jnp.int32)
+    codes_in = jnp.stack(
+        [
+            shift_ent(codes_out[(my_ent + k) % ent_count], k, ent_count)
+            for k in range(1, ent_count)
+        ]
+    )
 
     groups = send_lists.reshape(ent_count, per_relay)
     slots = bit_reverse(groups ^ lax.axis_index("grp"), grp_bits)
@@ -174,10 +177,10 @@
 
     empty = jnp.zeros((half, block, width), jnp.float32)
     own_row, keep, send = relay_tiles(
-        my_ent.reshape(1).astype(jnp.int32), codes_of(outgoing), outgoing, empty, empty
+        my_ent.reshape(1).astype(jnp.int32), codes_out[my_ent][None], outgoing, empty, empty
     )
     remote_srcs = (my_ent - jnp.arange(1, ent_count, dtype=jnp.int32)) % ent_count
-    row_parts, keep, send = relay_tiles(remote_srcs, codes_of(arrived), arrived, keep, send)
+    row_parts, keep, send = relay_tiles(remote_srcs, codes_in, arrived, keep, send)
 
     rows = own_row[0]
     for k in range(1, ent_count):

time: 64.9 us -> 71.3 us (1.099)
  starting transfers between devices: 14.9 us -> 20.3 us
  local copies, waits for them, and re-layouts: 4.14 us -> 5.24 us
    ppermute x3 -> x6, waiting for transfers between devices: 4.53 us -> 19.9 us  [shift_ent(): lax.ppermute(x, 'ent', [(i, (i + shift) % ent_count) for i in range(ent_c...]
    ppermute x3, waiting for transfers between devices: 9.5 us -> 0.09 us  [grp_gather(): got = lax.ppermute(held, 'grp', [(i, i ^ bit) for i in range(grp_count)])]
    ppermute x3 -> x6, starting transfers between devices: 2.14 us -> 7.5 us  [shift_ent(): lax.ppermute(x, 'ent', [(i, (i + shift) % ent_count) for i in range(ent_c...]
    all_to_all x1, waiting for transfers between devices: 4.93 us -> 0.01 us  [on_device(): lax.all_to_all(outgoing, 'ent', split_axis=0, concat_axis=0, tiled=True)]
    unnamed x12 -> x14, local copies, waits for them, and re-layouts: 0.93 us -> 2.9 us
    convert_element_type x4 -> x0, other arithmetic: 1.48 us -> none  [the longest x2 1.41 us: codes_of(): (heads[:, :per_relay] * 2 + heads[:, per_relay:2 * per_relay]).astype(jnp...]
    gather x1 -> x0, local copies, waits for them, and re-layouts: 1.45 us -> none  [on_device(): tile_rels.reshape(tiles)[tile_of].astype(jnp.float32)]
  transfers between devices with their start and end apart: 10 -> 13, of which waited for: 7 -> 5; matrix products, arithmetic and copies ran while one was open for 6% -> 7% of each run, Pallas kernels for 8% -> 7%
where the time goes in v13:
time: 71.3 us; the launch traced here: 70.9 us
  waiting for transfers between devices  26.4 us (37%)
  starting transfers between devices  20.3 us (28%)
  Pallas kernels  12 us (17%)
  other arithmetic  6.24 us (9%)
  local copies, waits for them, and re-layouts  5.24 us (7%)
  between operations  0.78 us (1%)
    ppermute x6, waiting for transfers between devices, shift_ent(): lax.ppermute(x, 'ent', [(i, (i + shift) % ent_count) for i in range(ent_c...  19.9 us
    pallas_call x2, Pallas kernels, relay_tiles(): pl.pallas_call(lambda *refs: tile_kernel(*refs, per_relay=per_relay, bloc...  12 us
    ppermute x6, starting transfers between devices, shift_ent(): lax.ppermute(x, 'ent', [(i, (i + shift) % ent_count) for i in range(ent_c...  7.5 us
    all_to_all x1, starting transfers between devices, on_device(): lax.all_to_all(outgoing, 'ent', split_axis=0, concat_axis=0, tiled=True)  6.45 us
    ppermute x2, waiting for transfers between devices, grp_reduce_scatter(): lax.ppermute(parts[half:], 'grp', [(i, i ^ bit) for i in range(grp_count)])  4.27 us
    ppermute x3, starting transfers between devices, grp_gather(): got = lax.ppermute(held, 'grp', [(i, i ^ bit) for i in range(grp_count)])  3.14 us
    ppermute x2, starting transfers between devices, grp_reduce_scatter(): lax.ppermute(parts[half:], 'grp', [(i, i ^ bit) for i in range(grp_count)])  3.14 us
    unnamed x14, local copies, waits for them, and re-layouts  2.9 us
  transfers between devices with their start and end apart: 13, of which 5 were waited for; matrix products, arithmetic and copies ran while one was open for 7% of the time, Pallas kernels for 7%

profile of v13, /device:TPU:0, one launch (start us, length us, event | category | flops | bytes accessed | tf_op | source)
XLA Modules:
  0.0 70.9 jit_solution(11810637357453758424)
XLA Ops:
  0.0 0.0 copy-start
  0.0 0.1 compare_select_fusion
  0.1 0.1 reshape.125
  0.2 1.2 %copy-done = s32[24,128,128]{2,1,0:T(8,128)S(1)} copy-done((s32[24,128,128]{2,1,0:T(8,128)S(1)}, s32[24,128,128]{2,1,0:T(8,128)}, u32[]{:S(2)}) %copy-start) | copy-done | bytes 1572888
  1.4 0.6 gather_fusion
  2.1 0.0 copy-start.3
  2.1 0.2 convert_element_type.13
  2.2 0.7 copy-done.3
  3.0 1.1 %pad_maximum_fusion.refs_4_ = bf16[4,1024,128]{2,1,0:T(8,128)(2,1)} fusion(bf16[4,256,128]{2,1,0:T(8,128)(2,1)S(1)} %broadcast_in_dim.34, bf16[4,768,128]{2,1,0:T(8,128)(2,1)S(1)} %bitcast.37), kind=kLoop, calls=%fused_computation.1 | loop fusion | flops 2097152 | bytes 2097152 | tf_op jit(solution)/shard_map/concatenate | solution.py:124
  4.0 0.0 copy-start.6
  4.0 0.0 copy-start.5
  4.0 6.4 %all-to-all-start = ((bf16[4,1024,128]{2,1,0:T(8,128)(2,1)}), bf16[4,1024,128]{2,1,0:T(8,128)(2,1)S(1)}, u32[]{:S(2)}, u32[]{:S(2)}) async-start(bf16[4,1024,128]{2,1,0:T(8,128)(2,1)} %pad_maximum_fusion.refs_4_), calls=%async_computation | async-start | bytes 2097152 | tf_op jit(solution)/shard_map/all_to_all | solution.py:127
  10.5 0.0 collective-permute-start
  10.5 0.1 broadcast_add_fusion
  10.6 0.1 copy.7
  10.7 0.0 copy-done.6
  10.7 0.2 select_reduce_fusion
  10.9 0.1 copy.8
  11.7 0.1 collective-permute-done
  11.8 1.6 %collective-permute-start.1 = (bf16[2,128,256]{2,1,0:T(8,128)(2,1)S(1)}, bf16[2,128,256]{2,1,0:T(8,128)(2,1)S(1)}, u32[]{:S(2)}, u32[]{:S(2)}) collective-permute-start(bf16[2,128,256]{2,1,0:T(8,128)(2,1)S(1)} %maximum_select_fusion.2), channel_id=1, source_target_pairs={{0,8},{4,12},{8,0},{12,4},{16,24},{20,28},{24,16},{28,20},{1,9},{5... | collective-permute-start | bytes 393224 | tf_op jit(solution)/shard_map/ppermute | solution.py:34
  13.3 0.1 convert_add_fusion
  13.4 0.5 constant_dynamic-slice_fusion.3
  13.9 2.9 %collective-permute-start.4 = (s32[6]{0:T(128)S(1)}, s32[6]{0:T(128)S(1)}, u32[]{:S(2)}, u32[]{:S(2)}) collective-permute-start(s32[6]{0:T(128)S(1)} %get-tuple-element.24), channel_id=1, source_target_pairs={{0,2},{1,3},{2,0},{3,1},{4,6},{5,7},{6,4},{7,5},{8,10},{9,11},{10,... | collective-permute-start | bytes 80 | tf_op jit(solution)/shard_map/ppermute | solution.py:44
  16.8 1.5 %collective-permute-start.5 = (s32[6]{0:T(128)S(1)}, s32[6]{0:T(128)S(1)}, u32[]{:S(2)}, u32[]{:S(2)}) collective-permute-start(s32[6]{0:T(128)S(1)} %get-tuple-element.23), channel_id=1, source_target_pairs={{0,3},{1,0},{2,1},{3,2},{4,7},{5,4},{6,5},{7,6},{8,11},{9,8},{10,9... | collective-permute-start | bytes 80 | tf_op jit(solution)/shard_map/ppermute | solution.py:44
  18.3 0.6 collective-permute-start.3
  18.8 0.0 collective-permute-done.1
  18.9 1.6 %collective-permute-start.2 = (bf16[4,128,256]{2,1,0:T(8,128)(2,1)S(1)}, bf16[4,128,256]{2,1,0:T(8,128)(2,1)S(1)}, u32[]{:S(2)}, u32[]{:S(2)}) collective-permute-start(bf16[4,128,256]{2,1,0:T(8,128)(2,1)S(1)} %maximum_select_fusion.1), channel_id=1, source_target_pairs={{0,16},{4,20},{8,24},{12,28},{16,0},{20,4},{24,8},{28,12},{1,17},{... | collective-permute-start | bytes 786440 | tf_op jit(solution)/shard_map/ppermute | solution.py:34
  20.4 0.0 copy-done.5
  20.4 0.6 shift-left_or_fusion.refs_3_
  21.1 0.6 and_select_fusion.refs_0_
  21.6 14.7 %collective-permute-done.4 = s32[6]{0:T(128)S(1)} collective-permute-done((s32[6]{0:T(128)S(1)}, s32[6]{0:T(128)S(1)}, u32[]{:S(2)}, u32[]{:S(2)}) %collective-permute-start.4) | collective-permute-done | bytes 56 | tf_op jit(solution)/shard_map/ppermute | solution.py:44
  36.3 0.0 collective-permute-done.5
  36.3 0.0 collective-permute-done.3
  36.3 0.6 pad_add_fusion.refs_1_
  36.9 0.0 collective-permute-done.2
  36.9 0.9 %maximum_select_fusion.refs_6_ = bf16[8,128,256]{2,1,0:T(8,128)(2,1)} fusion(bf16[4,128,256]{2,1,0:T(8,128)(2,1)S(1)} %collective-permute-done.2, bf16[4,128,256]{2,1,0:T(8,128)(2,1)S(1)} %maximum_select_fusion.1, pred[]{:T(512)S(6)} %eq.36), kind=kLoop, calls=%fused_computation.2 | loop fusion | flops 786432 | bytes 1048577 | tf_op jit(solution)/shard_map/jit(_where)/select_n | solution.py:36
  37.8 0.8 %broadcast_in_dim.36.refs_7_.refs_8_ = f32[4,128,256]{2,1,0:T(8,128)} broadcast(f32[]{:T(128)} %constant.102.clone.1), dimensions={} | broadcast | bytes 524292 | tf_op jit(solution)/shard_map/broadcast_in_dim | solution.py:178
  38.6 4.9 %shard_map.64 = (f32[1,128,256]{2,1,0:T(8,128)}, f32[4,128,256]{2,1,0:T(8,128)}, f32[4,128,256]{2,1,0:T(8,128)}) custom-call(s32[1]{0:T(128)} %bitcast.refs_0_, s32[1,6]{1,0:T(1,128)} %get-tuple-element.22.refs_1_, s32[4,6]{1,0:T(4,128)} %bitcast.40, s32[4,6]{1,0:T(4,128)} %shift-left_or_fusion.refs_3_, bf16[4,1024,128]{2,1,0:T(8,128)(2,1)} %pad_maximum_fusion.refs_4_, ...), custom_call_target="tpu_custom_call" | custom-call | tf_op jit(solution)/shard_map/pallas_call | solution.py:153
  43.5 0.0 all-to-all-done.refs_4_
  43.5 0.0 copy-start.1
  43.5 1.0 %copy-done.1 = bf16[4,1024,128]{2,1,0:T(8,128)(2,1)} copy-done((bf16[4,1024,128]{2,1,0:T(8,128)(2,1)}, bf16[4,1024,128]{2,1,0:T(8,128)(2,1)S(1)}, u32[]{:S(2)}) %copy-start.1) | copy-done | bytes 1048600
  44.5 7.1 %shard_map.65 = (f32[3,128,256]{2,1,0:T(8,128)}, f32[4,128,256]{2,1,0:T(8,128)}, f32[4,128,256]{2,1,0:T(8,128)}) custom-call(s32[3]{0:T(128)} %and_select_fusion.refs_0_, s32[3,6]{1,0:T(4,128)} %pad_add_fusion.refs_1_, s32[4,6]{1,0:T(4,128)} %bitcast.41, s32[4,6]{1,0:T(4,128)} %shift-left_or_fusion.refs_3_, bf16[4,1024,128]{2,1,0:T(8,128)(2,1)} %copy-done.1, ...), custom_call_target="tpu_custom_call" | custom-call | tf_op jit(solution)/shard_map/pallas_call | solution.py:153
  51.6 0.0 copy-start.2
  51.6 0.1 collective-permute-start.9
  51.7 2.1 %collective-permute-done.9 = f32[4,128,256]{2,1,0:T(8,128)S(1)} collective-permute-done((f32[4,128,256]{2,1,0:T(8,128)}, f32[4,128,256]{2,1,0:T(8,128)S(1)}, u32[]{:S(2)}, u32[]{:S(2)}) %collective-permute-start.9) | collective-permute-done | bytes 524320 | tf_op jit(solution)/shard_map/ppermute | solution.py:19
  53.8 1.1 %add.153 = f32[4,128,256]{2,1,0:T(8,128)S(1)} add(f32[4,128,256]{2,1,0:T(8,128)} %get-tuple-element.15, f32[4,128,256]{2,1,0:T(8,128)S(1)} %collective-permute-done.9) | non-fusion elementwise | flops 131072 | bytes 1572864 | tf_op jit(solution)/shard_map/add | solution.py:19
  54.9 0.0 copy-start.4
  54.9 1.6 %collective-permute-start.10 = (f32[2,128,256]{2,1,0:T(8,128)S(1)}, f32[2,128,256]{2,1,0:T(8,128)S(1)}, u32[]{:S(2)}, u32[]{:S(2)}) collective-permute-start(f32[2,128,256]{2,1,0:T(8,128)S(1)} %slice.39), channel_id=1, source_target_pairs={{0,8},{4,12},{8,0},{12,4},{16,24},{20,28},{24,16},{28,20},{1,9},{5... | collective-permute-start | bytes 786440 | tf_op jit(solution)/shard_map/ppermute | solution.py:23
  56.5 0.0 copy-done.2
  56.5 1.5 %collective-permute-start.6 = (f32[128,256]{1,0:T(8,128)S(1)}, f32[128,256]{1,0:T(8,128)S(1)}, u32[]{:S(2)}, u32[]{:S(2)}) collective-permute-start(f32[128,256]{1,0:T(8,128)S(1)} %get-tuple-element.17), channel_id=1, source_target_pairs={{0,3},{1,0},{2,1},{3,2},{4,7},{5,4},{6,5},{7,6},{8,11},{9,8},{10,9... | collective-permute-start | bytes 393224 | tf_op jit(solution)/shard_map/ppermute | solution.py:44
  58.0 0.5 collective-permute-start.7
  58.5 0.6 collective-permute-start.8
  59.1 4.3 %collective-permute-done.10 = f32[2,128,256]{2,1,0:T(8,128)S(1)} collective-permute-done((f32[2,128,256]{2,1,0:T(8,128)S(1)}, f32[2,128,256]{2,1,0:T(8,128)S(1)}, u32[]{:S(2)}, u32[]{:S(2)}) %collective-permute-start.10) | collective-permute-done | bytes 262176 | tf_op jit(solution)/shard_map/ppermute | solution.py:23
  63.4 1.6 %collective-permute-start.11 = (f32[1,128,256]{2,1,0:T(8,128)S(1)}, f32[1,128,256]{2,1,0:T(8,128)S(1)}, u32[]{:S(2)}, u32[]{:S(2)}) collective-permute-start(f32[1,128,256]{2,1,0:T(8,128)S(1)} %slice.41), channel_id=1, source_target_pairs={{0,16},{4,20},{8,24},{12,28},{16,0},{20,4},{24,8},{28,12},{1,17},{... | collective-permute-start | bytes 393224 | tf_op jit(solution)/shard_map/ppermute | solution.py:23
  65.0 0.0 collective-permute-done.6
  65.0 5.2 %collective-permute-done.7 = f32[128,256]{1,0:T(8,128)S(1)} collective-permute-done((f32[128,256]{1,0:T(8,128)S(1)}, f32[128,256]{1,0:T(8,128)S(1)}, u32[]{:S(2)}, u32[]{:S(2)}) %collective-permute-start.7) | collective-permute-done | bytes 131104 | tf_op jit(solution)/shard_map/ppermute | solution.py:44
  70.2 0.0 collective-permute-done.8
  70.2 0.0 collective-permute-done.11
  70.2 0.0 copy-done.4
  70.2 0.7 fusion.1
  (12 shorter events, 0.2 us)
Async XLA Ops:
  0.0 1.4 %copy-start = (s32[24,128,128]{2,1,0:T(8,128)S(1)}, s32[24,128,128]{2,1,0:T(8,128)}, u32[]{:S(2)}) copy-start(s32[24,128,128]{2,1,0:T(8,128)} %param.8) | copy-start | bytes 4718596
  2.1 0.8 %copy-start.3 = (bf16[128,256]{1,0:T(8,128)(2,1)S(1)}, bf16[128,256]{1,0:T(8,128)(2,1)}, u32[]{:S(2)}) copy-start(bf16[128,256]{1,0:T(8,128)(2,1)} %param.6) | copy-start | bytes 196612
  4.0 6.6 %copy-start.6 = (s32[1,24]{1,0:T(1,128)S(1)}, s32[1,24]{1,0:T(1,128)}, u32[]{:S(2)}) copy-start(s32[1,24]{1,0:T(1,128)} %param.9) | copy-start | bytes 292
  4.0 16.4 %copy-start.5 = (s32[1,4,6]{2,1,0:T(4,128)S(1)}, s32[1,4,6]{2,1,0:T(4,128)}, u32[]{:S(2)}) copy-start(s32[1,4,6]{2,1,0:T(4,128)} %param.11) | copy-start | bytes 292
  4.0 39.5 %all-to-all-start = ((bf16[4,1024,128]{2,1,0:T(8,128)(2,1)}), bf16[4,1024,128]{2,1,0:T(8,128)(2,1)S(1)}, u32[]{:S(2)}, u32[]{:S(2)}) async-start(bf16[4,1024,128]{2,1,0:T(8,128)(2,1)} %pad_maximum_fusion.refs_4_), calls=%async_computation | async-start | bytes 2097152 | tf_op jit(solution)/shard_map/all_to_all | solution.py:127
  10.5 1.3 %collective-permute-start = (bf16[1,128,256]{2,1,0:T(8,128)(2,1)S(1)}, bf16[1,128,256]{2,1,0:T(8,128)(2,1)S(1)}, u32[]{:S(2)}, u32[]{:S(2)}) collective-permute-start(bf16[1,128,256]{2,1,0:T(8,128)(2,1)S(1)} %bitcast.38), channel_id=1, source_target_pairs={{0,4},{4,0},{8,12},{12,8},{16,20},{20,16},{24,28},{28,24},{1,5},{5... | collective-permute-start | bytes 196616 | tf_op jit(solution)/shard_map/ppermute | solution.py:34
  11.8 7.1 %collective-permute-start.1 = (bf16[2,128,256]{2,1,0:T(8,128)(2,1)S(1)}, bf16[2,128,256]{2,1,0:T(8,128)(2,1)S(1)}, u32[]{:S(2)}, u32[]{:S(2)}) collective-permute-start(bf16[2,128,256]{2,1,0:T(8,128)(2,1)S(1)} %maximum_select_fusion.2), channel_id=1, source_target_pairs={{0,8},{4,12},{8,0},{12,4},{16,24},{20,28},{24,16},{28,20},{1,9},{5... | collective-permute-start | bytes 393224 | tf_op jit(solution)/shard_map/ppermute | solution.py:34
  13.9 22.4 %collective-permute-start.4 = (s32[6]{0:T(128)S(1)}, s32[6]{0:T(128)S(1)}, u32[]{:S(2)}, u32[]{:S(2)}) collective-permute-start(s32[6]{0:T(128)S(1)} %get-tuple-element.24), channel_id=1, source_target_pairs={{0,2},{1,3},{2,0},{3,1},{4,6},{5,7},{6,4},{7,5},{8,10},{9,11},{10,... | collective-permute-start | bytes 80 | tf_op jit(solution)/shard_map/ppermute | solution.py:44
  16.8 19.5 %collective-permute-start.5 = (s32[6]{0:T(128)S(1)}, s32[6]{0:T(128)S(1)}, u32[]{:S(2)}, u32[]{:S(2)}) collective-permute-start(s32[6]{0:T(128)S(1)} %get-tuple-element.23), channel_id=1, source_target_pairs={{0,3},{1,0},{2,1},{3,2},{4,7},{5,4},{6,5},{7,6},{8,11},{9,8},{10,9... | collective-permute-start | bytes 80 | tf_op jit(solution)/shard_map/ppermute | solution.py:44
  18.3 18.0 %collective-permute-start.3 = (s32[6]{0:T(128)S(1)}, s32[6]{0:T(128)S(1)}, u32[]{:S(2)}, u32[]{:S(2)}) collective-permute-start(s32[6]{0:T(128)S(1)} %get-tuple-element.25), channel_id=1, source_target_pairs={{0,1},{1,2},{2,3},{3,0},{4,5},{5,6},{6,7},{7,4},{8,9},{9,10},{10,1... | collective-permute-start | bytes 80 | tf_op jit(solution)/shard_map/ppermute | solution.py:44
  18.9 18.0 %collective-permute-start.2 = (bf16[4,128,256]{2,1,0:T(8,128)(2,1)S(1)}, bf16[4,128,256]{2,1,0:T(8,128)(2,1)S(1)}, u32[]{:S(2)}, u32[]{:S(2)}) collective-permute-start(bf16[4,128,256]{2,1,0:T(8,128)(2,1)S(1)} %maximum_select_fusion.1), channel_id=1, source_target_pairs={{0,16},{4,20},{8,24},{12,28},{16,0},{20,4},{24,8},{28,12},{1,17},{... | collective-permute-start | bytes 786440 | tf_op jit(solution)/shard_map/ppermute | solution.py:34
  43.5 1.0 %copy-start.1 = (bf16[4,1024,128]{2,1,0:T(8,128)(2,1)}, bf16[4,1024,128]{2,1,0:T(8,128)(2,1)S(1)}, u32[]{:S(2)}) copy-start(bf16[4,1024,128]{2,1,0:T(8,128)(2,1)S(1)} %all-to-all-done.refs_4_) | copy-start | bytes 3145732
  51.6 4.9 %copy-start.2 = (f32[3,128,256]{2,1,0:T(8,128)S(1)}, f32[3,128,256]{2,1,0:T(8,128)}, u32[]{:S(2)}) copy-start(f32[3,128,256]{2,1,0:T(8,128)} %get-tuple-element.14) | copy-start | bytes 1179652
  51.6 2.2 %collective-permute-start.9 = (f32[4,128,256]{2,1,0:T(8,128)}, f32[4,128,256]{2,1,0:T(8,128)S(1)}, u32[]{:S(2)}, u32[]{:S(2)}) collective-permute-start(f32[4,128,256]{2,1,0:T(8,128)} %get-tuple-element.16), channel_id=1, source_target_pairs={{0,4},{4,0},{8,12},{12,8},{16,20},{20,16},{24,28},{28,24},{1,5},{5... | collective-permute-start | bytes 1572872 | tf_op jit(solution)/shard_map/ppermute | solution.py:19
  54.9 15.3 %copy-start.4 = (f32[1,128,256]{2,1,0:T(8,128)S(1)}, f32[1,128,256]{2,1,0:T(8,128)}, u32[]{:S(2)}) copy-start(f32[1,128,256]{2,1,0:T(8,128)} %get-tuple-element.11) | copy-start | bytes 393220
  54.9 8.4 %collective-permute-start.10 = (f32[2,128,256]{2,1,0:T(8,128)S(1)}, f32[2,128,256]{2,1,0:T(8,128)S(1)}, u32[]{:S(2)}, u32[]{:S(2)}) collective-permute-start(f32[2,128,256]{2,1,0:T(8,128)S(1)} %slice.39), channel_id=1, source_target_pairs={{0,8},{4,12},{8,0},{12,4},{16,24},{20,28},{24,16},{28,20},{1,9},{5... | collective-permute-start | bytes 786440 | tf_op jit(solution)/shard_map/ppermute | solution.py:23
  56.5 8.5 %collective-permute-start.6 = (f32[128,256]{1,0:T(8,128)S(1)}, f32[128,256]{1,0:T(8,128)S(1)}, u32[]{:S(2)}, u32[]{:S(2)}) collective-permute-start(f32[128,256]{1,0:T(8,128)S(1)} %get-tuple-element.17), channel_id=1, source_target_pairs={{0,3},{1,0},{2,1},{3,2},{4,7},{5,4},{6,5},{7,6},{8,11},{9,8},{10,9... | collective-permute-start | bytes 393224 | tf_op jit(solution)/shard_map/ppermute | solution.py:44
  58.0 12.1 %collective-permute-start.7 = (f32[128,256]{1,0:T(8,128)S(1)}, f32[128,256]{1,0:T(8,128)S(1)}, u32[]{:S(2)}, u32[]{:S(2)}) collective-permute-start(f32[128,256]{1,0:T(8,128)S(1)} %get-tuple-element.19), channel_id=1, source_target_pairs={{0,2},{1,3},{2,0},{3,1},{4,6},{5,7},{6,4},{7,5},{8,10},{9,11},{10,... | collective-permute-start | bytes 393224 | tf_op jit(solution)/shard_map/ppermute | solution.py:44
  58.5 11.7 %collective-permute-start.8 = (f32[128,256]{1,0:T(8,128)S(1)}, f32[128,256]{1,0:T(8,128)S(1)}, u32[]{:S(2)}, u32[]{:S(2)}) collective-permute-start(f32[128,256]{1,0:T(8,128)S(1)} %get-tuple-element.18), channel_id=1, source_target_pairs={{0,1},{1,2},{2,3},{3,0},{4,5},{5,6},{6,7},{7,4},{8,9},{9,10},{10,1... | collective-permute-start | bytes 393224 | tf_op jit(solution)/shard_map/ppermute | solution.py:44
  63.4 6.8 %collective-permute-start.11 = (f32[1,128,256]{2,1,0:T(8,128)S(1)}, f32[1,128,256]{2,1,0:T(8,128)S(1)}, u32[]{:S(2)}, u32[]{:S(2)}) collective-permute-start(f32[1,128,256]{2,1,0:T(8,128)S(1)} %slice.41), channel_id=1, source_target_pairs={{0,16},{4,20},{8,24},{12,28},{16,0},{20,4},{24,8},{28,12},{1,17},{... | collective-permute-start | bytes 393224 | tf_op jit(solution)/shard_map/ppermute | solution.py:23

commit v14 on v12

--- a/solution.py
+++ b/solution.py
@@ -16,14 +16,15 @@
 
 
 def grp_reduce_scatter(keep, send, grp_count):
-    parts = keep + lax.ppermute(send, "grp", [(i, i ^ 1) for i in range(grp_count)])
+    got = lax.ppermute(send, "grp", [(i, i ^ 1) for i in range(grp_count)])
     bit = 2
     while bit < grp_count:
-        half = parts.shape[0] // 2
-        got = lax.ppermute(parts[half:], "grp", [(i, i ^ bit) for i in range(grp_count)])
-        parts = parts[:half] + got
+        half = keep.shape[0] // 2
+        outgoing = keep[half:] + got[half:]
+        keep = keep[:half] + got[:half]
+        got = lax.ppermute(outgoing, "grp", [(i, i ^ bit) for i in range(grp_count)])
         bit *= 2
-    return parts[0]
+    return (keep + got)[0]
 
 
 def grp_gather(block, grp_count):

time: 64.6 us -> 64.6 us (level)
  no operation moved by 1% of the time
where the time goes in v14:
time: 64.6 us; the launch traced here: 64.2 us
  waiting for transfers between devices  25.8 us (40%)
  starting transfers between devices  15 us (23%)
  Pallas kernels  12 us (19%)
  other arithmetic  7.84 us (12%)
  local copies, waits for them, and re-layouts  2.78 us (4%)
  between operations  0.76 us (1%)
    pallas_call x2, Pallas kernels, relay_tiles(): pl.pallas_call(lambda *refs: tile_kernel(*refs, per_relay=per_relay, bloc...  12 us
    ppermute x3, waiting for transfers between devices, grp_gather(): got = lax.ppermute(held, 'grp', [(i, i ^ bit) for i in range(grp_count)])  9.55 us
    all_to_all x1, starting transfers between devices, on_device(): lax.all_to_all(outgoing, 'ent', split_axis=0, concat_axis=0, tiled=True)  6.45 us
    all_to_all x1, waiting for transfers between devices, on_device(): lax.all_to_all(outgoing, 'ent', split_axis=0, concat_axis=0, tiled=True)  4.93 us
    ppermute x2, waiting for transfers between devices, grp_reduce_scatter(): lax.ppermute(outgoing, 'grp', [(i, i ^ bit) for i in range(grp_count)])  4.67 us
    ppermute x3, waiting for transfers between devices, shift_ent(): lax.ppermute(x, 'ent', [(i, (i + shift) % ent_count) for i in range(ent_c...  4.58 us
    ppermute x3, starting transfers between devices, grp_gather(): got = lax.ppermute(held, 'grp', [(i, i ^ bit) for i in range(grp_count)])  3.14 us
    ppermute x2, starting transfers between devices, grp_reduce_scatter(): lax.ppermute(outgoing, 'grp', [(i, i ^ bit) for i in range(grp_count)])  3.14 us
  transfers between devices with their start and end apart: 10, of which 7 were waited for; matrix products, arithmetic and copies ran while one was open for 6% of the time, Pallas kernels for 8%

profile of v14, /device:TPU:0, one launch (start us, length us, event | category | flops | bytes accessed | tf_op | source)
XLA Modules:
  0.0 64.2 jit_solution(9448885133931168899)
XLA Ops:
  0.0 0.0 copy-start
  0.0 0.1 broadcast_add_fusion
  0.1 0.1 compare_select_fusion
  0.2 0.1 copy.7
  0.3 1.0 %select_reduce_fusion = s32[4,6]{0,1:T(8,128)S(1)} fusion(s32[24]{0:T(128)} %bitcast.35, s32[4,6]{0,1:T(8,128)S(1)} %copy.7), kind=kLoop, calls=%fused_computation.19 | loop fusion | flops 1704 | bytes 288 | tf_op jit(solution)/shard_map/reduce_sum | solution.py:128
  1.3 0.1 copy.8
  2.0 0.1 convert_convert_fusion
  2.1 0.1 reshape.129
  2.2 0.0 copy-done
  2.2 0.7 %gather_fusion = s32[24,128,128]{2,1,0:T(8,128)S(1)} fusion(s32[24,128,128]{2,1,0:T(8,128)S(1)} %copy-done, s32[1024]{0:T(1024)S(1)} %pad_clamp_fusion), kind=kCustom, calls=%fused_computation | custom fusion | bytes 3145824 | tf_op jit(solution)/shard_map/gather | solution.py:124
  2.9 0.0 copy-start.3
  2.9 0.2 convert_element_type.42
  3.1 0.7 %copy-done.3 = bf16[128,256]{1,0:T(8,128)(2,1)S(1)} copy-done((bf16[128,256]{1,0:T(8,128)(2,1)S(1)}, bf16[128,256]{1,0:T(8,128)(2,1)}, u32[]{:S(2)}) %copy-start.3) | copy-done | bytes 65560
  3.7 0.1 fusion.10
  3.9 1.1 %pad_maximum_fusion.refs_4_ = bf16[4,1040,128]{2,1,0:T(8,128)(2,1)} fusion(bf16[4,16,128]{2,1,0:T(8,128)(2,1)S(1)} %broadcast_in_dim.41, bf16[4,256,128]{2,1,0:T(8,128)(2,1)S(1)} %broadcast_in_dim.40, bf16[4,768,128]{2,1,0:T(8,128)(2,1)S(1)} %bitcast.29), kind=kLoop, calls=%fused_computation.1 | loop fusion | flops 3194880 | bytes 2129920 | tf_op jit(solution)/shard_map/concatenate | solution.py:141
  4.9 0.0 copy-start.5
  4.9 6.4 %all-to-all-start = ((bf16[4,1040,128]{2,1,0:T(8,128)(2,1)}), bf16[4,1040,128]{2,1,0:T(8,128)(2,1)S(1)}, u32[]{:S(2)}, u32[]{:S(2)}) async-start(bf16[4,1040,128]{2,1,0:T(8,128)(2,1)} %pad_maximum_fusion.refs_4_), calls=%async_computation | async-start | bytes 2129920 | tf_op jit(solution)/shard_map/all_to_all | solution.py:144
  11.4 0.0 collective-permute-start
  11.4 1.3 %collective-permute-done = bf16[1,128,256]{2,1,0:T(8,128)(2,1)S(1)} collective-permute-done((bf16[1,128,256]{2,1,0:T(8,128)(2,1)S(1)}, bf16[1,128,256]{2,1,0:T(8,128)(2,1)S(1)}, u32[]{:S(2)}, u32[]{:S(2)}) %collective-permute-start) | collective-permute-done | bytes 65568 | tf_op jit(solution)/shard_map/ppermute | solution.py:35
  12.6 1.6 %collective-permute-start.1 = (bf16[2,128,256]{2,1,0:T(8,128)(2,1)S(1)}, bf16[2,128,256]{2,1,0:T(8,128)(2,1)S(1)}, u32[]{:S(2)}, u32[]{:S(2)}) collective-permute-start(bf16[2,128,256]{2,1,0:T(8,128)(2,1)S(1)} %maximum_select_fusion.2), channel_id=1, source_target_pairs={{0,8},{4,12},{8,0},{12,4},{16,24},{20,28},{24,16},{28,20},{1,9},{5... | collective-permute-start | bytes 393224 | tf_op jit(solution)/shard_map/ppermute | solution.py:35
  14.2 0.7 %add_convert_fusion.1.refs_1_ = s32[4,6]{1,0:T(4,128)} fusion(f32[4,128]{1,0:T(4,128)S(1)} %get-tuple-element.17), kind=kLoop, calls=%fused_computation.33 | loop fusion | flops 72 | bytes 288 | tf_op jit(solution)/shard_map/convert_element_type | solution.py:149
  14.9 3.4 %collective-permute-done.1 = bf16[2,128,256]{2,1,0:T(8,128)(2,1)S(1)} collective-permute-done((bf16[2,128,256]{2,1,0:T(8,128)(2,1)S(1)}, bf16[2,128,256]{2,1,0:T(8,128)(2,1)S(1)}, u32[]{:S(2)}, u32[]{:S(2)}) %collective-permute-start.1) | collective-permute-done | bytes 131104 | tf_op jit(solution)/shard_map/ppermute | solution.py:35
  18.3 1.6 %collective-permute-start.2 = (bf16[4,128,256]{2,1,0:T(8,128)(2,1)S(1)}, bf16[4,128,256]{2,1,0:T(8,128)(2,1)S(1)}, u32[]{:S(2)}, u32[]{:S(2)}) collective-permute-start(bf16[4,128,256]{2,1,0:T(8,128)(2,1)S(1)} %maximum_select_fusion.1), channel_id=1, source_target_pairs={{0,16},{4,20},{8,24},{12,28},{16,0},{20,4},{24,8},{28,12},{1,17},{... | collective-permute-start | bytes 786440 | tf_op jit(solution)/shard_map/ppermute | solution.py:35
  19.9 0.5 and_select_fusion.refs_0_
  20.4 0.0 copy-done.5
  20.4 0.6 shift-left_or_fusion.refs_3_
  21.0 4.9 %collective-permute-done.2 = bf16[4,128,256]{2,1,0:T(8,128)(2,1)S(1)} collective-permute-done((bf16[4,128,256]{2,1,0:T(8,128)(2,1)S(1)}, bf16[4,128,256]{2,1,0:T(8,128)(2,1)S(1)}, u32[]{:S(2)}, u32[]{:S(2)}) %collective-permute-start.2) | collective-permute-done | bytes 262176 | tf_op jit(solution)/shard_map/ppermute | solution.py:35
  25.9 0.9 %maximum_select_fusion.refs_6_ = bf16[8,128,256]{2,1,0:T(8,128)(2,1)} fusion(bf16[4,128,256]{2,1,0:T(8,128)(2,1)S(1)} %collective-permute-done.2, bf16[4,128,256]{2,1,0:T(8,128)(2,1)S(1)} %maximum_select_fusion.1, pred[]{:T(512)S(6)} %eq.33), kind=kLoop, calls=%fused_computation.2 | loop fusion | flops 786432 | bytes 1048577 | tf_op jit(solution)/shard_map/jit(_where)/select_n | solution.py:37
  26.8 0.8 %broadcast_in_dim.43.refs_7_.refs_8_ = f32[4,128,256]{2,1,0:T(8,128)} broadcast(f32[]{:T(128)} %constant.94.clone.1), dimensions={} | broadcast | bytes 524292 | tf_op jit(solution)/shard_map/broadcast_in_dim | solution.py:184
  27.6 4.9 %shard_map.64 = (f32[1,128,256]{2,1,0:T(8,128)}, f32[4,128,256]{2,1,0:T(8,128)}, f32[4,128,256]{2,1,0:T(8,128)}) custom-call(s32[1]{0:T(128)} %bitcast.refs_0_, s32[4,6]{1,0:T(4,128)} %add_convert_fusion.1.refs_1_, s32[4,6]{1,0:T(4,128)} %bitcast.32, s32[4,6]{1,0:T(4,128)} %shift-left_or_fusion.refs_3_, bf16[4,1040,128]{2,1,0:T(8,128)(2,1)} %pad_maximum_fusion.refs_4_, ...), custom_call_target="tpu_custom_call" | custom-call | tf_op jit(solution)/shard_map/pallas_call | solution.py:159
  32.5 4.9 %all-to-all-done.refs_4_ = bf16[4,1040,128]{2,1,0:T(8,128)(2,1)S(1)} async-done(((bf16[4,1040,128]{2,1,0:T(8,128)(2,1)}), bf16[4,1040,128]{2,1,0:T(8,128)(2,1)S(1)}, u32[]{:S(2)}, u32[]{:S(2)}) %all-to-all-start) | async-done | bytes 1064992 | tf_op jit(solution)/shard_map/all_to_all | solution.py:144
  37.4 0.0 copy-start.1
  37.5 0.7 %add_convert_fusion.refs_1_ = s32[4,6]{1,0:T(4,128)} fusion(f32[4,128]{1,0:T(4,128)S(1)} %bitcast.34), kind=kLoop, calls=%fused_computation.31 | loop fusion | flops 72 | bytes 288 | tf_op jit(solution)/shard_map/convert_element_type | solution.py:149
  38.2 0.3 copy-done.1
  38.4 7.1 %shard_map.65 = (f32[3,128,256]{2,1,0:T(8,128)}, f32[4,128,256]{2,1,0:T(8,128)}, f32[4,128,256]{2,1,0:T(8,128)}) custom-call(s32[3]{0:T(128)} %and_select_fusion.refs_0_, s32[4,6]{1,0:T(4,128)} %add_convert_fusion.refs_1_, s32[4,6]{1,0:T(4,128)} %bitcast.33, s32[4,6]{1,0:T(4,128)} %shift-left_or_fusion.refs_3_, bf16[4,1040,128]{2,1,0:T(8,128)(2,1)} %copy-done.1, ...), custom_call_target="tpu_custom_call" | custom-call | tf_op jit(solution)/shard_map/pallas_call | solution.py:159
  45.6 0.0 copy-start.2
  45.6 0.0 copy-start.4
  45.6 0.1 collective-permute-start.6
  45.7 2.1 %collective-permute-done.6 = f32[4,128,256]{2,1,0:T(8,128)S(1)} collective-permute-done((f32[4,128,256]{2,1,0:T(8,128)}, f32[4,128,256]{2,1,0:T(8,128)S(1)}, u32[]{:S(2)}, u32[]{:S(2)}) %collective-permute-start.6) | collective-permute-done | bytes 524320 | tf_op jit(solution)/shard_map/ppermute | solution.py:19
  47.8 1.1 %slice_add_fusion.1 = (f32[2,128,256]{2,1,0:T(8,128)S(1)}, f32[2,128,256]{2,1,0:T(8,128)S(1)}) fusion(f32[4,128,256]{2,1,0:T(8,128)S(1)} %collective-permute-done.6, f32[4,128,256]{2,1,0:T(8,128)} %get-tuple-element.15), kind=kLoop, calls=%fused_computation.4 | loop fusion | flops 131072 | bytes 1572864 | tf_op jit(solution)/shard_map/add | solution.py:24
  48.9 1.6 %collective-permute-start.7 = (f32[2,128,256]{2,1,0:T(8,128)S(1)}, f32[2,128,256]{2,1,0:T(8,128)S(1)}, u32[]{:S(2)}, u32[]{:S(2)}) collective-permute-start(f32[2,128,256]{2,1,0:T(8,128)S(1)} %get-tuple-element.20), channel_id=1, source_target_pairs={{0,8},{4,12},{8,0},{12,4},{16,24},{20,28},{24,16},{28,20},{1,9},{5... | collective-permute-start | bytes 786440 | tf_op jit(solution)/shard_map/ppermute | solution.py:25
  50.4 0.0 copy-done.2
  50.5 1.5 %collective-permute-start.3 = (f32[128,256]{1,0:T(8,128)S(1)}, f32[128,256]{1,0:T(8,128)S(1)}, u32[]{:S(2)}, u32[]{:S(2)}) collective-permute-start(f32[128,256]{1,0:T(8,128)S(1)} %get-tuple-element.21), channel_id=1, source_target_pairs={{0,3},{1,0},{2,1},{3,2},{4,7},{5,4},{6,5},{7,6},{8,11},{9,8},{10,9... | collective-permute-start | bytes 393224 | tf_op jit(solution)/shard_map/ppermute | solution.py:45
  52.0 0.0 collective-permute-start.4
  52.0 0.6 collective-permute-start.5
  52.6 4.7 %collective-permute-done.7 = f32[2,128,256]{2,1,0:T(8,128)S(1)} collective-permute-done((f32[2,128,256]{2,1,0:T(8,128)S(1)}, f32[2,128,256]{2,1,0:T(8,128)S(1)}, u32[]{:S(2)}, u32[]{:S(2)}) %collective-permute-start.7) | collective-permute-done | bytes 262176 | tf_op jit(solution)/shard_map/ppermute | solution.py:25
  57.3 1.6 %collective-permute-start.8 = (f32[1,128,256]{2,1,0:T(8,128)S(1)}, f32[1,128,256]{2,1,0:T(8,128)S(1)}, u32[]{:S(2)}, u32[]{:S(2)}) collective-permute-start(f32[1,128,256]{2,1,0:T(8,128)S(1)} %slice_add_fusion.2), channel_id=1, source_target_pairs={{0,16},{4,20},{8,24},{12,28},{16,0},{20,4},{24,8},{28,12},{1,17},{... | collective-permute-start | bytes 393224 | tf_op jit(solution)/shard_map/ppermute | solution.py:25
  58.9 0.0 collective-permute-done.3
  58.9 4.6 %collective-permute-done.4 = f32[128,256]{1,0:T(8,128)S(1)} collective-permute-done((f32[128,256]{1,0:T(8,128)S(1)}, f32[128,256]{1,0:T(8,128)S(1)}, u32[]{:S(2)}, u32[]{:S(2)}) %collective-permute-start.4) | collective-permute-done | bytes 131104 | tf_op jit(solution)/shard_map/ppermute | solution.py:45
  63.5 0.0 collective-permute-done.5
  63.5 0.0 collective-permute-done.8
  63.5 0.0 copy-done.4
  63.5 0.7 %fusion.2 = f32[128,256]{1,0:T(8,128)} fusion(f32[1,128,256]{2,1,0:T(8,128)S(1)} %collective-permute-done.8, f32[2,128,256]{2,1,0:T(8,128)S(1)} %collective-permute-done.7, f32[2,128,256]{2,1,0:T(8,128)S(1)} %get-tuple-element.19, f32[128,256]{1,0:T(8,128)S(1)} %collective-permute-done.5, f32[128,256]{1,0:T(8,128)S(1)} %collective-permute-done.4, ...), kind=kLoop, calls=%fused_computation.10 | loop fusion | flops 196608 | bytes 1048576 | tf_op jit(solution)/shard_map/add | solution.py:195
  (13 shorter events, 0.2 us)
Async XLA Ops:
  0.0 2.2 %copy-start = (s32[24,128,128]{2,1,0:T(8,128)S(1)}, s32[24,128,128]{2,1,0:T(8,128)}, u32[]{:S(2)}) copy-start(s32[24,128,128]{2,1,0:T(8,128)} %param.8) | copy-start | bytes 4718596
  2.9 0.8 %copy-start.3 = (bf16[128,256]{1,0:T(8,128)(2,1)S(1)}, bf16[128,256]{1,0:T(8,128)(2,1)}, u32[]{:S(2)}) copy-start(bf16[128,256]{1,0:T(8,128)(2,1)} %param.6) | copy-start | bytes 196612
  4.9 15.5 %copy-start.5 = (s32[1,4,6]{2,1,0:T(4,128)S(1)}, s32[1,4,6]{2,1,0:T(4,128)}, u32[]{:S(2)}) copy-start(s32[1,4,6]{2,1,0:T(4,128)} %param.11) | copy-start | bytes 292
  4.9 32.5 %all-to-all-start = ((bf16[4,1040,128]{2,1,0:T(8,128)(2,1)}), bf16[4,1040,128]{2,1,0:T(8,128)(2,1)S(1)}, u32[]{:S(2)}, u32[]{:S(2)}) async-start(bf16[4,1040,128]{2,1,0:T(8,128)(2,1)} %pad_maximum_fusion.refs_4_), calls=%async_computation | async-start | bytes 2129920 | tf_op jit(solution)/shard_map/all_to_all | solution.py:144
  11.4 1.3 %collective-permute-start = (bf16[1,128,256]{2,1,0:T(8,128)(2,1)S(1)}, bf16[1,128,256]{2,1,0:T(8,128)(2,1)S(1)}, u32[]{:S(2)}, u32[]{:S(2)}) collective-permute-start(bf16[1,128,256]{2,1,0:T(8,128)(2,1)S(1)} %bitcast.30), channel_id=1, source_target_pairs={{0,4},{4,0},{8,12},{12,8},{16,20},{20,16},{24,28},{28,24},{1,5},{5... | collective-permute-start | bytes 196616 | tf_op jit(solution)/shard_map/ppermute | solution.py:35
  12.6 5.6 %collective-permute-start.1 = (bf16[2,128,256]{2,1,0:T(8,128)(2,1)S(1)}, bf16[2,128,256]{2,1,0:T(8,128)(2,1)S(1)}, u32[]{:S(2)}, u32[]{:S(2)}) collective-permute-start(bf16[2,128,256]{2,1,0:T(8,128)(2,1)S(1)} %maximum_select_fusion.2), channel_id=1, source_target_pairs={{0,8},{4,12},{8,0},{12,4},{16,24},{20,28},{24,16},{28,20},{1,9},{5... | collective-permute-start | bytes 393224 | tf_op jit(solution)/shard_map/ppermute | solution.py:35
  18.3 7.6 %collective-permute-start.2 = (bf16[4,128,256]{2,1,0:T(8,128)(2,1)S(1)}, bf16[4,128,256]{2,1,0:T(8,128)(2,1)S(1)}, u32[]{:S(2)}, u32[]{:S(2)}) collective-permute-start(bf16[4,128,256]{2,1,0:T(8,128)(2,1)S(1)} %maximum_select_fusion.1), channel_id=1, source_target_pairs={{0,16},{4,20},{8,24},{12,28},{16,0},{20,4},{24,8},{28,12},{1,17},{... | collective-permute-start | bytes 786440 | tf_op jit(solution)/shard_map/ppermute | solution.py:35
  37.4 1.0 %copy-start.1 = (bf16[4,1040,128]{2,1,0:T(8,128)(2,1)}, bf16[4,1040,128]{2,1,0:T(8,128)(2,1)S(1)}, u32[]{:S(2)}) copy-start(bf16[4,1040,128]{2,1,0:T(8,128)(2,1)S(1)} %all-to-all-done.refs_4_) | copy-start | bytes 3194884
  45.6 4.9 %copy-start.2 = (f32[3,128,256]{2,1,0:T(8,128)S(1)}, f32[3,128,256]{2,1,0:T(8,128)}, u32[]{:S(2)}) copy-start(f32[3,128,256]{2,1,0:T(8,128)} %get-tuple-element.14) | copy-start | bytes 1179652
  45.6 17.9 %copy-start.4 = (f32[1,128,256]{2,1,0:T(8,128)S(1)}, f32[1,128,256]{2,1,0:T(8,128)}, u32[]{:S(2)}) copy-start(f32[1,128,256]{2,1,0:T(8,128)} %get-tuple-element.11) | copy-start | bytes 393220
  45.6 2.2 %collective-permute-start.6 = (f32[4,128,256]{2,1,0:T(8,128)}, f32[4,128,256]{2,1,0:T(8,128)S(1)}, u32[]{:S(2)}, u32[]{:S(2)}) collective-permute-start(f32[4,128,256]{2,1,0:T(8,128)} %get-tuple-element.16), channel_id=1, source_target_pairs={{0,4},{4,0},{8,12},{12,8},{16,20},{20,16},{24,28},{28,24},{1,5},{5... | collective-permute-start | bytes 1572872 | tf_op jit(solution)/shard_map/ppermute | solution.py:19
  48.9 8.4 %collective-permute-start.7 = (f32[2,128,256]{2,1,0:T(8,128)S(1)}, f32[2,128,256]{2,1,0:T(8,128)S(1)}, u32[]{:S(2)}, u32[]{:S(2)}) collective-permute-start(f32[2,128,256]{2,1,0:T(8,128)S(1)} %get-tuple-element.20), channel_id=1, source_target_pairs={{0,8},{4,12},{8,0},{12,4},{16,24},{20,28},{24,16},{28,20},{1,9},{5... | collective-permute-start | bytes 786440 | tf_op jit(solution)/shard_map/ppermute | solution.py:25
  50.5 8.4 %collective-permute-start.3 = (f32[128,256]{1,0:T(8,128)S(1)}, f32[128,256]{1,0:T(8,128)S(1)}, u32[]{:S(2)}, u32[]{:S(2)}) collective-permute-start(f32[128,256]{1,0:T(8,128)S(1)} %get-tuple-element.21), channel_id=1, source_target_pairs={{0,3},{1,0},{2,1},{3,2},{4,7},{5,4},{6,5},{7,6},{8,11},{9,8},{10,9... | collective-permute-start | bytes 393224 | tf_op jit(solution)/shard_map/ppermute | solution.py:45
  52.0 11.5 %collective-permute-start.4 = (f32[128,256]{1,0:T(8,128)S(1)}, f32[128,256]{1,0:T(8,128)S(1)}, u32[]{:S(2)}, u32[]{:S(2)}) collective-permute-start(f32[128,256]{1,0:T(8,128)S(1)} %get-tuple-element.23), channel_id=1, source_target_pairs={{0,2},{1,3},{2,0},{3,1},{4,6},{5,7},{6,4},{7,5},{8,10},{9,11},{10,... | collective-permute-start | bytes 393224 | tf_op jit(solution)/shard_map/ppermute | solution.py:45
  52.0 11.5 %collective-permute-start.5 = (f32[128,256]{1,0:T(8,128)S(1)}, f32[128,256]{1,0:T(8,128)S(1)}, u32[]{:S(2)}, u32[]{:S(2)}) collective-permute-start(f32[128,256]{1,0:T(8,128)S(1)} %get-tuple-element.22), channel_id=1, source_target_pairs={{0,1},{1,2},{2,3},{3,0},{4,5},{5,6},{6,7},{7,4},{8,9},{9,10},{10,1... | collective-permute-start | bytes 393224 | tf_op jit(solution)/shard_map/ppermute | solution.py:45
  57.3 6.2 %collective-permute-start.8 = (f32[1,128,256]{2,1,0:T(8,128)S(1)}, f32[1,128,256]{2,1,0:T(8,128)S(1)}, u32[]{:S(2)}, u32[]{:S(2)}) collective-permute-start(f32[1,128,256]{2,1,0:T(8,128)S(1)} %slice_add_fusion.2), channel_id=1, source_target_pairs={{0,16},{4,20},{8,24},{12,28},{16,0},{20,4},{24,8},{28,12},{1,17},{... | collective-permute-start | bytes 393224 | tf_op jit(solution)/shard_map/ppermute | solution.py:25

commit v15 on v12

--- a/solution.py
+++ b/solution.py
@@ -45,63 +45,62 @@
 
 
 def tile_kernel(srcs_ref, codes_ref, groups_ref, slots_ref, in_ref, core_ref, panel_ref,
-                keep_in_ref, send_in_ref, row_ref, keep_ref, send_ref, *, per_relay, block):
-    e = srcs_ref[pl.program_id(0)]
-
-    @pl.when(pl.program_id(0) == 0)
-    def _():
-        keep_ref[...] = keep_in_ref[...]
-        send_ref[...] = send_in_ref[...]
-
+                keep_in_ref, send_in_ref, row_ref, keep_ref, send_ref, *, per_relay, block, steps):
+    keep_ref[...] = keep_in_ref[...]
+    send_ref[...] = send_in_ref[...]
     nt = (((1,), (1,)), ((), ()))
     base = per_relay * block
-    own = jnp.concatenate(
-        [in_ref[0, base : base + block, :], in_ref[0, base + block : base + 2 * block, :]], axis=1
-    )
     half = keep_ref.shape[0]
-    codes = [codes_ref[e, j] for j in range(per_relay)]
-    rels = [c // 2 for c in codes]
-    groups = [groups_ref[e, j] for j in range(per_relay)]
-    mapped = [
-        jnp.dot(own, core_ref[r], preferred_element_type=jnp.float32).astype(jnp.bfloat16)
-        for r in rels
-    ]
-    predicted = [
-        lax.dot_general(m, panel_ref[g], nt, preferred_element_type=jnp.float32)
-        for m, g in zip(mapped, groups)
-    ]
-    resids = []
-    for j in range(per_relay):
-        scale = LOSS_SCALE * (codes[j] % 2).astype(jnp.float32)
-        adj = in_ref[0, j * block : (j + 1) * block, :].astype(jnp.float32)
-        resids.append(((predicted[j] - adj) * scale).astype(jnp.bfloat16))
-    products = [
-        jnp.dot(r, panel_ref[g], preferred_element_type=jnp.float32).astype(jnp.bfloat16)
-        for r, g in zip(resids, groups)
-    ]
-    columns = [
-        jnp.dot(
-            r.astype(jnp.float32).T.astype(jnp.bfloat16), m, preferred_element_type=jnp.float32
-        ).astype(jnp.bfloat16)
-        for r, m in zip(resids, mapped)
-    ]
-    acc = None
-    for p, r in zip(products, rels):
-        part = lax.dot_general(p, core_ref[r], nt, preferred_element_type=jnp.float32)
-        acc = part if acc is None else acc + part
-    for j, c in enumerate(columns):
-        slot = slots_ref[e, j]
-        column = c.astype(jnp.float32)
-
-        @pl.when(slot < half)
-        def _():
-            keep_ref[jnp.minimum(slot, half - 1)] += column
-
-        @pl.when(slot >= half)
-        def _():
-            send_ref[jnp.maximum(slot - half, 0)] += column
-
-    row_ref[0] = acc
+    for i in range(steps):
+        e = srcs_ref[i]
+        own = jnp.concatenate(
+            [in_ref[e, base : base + block, :], in_ref[e, base + block : base + 2 * block, :]],
+            axis=1,
+        )
+        codes = [codes_ref[e, j] for j in range(per_relay)]
+        rels = [c // 2 for c in codes]
+        groups = [groups_ref[e, j] for j in range(per_relay)]
+        mapped = [
+            jnp.dot(own, core_ref[r], preferred_element_type=jnp.float32).astype(jnp.bfloat16)
+            for r in rels
+        ]
+        predicted = [
+            lax.dot_general(m, panel_ref[g], nt, preferred_element_type=jnp.float32)
+            for m, g in zip(mapped, groups)
+        ]
+        resids = []
+        for j in range(per_relay):
+            scale = LOSS_SCALE * (codes[j] % 2).astype(jnp.float32)
+            adj = in_ref[e, j * block : (j + 1) * block, :].astype(jnp.float32)
+            resids.append(((predicted[j] - adj) * scale).astype(jnp.bfloat16))
+        products = [
+            jnp.dot(r, panel_ref[g], preferred_element_type=jnp.float32).astype(jnp.bfloat16)
+            for r, g in zip(resids, groups)
+        ]
+        columns = [
+            jnp.dot(
+                r.astype(jnp.float32).T.astype(jnp.bfloat16), m,
+                preferred_element_type=jnp.float32,
+            ).astype(jnp.bfloat16)
+            for r, m in zip(resids, mapped)
+        ]
+        acc = None
+        for p, r in zip(products, rels):
+            part = lax.dot_general(p, core_ref[r], nt, preferred_element_type=jnp.float32)
+            acc = part if acc is None else acc + part
+        for j, c in enumerate(columns):
+            slot = slots_ref[e, j]
+            column = c.astype(jnp.float32)
+
+            @pl.when(slot < half)
+            def _():
+                keep_ref[jnp.minimum(slot, half - 1)] += column
+
+            @pl.when(slot >= half)
+            def _():
+                send_ref[jnp.maximum(slot - half, 0)] += column
+
+        row_ref[i] = acc
 
 
 def on_device(factor, cores, adjacency, tile_rels, tile_count, send_lists):
@@ -156,19 +155,19 @@
         steps = srcs.shape[0]
         any_map = lambda i, *refs: (0, 0, 0)
         return pl.pallas_call(
-            lambda *refs: tile_kernel(*refs, per_relay=per_relay, block=block),
+            lambda *refs: tile_kernel(*refs, per_relay=per_relay, block=block, steps=steps),
             grid_spec=pltpu.PrefetchScalarGridSpec(
                 num_scalar_prefetch=4,
-                grid=(steps,),
+                grid=(1,),
                 in_specs=[
-                    pl.BlockSpec((1, rows_in, block), lambda i, e, c, g, s: (e[i], 0, 0)),
+                    pl.BlockSpec((ent_count, rows_in, block), any_map),
                     pl.BlockSpec(memory_space=pltpu.VMEM),
                     pl.BlockSpec(memory_space=pltpu.VMEM),
                     pl.BlockSpec((half, block, width), any_map),
                     pl.BlockSpec((half, block, width), any_map),
                 ],
                 out_specs=[
-                    pl.BlockSpec((1, block, width), lambda i, *refs: (i, 0, 0)),
+                    pl.BlockSpec((steps, block, width), any_map),
                     pl.BlockSpec((half, block, width), any_map),
                     pl.BlockSpec((half, block, width), any_map),
                 ],

time: 64.6 us -> 65.3 us (1.011)
  Pallas kernels: 12 us -> 13 us
    pallas_call x2, Pallas kernels: 12 us -> 13 us  [relay_tiles(): pl.pallas_call(lambda *refs: tile_kernel(*refs, per_relay=per_relay, bloc...]
where the time goes in v15:
time: 65.3 us; the launch traced here: 65 us
  waiting for transfers between devices  25.6 us (39%)
  starting transfers between devices  14.9 us (23%)
  Pallas kernels  13 us (20%)
  other arithmetic  7.88 us (12%)
  local copies, waits for them, and re-layouts  2.79 us (4%)
  between operations  0.77 us (1%)
    pallas_call x2, Pallas kernels, relay_tiles(): pl.pallas_call(lambda *refs: tile_kernel(*refs, per_relay=per_relay, bloc...  13 us
    ppermute x3, waiting for transfers between devices, grp_gather(): got = lax.ppermute(held, 'grp', [(i, i ^ bit) for i in range(grp_count)])  9.57 us
    all_to_all x1, starting transfers between devices, on_device(): lax.all_to_all(outgoing, 'ent', split_axis=0, concat_axis=0, tiled=True)  6.45 us
    all_to_all x1, waiting for transfers between devices, on_device(): lax.all_to_all(outgoing, 'ent', split_axis=0, concat_axis=0, tiled=True)  4.68 us
    ppermute x2, waiting for transfers between devices, grp_reduce_scatter(): lax.ppermute(parts[half:], 'grp', [(i, i ^ bit) for i in range(grp_count)])  4.68 us
    ppermute x3, waiting for transfers between devices, shift_ent(): lax.ppermute(x, 'ent', [(i, (i + shift) % ent_count) for i in range(ent_c...  4.54 us
    ppermute x3, starting transfers between devices, grp_gather(): got = lax.ppermute(held, 'grp', [(i, i ^ bit) for i in range(grp_count)])  3.14 us
    ppermute x2, starting transfers between devices, grp_reduce_scatter(): lax.ppermute(parts[half:], 'grp', [(i, i ^ bit) for i in range(grp_count)])  3.13 us
  transfers between devices with their start and end apart: 10, of which 7 were waited for; matrix products, arithmetic and copies ran while one was open for 6% of the time, Pallas kernels for 8%

profile of v15, /device:TPU:0, one launch (start us, length us, event | category | flops | bytes accessed | tf_op | source)
XLA Modules:
  0.0 65.0 jit_solution(10060363470103969414)
XLA Ops:
  0.0 0.0 copy-start
  0.0 0.1 broadcast_add_fusion
  0.1 0.1 compare_select_fusion
  0.2 0.1 copy.7
  0.3 1.0 %select_reduce_fusion = s32[4,6]{0,1:T(8,128)S(1)} fusion(s32[24]{0:T(128)} %bitcast.35, s32[4,6]{0,1:T(8,128)S(1)} %copy.7), kind=kLoop, calls=%fused_computation.16 | loop fusion | flops 1704 | bytes 288 | tf_op jit(solution)/shard_map/reduce_sum | solution.py:126
  1.3 0.1 copy.8
  2.0 0.1 convert_convert_fusion
  2.1 0.1 reshape.129
  2.2 0.0 copy-done
  2.2 0.7 %gather_fusion = s32[24,128,128]{2,1,0:T(8,128)S(1)} fusion(s32[24,128,128]{2,1,0:T(8,128)S(1)} %copy-done, s32[1024]{0:T(1024)S(1)} %pad_clamp_fusion), kind=kCustom, calls=%fused_computation | custom fusion | bytes 3145824 | tf_op jit(solution)/shard_map/gather | solution.py:122
  2.9 0.0 copy-start.3
  2.9 0.2 convert_element_type.42
  3.1 0.7 %copy-done.3 = bf16[128,256]{1,0:T(8,128)(2,1)S(1)} copy-done((bf16[128,256]{1,0:T(8,128)(2,1)S(1)}, bf16[128,256]{1,0:T(8,128)(2,1)}, u32[]{:S(2)}) %copy-start.3) | copy-done | bytes 65560
  3.7 0.1 fusion.9
  3.9 1.1 %pad_maximum_fusion.refs_4_ = bf16[4,1040,128]{2,1,0:T(8,128)(2,1)} fusion(bf16[4,16,128]{2,1,0:T(8,128)(2,1)S(1)} %broadcast_in_dim.41, bf16[4,256,128]{2,1,0:T(8,128)(2,1)S(1)} %broadcast_in_dim.40, bf16[4,768,128]{2,1,0:T(8,128)(2,1)S(1)} %bitcast.29), kind=kLoop, calls=%fused_computation.1 | loop fusion | flops 3194880 | bytes 2129920 | tf_op jit(solution)/shard_map/concatenate | solution.py:139
  4.9 0.0 copy-start.5
  4.9 6.4 %all-to-all-start = ((bf16[4,1040,128]{2,1,0:T(8,128)(2,1)}), bf16[4,1040,128]{2,1,0:T(8,128)(2,1)S(1)}, u32[]{:S(2)}, u32[]{:S(2)}) async-start(bf16[4,1040,128]{2,1,0:T(8,128)(2,1)} %pad_maximum_fusion.refs_4_), calls=%async_computation | async-start | bytes 2129920 | tf_op jit(solution)/shard_map/all_to_all | solution.py:142
  11.4 0.0 collective-permute-start
  11.4 1.3 %collective-permute-done = bf16[1,128,256]{2,1,0:T(8,128)(2,1)S(1)} collective-permute-done((bf16[1,128,256]{2,1,0:T(8,128)(2,1)S(1)}, bf16[1,128,256]{2,1,0:T(8,128)(2,1)S(1)}, u32[]{:S(2)}, u32[]{:S(2)}) %collective-permute-start) | collective-permute-done | bytes 65568 | tf_op jit(solution)/shard_map/ppermute | solution.py:34
  12.7 1.6 %collective-permute-start.1 = (bf16[2,128,256]{2,1,0:T(8,128)(2,1)S(1)}, bf16[2,128,256]{2,1,0:T(8,128)(2,1)S(1)}, u32[]{:S(2)}, u32[]{:S(2)}) collective-permute-start(bf16[2,128,256]{2,1,0:T(8,128)(2,1)S(1)} %maximum_select_fusion.2), channel_id=1, source_target_pairs={{0,8},{4,12},{8,0},{12,4},{16,24},{20,28},{24,16},{28,20},{1,9},{5... | collective-permute-start | bytes 393224 | tf_op jit(solution)/shard_map/ppermute | solution.py:34
  14.2 0.7 %add_convert_fusion.1.refs_1_ = s32[4,6]{1,0:T(4,128)} fusion(f32[4,128]{1,0:T(4,128)S(1)} %get-tuple-element.17), kind=kLoop, calls=%fused_computation.30 | loop fusion | flops 72 | bytes 288 | tf_op jit(solution)/shard_map/convert_element_type | solution.py:147
  14.9 3.4 %collective-permute-done.1 = bf16[2,128,256]{2,1,0:T(8,128)(2,1)S(1)} collective-permute-done((bf16[2,128,256]{2,1,0:T(8,128)(2,1)S(1)}, bf16[2,128,256]{2,1,0:T(8,128)(2,1)S(1)}, u32[]{:S(2)}, u32[]{:S(2)}) %collective-permute-start.1) | collective-permute-done | bytes 131104 | tf_op jit(solution)/shard_map/ppermute | solution.py:34
  18.3 1.6 %collective-permute-start.2 = (bf16[4,128,256]{2,1,0:T(8,128)(2,1)S(1)}, bf16[4,128,256]{2,1,0:T(8,128)(2,1)S(1)}, u32[]{:S(2)}, u32[]{:S(2)}) collective-permute-start(bf16[4,128,256]{2,1,0:T(8,128)(2,1)S(1)} %maximum_select_fusion.1), channel_id=1, source_target_pairs={{0,16},{4,20},{8,24},{12,28},{16,0},{20,4},{24,8},{28,12},{1,17},{... | collective-permute-start | bytes 786440 | tf_op jit(solution)/shard_map/ppermute | solution.py:34
  19.9 0.5 and_select_fusion.refs_0_
  20.4 0.0 copy-done.5
  20.4 0.6 shift-left_or_fusion.refs_3_
  21.0 4.9 %collective-permute-done.2 = bf16[4,128,256]{2,1,0:T(8,128)(2,1)S(1)} collective-permute-done((bf16[4,128,256]{2,1,0:T(8,128)(2,1)S(1)}, bf16[4,128,256]{2,1,0:T(8,128)(2,1)S(1)}, u32[]{:S(2)}, u32[]{:S(2)}) %collective-permute-start.2) | collective-permute-done | bytes 262176 | tf_op jit(solution)/shard_map/ppermute | solution.py:34
  25.9 0.9 %maximum_select_fusion.refs_6_ = bf16[8,128,256]{2,1,0:T(8,128)(2,1)} fusion(bf16[4,128,256]{2,1,0:T(8,128)(2,1)S(1)} %collective-permute-done.2, bf16[4,128,256]{2,1,0:T(8,128)(2,1)S(1)} %maximum_select_fusion.1, pred[]{:T(512)S(6)} %eq.33), kind=kLoop, calls=%fused_computation.2 | loop fusion | flops 786432 | bytes 1048577 | tf_op jit(solution)/shard_map/jit(_where)/select_n | solution.py:36
  26.8 0.8 %broadcast_in_dim.43.refs_7_.refs_8_ = f32[4,128,256]{2,1,0:T(8,128)} broadcast(f32[]{:T(128)} %constant.94.clone.1), dimensions={} | broadcast | bytes 524292 | tf_op jit(solution)/shard_map/broadcast_in_dim | solution.py:182
  27.6 5.1 %shard_map.64 = (f32[1,128,256]{2,1,0:T(8,128)}, f32[4,128,256]{2,1,0:T(8,128)}, f32[4,128,256]{2,1,0:T(8,128)}) custom-call(s32[1]{0:T(128)} %bitcast.refs_0_, s32[4,6]{1,0:T(4,128)} %add_convert_fusion.1.refs_1_, s32[4,6]{1,0:T(4,128)} %bitcast.32, s32[4,6]{1,0:T(4,128)} %shift-left_or_fusion.refs_3_, bf16[4,1040,128]{2,1,0:T(8,128)(2,1)} %pad_maximum_fusion.refs_4_, ...), custom_call_target="tpu_custom_call" | custom-call | tf_op jit(solution)/shard_map/pallas_call | solution.py:157
  32.8 4.7 %all-to-all-done.refs_4_ = bf16[4,1040,128]{2,1,0:T(8,128)(2,1)S(1)} async-done(((bf16[4,1040,128]{2,1,0:T(8,128)(2,1)}), bf16[4,1040,128]{2,1,0:T(8,128)(2,1)S(1)}, u32[]{:S(2)}, u32[]{:S(2)}) %all-to-all-start) | async-done | bytes 1064992 | tf_op jit(solution)/shard_map/all_to_all | solution.py:142
  37.5 0.0 copy-start.1
  37.5 0.7 %add_convert_fusion.refs_1_ = s32[4,6]{1,0:T(4,128)} fusion(f32[4,128]{1,0:T(4,128)S(1)} %bitcast.34), kind=kLoop, calls=%fused_computation.28 | loop fusion | flops 72 | bytes 288 | tf_op jit(solution)/shard_map/convert_element_type | solution.py:147
  38.2 0.2 copy-done.1
  38.5 7.9 %shard_map.65 = (f32[3,128,256]{2,1,0:T(8,128)}, f32[4,128,256]{2,1,0:T(8,128)}, f32[4,128,256]{2,1,0:T(8,128)}) custom-call(s32[3]{0:T(128)} %and_select_fusion.refs_0_, s32[4,6]{1,0:T(4,128)} %add_convert_fusion.refs_1_, s32[4,6]{1,0:T(4,128)} %bitcast.33, s32[4,6]{1,0:T(4,128)} %shift-left_or_fusion.refs_3_, bf16[4,1040,128]{2,1,0:T(8,128)(2,1)} %copy-done.1, ...), custom_call_target="tpu_custom_call" | custom-call | tf_op jit(solution)/shard_map/pallas_call | solution.py:157
  46.4 0.0 copy-start.2
  46.4 0.0 collective-permute-start.6
  46.4 2.1 %collective-permute-done.6 = f32[4,128,256]{2,1,0:T(8,128)S(1)} collective-permute-done((f32[4,128,256]{2,1,0:T(8,128)}, f32[4,128,256]{2,1,0:T(8,128)S(1)}, u32[]{:S(2)}, u32[]{:S(2)}) %collective-permute-start.6) | collective-permute-done | bytes 524320 | tf_op jit(solution)/shard_map/ppermute | solution.py:19
  48.5 1.1 %add.119 = f32[4,128,256]{2,1,0:T(8,128)S(1)} add(f32[4,128,256]{2,1,0:T(8,128)} %get-tuple-element.15, f32[4,128,256]{2,1,0:T(8,128)S(1)} %collective-permute-done.6) | non-fusion elementwise | flops 131072 | bytes 1572864 | tf_op jit(solution)/shard_map/add | solution.py:19
  49.6 0.0 copy-start.4
  49.7 1.6 %collective-permute-start.7 = (f32[2,128,256]{2,1,0:T(8,128)S(1)}, f32[2,128,256]{2,1,0:T(8,128)S(1)}, u32[]{:S(2)}, u32[]{:S(2)}) collective-permute-start(f32[2,128,256]{2,1,0:T(8,128)S(1)} %slice.61), channel_id=1, source_target_pairs={{0,8},{4,12},{8,0},{12,4},{16,24},{20,28},{24,16},{28,20},{1,9},{5... | collective-permute-start | bytes 786440 | tf_op jit(solution)/shard_map/ppermute | solution.py:23
  51.2 0.0 copy-done.2
  51.2 1.5 %collective-permute-start.3 = (f32[128,256]{1,0:T(8,128)S(1)}, f32[128,256]{1,0:T(8,128)S(1)}, u32[]{:S(2)}, u32[]{:S(2)}) collective-permute-start(f32[128,256]{1,0:T(8,128)S(1)} %get-tuple-element.19), channel_id=1, source_target_pairs={{0,3},{1,0},{2,1},{3,2},{4,7},{5,4},{6,5},{7,6},{8,11},{9,8},{10,9... | collective-permute-start | bytes 393224 | tf_op jit(solution)/shard_map/ppermute | solution.py:44
  52.8 0.0 collective-permute-start.4
  52.8 0.6 collective-permute-start.5
  53.4 4.7 %collective-permute-done.7 = f32[2,128,256]{2,1,0:T(8,128)S(1)} collective-permute-done((f32[2,128,256]{2,1,0:T(8,128)S(1)}, f32[2,128,256]{2,1,0:T(8,128)S(1)}, u32[]{:S(2)}, u32[]{:S(2)}) %collective-permute-start.7) | collective-permute-done | bytes 262176 | tf_op jit(solution)/shard_map/ppermute | solution.py:23
  58.1 1.6 %collective-permute-start.8 = (f32[1,128,256]{2,1,0:T(8,128)S(1)}, f32[1,128,256]{2,1,0:T(8,128)S(1)}, u32[]{:S(2)}, u32[]{:S(2)}) collective-permute-start(f32[1,128,256]{2,1,0:T(8,128)S(1)} %slice.63), channel_id=1, source_target_pairs={{0,16},{4,20},{8,24},{12,28},{16,0},{20,4},{24,8},{28,12},{1,17},{... | collective-permute-start | bytes 393224 | tf_op jit(solution)/shard_map/ppermute | solution.py:23
  59.7 0.0 collective-permute-done.3
  59.7 4.5 %collective-permute-done.4 = f32[128,256]{1,0:T(8,128)S(1)} collective-permute-done((f32[128,256]{1,0:T(8,128)S(1)}, f32[128,256]{1,0:T(8,128)S(1)}, u32[]{:S(2)}, u32[]{:S(2)}) %collective-permute-start.4) | collective-permute-done | bytes 131104 | tf_op jit(solution)/shard_map/ppermute | solution.py:44
  64.2 0.0 collective-permute-done.5
  64.2 0.0 collective-permute-done.8
  64.3 0.0 copy-done.4
  64.3 0.7 %fusion.1 = f32[128,256]{1,0:T(8,128)} fusion(f32[1,128,256]{2,1,0:T(8,128)S(1)} %collective-permute-done.8, f32[2,128,256]{2,1,0:T(8,128)S(1)} %slice_add_fusion, f32[128,256]{1,0:T(8,128)S(1)} %collective-permute-done.5, f32[128,256]{1,0:T(8,128)S(1)} %collective-permute-done.4, f32[128,256]{1,0:T(8,128)S(1)} %collective-permute-done.3, ...), kind=kLoop, calls=%fused_computation.7 | loop fusion | flops 163840 | bytes 917504 | tf_op jit(solution)/shard_map/add | solution.py:193
  (15 shorter events, 0.2 us)
Async XLA Ops:
  0.0 2.2 %copy-start = (s32[24,128,128]{2,1,0:T(8,128)S(1)}, s32[24,128,128]{2,1,0:T(8,128)}, u32[]{:S(2)}) copy-start(s32[24,128,128]{2,1,0:T(8,128)} %param.8) | copy-start | bytes 4718596
  2.9 0.8 %copy-start.3 = (bf16[128,256]{1,0:T(8,128)(2,1)S(1)}, bf16[128,256]{1,0:T(8,128)(2,1)}, u32[]{:S(2)}) copy-start(bf16[128,256]{1,0:T(8,128)(2,1)} %param.6) | copy-start | bytes 196612
  4.9 15.5 %copy-start.5 = (s32[1,4,6]{2,1,0:T(4,128)S(1)}, s32[1,4,6]{2,1,0:T(4,128)}, u32[]{:S(2)}) copy-start(s32[1,4,6]{2,1,0:T(4,128)} %param.11) | copy-start | bytes 292
  4.9 32.5 %all-to-all-start = ((bf16[4,1040,128]{2,1,0:T(8,128)(2,1)}), bf16[4,1040,128]{2,1,0:T(8,128)(2,1)S(1)}, u32[]{:S(2)}, u32[]{:S(2)}) async-start(bf16[4,1040,128]{2,1,0:T(8,128)(2,1)} %pad_maximum_fusion.refs_4_), calls=%async_computation | async-start | bytes 2129920 | tf_op jit(solution)/shard_map/all_to_all | solution.py:142
  11.4 1.3 %collective-permute-start = (bf16[1,128,256]{2,1,0:T(8,128)(2,1)S(1)}, bf16[1,128,256]{2,1,0:T(8,128)(2,1)S(1)}, u32[]{:S(2)}, u32[]{:S(2)}) collective-permute-start(bf16[1,128,256]{2,1,0:T(8,128)(2,1)S(1)} %bitcast.30), channel_id=1, source_target_pairs={{0,4},{4,0},{8,12},{12,8},{16,20},{20,16},{24,28},{28,24},{1,5},{5... | collective-permute-start | bytes 196616 | tf_op jit(solution)/shard_map/ppermute | solution.py:34
  12.7 5.6 %collective-permute-start.1 = (bf16[2,128,256]{2,1,0:T(8,128)(2,1)S(1)}, bf16[2,128,256]{2,1,0:T(8,128)(2,1)S(1)}, u32[]{:S(2)}, u32[]{:S(2)}) collective-permute-start(bf16[2,128,256]{2,1,0:T(8,128)(2,1)S(1)} %maximum_select_fusion.2), channel_id=1, source_target_pairs={{0,8},{4,12},{8,0},{12,4},{16,24},{20,28},{24,16},{28,20},{1,9},{5... | collective-permute-start | bytes 393224 | tf_op jit(solution)/shard_map/ppermute | solution.py:34
  18.3 7.6 %collective-permute-start.2 = (bf16[4,128,256]{2,1,0:T(8,128)(2,1)S(1)}, bf16[4,128,256]{2,1,0:T(8,128)(2,1)S(1)}, u32[]{:S(2)}, u32[]{:S(2)}) collective-permute-start(bf16[4,128,256]{2,1,0:T(8,128)(2,1)S(1)} %maximum_select_fusion.1), channel_id=1, source_target_pairs={{0,16},{4,20},{8,24},{12,28},{16,0},{20,4},{24,8},{28,12},{1,17},{... | collective-permute-start | bytes 786440 | tf_op jit(solution)/shard_map/ppermute | solution.py:34
  37.5 1.0 %copy-start.1 = (bf16[4,1040,128]{2,1,0:T(8,128)(2,1)}, bf16[4,1040,128]{2,1,0:T(8,128)(2,1)S(1)}, u32[]{:S(2)}) copy-start(bf16[4,1040,128]{2,1,0:T(8,128)(2,1)S(1)} %all-to-all-done.refs_4_) | copy-start | bytes 3194884
  46.4 4.8 %copy-start.2 = (f32[3,128,256]{2,1,0:T(8,128)S(1)}, f32[3,128,256]{2,1,0:T(8,128)}, u32[]{:S(2)}) copy-start(f32[3,128,256]{2,1,0:T(8,128)} %get-tuple-element.14) | copy-start | bytes 1179652
  46.4 2.1 %collective-permute-start.6 = (f32[4,128,256]{2,1,0:T(8,128)}, f32[4,128,256]{2,1,0:T(8,128)S(1)}, u32[]{:S(2)}, u32[]{:S(2)}) collective-permute-start(f32[4,128,256]{2,1,0:T(8,128)} %get-tuple-element.16), channel_id=1, source_target_pairs={{0,4},{4,0},{8,12},{12,8},{16,20},{20,16},{24,28},{28,24},{1,5},{5... | collective-permute-start | bytes 1572872 | tf_op jit(solution)/shard_map/ppermute | solution.py:19
  49.6 14.6 %copy-start.4 = (f32[1,128,256]{2,1,0:T(8,128)S(1)}, f32[1,128,256]{2,1,0:T(8,128)}, u32[]{:S(2)}) copy-start(f32[1,128,256]{2,1,0:T(8,128)} %get-tuple-element.11) | copy-start | bytes 393220
  49.7 8.4 %collective-permute-start.7 = (f32[2,128,256]{2,1,0:T(8,128)S(1)}, f32[2,128,256]{2,1,0:T(8,128)S(1)}, u32[]{:S(2)}, u32[]{:S(2)}) collective-permute-start(f32[2,128,256]{2,1,0:T(8,128)S(1)} %slice.61), channel_id=1, source_target_pairs={{0,8},{4,12},{8,0},{12,4},{16,24},{20,28},{24,16},{28,20},{1,9},{5... | collective-permute-start | bytes 786440 | tf_op jit(solution)/shard_map/ppermute | solution.py:23
  51.2 8.5 %collective-permute-start.3 = (f32[128,256]{1,0:T(8,128)S(1)}, f32[128,256]{1,0:T(8,128)S(1)}, u32[]{:S(2)}, u32[]{:S(2)}) collective-permute-start(f32[128,256]{1,0:T(8,128)S(1)} %get-tuple-element.19), channel_id=1, source_target_pairs={{0,3},{1,0},{2,1},{3,2},{4,7},{5,4},{6,5},{7,6},{8,11},{9,8},{10,9... | collective-permute-start | bytes 393224 | tf_op jit(solution)/shard_map/ppermute | solution.py:44
  52.8 11.5 %collective-permute-start.4 = (f32[128,256]{1,0:T(8,128)S(1)}, f32[128,256]{1,0:T(8,128)S(1)}, u32[]{:S(2)}, u32[]{:S(2)}) collective-permute-start(f32[128,256]{1,0:T(8,128)S(1)} %get-tuple-element.21), channel_id=1, source_target_pairs={{0,2},{1,3},{2,0},{3,1},{4,6},{5,7},{6,4},{7,5},{8,10},{9,11},{10,... | collective-permute-start | bytes 393224 | tf_op jit(solution)/shard_map/ppermute | solution.py:44
  52.8 11.5 %collective-permute-start.5 = (f32[128,256]{1,0:T(8,128)S(1)}, f32[128,256]{1,0:T(8,128)S(1)}, u32[]{:S(2)}, u32[]{:S(2)}) collective-permute-start(f32[128,256]{1,0:T(8,128)S(1)} %get-tuple-element.20), channel_id=1, source_target_pairs={{0,1},{1,2},{2,3},{3,0},{4,5},{5,6},{6,7},{7,4},{8,9},{9,10},{10,1... | collective-permute-start | bytes 393224 | tf_op jit(solution)/shard_map/ppermute | solution.py:44
  58.1 6.1 %collective-permute-start.8 = (f32[1,128,256]{2,1,0:T(8,128)S(1)}, f32[1,128,256]{2,1,0:T(8,128)S(1)}, u32[]{:S(2)}, u32[]{:S(2)}) collective-permute-start(f32[1,128,256]{2,1,0:T(8,128)S(1)} %slice.63), channel_id=1, source_target_pairs={{0,16},{4,20},{8,24},{12,28},{16,0},{20,4},{24,8},{28,12},{1,17},{... | collective-permute-start | bytes 393224 | tf_op jit(solution)/shard_map/ppermute | solution.py:23

commit v16 on v11

--- a/solution.py
+++ b/solution.py
@@ -104,6 +104,23 @@
     row_ref[0] = acc
 
 
+def build_kernel(tile_ref, rels_ref, count_ref, adj_ref, factor_ref, out_ref, *, per_relay,
+                 block):
+    u = pl.program_id(0)
+    base = per_relay * block
+    lane = lax.broadcasted_iota(jnp.int32, (16, block), 1)
+    head = jnp.zeros((16, block), jnp.float32)
+    for j in range(per_relay):
+        t = tile_ref[u * per_relay + j]
+        out_ref[0, j * block : (j + 1) * block, :] = adj_ref[t].astype(jnp.bfloat16)
+        head = jnp.where(lane == j, rels_ref[t].astype(jnp.float32), head)
+        live = (t < count_ref[0]).astype(jnp.float32)
+        head = jnp.where(lane == per_relay + j, live, head)
+    out_ref[0, base : base + block, :] = factor_ref[:, :block]
+    out_ref[0, base + block : base + 2 * block, :] = factor_ref[:, block:]
+    out_ref[0, base + 2 * block :, :] = head.astype(jnp.bfloat16)
+
+
 def on_device(factor, cores, adjacency, tile_rels, tile_count, send_lists):
     ent_count = lax.axis_size("ent")
     grp_count = lax.axis_size("grp")
@@ -120,18 +137,20 @@
     relay_ids = jnp.arange(ent_count, dtype=jnp.int32)
     slot_ids = jnp.arange(per_relay, dtype=jnp.int32)
     tile_of = slot_ids[None, :] * ent_count + (relay_ids[:, None] - my_ent) % ent_count
-    adj_out = adjacency[tile_of].astype(jnp.bfloat16).reshape(ent_count, per_relay * block, block)
-    halves = jnp.concatenate([factor[:, :block], factor[:, block:]], axis=0)
-    head = jnp.concatenate(
-        [tile_rels.reshape(tiles)[tile_of].astype(jnp.float32),
-         (tile_of < tile_count.reshape(())).astype(jnp.float32)],
-        axis=1,
-    )
-    head = jnp.pad(head, ((0, 0), (0, block - 2 * per_relay)))
-    head = jnp.broadcast_to(head[:, None, :], (ent_count, head_rows, block)).astype(jnp.bfloat16)
-    outgoing = jnp.concatenate(
-        [adj_out, jnp.broadcast_to(halves[None], (ent_count,) + halves.shape), head], axis=1
-    )
+    rows_out = per_relay * block + 2 * block + head_rows
+    outgoing = pl.pallas_call(
+        lambda *refs: build_kernel(*refs, per_relay=per_relay, block=block),
+        grid_spec=pltpu.PrefetchScalarGridSpec(
+            num_scalar_prefetch=3,
+            grid=(ent_count,),
+            in_specs=[
+                pl.BlockSpec((tiles, block, block), lambda u, *refs: (0, 0, 0)),
+                pl.BlockSpec((block, width), lambda u, *refs: (0, 0)),
+            ],
+            out_specs=pl.BlockSpec((1, rows_out, block), lambda u, *refs: (u, 0, 0)),
+        ),
+        out_shape=jax.ShapeDtypeStruct((ent_count, rows_out, block), jnp.bfloat16),
+    )(tile_of.reshape(count), tile_rels.reshape(tiles), tile_count.reshape(1), adjacency, factor)
     arrived = lax.all_to_all(outgoing, "ent", split_axis=0, concat_axis=0, tiled=True)
     group_blocks = grp_gather(factor, grp_count)
 

time: 64.9 us -> 64.7 us (level)
  Pallas kernels: 12.1 us -> 15.7 us
  local copies, waits for them, and re-layouts: 4.14 us -> 2.41 us
  other arithmetic: 6.86 us -> 5.51 us
  waiting for transfers between devices: 25.8 us -> 25 us
    pallas_call x0 -> x1, Pallas kernels: none -> 3.68 us  [on_device(): pl.pallas_call(lambda *refs: build_kernel(*refs, per_relay=per_relay, blo...]
    gather x2 -> x0, local copies, waits for them, and re-layouts: 2.1 us -> none  [the longest x1 1.45 us: on_device(): tile_rels.reshape(tiles)[tile_of].astype(jnp.float32)]
    concatenate x2 -> x0, other arithmetic: 1.08 us -> none  [the longest x1 1.08 us: on_device(): jnp.concatenate([adj_out, jnp.broadcast_to(halves[None], (ent_count,) + h...]
    all_to_all x1, waiting for transfers between devices: 4.93 us -> 4.13 us  [on_device(): lax.all_to_all(outgoing, 'ent', split_axis=0, concat_axis=0, tiled=True)]
    unnamed x12 -> x10, local copies, waits for them, and re-layouts: 0.93 us -> 0.22 us
    slice x1, local copies, waits for them, and re-layouts: 0.01 us -> 0.7 us  [codes_of(): heads = buf[:, -head_rows].astype(jnp.float32)]
  transfers between devices with their start and end apart: 10 -> 10, of which waited for: 7 -> 6; matrix products, arithmetic and copies ran while one was open for 6% -> 7% of each run, Pallas kernels for 8% -> 8%
where the time goes in v16:
time: 64.7 us; the launch traced here: 64.3 us
  waiting for transfers between devices  25 us (39%)
  Pallas kernels  15.7 us (24%)
  starting transfers between devices  15 us (23%)
  other arithmetic  5.51 us (9%)
  local copies, waits for them, and re-layouts  2.41 us (4%)
  between operations  0.74 us (1%)
    pallas_call x2, Pallas kernels, relay_tiles(): pl.pallas_call(lambda *refs: tile_kernel(*refs, per_relay=per_relay, bloc...  12 us
    ppermute x3, waiting for transfers between devices, grp_gather(): got = lax.ppermute(held, 'grp', [(i, i ^ bit) for i in range(grp_count)])  9.55 us
    all_to_all x1, starting transfers between devices, on_device(): lax.all_to_all(outgoing, 'ent', split_axis=0, concat_axis=0, tiled=True)  6.45 us
    ppermute x2, waiting for transfers between devices, grp_reduce_scatter(): lax.ppermute(parts[half:], 'grp', [(i, i ^ bit) for i in range(grp_count)])  4.67 us
    ppermute x3, waiting for transfers between devices, shift_ent(): lax.ppermute(x, 'ent', [(i, (i + shift) % ent_count) for i in range(ent_c...  4.54 us
    all_to_all x1, waiting for transfers between devices, on_device(): lax.all_to_all(outgoing, 'ent', split_axis=0, concat_axis=0, tiled=True)  4.13 us
    pallas_call x1, Pallas kernels, on_device(): pl.pallas_call(lambda *refs: build_kernel(*refs, per_relay=per_relay, blo...  3.68 us
    ppermute x3, starting transfers between devices, grp_gather(): got = lax.ppermute(held, 'grp', [(i, i ^ bit) for i in range(grp_count)])  3.14 us
  transfers between devices with their start and end apart: 10, of which 6 were waited for; matrix products, arithmetic and copies ran while one was open for 7% of the time, Pallas kernels for 8%

profile of v16, /device:TPU:0, one launch (start us, length us, event | category | flops | bytes accessed | tf_op | source)
XLA Modules:
  0.0 64.3 jit_solution(18320440848525194883)
XLA Ops:
  0.0 0.1 broadcast_add_fusion
  0.1 0.6 add.81.refs_0_
  1.3 3.7 %shard_map.64.refs_4_ = bf16[4,1040,128]{2,1,0:T(8,128)(2,1)} custom-call(s32[24]{0:T(128)} %add.81.refs_0_, s32[24]{0:T(128)} %bitcast.34, s32[1]{0:T(128)S(6)} %copy.12.refs_2_, s32[24,128,128]{2,1,0:T(8,128)} %refs_3_.1, bf16[128,256]{1,0:T(8,128)(2,1)} %refs_4_.1), custom_call_target="tpu_custom_call" | custom-call | tf_op jit(solution)/shard_map/pallas_call | solution.py:141
  5.0 0.0 copy-start.2
  5.0 0.0 copy-start.4
  5.0 6.4 %all-to-all-start = ((bf16[4,1040,128]{2,1,0:T(8,128)(2,1)}), bf16[4,1040,128]{2,1,0:T(8,128)(2,1)S(1)}, u32[]{:S(2)}, u32[]{:S(2)}) async-start(bf16[4,1040,128]{2,1,0:T(8,128)(2,1)} %shard_map.64.refs_4_), calls=%async_computation | async-start | bytes 2129920 | tf_op jit(solution)/shard_map/all_to_all | solution.py:154
  11.5 0.0 copy-done.2
  11.5 0.0 collective-permute-start
  11.5 0.0 copy-done.4
  11.5 0.6 shift-left_or_fusion.refs_3_
  12.1 0.7 %slice.52 = bf16[4,1,128]{2,1,0:T(2,128)(2,1)S(1)} slice(bf16[4,1040,128]{2,1,0:T(8,128)(2,1)} %shard_map.64.refs_4_), slice={[0:4], [1024:1025], [0:128]} | slice | bytes 2048 | tf_op jit(solution)/shard_map/slice | solution.py:158
  12.8 0.0 collective-permute-done
  12.8 1.6 %collective-permute-start.1 = (bf16[2,128,256]{2,1,0:T(8,128)(2,1)S(1)}, bf16[2,128,256]{2,1,0:T(8,128)(2,1)S(1)}, u32[]{:S(2)}, u32[]{:S(2)}) collective-permute-start(bf16[2,128,256]{2,1,0:T(8,128)(2,1)S(1)} %maximum_select_fusion.2), channel_id=1, source_target_pairs={{0,8},{4,12},{8,0},{12,4},{16,24},{20,28},{24,16},{28,20},{1,9},{5... | collective-permute-start | bytes 393224 | tf_op jit(solution)/shard_map/ppermute | solution.py:34
  14.4 4.4 %collective-permute-done.1 = bf16[2,128,256]{2,1,0:T(8,128)(2,1)S(1)} collective-permute-done((bf16[2,128,256]{2,1,0:T(8,128)(2,1)S(1)}, bf16[2,128,256]{2,1,0:T(8,128)(2,1)S(1)}, u32[]{:S(2)}, u32[]{:S(2)}) %collective-permute-start.1) | collective-permute-done | bytes 131104 | tf_op jit(solution)/shard_map/ppermute | solution.py:34
  18.8 1.6 %collective-permute-start.2 = (bf16[4,128,256]{2,1,0:T(8,128)(2,1)S(1)}, bf16[4,128,256]{2,1,0:T(8,128)(2,1)S(1)}, u32[]{:S(2)}, u32[]{:S(2)}) collective-permute-start(bf16[4,128,256]{2,1,0:T(8,128)(2,1)S(1)} %maximum_select_fusion.1), channel_id=1, source_target_pairs={{0,16},{4,20},{8,24},{12,28},{16,0},{20,4},{24,8},{28,12},{1,17},{... | collective-permute-start | bytes 786440 | tf_op jit(solution)/shard_map/ppermute | solution.py:34
  20.4 0.6 and_select_fusion.refs_0_
  21.0 0.7 %add_convert_fusion.1.refs_1_ = s32[4,6]{1,0:T(4,128)} fusion(f32[4,128]{1,0:T(4,128)S(1)} %fusion.4), kind=kLoop, calls=%fused_computation.20 | loop fusion | flops 72 | bytes 288 | tf_op jit(solution)/shard_map/convert_element_type | solution.py:159
  21.6 5.2 %collective-permute-done.2 = bf16[4,128,256]{2,1,0:T(8,128)(2,1)S(1)} collective-permute-done((bf16[4,128,256]{2,1,0:T(8,128)(2,1)S(1)}, bf16[4,128,256]{2,1,0:T(8,128)(2,1)S(1)}, u32[]{:S(2)}, u32[]{:S(2)}) %collective-permute-start.2) | collective-permute-done | bytes 262176 | tf_op jit(solution)/shard_map/ppermute | solution.py:34
  26.8 0.9 %maximum_select_fusion.refs_6_ = bf16[8,128,256]{2,1,0:T(8,128)(2,1)} fusion(bf16[4,128,256]{2,1,0:T(8,128)(2,1)S(1)} %collective-permute-done.2, bf16[4,128,256]{2,1,0:T(8,128)(2,1)S(1)} %maximum_select_fusion.1, pred[]{:T(512)S(6)} %eq.17), kind=kLoop, calls=%fused_computation | loop fusion | flops 786432 | bytes 1048577 | tf_op jit(solution)/shard_map/jit(_where)/select_n | solution.py:36
  27.7 0.8 %broadcast_in_dim.9.refs_7_.refs_8_ = f32[4,128,256]{2,1,0:T(8,128)} broadcast(f32[]{:T(128)} %constant.89.clone.1), dimensions={} | broadcast | bytes 524292 | tf_op jit(solution)/shard_map/broadcast_in_dim | solution.py:194
  28.5 4.9 %shard_map.65 = (f32[1,128,256]{2,1,0:T(8,128)}, f32[4,128,256]{2,1,0:T(8,128)}, f32[4,128,256]{2,1,0:T(8,128)}) custom-call(s32[1]{0:T(128)} %bitcast.refs_0_, s32[4,6]{1,0:T(4,128)} %add_convert_fusion.1.refs_1_, s32[4,6]{1,0:T(4,128)} %bitcast.31, s32[4,6]{1,0:T(4,128)} %shift-left_or_fusion.refs_3_, bf16[4,1040,128]{2,1,0:T(8,128)(2,1)} %shard_map.64.refs_4_, ...), custom_call_target="tpu_custom_call" | custom-call | tf_op jit(solution)/shard_map/pallas_call | solution.py:169
  33.4 4.1 %all-to-all-done.refs_4_ = bf16[4,1040,128]{2,1,0:T(8,128)(2,1)S(1)} async-done(((bf16[4,1040,128]{2,1,0:T(8,128)(2,1)}), bf16[4,1040,128]{2,1,0:T(8,128)(2,1)S(1)}, u32[]{:S(2)}, u32[]{:S(2)}) %all-to-all-start) | async-done | bytes 1064992 | tf_op jit(solution)/shard_map/all_to_all | solution.py:154
  37.5 0.0 copy-start
  37.6 0.8 %add_convert_fusion.refs_1_ = s32[4,6]{1,0:T(4,128)} fusion(f32[4,128]{1,0:T(4,128)S(1)} %bitcast.33), kind=kLoop, calls=%fused_computation.18 | loop fusion | flops 72 | bytes 288 | tf_op jit(solution)/shard_map/convert_element_type | solution.py:159
  38.3 0.2 copy-done
  38.5 7.1 %shard_map.66 = (f32[3,128,256]{2,1,0:T(8,128)}, f32[4,128,256]{2,1,0:T(8,128)}, f32[4,128,256]{2,1,0:T(8,128)}) custom-call(s32[3]{0:T(128)} %and_select_fusion.refs_0_, s32[4,6]{1,0:T(4,128)} %add_convert_fusion.refs_1_, s32[4,6]{1,0:T(4,128)} %bitcast.32, s32[4,6]{1,0:T(4,128)} %shift-left_or_fusion.refs_3_, bf16[4,1040,128]{2,1,0:T(8,128)(2,1)} %copy-done, ...), custom_call_target="tpu_custom_call" | custom-call | tf_op jit(solution)/shard_map/pallas_call | solution.py:169
  45.7 0.0 copy-start.1
  45.7 0.1 collective-permute-start.6
  45.8 2.1 %collective-permute-done.6 = f32[4,128,256]{2,1,0:T(8,128)S(1)} collective-permute-done((f32[4,128,256]{2,1,0:T(8,128)}, f32[4,128,256]{2,1,0:T(8,128)S(1)}, u32[]{:S(2)}, u32[]{:S(2)}) %collective-permute-start.6) | collective-permute-done | bytes 524320 | tf_op jit(solution)/shard_map/ppermute | solution.py:19
  47.9 1.1 %add.92 = f32[4,128,256]{2,1,0:T(8,128)S(1)} add(f32[4,128,256]{2,1,0:T(8,128)} %get-tuple-element.15, f32[4,128,256]{2,1,0:T(8,128)S(1)} %collective-permute-done.6) | non-fusion elementwise | flops 131072 | bytes 1572864 | tf_op jit(solution)/shard_map/add | solution.py:19
  49.0 0.0 copy-start.3
  49.0 1.6 %collective-permute-start.7 = (f32[2,128,256]{2,1,0:T(8,128)S(1)}, f32[2,128,256]{2,1,0:T(8,128)S(1)}, u32[]{:S(2)}, u32[]{:S(2)}) collective-permute-start(f32[2,128,256]{2,1,0:T(8,128)S(1)} %slice.55), channel_id=1, source_target_pairs={{0,8},{4,12},{8,0},{12,4},{16,24},{20,28},{24,16},{28,20},{1,9},{5... | collective-permute-start | bytes 786440 | tf_op jit(solution)/shard_map/ppermute | solution.py:23
  50.6 0.0 copy-done.1
  50.6 1.5 %collective-permute-start.3 = (f32[128,256]{1,0:T(8,128)S(1)}, f32[128,256]{1,0:T(8,128)S(1)}, u32[]{:S(2)}, u32[]{:S(2)}) collective-permute-start(f32[128,256]{1,0:T(8,128)S(1)} %get-tuple-element.17), channel_id=1, source_target_pairs={{0,3},{1,0},{2,1},{3,2},{4,7},{5,4},{6,5},{7,6},{8,11},{9,8},{10,9... | collective-permute-start | bytes 393224 | tf_op jit(solution)/shard_map/ppermute | solution.py:44
  52.1 0.0 collective-permute-start.4
  52.1 0.6 collective-permute-start.5
  52.8 4.7 %collective-permute-done.7 = f32[2,128,256]{2,1,0:T(8,128)S(1)} collective-permute-done((f32[2,128,256]{2,1,0:T(8,128)S(1)}, f32[2,128,256]{2,1,0:T(8,128)S(1)}, u32[]{:S(2)}, u32[]{:S(2)}) %collective-permute-start.7) | collective-permute-done | bytes 262176 | tf_op jit(solution)/shard_map/ppermute | solution.py:23
  57.5 1.6 %collective-permute-start.8 = (f32[1,128,256]{2,1,0:T(8,128)S(1)}, f32[1,128,256]{2,1,0:T(8,128)S(1)}, u32[]{:S(2)}, u32[]{:S(2)}) collective-permute-start(f32[1,128,256]{2,1,0:T(8,128)S(1)} %slice.57), channel_id=1, source_target_pairs={{0,16},{4,20},{8,24},{12,28},{16,0},{20,4},{24,8},{28,12},{1,17},{... | collective-permute-start | bytes 393224 | tf_op jit(solution)/shard_map/ppermute | solution.py:23
  59.1 0.0 collective-permute-done.3
  59.1 4.5 %collective-permute-done.4 = f32[128,256]{1,0:T(8,128)S(1)} collective-permute-done((f32[128,256]{1,0:T(8,128)S(1)}, f32[128,256]{1,0:T(8,128)S(1)}, u32[]{:S(2)}, u32[]{:S(2)}) %collective-permute-start.4) | collective-permute-done | bytes 131104 | tf_op jit(solution)/shard_map/ppermute | solution.py:44
  63.6 0.0 collective-permute-done.5
  63.6 0.0 collective-permute-done.8
  63.6 0.0 copy-done.3
  63.6 0.7 %fusion.1 = f32[128,256]{1,0:T(8,128)} fusion(f32[1,128,256]{2,1,0:T(8,128)S(1)} %collective-permute-done.8, f32[2,128,256]{2,1,0:T(8,128)S(1)} %slice_add_fusion, f32[128,256]{1,0:T(8,128)S(1)} %collective-permute-done.5, f32[128,256]{1,0:T(8,128)S(1)} %collective-permute-done.4, f32[128,256]{1,0:T(8,128)S(1)} %collective-permute-done.3, ...), kind=kLoop, calls=%fused_computation.5 | loop fusion | flops 163840 | bytes 917504 | tf_op jit(solution)/shard_map/add | solution.py:205
  (10 shorter events, 0.1 us)
Async XLA Ops:
  5.0 6.5 %copy-start.2 = (bf16[128,256]{1,0:T(8,128)(2,1)S(1)}, bf16[128,256]{1,0:T(8,128)(2,1)}, u32[]{:S(2)}) copy-start(bf16[128,256]{1,0:T(8,128)(2,1)} %refs_4_.1) | copy-start | bytes 196612
  5.0 6.5 %copy-start.4 = (s32[1,4,6]{2,1,0:T(4,128)S(1)}, s32[1,4,6]{2,1,0:T(4,128)}, u32[]{:S(2)}) copy-start(s32[1,4,6]{2,1,0:T(4,128)} %param.11) | copy-start | bytes 292
  5.0 32.5 %all-to-all-start = ((bf16[4,1040,128]{2,1,0:T(8,128)(2,1)}), bf16[4,1040,128]{2,1,0:T(8,128)(2,1)S(1)}, u32[]{:S(2)}, u32[]{:S(2)}) async-start(bf16[4,1040,128]{2,1,0:T(8,128)(2,1)} %shard_map.64.refs_4_), calls=%async_computation | async-start | bytes 2129920 | tf_op jit(solution)/shard_map/all_to_all | solution.py:154
  11.5 1.3 %collective-permute-start = (bf16[1,128,256]{2,1,0:T(8,128)(2,1)S(1)}, bf16[1,128,256]{2,1,0:T(8,128)(2,1)S(1)}, u32[]{:S(2)}, u32[]{:S(2)}) collective-permute-start(bf16[1,128,256]{2,1,0:T(8,128)(2,1)S(1)} %bitcast.29), channel_id=1, source_target_pairs={{0,4},{4,0},{8,12},{12,8},{16,20},{20,16},{24,28},{28,24},{1,5},{5... | collective-permute-start | bytes 196616 | tf_op jit(solution)/shard_map/ppermute | solution.py:34
  12.8 6.0 %collective-permute-start.1 = (bf16[2,128,256]{2,1,0:T(8,128)(2,1)S(1)}, bf16[2,128,256]{2,1,0:T(8,128)(2,1)S(1)}, u32[]{:S(2)}, u32[]{:S(2)}) collective-permute-start(bf16[2,128,256]{2,1,0:T(8,128)(2,1)S(1)} %maximum_select_fusion.2), channel_id=1, source_target_pairs={{0,8},{4,12},{8,0},{12,4},{16,24},{20,28},{24,16},{28,20},{1,9},{5... | collective-permute-start | bytes 393224 | tf_op jit(solution)/shard_map/ppermute | solution.py:34
  18.8 8.0 %collective-permute-start.2 = (bf16[4,128,256]{2,1,0:T(8,128)(2,1)S(1)}, bf16[4,128,256]{2,1,0:T(8,128)(2,1)S(1)}, u32[]{:S(2)}, u32[]{:S(2)}) collective-permute-start(bf16[4,128,256]{2,1,0:T(8,128)(2,1)S(1)} %maximum_select_fusion.1), channel_id=1, source_target_pairs={{0,16},{4,20},{8,24},{12,28},{16,0},{20,4},{24,8},{28,12},{1,17},{... | collective-permute-start | bytes 786440 | tf_op jit(solution)/shard_map/ppermute | solution.py:34
  37.5 1.0 %copy-start = (bf16[4,1040,128]{2,1,0:T(8,128)(2,1)}, bf16[4,1040,128]{2,1,0:T(8,128)(2,1)S(1)}, u32[]{:S(2)}) copy-start(bf16[4,1040,128]{2,1,0:T(8,128)(2,1)S(1)} %all-to-all-done.refs_4_) | copy-start | bytes 3194884
  45.7 4.9 %copy-start.1 = (f32[3,128,256]{2,1,0:T(8,128)S(1)}, f32[3,128,256]{2,1,0:T(8,128)}, u32[]{:S(2)}) copy-start(f32[3,128,256]{2,1,0:T(8,128)} %get-tuple-element.14) | copy-start | bytes 1179652
  45.7 2.2 %collective-permute-start.6 = (f32[4,128,256]{2,1,0:T(8,128)}, f32[4,128,256]{2,1,0:T(8,128)S(1)}, u32[]{:S(2)}, u32[]{:S(2)}) collective-permute-start(f32[4,128,256]{2,1,0:T(8,128)} %get-tuple-element.16), channel_id=1, source_target_pairs={{0,4},{4,0},{8,12},{12,8},{16,20},{20,16},{24,28},{28,24},{1,5},{5... | collective-permute-start | bytes 1572872 | tf_op jit(solution)/shard_map/ppermute | solution.py:19
  49.0 14.6 %copy-start.3 = (f32[1,128,256]{2,1,0:T(8,128)S(1)}, f32[1,128,256]{2,1,0:T(8,128)}, u32[]{:S(2)}) copy-start(f32[1,128,256]{2,1,0:T(8,128)} %get-tuple-element.11) | copy-start | bytes 393220
  49.0 8.4 %collective-permute-start.7 = (f32[2,128,256]{2,1,0:T(8,128)S(1)}, f32[2,128,256]{2,1,0:T(8,128)S(1)}, u32[]{:S(2)}, u32[]{:S(2)}) collective-permute-start(f32[2,128,256]{2,1,0:T(8,128)S(1)} %slice.55), channel_id=1, source_target_pairs={{0,8},{4,12},{8,0},{12,4},{16,24},{20,28},{24,16},{28,20},{1,9},{5... | collective-permute-start | bytes 786440 | tf_op jit(solution)/shard_map/ppermute | solution.py:23
  50.6 8.5 %collective-permute-start.3 = (f32[128,256]{1,0:T(8,128)S(1)}, f32[128,256]{1,0:T(8,128)S(1)}, u32[]{:S(2)}, u32[]{:S(2)}) collective-permute-start(f32[128,256]{1,0:T(8,128)S(1)} %get-tuple-element.17), channel_id=1, source_target_pairs={{0,3},{1,0},{2,1},{3,2},{4,7},{5,4},{6,5},{7,6},{8,11},{9,8},{10,9... | collective-permute-start | bytes 393224 | tf_op jit(solution)/shard_map/ppermute | solution.py:44
  52.1 11.5 %collective-permute-start.4 = (f32[128,256]{1,0:T(8,128)S(1)}, f32[128,256]{1,0:T(8,128)S(1)}, u32[]{:S(2)}, u32[]{:S(2)}) collective-permute-start(f32[128,256]{1,0:T(8,128)S(1)} %get-tuple-element.19), channel_id=1, source_target_pairs={{0,2},{1,3},{2,0},{3,1},{4,6},{5,7},{6,4},{7,5},{8,10},{9,11},{10,... | collective-permute-start | bytes 393224 | tf_op jit(solution)/shard_map/ppermute | solution.py:44
  52.1 11.5 %collective-permute-start.5 = (f32[128,256]{1,0:T(8,128)S(1)}, f32[128,256]{1,0:T(8,128)S(1)}, u32[]{:S(2)}, u32[]{:S(2)}) collective-permute-start(f32[128,256]{1,0:T(8,128)S(1)} %get-tuple-element.18), channel_id=1, source_target_pairs={{0,1},{1,2},{2,3},{3,0},{4,5},{5,6},{6,7},{7,4},{8,9},{9,10},{10,1... | collective-permute-start | bytes 393224 | tf_op jit(solution)/shard_map/ppermute | solution.py:44
  57.5 6.1 %collective-permute-start.8 = (f32[1,128,256]{2,1,0:T(8,128)S(1)}, f32[1,128,256]{2,1,0:T(8,128)S(1)}, u32[]{:S(2)}, u32[]{:S(2)}) collective-permute-start(f32[1,128,256]{2,1,0:T(8,128)S(1)} %slice.57), channel_id=1, source_target_pairs={{0,16},{4,20},{8,24},{12,28},{16,0},{20,4},{24,8},{28,12},{1,17},{... | collective-permute-start | bytes 393224 | tf_op jit(solution)/shard_map/ppermute | solution.py:23
